TPU v7x, 256 devices: a whole 4x4x8 slice. The times are simulated.
256 devices in a mesh: lon: 16 (over z, core), lat: 16 (over x, y).
Axes of the slice: x: 4, y: 4, z: 8, core: 2. Of those that a mesh axis runs over, the one named last changes fastest.
Arguments:
- state: float32 [16, 512, 4096], P(None, 'lat', 'lon'), may hold values from -6 to 6
- coef_lon: float32 [512, 4096], P('lat', 'lon'), may hold values from 0.2 to 0.24
- coef_lat: float32 [512, 4096], P('lat', 'lon'), may hold values from 0.2 to 0.24
- land_sea: int32 [512, 4096], P('lat', 'lon'), may hold values 0 or 1
- send_cols: int32 [16, 65536], P('lat', 'lon'), may hold values from 0 to 8191
- send_count: int32 [16, 256], P('lat', 'lon'), may hold values from 32 to 256, as said below
- obs_value: float32 [16, 16, 65536], P(None, 'lat', 'lon'), may hold values from -6 to 6
- obs_weight: float32 [16, 16, 65536], P(None, 'lat', 'lon'), may hold values from 0.25 to 4
Outputs:
- increment: float32 [16, 512, 4096], P(None, 'lat', 'lon')
Inputs may be any that keep to these rules, and one draw needn't show every extreme that they name: `send_count`: at most 256 live slots go from one device to one peer; in every latitude band some receiving device gets 256 from every device of the band, which one drawn from the seed. `send_cols`: entries index a column of the sending device's own block, row-major over its 32 x 256 cells.
All inputs are finite; a program needn't handle non-finite values. No bound on the sum of `land_sea` on one device may be relied on, other than what follows from the above.
Results may differ from a plain program's by a relative error of at most 0.00002.
Values sent between devices are 32-bit elements; how exact they have to be, the bound alone decides.
No kernel may reach another device: no remote copies, remote signals or barrier semaphores. Data moves between devices by JAX's collectives and lax.ppermute only.
A program may use at most 64 MiB of HBM per device.

v0:
```python
import jax
import jax.numpy as jnp
from jax import lax
from jax.sharding import PartitionSpec as P

PASSES = 8


def with_halo(block, sides, width):
    for axis, dim in sides:
        count = lax.axis_size(axis)
        forward = [(i, i + 1) for i in range(count - 1)]
        forward.append((count - 1, 0))
        backward = [(target, source) for source, target in forward]
        low = lax.ppermute(
            lax.slice_in_dim(block, block.shape[dim] - width, None, axis=dim), axis, forward
        )
        high = lax.ppermute(lax.slice_in_dim(block, 0, width, axis=dim), axis, backward)
        block = jnp.concatenate([low, block, high], axis=dim)
    return block


def one_pass(layer_field, east_face, north_face):
    flux_east = east_face * (layer_field[:, :, 1:] - layer_field[:, :, :-1])
    flux_north = north_face * (layer_field[:, 1:, :] - layer_field[:, :-1, :])
    return (
        layer_field[:, 1:-1, 1:-1]
        + flux_east[:, 1:-1, 1:]
        - flux_east[:, 1:-1, :-1]
        + flux_north[:, 1:, 1:-1]
        - flux_north[:, :-1, 1:-1]
    )


def body(state, coef_lon, coef_lat, land_sea, send_cols, send_count, obs_value, obs_weight):
    levels, rows_here, cols_here = state.shape
    lon_count = lax.axis_size("lon")
    lat_count = lax.axis_size("lat")
    slots = send_cols.shape[1]
    capacity = slots // lon_count
    columns = state.reshape(levels, rows_here * cols_here)
    targets = send_cols[0]
    slot_index = jnp.arange(slots, dtype=jnp.int32)
    limits = jnp.broadcast_to(send_count[0][:, None], (lon_count, capacity)).reshape(slots)
    usable = jnp.where(slot_index % capacity < limits, 1.0, 0.0).astype(jnp.float32)
    at_column = jnp.take(columns, targets, axis=1)
    remote = lax.all_to_all(at_column, "lon", split_axis=1, concat_axis=1, tiled=True)
    local_terms = obs_weight[:, 0, :] * (obs_value[:, 0, :] - remote)
    weighted = lax.all_to_all(local_terms, "lon", split_axis=1, concat_axis=1, tiled=True) * usable
    sea = land_sea.astype(jnp.float32)
    gradient = jnp.zeros((levels, rows_here * cols_here), jnp.float32).at[:, targets].add(weighted)
    gradient = gradient.reshape(levels, rows_here, cols_here) * sea[None]
    rim_width = PASSES
    stacked = jnp.stack([sea, coef_lon, coef_lat])
    padded = with_halo(stacked, (("lon", 2), ("lat", 1)), rim_width)
    lat_index = lax.axis_index("lat")
    row_place = jnp.arange(rows_here + 2 * rim_width, dtype=jnp.int32)
    outside = (row_place < rim_width) & (lat_index == 0) | (row_place >= rows_here + rim_width) & (
        lat_index == lat_count - 1
    )
    inside = jnp.where(outside, 0.0, 1.0).astype(jnp.float32)[:, None]
    sea_rim = padded[0] * inside
    east_face = padded[1][:, :-1] * sea_rim[:, :-1] * sea_rim[:, 1:]
    north_face = padded[2][:-1, :] * sea_rim[:-1, :] * sea_rim[1:, :]
    field = with_halo(gradient, (("lon", 2), ("lat", 1)), rim_width)
    for step_number in range(PASSES):
        high, wide = field.shape[1], field.shape[2]
        field = one_pass(
            field,
            east_face[step_number : step_number + high, step_number : step_number + wide - 1],
            north_face[step_number : step_number + high - 1, step_number : step_number + wide],
        )
    gradient = field
    return gradient


def solution(mesh):
    placed = (
        P(None, "lat", "lon"),
        P("lat", "lon"),
        P("lat", "lon"),
        P("lat", "lon"),
        P("lat", "lon"),
        P("lat", "lon"),
        P(None, "lat", "lon"),
        P(None, "lat", "lon"),
    )
    return jax.shard_map(
        body, mesh=mesh, in_specs=placed, out_specs=P(None, "lat", "lon"), check_vma=False
    )
```

profile of v0, /device:TPU:1, one launch (start us, length us, event | category | flops | bytes accessed | tf_op | source)
XLA Modules:
  0.0 120.7 jit_solution(9083581683232877468)
XLA Ops:
  0.0 0.8 convert_bitcast_fusion
  0.8 0.8 pad_maximum_fusion.5
  1.6 3.0 %collective-permute-start.4 = (f32[3,32,8]{2,1,0:T(8,128)S(1)}, f32[3,32,8]{2,1,0:T(8,128)S(1)}, u32[]{:S(2)}, u32[]{:S(2)}) collective-permute-start(f32[3,32,8]{2,1,0:T(8,128)S(1)} %get-tuple-element.11), channel_id=1, source_target_pairs={{0,16},{16,32},{32,48},{48,64},{64,80},{80,96},{96,112},{112,128},... | collective-permute-start | bytes 9224 | tf_op jit(solution)/shard_map/ppermute | solution.py:15
  4.7 0.2 collective-permute-start.5
  4.9 0.7 compare_select_fusion
  5.6 3.5 %copy.20 = f32[16,32,256]{0,2,1:T(8,128)} copy(f32[16,32,256]{2,1,0:T(8,128)} %param.8) | data formatting | bytes 1048576 | tf_op args[0]
  9.2 13.0 %gather_fusion = f32[4096,16]{1,0:T(8,128)S(1)} fusion(f32[16,8192]{0,1:T(8,128)} %bitcast.40, s32[4096]{0:T(1024)S(1)} %broadcast_clamp_fusion), kind=kCustom, calls=%fused_computation | custom fusion | bytes 540672 | tf_op jit(solution)/shard_map/jit(_take)/gather | solution.py:46
  22.2 0.6 copy.21
  22.7 0.5 broadcast.110
  23.2 0.7 reduce.5
  24.0 0.7 broadcast_select_fusion
  24.7 9.7 %all-to-all-start = ((f32[16,16,256]{2,0,1:T(8,128)}), f32[16,16,256]{2,0,1:T(8,128)S(1)}, u32[]{:S(2)}, u32[]{:S(2)}) async-start(f32[16,16,256]{2,0,1:T(8,128)} %broadcast_select_fusion), calls=%async_computation | async-start | bytes 524288 | tf_op jit(solution)/shard_map/all_to_all | solution.py:47
  34.6 0.6 reduce
  35.3 0.6 reduce.1
  36.1 0.1 pad_maximum_fusion.10
  36.2 1.4 %collective-permute-start.6 = (f32[3,8,272]{2,1,0:T(8,128)S(1)}, f32[3,8,272]{2,1,0:T(8,128)S(1)}, u32[]{:S(2)}, u32[]{:S(2)}) collective-permute-start(f32[3,8,272]{2,1,0:T(8,128)S(1)} %get-tuple-element.9), channel_id=1, source_target_pairs={{0,1},{1,2},{2,3},{3,4},{4,5},{5,6},{6,7},{7,8},{8,9},{9,10},{10,1... | collective-permute-start | bytes 78344 | tf_op jit(solution)/shard_map/ppermute | solution.py:15
  37.6 3.7 %collective-permute-start.7 = (f32[3,8,272]{2,1,0:T(8,128)S(1)}, f32[3,8,272]{2,1,0:T(8,128)S(1)}, u32[]{:S(2)}, u32[]{:S(2)}) collective-permute-start(f32[3,8,272]{2,1,0:T(8,128)S(1)} %get-tuple-element.10), channel_id=1, source_target_pairs={{1,0},{2,1},{3,2},{4,3},{5,4},{6,5},{7,6},{8,7},{9,8},{10,9},{11,1... | collective-permute-start | bytes 78344 | tf_op jit(solution)/shard_map/ppermute | solution.py:18
  41.3 4.9 %all-to-all-done = f32[16,16,256]{2,0,1:T(8,128)S(1)} async-done(((f32[16,16,256]{2,0,1:T(8,128)}), f32[16,16,256]{2,0,1:T(8,128)S(1)}, u32[]{:S(2)}, u32[]{:S(2)}) %all-to-all-start) | async-done | bytes 262176 | tf_op jit(solution)/shard_map/all_to_all | solution.py:47
  46.1 0.2 fusion.18
  46.3 0.9 copy.23
  47.2 3.4 %all-to-all-start.1 = ((f32[16,16,256]{2,0,1:T(8,128)}), f32[16,16,256]{2,0,1:T(8,128)S(1)}, u32[]{:S(2)}, u32[]{:S(2)}) async-start(f32[16,16,256]{2,0,1:T(8,128)} %copy.23), calls=%async_computation.1 | async-start | bytes 524288 | tf_op jit(solution)/shard_map/all_to_all | solution.py:49
  50.6 0.1 pad_maximum_fusion.1
  50.8 10.9 %all-to-all-done.1 = f32[16,16,256]{2,0,1:T(8,128)S(1)} async-done(((f32[16,16,256]{2,0,1:T(8,128)}), f32[16,16,256]{2,0,1:T(8,128)S(1)}, u32[]{:S(2)}, u32[]{:S(2)}) %all-to-all-start.1) | async-done | bytes 262176 | tf_op jit(solution)/shard_map/all_to_all | solution.py:49
  61.8 0.6 copy.25
  62.4 24.5 %scatter_custom_fusion = f32[16,8192]{0,1:T(8,128)} fusion(s32[4096]{0:T(1024)S(1)} %bitcast.53, f32[4096,16]{1,0:T(8,128)S(1)} %copy.25, f32[]{:T(128)} %constant.19.clone.1), kind=kCustom, calls=%fused_computation.2 | custom fusion | flops 65536 | bytes 524292 | tf_op jit(solution)/shard_map/scatter-add | solution.py:51
  86.9 2.9 %copy.26 = f32[16,32,256]{2,1,0:T(8,128)S(1)} copy(f32[16,32,256]{0,2,1:T(8,128)} %bitcast.39) | data formatting | bytes 1048576 | tf_op jit(solution)/shard_map/reshape | solution.py:52
  89.8 0.1 fusion.25
  90.0 0.5 collective-permute-start.1
  90.6 0.1 slice.438
  90.7 0.1 slice.449
  90.8 2.5 %collective-permute-done = f32[16,32,8]{2,1,0:T(8,128)S(1)} collective-permute-done((f32[16,32,8]{2,1,0:T(8,128)S(1)}, f32[16,32,8]{2,1,0:T(8,128)S(1)}, u32[]{:S(2)}, u32[]{:S(2)}) %collective-permute-start) | collective-permute-done | bytes 16416 | tf_op jit(solution)/shard_map/ppermute | solution.py:15
  93.3 2.8 %collective-permute-done.1 = f32[16,32,8]{2,1,0:T(8,128)S(1)} collective-permute-done((f32[16,32,8]{2,1,0:T(8,128)S(1)}, f32[16,32,8]{2,1,0:T(8,128)S(1)}, u32[]{:S(2)}, u32[]{:S(2)}) %collective-permute-start.1) | collective-permute-done | bytes 16416 | tf_op jit(solution)/shard_map/ppermute | solution.py:18
  96.1 0.2 pad_maximum_fusion.4
  96.3 1.4 %collective-permute-start.2 = (f32[16,8,272]{2,1,0:T(8,128)S(1)}, f32[16,8,272]{2,1,0:T(8,128)S(1)}, u32[]{:S(2)}, u32[]{:S(2)}) collective-permute-start(f32[16,8,272]{2,1,0:T(8,128)S(1)} %get-tuple-element.5), channel_id=1, source_target_pairs={{0,1},{1,2},{2,3},{3,4},{4,5},{5,6},{6,7},{7,8},{8,9},{9,10},{10,1... | collective-permute-start | bytes 417800 | tf_op jit(solution)/shard_map/ppermute | solution.py:15
  97.7 3.9 %collective-permute-start.3 = (f32[16,8,272]{2,1,0:T(8,128)S(1)}, f32[16,8,272]{2,1,0:T(8,128)S(1)}, u32[]{:S(2)}, u32[]{:S(2)}) collective-permute-start(f32[16,8,272]{2,1,0:T(8,128)S(1)} %get-tuple-element.6), channel_id=1, source_target_pairs={{1,0},{2,1},{3,2},{4,3},{5,4},{6,5},{7,6},{8,7},{9,8},{10,9},{11,1... | collective-permute-start | bytes 417800 | tf_op jit(solution)/shard_map/ppermute | solution.py:18
  101.6 0.1 slice.443
  101.7 0.1 slice.454
  101.8 0.1 slice.460
  102.7 3.0 %collective-permute-done.2 = f32[16,8,272]{2,1,0:T(8,128)S(1)} collective-permute-done((f32[16,8,272]{2,1,0:T(8,128)S(1)}, f32[16,8,272]{2,1,0:T(8,128)S(1)}, u32[]{:S(2)}, u32[]{:S(2)}) %collective-permute-start.2) | collective-permute-done | bytes 139296 | tf_op jit(solution)/shard_map/ppermute | solution.py:15
  105.7 0.3 pad_maximum_fusion
  106.0 0.4 fusion.9
  106.4 0.2 fusion.8
  106.6 1.4 %slice_subtract_fusion.10 = f32[16,46,270]{2,1,0:T(8,128)S(1)} fusion(f32[16,47,272]{2,1,0:T(8,128)S(1)} %fusion.8, f32[16,48,271]{2,1,0:T(8,128)S(1)} %fusion.9, f32[16,48,272]{2,1,0:T(8,128)S(1)} %pad_maximum_fusion), kind=kLoop, calls=%fused_computation.24 | loop fusion | flops 794880 | bytes 4769280 | tf_op jit(solution)/shard_map/sub | solution.py:27
  108.0 0.4 fusion.7
  108.4 0.2 fusion.6
  108.6 1.4 %slice_subtract_fusion.6 = f32[16,44,268]{2,1,0:T(8,128)S(1)} fusion(f32[16,45,270]{2,1,0:T(8,128)S(1)} %fusion.6, f32[16,46,269]{2,1,0:T(8,128)S(1)} %fusion.7, f32[16,46,270]{2,1,0:T(8,128)S(1)} %slice_subtract_fusion.10), kind=kLoop, calls=%fused_computation.16 | loop fusion | flops 754688 | bytes 4528128 | tf_op jit(solution)/shard_map/sub | solution.py:27
  110.0 0.4 fusion.5
  110.4 0.2 fusion.4
  110.6 1.4 %slice_subtract_fusion.2 = f32[16,42,266]{2,1,0:T(8,128)S(1)} fusion(f32[16,43,268]{2,1,0:T(8,128)S(1)} %fusion.4, f32[16,44,267]{2,1,0:T(8,128)S(1)} %fusion.5, f32[16,44,268]{2,1,0:T(8,128)S(1)} %slice_subtract_fusion.6), kind=kLoop, calls=%fused_computation.8 | loop fusion | flops 715008 | bytes 4290048 | tf_op jit(solution)/shard_map/sub | solution.py:27
  112.0 0.4 fusion.3
  112.4 0.2 fusion.2
  112.5 1.2 %slice_subtract_fusion.28 = f32[16,40,264]{2,1,0:T(8,128)S(1)} fusion(f32[16,41,266]{2,1,0:T(8,128)S(1)} %fusion.2, f32[16,42,265]{2,1,0:T(8,128)S(1)} %fusion.3, f32[16,42,266]{2,1,0:T(8,128)S(1)} %slice_subtract_fusion.2), kind=kLoop, calls=%fused_computation.61 | loop fusion | flops 675840 | bytes 4055040 | tf_op jit(solution)/shard_map/sub | solution.py:27
  113.8 0.3 fusion.17
  114.1 0.1 fusion.16
  114.2 1.2 %slice_subtract_fusion.24 = f32[16,38,262]{2,1,0:T(8,128)S(1)} fusion(f32[16,39,264]{2,1,0:T(8,128)S(1)} %fusion.16, f32[16,40,263]{2,1,0:T(8,128)S(1)} %fusion.17, f32[16,40,264]{2,1,0:T(8,128)S(1)} %slice_subtract_fusion.28), kind=kLoop, calls=%fused_computation.53 | loop fusion | flops 637184 | bytes 3823104 | tf_op jit(solution)/shard_map/sub | solution.py:27
  115.4 0.3 fusion.15
  115.8 0.1 fusion.14
  115.9 1.2 %slice_subtract_fusion.20 = f32[16,36,260]{2,1,0:T(8,128)S(1)} fusion(f32[16,37,262]{2,1,0:T(8,128)S(1)} %fusion.14, f32[16,38,261]{2,1,0:T(8,128)S(1)} %fusion.15, f32[16,38,262]{2,1,0:T(8,128)S(1)} %slice_subtract_fusion.24), kind=kLoop, calls=%fused_computation.45 | loop fusion | flops 599040 | bytes 3594240 | tf_op jit(solution)/shard_map/sub | solution.py:27
  117.1 0.3 fusion.13
  117.4 0.1 fusion.12
  117.6 1.2 %slice_subtract_fusion.16 = f32[16,34,258]{2,1,0:T(8,128)S(1)} fusion(f32[16,35,260]{2,1,0:T(8,128)S(1)} %fusion.12, f32[16,36,259]{2,1,0:T(8,128)S(1)} %fusion.13, f32[16,36,260]{2,1,0:T(8,128)S(1)} %slice_subtract_fusion.20), kind=kLoop, calls=%fused_computation.37 | loop fusion | flops 561408 | bytes 3368448 | tf_op jit(solution)/shard_map/sub | solution.py:27
  118.8 0.3 fusion.11
  119.1 0.1 fusion.10
  119.3 1.5 %slice_subtract_fusion.30 = f32[16,32,256]{2,1,0:T(8,128)} fusion(f32[16,33,258]{2,1,0:T(8,128)S(1)} %fusion.10, f32[16,34,257]{2,1,0:T(8,128)S(1)} %fusion.11, f32[16,34,258]{2,1,0:T(8,128)S(1)} %slice_subtract_fusion.16), kind=kLoop, calls=%fused_computation.65 | loop fusion | flops 524288 | bytes 3145728 | tf_op jit(solution)/shard_map/sub | solution.py:27
  (44 shorter events, 1.4 us)
Async XLA Ops:
  0.0 34.4 %copy-start = (s32[1,16]{1,0:T(1,128)S(1)}, s32[1,16]{1,0:T(1,128)}, u32[]{:S(2)}) copy-start(s32[1,16]{1,0:T(1,128)} %param.13) | copy-start | bytes 196
  1.6 34.4 %collective-permute-start.4 = (f32[3,32,8]{2,1,0:T(8,128)S(1)}, f32[3,32,8]{2,1,0:T(8,128)S(1)}, u32[]{:S(2)}, u32[]{:S(2)}) collective-permute-start(f32[3,32,8]{2,1,0:T(8,128)S(1)} %get-tuple-element.11), channel_id=1, source_target_pairs={{0,16},{16,32},{32,48},{48,64},{64,80},{80,96},{96,112},{112,128},... | collective-permute-start | bytes 9224 | tf_op jit(solution)/shard_map/ppermute | solution.py:15
  4.7 31.4 %collective-permute-start.5 = (f32[3,32,8]{2,1,0:T(8,128)S(1)}, f32[3,32,8]{2,1,0:T(8,128)S(1)}, u32[]{:S(2)}, u32[]{:S(2)}) collective-permute-start(f32[3,32,8]{2,1,0:T(8,128)S(1)} %get-tuple-element.12), channel_id=1, source_target_pairs={{16,0},{32,16},{48,32},{64,48},{80,64},{96,80},{112,96},{128,112},... | collective-permute-start | bytes 9224 | tf_op jit(solution)/shard_map/ppermute | solution.py:18
  22.1 1.1 copy-start.5
  22.7 11.8 %copy-start.3 = (f32[16,1,4096]{2,1,0:T(1,128)S(1)}, f32[16,1,4096]{2,1,0:T(1,128)}, u32[]{:S(2)}) copy-start(f32[16,1,4096]{2,1,0:T(1,128)} %param.15) | copy-start | bytes 786436
  22.7 12.6 %copy-start.4 = (f32[16,1,4096]{2,1,0:T(1,128)S(1)}, f32[16,1,4096]{2,1,0:T(1,128)}, u32[]{:S(2)}) copy-start(f32[16,1,4096]{2,1,0:T(1,128)} %param.14) | copy-start | bytes 786436
  24.7 21.4 %all-to-all-start = ((f32[16,16,256]{2,0,1:T(8,128)}), f32[16,16,256]{2,0,1:T(8,128)S(1)}, u32[]{:S(2)}, u32[]{:S(2)}) async-start(f32[16,16,256]{2,0,1:T(8,128)} %broadcast_select_fusion), calls=%async_computation | async-start | bytes 524288 | tf_op jit(solution)/shard_map/all_to_all | solution.py:47
  34.4 1.6 %copy-start.1 = (f32[32,256]{1,0:T(8,128)S(1)}, f32[32,256]{1,0:T(8,128)}, u32[]{:S(2)}) copy-start(f32[32,256]{1,0:T(8,128)} %param.10) | copy-start | bytes 98308
  34.4 1.6 %copy-start.2 = (f32[32,256]{1,0:T(8,128)S(1)}, f32[32,256]{1,0:T(8,128)}, u32[]{:S(2)}) copy-start(f32[32,256]{1,0:T(8,128)} %param.9) | copy-start | bytes 98308
  36.2 14.4 %collective-permute-start.6 = (f32[3,8,272]{2,1,0:T(8,128)S(1)}, f32[3,8,272]{2,1,0:T(8,128)S(1)}, u32[]{:S(2)}, u32[]{:S(2)}) collective-permute-start(f32[3,8,272]{2,1,0:T(8,128)S(1)} %get-tuple-element.9), channel_id=1, source_target_pairs={{0,1},{1,2},{2,3},{3,4},{4,5},{5,6},{6,7},{7,8},{8,9},{9,10},{10,1... | collective-permute-start | bytes 78344 | tf_op jit(solution)/shard_map/ppermute | solution.py:15
  37.6 13.1 %collective-permute-start.7 = (f32[3,8,272]{2,1,0:T(8,128)S(1)}, f32[3,8,272]{2,1,0:T(8,128)S(1)}, u32[]{:S(2)}, u32[]{:S(2)}) collective-permute-start(f32[3,8,272]{2,1,0:T(8,128)S(1)} %get-tuple-element.10), channel_id=1, source_target_pairs={{1,0},{2,1},{3,2},{4,3},{5,4},{6,5},{7,6},{8,7},{9,8},{10,9},{11,1... | collective-permute-start | bytes 78344 | tf_op jit(solution)/shard_map/ppermute | solution.py:18
  47.2 14.6 %all-to-all-start.1 = ((f32[16,16,256]{2,0,1:T(8,128)}), f32[16,16,256]{2,0,1:T(8,128)S(1)}, u32[]{:S(2)}, u32[]{:S(2)}) async-start(f32[16,16,256]{2,0,1:T(8,128)} %copy.23), calls=%async_computation.1 | async-start | bytes 524288 | tf_op jit(solution)/shard_map/all_to_all | solution.py:49
  90.0 3.3 %collective-permute-start = (f32[16,32,8]{2,1,0:T(8,128)S(1)}, f32[16,32,8]{2,1,0:T(8,128)S(1)}, u32[]{:S(2)}, u32[]{:S(2)}) collective-permute-start(f32[16,32,8]{2,1,0:T(8,128)S(1)} %get-tuple-element.7), channel_id=1, source_target_pairs={{0,16},{16,32},{32,48},{48,64},{64,80},{80,96},{96,112},{112,128},... | collective-permute-start | bytes 49160 | tf_op jit(solution)/shard_map/ppermute | solution.py:15
  90.0 6.1 %collective-permute-start.1 = (f32[16,32,8]{2,1,0:T(8,128)S(1)}, f32[16,32,8]{2,1,0:T(8,128)S(1)}, u32[]{:S(2)}, u32[]{:S(2)}) collective-permute-start(f32[16,32,8]{2,1,0:T(8,128)S(1)} %get-tuple-element.8), channel_id=1, source_target_pairs={{16,0},{32,16},{48,32},{64,48},{80,64},{96,80},{112,96},{128,112},... | collective-permute-start | bytes 49160 | tf_op jit(solution)/shard_map/ppermute | solution.py:18
  96.3 9.4 %collective-permute-start.2 = (f32[16,8,272]{2,1,0:T(8,128)S(1)}, f32[16,8,272]{2,1,0:T(8,128)S(1)}, u32[]{:S(2)}, u32[]{:S(2)}) collective-permute-start(f32[16,8,272]{2,1,0:T(8,128)S(1)} %get-tuple-element.5), channel_id=1, source_target_pairs={{0,1},{1,2},{2,3},{3,4},{4,5},{5,6},{6,7},{7,8},{8,9},{9,10},{10,1... | collective-permute-start | bytes 417800 | tf_op jit(solution)/shard_map/ppermute | solution.py:15
  97.7 8.0 %collective-permute-start.3 = (f32[16,8,272]{2,1,0:T(8,128)S(1)}, f32[16,8,272]{2,1,0:T(8,128)S(1)}, u32[]{:S(2)}, u32[]{:S(2)}) collective-permute-start(f32[16,8,272]{2,1,0:T(8,128)S(1)} %get-tuple-element.6), channel_id=1, source_target_pairs={{1,0},{2,1},{3,2},{4,3},{5,4},{6,5},{7,6},{8,7},{9,8},{10,9},{11,1... | collective-permute-start | bytes 417800 | tf_op jit(solution)/shard_map/ppermute | solution.py:18
where the time goes:
time: 121 us
  other arithmetic  45.3 us (37%)
  starting transfers between devices  27.3 us (23%)
  waiting for transfers between devices  24.1 us (20%)
  local copies, waits for them, and re-layouts  23.6 us (20%)
    scatter-add x1, other arithmetic, body(): jnp.zeros((levels, rows_here * cols_here), jnp.float32).at[:, targets]  24.5 us
    gather x2, local copies, waits for them, and re-layouts, body(): at_column = jnp.take(columns, targets, axis=1)  13.5 us
    all_to_all x1, waiting for transfers between devices, body(): lax.all_to_all(local_terms, 'lon', split_axis=1, concat_axis=1, tiled=True)  10.9 us
    sub x8, other arithmetic, one_pass(): layer_field[:, 1:-1, 1:-1] + flux_east[:, 1:-1, 1:]  10.6 us
    all_to_all x1, starting transfers between devices, body(): lax.all_to_all(at_column, 'lon', split_axis=1, concat_axis=1, tiled=True)  9.7 us
    ppermute x4, starting transfers between devices, with_halo(): lax.ppermute(lax.slice_in_dim(block, 0, width, axis=dim), axis, backward)  8.31 us
    ppermute x4, starting transfers between devices, with_halo(): lax.ppermute(lax.slice_in_dim(block, block.shape[dim] - width, None, axis...  5.82 us
    ppermute x4, waiting for transfers between devices, with_halo(): lax.ppermute(lax.slice_in_dim(block, block.shape[dim] - width, None, axis...  5.55 us
  transfers between devices with their start and end apart: 10, of which 5 were waited for; matrix products, arithmetic and copies ran while one was open for 20% of the time, Pallas kernels for 0%

commit v1 on v0

--- a/solution.py
+++ b/solution.py
@@ -43,10 +43,10 @@
     slot_index = jnp.arange(slots, dtype=jnp.int32)
     limits = jnp.broadcast_to(send_count[0][:, None], (lon_count, capacity)).reshape(slots)
     usable = jnp.where(slot_index % capacity < limits, 1.0, 0.0).astype(jnp.float32)
+    held = jnp.stack([obs_value[:, 0, :], obs_weight[:, 0, :]])
+    at_owner = lax.all_to_all(held, "lon", split_axis=2, concat_axis=2, tiled=True)
     at_column = jnp.take(columns, targets, axis=1)
-    remote = lax.all_to_all(at_column, "lon", split_axis=1, concat_axis=1, tiled=True)
-    local_terms = obs_weight[:, 0, :] * (obs_value[:, 0, :] - remote)
-    weighted = lax.all_to_all(local_terms, "lon", split_axis=1, concat_axis=1, tiled=True) * usable
+    weighted = at_owner[1] * (at_owner[0] - at_column) * usable
     sea = land_sea.astype(jnp.float32)
     gradient = jnp.zeros((levels, rows_here * cols_here), jnp.float32).at[:, targets].add(weighted)
     gradient = gradient.reshape(levels, rows_here, cols_here) * sea[None]

time: 121 us -> 153 us (1.26)
  other arithmetic: 45.3 us -> 68.8 us
  local copies, waits for them, and re-layouts: 23.6 us -> 35.8 us
  starting transfers between devices: 27.3 us -> 21 us
  waiting for transfers between devices: 24.1 us -> 25.9 us
    scatter-add x1, other arithmetic: 24.5 us -> 51.2 us  [body(): jnp.zeros((levels, rows_here * cols_here), jnp.float32).at[:, targets]]
    all_to_all x2 -> x1, waiting for transfers between devices: 15.8 us -> 0.01 us  [body(): lax.all_to_all(held, 'lon', split_axis=2, concat_axis=2, tiled=True)]
    unnamed x18, local copies, waits for them, and re-layouts: 4.34 us -> 19 us
    ppermute x4, waiting for transfers between devices: 2.8 us -> 17.5 us  [with_halo(): lax.ppermute(lax.slice_in_dim(block, 0, width, axis=dim), axis, backward)]
    gather x2 -> x0, local copies, waits for them, and re-layouts: 13.5 us -> none  [body(): at_column = jnp.take(columns, targets, axis=1)]
    slice x0 -> x1, local copies, waits for them, and re-layouts: none -> 7.62 us  [body(): weighted = at_owner[1] * (at_owner[0] - at_column) * usable]
    another operation x0 -> x1, local copies, waits for them, and re-layouts: none -> 4.36 us  [body(): held = jnp.stack([obs_value[:, 0, :], obs_weight[:, 0, :]])]
    ppermute x4, starting transfers between devices: 5.82 us -> 1.65 us  [with_halo(): lax.ppermute(lax.slice_in_dim(block, block.shape[dim] - width, None, axis...]
  transfers between devices with their start and end apart: 10 -> 9, of which waited for: 5 -> 5; matrix products, arithmetic and copies ran while one was open for 20% -> 3% of each run, Pallas kernels for 0% -> 0%
where the time goes in v1:
time: 153 us; the launch traced here: 152 us
  other arithmetic  68.8 us (45%)
  local copies, waits for them, and re-layouts  35.8 us (23%)
  waiting for transfers between devices  25.9 us (17%)
  starting transfers between devices  21 us (14%)
    scatter-add x1, other arithmetic, body(): jnp.zeros((levels, rows_here * cols_here), jnp.float32).at[:, targets]  51.2 us
    unnamed x18, local copies, waits for them, and re-layouts  19 us
    ppermute x4, waiting for transfers between devices, with_halo(): lax.ppermute(lax.slice_in_dim(block, 0, width, axis=dim), axis, backward)  17.5 us
    sub x8, other arithmetic, one_pass(): layer_field[:, 1:-1, 1:-1] + flux_east[:, 1:-1, 1:]  10.6 us
    all_to_all x1, starting transfers between devices, body(): lax.all_to_all(held, 'lon', split_axis=2, concat_axis=2, tiled=True)  10.1 us
    ppermute x4, starting transfers between devices, with_halo(): lax.ppermute(lax.slice_in_dim(block, 0, width, axis=dim), axis, backward)  9.27 us
    ppermute x4, waiting for transfers between devices, with_halo(): lax.ppermute(lax.slice_in_dim(block, block.shape[dim] - width, None, axis...  8.46 us
    slice x1, local copies, waits for them, and re-layouts, body(): weighted = at_owner[1] * (at_owner[0] - at_column) * usable  7.62 us
  transfers between devices with their start and end apart: 9, of which 5 were waited for; matrix products, arithmetic and copies ran while one was open for 3% of the time, Pallas kernels for 0%

profile of v1, /device:TPU:1, one launch (start us, length us, event | category | flops | bytes accessed | tf_op | source)
XLA Modules:
  0.0 151.9 jit_solution(4161188813281966988)
XLA Ops:
  0.0 1.3 copy_bitcast_fusion
  1.4 4.4 %copy.17 = f32[2,16,4096]{1,0,2:T(2,128)} copy(f32[2,16,4096]{2,1,0:T(8,128)S(1)} %pad_maximum_fusion.1) | data formatting | bytes 1048576 | tf_op jit(solution)/shard_map/stack | solution.py:46
  5.8 8.0 %reshape.116 = f32[16,1,8192]{2,1,0:T(1,128)} reshape(f32[4096,2,16]{2,1,0:T(2,128)} %bitcast.49) | data formatting | bytes 1048576
  13.7 10.1 %all-to-all-start = ((f32[16,1,8192]{2,1,0:T(1,128)}), f32[16,1,8192]{2,1,0:T(1,128)S(1)}, u32[]{:S(2)}, u32[]{:S(2)}) async-start(f32[16,1,8192]{2,1,0:T(1,128)} %reshape.116), calls=%async_computation | async-start | bytes 1048576 | tf_op jit(solution)/shard_map/all_to_all | solution.py:47
  24.0 0.1 collective-permute-start.5
  24.1 1.6 %collective-permute-start.4 = (f32[3,32,8]{2,1,0:T(8,128)S(1)}, f32[3,32,8]{2,1,0:T(8,128)S(1)}, u32[]{:S(2)}, u32[]{:S(2)}) collective-permute-start(f32[3,32,8]{2,1,0:T(8,128)S(1)} %get-tuple-element.13), channel_id=1, source_target_pairs={{0,16},{16,32},{32,48},{48,64},{64,80},{80,96},{96,112},{112,128},... | collective-permute-start | bytes 9224 | tf_op jit(solution)/shard_map/ppermute | solution.py:15
  25.9 12.6 %collective-permute-done.5 = f32[3,32,8]{2,1,0:T(8,128)S(1)} collective-permute-done((f32[3,32,8]{2,1,0:T(8,128)S(1)}, f32[3,32,8]{2,1,0:T(8,128)S(1)}, u32[]{:S(2)}, u32[]{:S(2)}) %collective-permute-start.5) | collective-permute-done | bytes 3104 | tf_op jit(solution)/shard_map/ppermute | solution.py:18
  38.5 0.1 pad_maximum_fusion.11
  38.6 5.0 %collective-permute-start.7 = (f32[3,8,272]{2,1,0:T(8,128)S(1)}, f32[3,8,272]{2,1,0:T(8,128)S(1)}, u32[]{:S(2)}, u32[]{:S(2)}) collective-permute-start(f32[3,8,272]{2,1,0:T(8,128)S(1)} %get-tuple-element.12), channel_id=1, source_target_pairs={{1,0},{2,1},{3,2},{4,3},{5,4},{6,5},{7,6},{8,7},{9,8},{10,9},{11,1... | collective-permute-start | bytes 78344 | tf_op jit(solution)/shard_map/ppermute | solution.py:18
  43.6 2.6 %copy.20 = f32[16,32,256]{0,2,1:T(8,128)} copy(f32[16,32,256]{2,1,0:T(8,128)S(1)} %copy-done.1) | data formatting | bytes 1048576 | tf_op args[0]
  46.3 3.5 %collective-permute-done.6 = f32[3,8,272]{2,1,0:T(8,128)S(1)} collective-permute-done((f32[3,8,272]{2,1,0:T(8,128)S(1)}, f32[3,8,272]{2,1,0:T(8,128)S(1)}, u32[]{:S(2)}, u32[]{:S(2)}) %collective-permute-start.6) | collective-permute-done | bytes 26144 | tf_op jit(solution)/shard_map/ppermute | solution.py:15
  49.7 0.1 pad_maximum_fusion.2
  50.0 0.5 broadcast.109
  50.5 1.9 %reduce = f32[16,8192]{1,0:T(8,128)S(1)} reduce(f32[16,1,8192]{2,1,0:T(1,128)S(1)} %all-to-all-done, f32[]{:T(128)} %broadcast.109), dimensions={1}, to_apply=%all_to_all.3.reduce_sub_computation | reduce | bytes 1048580 | tf_op jit(solution)/shard_map/all_to_all | solution.py:47
  52.4 7.0 %reshape.117 = f32[4096,2,16]{2,1,0:T(2,128)} reshape(f32[16,8192]{1,0:T(8,128)S(1)} %reduce) | data formatting | bytes 1048576
  59.4 7.6 %fusion.33 = (f32[1,16,4096]{1,0,2:T(1,128)S(1)}, f32[1,16,4096]{1,0,2:T(1,128)}) fusion(f32[2,16,4096]{1,0,2:T(2,128)} %bitcast.52), kind=kLoop, calls=%fused_computation.114 | loop fusion | bytes 1048576 | tf_op jit(solution)/shard_map/slice | solution.py:49
  67.0 51.2 %scatter_custom_fusion = f32[16,8192]{0,1:T(8,128)} fusion(s32[4096]{0:T(1024)S(1)} %bitcast.63, f32[16,4096]{0,1:T(8,128)} %bitcast.54, f32[16,4096]{0,1:T(8,128)S(1)} %bitcast.53, f32[]{:T(128)} %constant.19.clone.1, f32[]{:T(128)} %constant.23.clone.1, f32[4096]{0:T(1024)S(1)} %fusion.31, pred[4096]{0:T(1024)(128)(4,1)S(1)} %compare_and_fusion, ...), kind=kCustom, calls=%fused_computation.2 | custom fusion | flops 327680 | bytes 3444744 | tf_op jit(solution)/shard_map/scatter-add | solution.py:51
  118.2 2.9 %copy.21 = f32[16,32,256]{2,1,0:T(8,128)S(1)} copy(f32[16,32,256]{0,2,1:T(8,128)} %bitcast.51) | data formatting | bytes 1048576 | tf_op jit(solution)/shard_map/reshape | solution.py:52
  121.1 0.1 fusion.34
  121.3 2.4 %collective-permute-start.1 = (f32[16,32,8]{2,1,0:T(8,128)S(1)}, f32[16,32,8]{2,1,0:T(8,128)S(1)}, u32[]{:S(2)}, u32[]{:S(2)}) collective-permute-start(f32[16,32,8]{2,1,0:T(8,128)S(1)} %get-tuple-element.10), channel_id=1, source_target_pairs={{16,0},{32,16},{48,32},{64,48},{80,64},{96,80},{112,96},{128,112},... | collective-permute-start | bytes 49160 | tf_op jit(solution)/shard_map/ppermute | solution.py:18
  123.7 0.1 slice.453
  123.8 0.1 slice.464
  123.8 3.2 %collective-permute-done.1 = f32[16,32,8]{2,1,0:T(8,128)S(1)} collective-permute-done((f32[16,32,8]{2,1,0:T(8,128)S(1)}, f32[16,32,8]{2,1,0:T(8,128)S(1)}, u32[]{:S(2)}, u32[]{:S(2)}) %collective-permute-start.1) | collective-permute-done | bytes 16416 | tf_op jit(solution)/shard_map/ppermute | solution.py:18
  127.1 0.2 pad_maximum_fusion.5
  127.3 1.8 %collective-permute-start.3 = (f32[16,8,272]{2,1,0:T(8,128)S(1)}, f32[16,8,272]{2,1,0:T(8,128)S(1)}, u32[]{:S(2)}, u32[]{:S(2)}) collective-permute-start(f32[16,8,272]{2,1,0:T(8,128)S(1)} %get-tuple-element.8), channel_id=1, source_target_pairs={{1,0},{2,1},{3,2},{4,3},{5,4},{6,5},{7,6},{8,7},{9,8},{10,9},{11,1... | collective-permute-start | bytes 417800 | tf_op jit(solution)/shard_map/ppermute | solution.py:18
  129.0 0.1 slice_multiply_fusion.2
  129.1 0.1 slice.448
  129.2 0.1 slice.459
  129.3 0.1 slice.475
  129.4 0.1 slice.470
  129.5 0.1 slice.486
  129.6 0.1 slice.481
  129.7 0.1 slice.497
  129.7 0.1 slice.492
  129.8 0.1 slice.508
  129.9 0.1 slice.503
  130.0 0.1 slice.519
  130.2 1.7 %collective-permute-done.3 = f32[16,8,272]{2,1,0:T(8,128)S(1)} collective-permute-done((f32[16,8,272]{2,1,0:T(8,128)S(1)}, f32[16,8,272]{2,1,0:T(8,128)S(1)}, u32[]{:S(2)}, u32[]{:S(2)}) %collective-permute-start.3) | collective-permute-done | bytes 139296 | tf_op jit(solution)/shard_map/ppermute | solution.py:18
  131.9 5.0 %collective-permute-done.2 = f32[16,8,272]{2,1,0:T(8,128)S(1)} collective-permute-done((f32[16,8,272]{2,1,0:T(8,128)S(1)}, f32[16,8,272]{2,1,0:T(8,128)S(1)}, u32[]{:S(2)}, u32[]{:S(2)}) %collective-permute-start.2) | collective-permute-done | bytes 139296 | tf_op jit(solution)/shard_map/ppermute | solution.py:15
  136.9 0.3 pad_maximum_fusion
  137.2 0.2 fusion.13
  137.4 0.4 fusion.14
  137.7 1.4 slice_subtract_fusion.10
  139.2 0.2 fusion.11
  139.4 0.4 fusion.12
  139.7 1.4 slice_subtract_fusion.6
  141.2 0.2 fusion.9
  141.4 0.4 fusion.10
  141.7 1.4 slice_subtract_fusion.2
  143.2 0.2 fusion.7
  143.3 0.4 fusion.8
  143.7 1.2 slice_subtract_fusion.28
  144.9 0.1 fusion.24
  145.1 0.3 fusion.25
  145.4 1.2 slice_subtract_fusion.24
  146.6 0.1 fusion.22
  146.8 0.3 fusion.23
  147.1 1.2 slice_subtract_fusion.20
  148.3 0.1 fusion.20
  148.4 0.3 fusion.21
  148.8 1.2 slice_subtract_fusion.16
  150.0 0.1 fusion.18
  150.1 0.3 fusion.19
  150.4 1.5 slice_subtract_fusion.30
  (35 shorter events, 0.5 us)
Async XLA Ops:
  0.0 25.8 %copy-start = (s32[1,16]{1,0:T(1,128)S(1)}, s32[1,16]{1,0:T(1,128)}, u32[]{:S(2)}) copy-start(s32[1,16]{1,0:T(1,128)} %param.13) | copy-start | bytes 196
  5.8 18.1 %copy-start.5 = (s32[32,256]{1,0:T(8,128)S(1)}, s32[32,256]{1,0:T(8,128)}, u32[]{:S(2)}) copy-start(s32[32,256]{1,0:T(8,128)} %param.11) | copy-start | bytes 98308
  5.8 18.1 %copy-start.2 = (f32[32,256]{1,0:T(8,128)S(1)}, f32[32,256]{1,0:T(8,128)}, u32[]{:S(2)}) copy-start(f32[32,256]{1,0:T(8,128)} %param.10) | copy-start | bytes 98308
  5.8 18.1 %copy-start.3 = (f32[32,256]{1,0:T(8,128)S(1)}, f32[32,256]{1,0:T(8,128)}, u32[]{:S(2)}) copy-start(f32[32,256]{1,0:T(8,128)} %param.9) | copy-start | bytes 98308
  13.7 12.0 %copy-start.4 = (s32[1,4096]{1,0:T(1,128)S(1)}, s32[1,4096]{1,0:T(1,128)}, u32[]{:S(2)}) copy-start(s32[1,4096]{1,0:T(1,128)} %param.12) | copy-start | bytes 49156
  13.7 29.9 %copy-start.1 = (f32[16,32,256]{2,1,0:T(8,128)S(1)}, f32[16,32,256]{2,1,0:T(8,128)}, u32[]{:S(2)}) copy-start(f32[16,32,256]{2,1,0:T(8,128)} %param.8) | copy-start | bytes 1572868
  13.7 36.2 %all-to-all-start = ((f32[16,1,8192]{2,1,0:T(1,128)}), f32[16,1,8192]{2,1,0:T(1,128)S(1)}, u32[]{:S(2)}, u32[]{:S(2)}) async-start(f32[16,1,8192]{2,1,0:T(1,128)} %reshape.116), calls=%async_computation | async-start | bytes 1048576 | tf_op jit(solution)/shard_map/all_to_all | solution.py:47
  24.0 14.5 %collective-permute-start.5 = (f32[3,32,8]{2,1,0:T(8,128)S(1)}, f32[3,32,8]{2,1,0:T(8,128)S(1)}, u32[]{:S(2)}, u32[]{:S(2)}) collective-permute-start(f32[3,32,8]{2,1,0:T(8,128)S(1)} %get-tuple-element.14), channel_id=1, source_target_pairs={{16,0},{32,16},{48,32},{64,48},{80,64},{96,80},{112,96},{128,112},... | collective-permute-start | bytes 9224 | tf_op jit(solution)/shard_map/ppermute | solution.py:18
  24.1 14.4 %collective-permute-start.4 = (f32[3,32,8]{2,1,0:T(8,128)S(1)}, f32[3,32,8]{2,1,0:T(8,128)S(1)}, u32[]{:S(2)}, u32[]{:S(2)}) collective-permute-start(f32[3,32,8]{2,1,0:T(8,128)S(1)} %get-tuple-element.13), channel_id=1, source_target_pairs={{0,16},{16,32},{32,48},{48,64},{64,80},{80,96},{96,112},{112,128},... | collective-permute-start | bytes 9224 | tf_op jit(solution)/shard_map/ppermute | solution.py:15
  38.6 7.7 %collective-permute-start.7 = (f32[3,8,272]{2,1,0:T(8,128)S(1)}, f32[3,8,272]{2,1,0:T(8,128)S(1)}, u32[]{:S(2)}, u32[]{:S(2)}) collective-permute-start(f32[3,8,272]{2,1,0:T(8,128)S(1)} %get-tuple-element.12), channel_id=1, source_target_pairs={{1,0},{2,1},{3,2},{4,3},{5,4},{6,5},{7,6},{8,7},{9,8},{10,9},{11,1... | collective-permute-start | bytes 78344 | tf_op jit(solution)/shard_map/ppermute | solution.py:18
  43.6 6.1 %collective-permute-start.6 = (f32[3,8,272]{2,1,0:T(8,128)S(1)}, f32[3,8,272]{2,1,0:T(8,128)S(1)}, u32[]{:S(2)}, u32[]{:S(2)}) collective-permute-start(f32[3,8,272]{2,1,0:T(8,128)S(1)} %get-tuple-element.11), channel_id=1, source_target_pairs={{0,1},{1,2},{2,3},{3,4},{4,5},{5,6},{6,7},{7,8},{8,9},{9,10},{10,1... | collective-permute-start | bytes 78344 | tf_op jit(solution)/shard_map/ppermute | solution.py:15
  121.3 5.8 %collective-permute-start.1 = (f32[16,32,8]{2,1,0:T(8,128)S(1)}, f32[16,32,8]{2,1,0:T(8,128)S(1)}, u32[]{:S(2)}, u32[]{:S(2)}) collective-permute-start(f32[16,32,8]{2,1,0:T(8,128)S(1)} %get-tuple-element.10), channel_id=1, source_target_pairs={{16,0},{32,16},{48,32},{64,48},{80,64},{96,80},{112,96},{128,112},... | collective-permute-start | bytes 49160 | tf_op jit(solution)/shard_map/ppermute | solution.py:18
  123.7 3.4 %collective-permute-start = (f32[16,32,8]{2,1,0:T(8,128)S(1)}, f32[16,32,8]{2,1,0:T(8,128)S(1)}, u32[]{:S(2)}, u32[]{:S(2)}) collective-permute-start(f32[16,32,8]{2,1,0:T(8,128)S(1)} %get-tuple-element.9), channel_id=1, source_target_pairs={{0,16},{16,32},{32,48},{48,64},{64,80},{80,96},{96,112},{112,128},... | collective-permute-start | bytes 49160 | tf_op jit(solution)/shard_map/ppermute | solution.py:15
  127.3 4.6 %collective-permute-start.3 = (f32[16,8,272]{2,1,0:T(8,128)S(1)}, f32[16,8,272]{2,1,0:T(8,128)S(1)}, u32[]{:S(2)}, u32[]{:S(2)}) collective-permute-start(f32[16,8,272]{2,1,0:T(8,128)S(1)} %get-tuple-element.8), channel_id=1, source_target_pairs={{1,0},{2,1},{3,2},{4,3},{5,4},{6,5},{7,6},{8,7},{9,8},{10,9},{11,1... | collective-permute-start | bytes 417800 | tf_op jit(solution)/shard_map/ppermute | solution.py:18
  129.0 7.8 %collective-permute-start.2 = (f32[16,8,272]{2,1,0:T(8,128)S(1)}, f32[16,8,272]{2,1,0:T(8,128)S(1)}, u32[]{:S(2)}, u32[]{:S(2)}) collective-permute-start(f32[16,8,272]{2,1,0:T(8,128)S(1)} %get-tuple-element.7), channel_id=1, source_target_pairs={{0,1},{1,2},{2,3},{3,4},{4,5},{5,6},{6,7},{7,8},{8,9},{9,10},{10,1... | collective-permute-start | bytes 417800 | tf_op jit(solution)/shard_map/ppermute | solution.py:15

commit v2 on v1

--- a/solution.py
+++ b/solution.py
@@ -43,10 +43,10 @@
     slot_index = jnp.arange(slots, dtype=jnp.int32)
     limits = jnp.broadcast_to(send_count[0][:, None], (lon_count, capacity)).reshape(slots)
     usable = jnp.where(slot_index % capacity < limits, 1.0, 0.0).astype(jnp.float32)
-    held = jnp.stack([obs_value[:, 0, :], obs_weight[:, 0, :]])
-    at_owner = lax.all_to_all(held, "lon", split_axis=2, concat_axis=2, tiled=True)
+    values = lax.all_to_all(obs_value[:, 0, :], "lon", split_axis=1, concat_axis=1, tiled=True)
+    weights = lax.all_to_all(obs_weight[:, 0, :], "lon", split_axis=1, concat_axis=1, tiled=True)
     at_column = jnp.take(columns, targets, axis=1)
-    weighted = at_owner[1] * (at_owner[0] - at_column) * usable
+    weighted = lax.optimization_barrier(weights * (values - at_column) * usable)
     sea = land_sea.astype(jnp.float32)
     gradient = jnp.zeros((levels, rows_here * cols_here), jnp.float32).at[:, targets].add(weighted)
     gradient = gradient.reshape(levels, rows_here, cols_here) * sea[None]

time: 153 us -> 127 us (0.83)
  other arithmetic: 68.8 us -> 48 us
  starting transfers between devices: 21 us -> 31 us
  waiting for transfers between devices: 25.9 us -> 18.4 us
  local copies, waits for them, and re-layouts: 35.8 us -> 28.7 us
    scatter-add x1, other arithmetic: 51.2 us -> 24.6 us  [body(): jnp.zeros((levels, rows_here * cols_here), jnp.float32).at[:, targets]]
    gather x0 -> x1, local copies, waits for them, and re-layouts: none -> 16.4 us  [body(): at_column = jnp.take(columns, targets, axis=1)]
    unnamed x18 -> x15, local copies, waits for them, and re-layouts: 19 us -> 2.73 us
    ppermute x4, waiting for transfers between devices: 17.5 us -> 2.8 us  [with_halo(): lax.ppermute(lax.slice_in_dim(block, 0, width, axis=dim), axis, backward)]
    all_to_all x1 -> x2, waiting for transfers between devices: 0.01 us -> 9.55 us  [the longest x1 9.55 us: body(): lax.all_to_all(obs_value[:, 0, :], 'lon', split_axis=1, concat_axis=1, ti...]
    slice x1 -> x0, local copies, waits for them, and re-layouts: 7.62 us -> none  [body(): weighted = at_owner[1] * (at_owner[0] - at_column) * usable]
    all_to_all x1 -> x2, starting transfers between devices: 10.1 us -> 17.3 us  [the longest x1 9.71 us: body(): lax.all_to_all(obs_weight[:, 0, :], 'lon', split_axis=1, concat_axis=1, t...]
    all_to_all x1 -> x4, local copies, waits for them, and re-layouts: 0.51 us -> 5.34 us  [the longest x2 2.68 us: body(): lax.all_to_all(obs_value[:, 0, :], 'lon', split_axis=1, concat_axis=1, ti...]
  transfers between devices with their start and end apart: 9 -> 10, of which waited for: 5 -> 4; matrix products, arithmetic and copies ran while one was open for 3% -> 21% of each run, Pallas kernels for 0% -> 0%
where the time goes in v2:
time: 127 us; the launch traced here: 126 us
  other arithmetic  48 us (38%)
  starting transfers between devices  31 us (24%)
  local copies, waits for them, and re-layouts  28.7 us (23%)
  waiting for transfers between devices  18.4 us (14%)
    scatter-add x1, other arithmetic, body(): jnp.zeros((levels, rows_here * cols_here), jnp.float32).at[:, targets]  24.6 us
    gather x1, local copies, waits for them, and re-layouts, body(): at_column = jnp.take(columns, targets, axis=1)  16.4 us
    sub x8, other arithmetic, one_pass(): layer_field[:, 1:-1, 1:-1] + flux_east[:, 1:-1, 1:]  10.6 us
    all_to_all x1, starting transfers between devices, body(): lax.all_to_all(obs_weight[:, 0, :], 'lon', split_axis=1, concat_axis=1, t...  9.71 us
    all_to_all x1, waiting for transfers between devices, body(): lax.all_to_all(obs_value[:, 0, :], 'lon', split_axis=1, concat_axis=1, ti...  9.55 us
    ppermute x4, starting transfers between devices, with_halo(): lax.ppermute(lax.slice_in_dim(block, 0, width, axis=dim), axis, backward)  9.17 us
    all_to_all x1, starting transfers between devices, body(): lax.all_to_all(obs_value[:, 0, :], 'lon', split_axis=1, concat_axis=1, ti...  7.55 us
    ppermute x4, waiting for transfers between devices, with_halo(): lax.ppermute(lax.slice_in_dim(block, block.shape[dim] - width, None, axis...  6 us
  transfers between devices with their start and end apart: 10, of which 4 were waited for; matrix products, arithmetic and copies ran while one was open for 21% of the time, Pallas kernels for 0%

profile of v2, /device:TPU:1, one launch (start us, length us, event | category | flops | bytes accessed | tf_op | source)
XLA Modules:
  0.0 126.5 jit_solution(7850044198623653422)
XLA Ops:
  0.0 0.8 convert_bitcast_fusion
  0.8 0.8 pad_maximum_fusion.5
  1.7 3.0 %collective-permute-start.4 = (f32[3,32,8]{2,1,0:T(8,128)S(1)}, f32[3,32,8]{2,1,0:T(8,128)S(1)}, u32[]{:S(2)}, u32[]{:S(2)}) collective-permute-start(f32[3,32,8]{2,1,0:T(8,128)S(1)} %get-tuple-element.11), channel_id=1, source_target_pairs={{0,16},{16,32},{32,48},{48,64},{64,80},{80,96},{96,112},{112,128},... | collective-permute-start | bytes 9224 | tf_op jit(solution)/shard_map/ppermute | solution.py:15
  4.8 0.2 collective-permute-start.5
  5.0 1.6 %reduce = f32[16,4096]{1,0:T(8,128)S(1)} reduce(f32[16,1,4096]{2,1,0:T(1,128)} %param.15, f32[]{:T(128)} %constant.53), dimensions={1}, to_apply=%param.15.reduce_sub_computation | reduce | bytes 524292 | tf_op args[7]
  6.6 0.7 copy.33
  7.3 9.7 %all-to-all-start = ((f32[16,16,256]{2,0,1:T(8,128)}), f32[16,16,256]{2,0,1:T(8,128)S(1)}, u32[]{:S(2)}, u32[]{:S(2)}) async-start(f32[16,16,256]{2,0,1:T(8,128)} %bitcast.44), calls=%async_computation | async-start | bytes 524288 | tf_op jit(solution)/shard_map/all_to_all | solution.py:47
  17.2 0.1 pad_maximum_fusion.10
  17.3 1.4 %collective-permute-start.6 = (f32[3,8,272]{2,1,0:T(8,128)S(1)}, f32[3,8,272]{2,1,0:T(8,128)S(1)}, u32[]{:S(2)}, u32[]{:S(2)}) collective-permute-start(f32[3,8,272]{2,1,0:T(8,128)S(1)} %get-tuple-element.9), channel_id=1, source_target_pairs={{0,1},{1,2},{2,3},{3,4},{4,5},{5,6},{6,7},{7,8},{8,9},{9,10},{10,1... | collective-permute-start | bytes 78344 | tf_op jit(solution)/shard_map/ppermute | solution.py:15
  18.7 3.7 %collective-permute-start.7 = (f32[3,8,272]{2,1,0:T(8,128)S(1)}, f32[3,8,272]{2,1,0:T(8,128)S(1)}, u32[]{:S(2)}, u32[]{:S(2)}) collective-permute-start(f32[3,8,272]{2,1,0:T(8,128)S(1)} %get-tuple-element.10), channel_id=1, source_target_pairs={{1,0},{2,1},{3,2},{4,3},{5,4},{6,5},{7,6},{8,7},{9,8},{10,9},{11,1... | collective-permute-start | bytes 78344 | tf_op jit(solution)/shard_map/ppermute | solution.py:18
  22.4 2.6 %copy.25 = f32[16,32,256]{0,2,1:T(8,128)} copy(f32[16,32,256]{2,1,0:T(8,128)S(1)} %copy-done.1) | data formatting | bytes 1048576 | tf_op args[0]
  25.1 0.6 reduce.1
  25.7 0.7 copy.32
  26.4 16.4 %gather_fusion = f32[4096,16]{1,0:T(8,128)} fusion(f32[16,8192]{0,1:T(8,128)} %bitcast.47, s32[4096]{0:T(1024)S(1)} %broadcast_clamp_fusion), kind=kCustom, calls=%fused_computation | custom fusion | bytes 540672 | tf_op jit(solution)/shard_map/jit(_take)/gather | solution.py:48
  42.9 7.6 %all-to-all-start.1 = ((f32[16,16,256]{2,0,1:T(8,128)}), f32[16,16,256]{2,0,1:T(8,128)S(1)}, u32[]{:S(2)}, u32[]{:S(2)}) async-start(f32[16,16,256]{2,0,1:T(8,128)} %bitcast.43), calls=%async_computation.1 | async-start | bytes 524288 | tf_op jit(solution)/shard_map/all_to_all | solution.py:46
  50.4 0.1 pad_maximum_fusion.1
  50.6 1.9 %copy.22 = f32[16,16,256]{0,2,1:T(8,128)} copy(f32[16,16,256]{2,0,1:T(8,128)S(1)} %all-to-all-done) | data formatting | bytes 524288 | tf_op jit(solution)/shard_map/all_to_all | solution.py:47
  52.6 9.5 %all-to-all-done.1 = f32[16,16,256]{2,0,1:T(8,128)S(1)} async-done(((f32[16,16,256]{2,0,1:T(8,128)}), f32[16,16,256]{2,0,1:T(8,128)S(1)}, u32[]{:S(2)}, u32[]{:S(2)}) %all-to-all-start.1) | async-done | bytes 262176 | tf_op jit(solution)/shard_map/all_to_all | solution.py:46
  62.1 1.9 %copy.24 = f32[16,16,256]{0,2,1:T(8,128)} copy(f32[16,16,256]{2,0,1:T(8,128)S(1)} %all-to-all-done.1) | data formatting | bytes 524288 | tf_op jit(solution)/shard_map/all_to_all | solution.py:46
  64.1 4.0 %fusion.3 = f32[16,4096]{0,1:T(8,128)S(1)} fusion(f32[16,16,256]{0,2,1:T(8,128)} %copy.24, f32[16,16,256]{0,2,1:T(8,128)} %copy.22, f32[4096,16]{1,0:T(8,128)} %gather_fusion, f32[4096]{0:T(1024)S(1)} %fusion.26, pred[4096]{0:T(1024)(128)(4,1)S(1)} %compare_and_fusion), kind=kLoop, calls=%fused_computation.6 | loop fusion | flops 262144 | bytes 1069056 | tf_op jit(solution)/shard_map/mul | solution.py:49
  68.1 24.6 %scatter_custom_fusion = f32[16,8192]{0,1:T(8,128)} fusion(s32[4096]{0:T(1024)S(1)} %bitcast.58, f32[16,4096]{0,1:T(8,128)S(1)} %fusion.3, f32[]{:T(128)} %constant.19.clone.1), kind=kCustom, calls=%fused_computation.2 | custom fusion | flops 65536 | bytes 2621444 | tf_op jit(solution)/shard_map/scatter-add | solution.py:51
  92.6 2.9 %copy.26 = f32[16,32,256]{2,1,0:T(8,128)S(1)} copy(f32[16,32,256]{0,2,1:T(8,128)} %bitcast.46) | data formatting | bytes 1048576 | tf_op jit(solution)/shard_map/reshape | solution.py:52
  95.6 0.1 fusion.27
  95.7 0.5 collective-permute-start.1
  96.3 0.1 slice.438
  96.4 0.1 slice.449
  96.5 2.5 %collective-permute-done = f32[16,32,8]{2,1,0:T(8,128)S(1)} collective-permute-done((f32[16,32,8]{2,1,0:T(8,128)S(1)}, f32[16,32,8]{2,1,0:T(8,128)S(1)}, u32[]{:S(2)}, u32[]{:S(2)}) %collective-permute-start) | collective-permute-done | bytes 16416 | tf_op jit(solution)/shard_map/ppermute | solution.py:15
  99.0 2.8 %collective-permute-done.1 = f32[16,32,8]{2,1,0:T(8,128)S(1)} collective-permute-done((f32[16,32,8]{2,1,0:T(8,128)S(1)}, f32[16,32,8]{2,1,0:T(8,128)S(1)}, u32[]{:S(2)}, u32[]{:S(2)}) %collective-permute-start.1) | collective-permute-done | bytes 16416 | tf_op jit(solution)/shard_map/ppermute | solution.py:18
  101.8 0.2 pad_maximum_fusion.4
  102.0 0.1 collective-permute-start.2
  102.1 4.8 %collective-permute-start.3 = (f32[16,8,272]{2,1,0:T(8,128)S(1)}, f32[16,8,272]{2,1,0:T(8,128)S(1)}, u32[]{:S(2)}, u32[]{:S(2)}) collective-permute-start(f32[16,8,272]{2,1,0:T(8,128)S(1)} %get-tuple-element.6), channel_id=1, source_target_pairs={{1,0},{2,1},{3,2},{4,3},{5,4},{6,5},{7,6},{8,7},{9,8},{10,9},{11,1... | collective-permute-start | bytes 417800 | tf_op jit(solution)/shard_map/ppermute | solution.py:18
  106.9 0.1 slice.443
  107.0 0.1 slice.454
  107.1 0.1 slice.460
  107.2 0.1 slice.465
  107.3 0.1 slice.471
  107.4 0.1 slice.476
  107.6 0.1 slice.493
  108.0 3.5 %collective-permute-done.2 = f32[16,8,272]{2,1,0:T(8,128)S(1)} collective-permute-done((f32[16,8,272]{2,1,0:T(8,128)S(1)}, f32[16,8,272]{2,1,0:T(8,128)S(1)}, u32[]{:S(2)}, u32[]{:S(2)}) %collective-permute-start.2) | collective-permute-done | bytes 139296 | tf_op jit(solution)/shard_map/ppermute | solution.py:15
  111.5 0.3 pad_maximum_fusion
  111.8 0.4 fusion.12
  112.2 0.2 fusion.11
  112.3 1.4 %slice_subtract_fusion.10 = f32[16,46,270]{2,1,0:T(8,128)S(1)} fusion(f32[16,47,272]{2,1,0:T(8,128)S(1)} %fusion.11, f32[16,48,271]{2,1,0:T(8,128)S(1)} %fusion.12, f32[16,48,272]{2,1,0:T(8,128)S(1)} %pad_maximum_fusion), kind=kLoop, calls=%fused_computation.28 | loop fusion | flops 794880 | bytes 4769280 | tf_op jit(solution)/shard_map/sub | solution.py:27
  113.8 0.4 fusion.10
  114.2 0.2 fusion.9
  114.3 1.4 %slice_subtract_fusion.6 = f32[16,44,268]{2,1,0:T(8,128)S(1)} fusion(f32[16,45,270]{2,1,0:T(8,128)S(1)} %fusion.9, f32[16,46,269]{2,1,0:T(8,128)S(1)} %fusion.10, f32[16,46,270]{2,1,0:T(8,128)S(1)} %slice_subtract_fusion.10), kind=kLoop, calls=%fused_computation.20 | loop fusion | flops 754688 | bytes 4528128 | tf_op jit(solution)/shard_map/sub | solution.py:27
  115.8 0.4 fusion.8
  116.2 0.2 fusion.7
  116.3 1.4 %slice_subtract_fusion.2 = f32[16,42,266]{2,1,0:T(8,128)S(1)} fusion(f32[16,43,268]{2,1,0:T(8,128)S(1)} %fusion.7, f32[16,44,267]{2,1,0:T(8,128)S(1)} %fusion.8, f32[16,44,268]{2,1,0:T(8,128)S(1)} %slice_subtract_fusion.6), kind=kLoop, calls=%fused_computation.12 | loop fusion | flops 715008 | bytes 4290048 | tf_op jit(solution)/shard_map/sub | solution.py:27
  117.8 0.4 fusion.6
  118.1 0.2 fusion.5
  118.3 1.2 slice_subtract_fusion.28
  119.5 0.3 fusion.20
  119.9 0.1 fusion.19
  120.0 1.2 slice_subtract_fusion.24
  121.2 0.3 fusion.18
  121.5 0.1 fusion.17
  121.7 1.2 slice_subtract_fusion.20
  122.9 0.3 fusion.16
  123.2 0.1 fusion.15
  123.4 1.2 slice_subtract_fusion.16
  124.6 0.3 fusion.14
  124.9 0.1 fusion.13
  125.0 1.5 %slice_subtract_fusion.30 = f32[16,32,256]{2,1,0:T(8,128)} fusion(f32[16,33,258]{2,1,0:T(8,128)S(1)} %fusion.13, f32[16,34,257]{2,1,0:T(8,128)S(1)} %fusion.14, f32[16,34,258]{2,1,0:T(8,128)S(1)} %slice_subtract_fusion.16), kind=kLoop, calls=%fused_computation.69 | loop fusion | flops 524288 | bytes 3145728 | tf_op jit(solution)/shard_map/sub | solution.py:27
  (37 shorter events, 0.9 us)
Async XLA Ops:
  0.0 17.1 %copy-start = (s32[1,16]{1,0:T(1,128)S(1)}, s32[1,16]{1,0:T(1,128)}, u32[]{:S(2)}) copy-start(s32[1,16]{1,0:T(1,128)} %param.13) | copy-start | bytes 196
  0.0 17.2 %copy-start.3 = (f32[32,256]{1,0:T(8,128)S(1)}, f32[32,256]{1,0:T(8,128)}, u32[]{:S(2)}) copy-start(f32[32,256]{1,0:T(8,128)} %param.9) | copy-start | bytes 98308
  0.0 17.2 %copy-start.2 = (f32[32,256]{1,0:T(8,128)S(1)}, f32[32,256]{1,0:T(8,128)}, u32[]{:S(2)}) copy-start(f32[32,256]{1,0:T(8,128)} %param.10) | copy-start | bytes 98308
  0.0 17.0 %copy-start.5 = (s32[1,4096]{1,0:T(1,128)S(1)}, s32[1,4096]{1,0:T(1,128)}, u32[]{:S(2)}) copy-start(s32[1,4096]{1,0:T(1,128)} %param.12) | copy-start | bytes 49156
  0.8 21.6 %copy-start.1 = (f32[16,32,256]{2,1,0:T(8,128)S(1)}, f32[16,32,256]{2,1,0:T(8,128)}, u32[]{:S(2)}) copy-start(f32[16,32,256]{2,1,0:T(8,128)} %param.8) | copy-start | bytes 1572868
  1.7 15.4 %collective-permute-start.4 = (f32[3,32,8]{2,1,0:T(8,128)S(1)}, f32[3,32,8]{2,1,0:T(8,128)S(1)}, u32[]{:S(2)}, u32[]{:S(2)}) collective-permute-start(f32[3,32,8]{2,1,0:T(8,128)S(1)} %get-tuple-element.11), channel_id=1, source_target_pairs={{0,16},{16,32},{32,48},{48,64},{64,80},{80,96},{96,112},{112,128},... | collective-permute-start | bytes 9224 | tf_op jit(solution)/shard_map/ppermute | solution.py:15
  4.8 12.4 %collective-permute-start.5 = (f32[3,32,8]{2,1,0:T(8,128)S(1)}, f32[3,32,8]{2,1,0:T(8,128)S(1)}, u32[]{:S(2)}, u32[]{:S(2)}) collective-permute-start(f32[3,32,8]{2,1,0:T(8,128)S(1)} %get-tuple-element.12), channel_id=1, source_target_pairs={{16,0},{32,16},{48,32},{64,48},{80,64},{96,80},{112,96},{128,112},... | collective-permute-start | bytes 9224 | tf_op jit(solution)/shard_map/ppermute | solution.py:18
  7.3 35.6 %all-to-all-start = ((f32[16,16,256]{2,0,1:T(8,128)}), f32[16,16,256]{2,0,1:T(8,128)S(1)}, u32[]{:S(2)}, u32[]{:S(2)}) async-start(f32[16,16,256]{2,0,1:T(8,128)} %bitcast.44), calls=%async_computation | async-start | bytes 524288 | tf_op jit(solution)/shard_map/all_to_all | solution.py:47
  17.3 33.1 %collective-permute-start.6 = (f32[3,8,272]{2,1,0:T(8,128)S(1)}, f32[3,8,272]{2,1,0:T(8,128)S(1)}, u32[]{:S(2)}, u32[]{:S(2)}) collective-permute-start(f32[3,8,272]{2,1,0:T(8,128)S(1)} %get-tuple-element.9), channel_id=1, source_target_pairs={{0,1},{1,2},{2,3},{3,4},{4,5},{5,6},{6,7},{7,8},{8,9},{9,10},{10,1... | collective-permute-start | bytes 78344 | tf_op jit(solution)/shard_map/ppermute | solution.py:15
  18.7 31.7 %collective-permute-start.7 = (f32[3,8,272]{2,1,0:T(8,128)S(1)}, f32[3,8,272]{2,1,0:T(8,128)S(1)}, u32[]{:S(2)}, u32[]{:S(2)}) collective-permute-start(f32[3,8,272]{2,1,0:T(8,128)S(1)} %get-tuple-element.10), channel_id=1, source_target_pairs={{1,0},{2,1},{3,2},{4,3},{5,4},{6,5},{7,6},{8,7},{9,8},{10,9},{11,1... | collective-permute-start | bytes 78344 | tf_op jit(solution)/shard_map/ppermute | solution.py:18
  22.4 2.6 %copy-start.4 = (f32[16,1,4096]{2,1,0:T(1,128)S(1)}, f32[16,1,4096]{2,1,0:T(1,128)}, u32[]{:S(2)}) copy-start(f32[16,1,4096]{2,1,0:T(1,128)} %param.14) | copy-start | bytes 786436
  42.9 19.3 %all-to-all-start.1 = ((f32[16,16,256]{2,0,1:T(8,128)}), f32[16,16,256]{2,0,1:T(8,128)S(1)}, u32[]{:S(2)}, u32[]{:S(2)}) async-start(f32[16,16,256]{2,0,1:T(8,128)} %bitcast.43), calls=%async_computation.1 | async-start | bytes 524288 | tf_op jit(solution)/shard_map/all_to_all | solution.py:46
  95.7 3.3 %collective-permute-start = (f32[16,32,8]{2,1,0:T(8,128)S(1)}, f32[16,32,8]{2,1,0:T(8,128)S(1)}, u32[]{:S(2)}, u32[]{:S(2)}) collective-permute-start(f32[16,32,8]{2,1,0:T(8,128)S(1)} %get-tuple-element.7), channel_id=1, source_target_pairs={{0,16},{16,32},{32,48},{48,64},{64,80},{80,96},{96,112},{112,128},... | collective-permute-start | bytes 49160 | tf_op jit(solution)/shard_map/ppermute | solution.py:15
  95.7 6.1 %collective-permute-start.1 = (f32[16,32,8]{2,1,0:T(8,128)S(1)}, f32[16,32,8]{2,1,0:T(8,128)S(1)}, u32[]{:S(2)}, u32[]{:S(2)}) collective-permute-start(f32[16,32,8]{2,1,0:T(8,128)S(1)} %get-tuple-element.8), channel_id=1, source_target_pairs={{16,0},{32,16},{48,32},{64,48},{80,64},{96,80},{112,96},{128,112},... | collective-permute-start | bytes 49160 | tf_op jit(solution)/shard_map/ppermute | solution.py:18
  102.0 9.4 %collective-permute-start.2 = (f32[16,8,272]{2,1,0:T(8,128)S(1)}, f32[16,8,272]{2,1,0:T(8,128)S(1)}, u32[]{:S(2)}, u32[]{:S(2)}) collective-permute-start(f32[16,8,272]{2,1,0:T(8,128)S(1)} %get-tuple-element.5), channel_id=1, source_target_pairs={{0,1},{1,2},{2,3},{3,4},{4,5},{5,6},{6,7},{7,8},{8,9},{9,10},{10,1... | collective-permute-start | bytes 417800 | tf_op jit(solution)/shard_map/ppermute | solution.py:15
  102.1 9.3 %collective-permute-start.3 = (f32[16,8,272]{2,1,0:T(8,128)S(1)}, f32[16,8,272]{2,1,0:T(8,128)S(1)}, u32[]{:S(2)}, u32[]{:S(2)}) collective-permute-start(f32[16,8,272]{2,1,0:T(8,128)S(1)} %get-tuple-element.6), channel_id=1, source_target_pairs={{1,0},{2,1},{3,2},{4,3},{5,4},{6,5},{7,6},{8,7},{9,8},{10,9},{11,1... | collective-permute-start | bytes 417800 | tf_op jit(solution)/shard_map/ppermute | solution.py:18

commit v3 on v2

--- a/solution.py
+++ b/solution.py
@@ -43,8 +43,14 @@
     slot_index = jnp.arange(slots, dtype=jnp.int32)
     limits = jnp.broadcast_to(send_count[0][:, None], (lon_count, capacity)).reshape(slots)
     usable = jnp.where(slot_index % capacity < limits, 1.0, 0.0).astype(jnp.float32)
-    values = lax.all_to_all(obs_value[:, 0, :], "lon", split_axis=1, concat_axis=1, tiled=True)
-    weights = lax.all_to_all(obs_weight[:, 0, :], "lon", split_axis=1, concat_axis=1, tiled=True)
+    chunked = (levels, lon_count, capacity)
+    held = jnp.concatenate(
+        [obs_value[:, 0, :].reshape(chunked), obs_weight[:, 0, :].reshape(chunked)], axis=2
+    ).reshape(levels, 2 * slots)
+    at_owner = lax.all_to_all(held, "lon", split_axis=1, concat_axis=1, tiled=True)
+    at_owner = at_owner.reshape(levels, lon_count, 2 * capacity)
+    values = at_owner[:, :, :capacity].reshape(levels, slots)
+    weights = at_owner[:, :, capacity:].reshape(levels, slots)
     at_column = jnp.take(columns, targets, axis=1)
     weighted = lax.optimization_barrier(weights * (values - at_column) * usable)
     sea = land_sea.astype(jnp.float32)

time: 127 us -> 112 us (0.88)
  waiting for transfers between devices: 18.4 us -> 9.74 us
  starting transfers between devices: 31 us -> 24.9 us
    all_to_all x2 -> x1, waiting for transfers between devices: 9.55 us -> 0.01 us  [body(): lax.all_to_all(held, 'lon', split_axis=1, concat_axis=1, tiled=True)]
    all_to_all x2 -> x1, starting transfers between devices: 17.3 us -> 9.69 us  [body(): lax.all_to_all(held, 'lon', split_axis=1, concat_axis=1, tiled=True)]
    all_to_all x4 -> x0, local copies, waits for them, and re-layouts: 5.34 us -> none  [the longest x2 2.68 us: body(): lax.all_to_all(obs_value[:, 0, :], 'lon', split_axis=1, concat_axis=1, ti...]
    slice x0 -> x3, local copies, waits for them, and re-layouts: none -> 3.92 us  [the longest x2 1.98 us: body(): weights = at_owner[:, :, capacity:].reshape(levels, slots)]
    ppermute x4, starting transfers between devices: 4.53 us -> 6.48 us  [with_halo(): lax.ppermute(lax.slice_in_dim(block, block.shape[dim] - width, None, axis...]
    unnamed x15 -> x17, local copies, waits for them, and re-layouts: 2.73 us -> 2.9 us
  transfers between devices with their start and end apart: 10 -> 9, of which waited for: 4 -> 3; matrix products, arithmetic and copies ran while one was open for 21% -> 22% of each run, Pallas kernels for 0% -> 0%
where the time goes in v3:
time: 112 us
  other arithmetic  48 us (43%)
  local copies, waits for them, and re-layouts  28.5 us (25%)
  starting transfers between devices  24.9 us (22%)
  waiting for transfers between devices  9.74 us (9%)
    scatter-add x1, other arithmetic, body(): jnp.zeros((levels, rows_here * cols_here), jnp.float32).at[:, targets]  24.6 us
    gather x1, local copies, waits for them, and re-layouts, body(): at_column = jnp.take(columns, targets, axis=1)  16.3 us
    sub x8, other arithmetic, one_pass(): layer_field[:, 1:-1, 1:-1] + flux_east[:, 1:-1, 1:]  10.6 us
    all_to_all x1, starting transfers between devices, body(): lax.all_to_all(held, 'lon', split_axis=1, concat_axis=1, tiled=True)  9.69 us
    ppermute x4, starting transfers between devices, with_halo(): lax.ppermute(lax.slice_in_dim(block, 0, width, axis=dim), axis, backward)  8.69 us
    ppermute x4, waiting for transfers between devices, with_halo(): lax.ppermute(lax.slice_in_dim(block, block.shape[dim] - width, None, axis...  7.25 us
    ppermute x4, starting transfers between devices, with_halo(): lax.ppermute(lax.slice_in_dim(block, block.shape[dim] - width, None, axis...  6.48 us
    mul x1, other arithmetic, body(): weighted = lax.optimization_barrier(weights * (values - at_column) * usable)  3.99 us
  transfers between devices with their start and end apart: 9, of which 3 were waited for; matrix products, arithmetic and copies ran while one was open for 22% of the time, Pallas kernels for 0%

profile of v3, /device:TPU:1, one launch (start us, length us, event | category | flops | bytes accessed | tf_op | source)
XLA Modules:
  0.0 111.5 jit_solution(14636840000144006930)
XLA Ops:
  0.0 0.8 convert_bitcast_fusion
  0.8 0.8 pad_maximum_fusion.6
  1.7 3.0 %collective-permute-start.4 = (f32[3,32,8]{2,1,0:T(8,128)S(1)}, f32[3,32,8]{2,1,0:T(8,128)S(1)}, u32[]{:S(2)}, u32[]{:S(2)}) collective-permute-start(f32[3,32,8]{2,1,0:T(8,128)S(1)} %get-tuple-element.13), channel_id=1, source_target_pairs={{0,16},{16,32},{32,48},{48,64},{64,80},{80,96},{96,112},{112,128},... | collective-permute-start | bytes 9224 | tf_op jit(solution)/shard_map/ppermute | solution.py:15
  4.7 0.2 collective-permute-start.5
  4.9 1.6 %reduce = f32[16,4096]{1,0:T(8,128)S(1)} reduce(f32[16,1,4096]{2,1,0:T(1,128)} %param.14, f32[]{:T(128)} %constant.53), dimensions={1}, to_apply=%param.14.reduce_sub_computation | reduce | bytes 524292 | tf_op args[6]
  6.5 0.1 copy.22
  6.6 0.6 reduce.1
  7.3 0.1 copy.23
  7.5 1.1 copy.17
  8.6 9.7 %all-to-all-start = ((f32[16,16,512]{2,0,1:T(8,128)}), f32[16,16,512]{2,0,1:T(8,128)S(1)}, u32[]{:S(2)}, u32[]{:S(2)}) async-start(f32[16,16,512]{2,0,1:T(8,128)} %copy.17), calls=%async_computation | async-start | bytes 1048576 | tf_op jit(solution)/shard_map/all_to_all | solution.py:50
  18.5 0.1 pad_maximum_fusion.11
  18.6 1.4 %collective-permute-start.6 = (f32[3,8,272]{2,1,0:T(8,128)S(1)}, f32[3,8,272]{2,1,0:T(8,128)S(1)}, u32[]{:S(2)}, u32[]{:S(2)}) collective-permute-start(f32[3,8,272]{2,1,0:T(8,128)S(1)} %get-tuple-element.11), channel_id=1, source_target_pairs={{0,1},{1,2},{2,3},{3,4},{4,5},{5,6},{6,7},{7,8},{8,9},{9,10},{10,1... | collective-permute-start | bytes 78344 | tf_op jit(solution)/shard_map/ppermute | solution.py:15
  20.0 3.7 %collective-permute-start.7 = (f32[3,8,272]{2,1,0:T(8,128)S(1)}, f32[3,8,272]{2,1,0:T(8,128)S(1)}, u32[]{:S(2)}, u32[]{:S(2)}) collective-permute-start(f32[3,8,272]{2,1,0:T(8,128)S(1)} %get-tuple-element.12), channel_id=1, source_target_pairs={{1,0},{2,1},{3,2},{4,3},{5,4},{6,5},{7,6},{8,7},{9,8},{10,9},{11,1... | collective-permute-start | bytes 78344 | tf_op jit(solution)/shard_map/ppermute | solution.py:18
  23.7 2.6 %copy.20 = f32[16,32,256]{0,2,1:T(8,128)} copy(f32[16,32,256]{2,1,0:T(8,128)S(1)} %copy-done.1) | data formatting | bytes 1048576 | tf_op args[0]
  26.3 16.3 %gather_fusion = f32[4096,16]{1,0:T(8,128)} fusion(f32[16,8192]{0,1:T(8,128)} %bitcast.43, s32[4096]{0:T(1024)S(1)} %broadcast_clamp_fusion), kind=kCustom, calls=%fused_computation | custom fusion | bytes 540672 | tf_op jit(solution)/shard_map/jit(_take)/gather | solution.py:54
  42.6 0.1 pad_maximum_fusion.2
  42.9 1.9 %copy.18 = f32[16,16,256]{0,2,1:T(8,128)} copy(f32[16,16,256]{2,0,1:T(8,128)S(1)} %get-tuple-element.9) | data formatting | bytes 524288 | tf_op jit(solution)/shard_map/slice | solution.py:53
  44.8 1.9 %copy.19 = f32[16,16,256]{0,2,1:T(8,128)} copy(f32[16,16,256]{2,0,1:T(8,128)S(1)} %get-tuple-element.10) | data formatting | bytes 524288 | tf_op jit(solution)/shard_map/slice | solution.py:52
  46.7 4.0 %fusion.3 = f32[16,4096]{0,1:T(8,128)S(1)} fusion(f32[16,16,256]{0,2,1:T(8,128)} %copy.19, f32[16,16,256]{0,2,1:T(8,128)} %copy.18, f32[4096,16]{1,0:T(8,128)} %gather_fusion, f32[4096]{0:T(1024)S(1)} %fusion.26, pred[4096]{0:T(1024)(128)(4,1)S(1)} %compare_and_fusion), kind=kLoop, calls=%fused_computation.6 | loop fusion | flops 262144 | bytes 1069056 | tf_op jit(solution)/shard_map/mul | solution.py:55
  50.7 24.6 %scatter_custom_fusion = f32[16,8192]{0,1:T(8,128)} fusion(s32[4096]{0:T(1024)S(1)} %bitcast.56, f32[16,4096]{0,1:T(8,128)S(1)} %fusion.3, f32[]{:T(128)} %constant.19.clone.1), kind=kCustom, calls=%fused_computation.2 | custom fusion | flops 65536 | bytes 2621444 | tf_op jit(solution)/shard_map/scatter-add | solution.py:57
  75.3 2.9 %copy.21 = f32[16,32,256]{2,1,0:T(8,128)S(1)} copy(f32[16,32,256]{0,2,1:T(8,128)} %bitcast.42) | data formatting | bytes 1048576 | tf_op jit(solution)/shard_map/reshape | solution.py:58
  78.2 0.1 fusion.27
  78.4 2.0 %collective-permute-start = (f32[16,32,8]{2,1,0:T(8,128)S(1)}, f32[16,32,8]{2,1,0:T(8,128)S(1)}, u32[]{:S(2)}, u32[]{:S(2)}) collective-permute-start(f32[16,32,8]{2,1,0:T(8,128)S(1)} %get-tuple-element.7), channel_id=1, source_target_pairs={{0,16},{16,32},{32,48},{48,64},{64,80},{80,96},{96,112},{112,128},... | collective-permute-start | bytes 49160 | tf_op jit(solution)/shard_map/ppermute | solution.py:15
  80.3 0.1 slice_multiply_fusion.2
  80.4 0.1 slice.448
  80.5 0.1 slice.459
  80.6 3.0 %collective-permute-done = f32[16,32,8]{2,1,0:T(8,128)S(1)} collective-permute-done((f32[16,32,8]{2,1,0:T(8,128)S(1)}, f32[16,32,8]{2,1,0:T(8,128)S(1)}, u32[]{:S(2)}, u32[]{:S(2)}) %collective-permute-start) | collective-permute-done | bytes 16416 | tf_op jit(solution)/shard_map/ppermute | solution.py:15
  83.7 2.5 %collective-permute-done.1 = f32[16,32,8]{2,1,0:T(8,128)S(1)} collective-permute-done((f32[16,32,8]{2,1,0:T(8,128)S(1)}, f32[16,32,8]{2,1,0:T(8,128)S(1)}, u32[]{:S(2)}, u32[]{:S(2)}) %collective-permute-start.1) | collective-permute-done | bytes 16416 | tf_op jit(solution)/shard_map/ppermute | solution.py:18
  86.1 0.2 pad_maximum_fusion.5
  86.3 0.1 collective-permute-start.2
  86.4 4.8 %collective-permute-start.3 = (f32[16,8,272]{2,1,0:T(8,128)S(1)}, f32[16,8,272]{2,1,0:T(8,128)S(1)}, u32[]{:S(2)}, u32[]{:S(2)}) collective-permute-start(f32[16,8,272]{2,1,0:T(8,128)S(1)} %get-tuple-element.6), channel_id=1, source_target_pairs={{1,0},{2,1},{3,2},{4,3},{5,4},{6,5},{7,6},{8,7},{9,8},{10,9},{11,1... | collective-permute-start | bytes 417800 | tf_op jit(solution)/shard_map/ppermute | solution.py:18
  91.2 0.1 slice.453
  91.3 0.1 slice.464
  91.4 0.1 slice.470
  91.5 0.1 slice.475
  91.6 0.1 slice.481
  91.8 0.1 slice.492
  92.1 0.1 slice.514
  92.3 4.2 %collective-permute-done.2 = f32[16,8,272]{2,1,0:T(8,128)S(1)} collective-permute-done((f32[16,8,272]{2,1,0:T(8,128)S(1)}, f32[16,8,272]{2,1,0:T(8,128)S(1)}, u32[]{:S(2)}, u32[]{:S(2)}) %collective-permute-start.2) | collective-permute-done | bytes 139296 | tf_op jit(solution)/shard_map/ppermute | solution.py:15
  96.5 0.3 pad_maximum_fusion
  96.8 0.4 fusion.12
  97.2 0.2 fusion.11
  97.4 1.4 %slice_subtract_fusion.10 = f32[16,46,270]{2,1,0:T(8,128)S(1)} fusion(f32[16,47,272]{2,1,0:T(8,128)S(1)} %fusion.11, f32[16,48,271]{2,1,0:T(8,128)S(1)} %fusion.12, f32[16,48,272]{2,1,0:T(8,128)S(1)} %pad_maximum_fusion), kind=kLoop, calls=%fused_computation.28 | loop fusion | flops 794880 | bytes 4769280 | tf_op jit(solution)/shard_map/sub | solution.py:27
  98.8 0.4 fusion.10
  99.2 0.2 fusion.9
  99.4 1.4 %slice_subtract_fusion.6 = f32[16,44,268]{2,1,0:T(8,128)S(1)} fusion(f32[16,45,270]{2,1,0:T(8,128)S(1)} %fusion.9, f32[16,46,269]{2,1,0:T(8,128)S(1)} %fusion.10, f32[16,46,270]{2,1,0:T(8,128)S(1)} %slice_subtract_fusion.10), kind=kLoop, calls=%fused_computation.20 | loop fusion | flops 754688 | bytes 4528128 | tf_op jit(solution)/shard_map/sub | solution.py:27
  100.8 0.4 fusion.8
  101.2 0.2 fusion.7
  101.4 1.4 %slice_subtract_fusion.2 = f32[16,42,266]{2,1,0:T(8,128)S(1)} fusion(f32[16,43,268]{2,1,0:T(8,128)S(1)} %fusion.7, f32[16,44,267]{2,1,0:T(8,128)S(1)} %fusion.8, f32[16,44,268]{2,1,0:T(8,128)S(1)} %slice_subtract_fusion.6), kind=kLoop, calls=%fused_computation.12 | loop fusion | flops 715008 | bytes 4290048 | tf_op jit(solution)/shard_map/sub | solution.py:27
  102.8 0.4 fusion.6
  103.2 0.2 fusion.5
  103.4 1.2 %slice_subtract_fusion.28 = f32[16,40,264]{2,1,0:T(8,128)S(1)} fusion(f32[16,41,266]{2,1,0:T(8,128)S(1)} %fusion.5, f32[16,42,265]{2,1,0:T(8,128)S(1)} %fusion.6, f32[16,42,266]{2,1,0:T(8,128)S(1)} %slice_subtract_fusion.2), kind=kLoop, calls=%fused_computation.65 | loop fusion | flops 675840 | bytes 4055040 | tf_op jit(solution)/shard_map/sub | solution.py:27
  104.6 0.3 fusion.20
  104.9 0.1 fusion.19
  105.0 1.2 %slice_subtract_fusion.24 = f32[16,38,262]{2,1,0:T(8,128)S(1)} fusion(f32[16,39,264]{2,1,0:T(8,128)S(1)} %fusion.19, f32[16,40,263]{2,1,0:T(8,128)S(1)} %fusion.20, f32[16,40,264]{2,1,0:T(8,128)S(1)} %slice_subtract_fusion.28), kind=kLoop, calls=%fused_computation.57 | loop fusion | flops 637184 | bytes 3823104 | tf_op jit(solution)/shard_map/sub | solution.py:27
  106.3 0.3 fusion.18
  106.6 0.1 fusion.17
  106.7 1.2 %slice_subtract_fusion.20 = f32[16,36,260]{2,1,0:T(8,128)S(1)} fusion(f32[16,37,262]{2,1,0:T(8,128)S(1)} %fusion.17, f32[16,38,261]{2,1,0:T(8,128)S(1)} %fusion.18, f32[16,38,262]{2,1,0:T(8,128)S(1)} %slice_subtract_fusion.24), kind=kLoop, calls=%fused_computation.49 | loop fusion | flops 599040 | bytes 3594240 | tf_op jit(solution)/shard_map/sub | solution.py:27
  107.9 0.3 fusion.16
  108.3 0.1 fusion.15
  108.4 1.2 %slice_subtract_fusion.16 = f32[16,34,258]{2,1,0:T(8,128)S(1)} fusion(f32[16,35,260]{2,1,0:T(8,128)S(1)} %fusion.15, f32[16,36,259]{2,1,0:T(8,128)S(1)} %fusion.16, f32[16,36,260]{2,1,0:T(8,128)S(1)} %slice_subtract_fusion.20), kind=kLoop, calls=%fused_computation.41 | loop fusion | flops 561408 | bytes 3368448 | tf_op jit(solution)/shard_map/sub | solution.py:27
  109.6 0.3 fusion.14
  109.9 0.1 fusion.13
  110.1 1.5 %slice_subtract_fusion.30 = f32[16,32,256]{2,1,0:T(8,128)} fusion(f32[16,33,258]{2,1,0:T(8,128)S(1)} %fusion.13, f32[16,34,257]{2,1,0:T(8,128)S(1)} %fusion.14, f32[16,34,258]{2,1,0:T(8,128)S(1)} %slice_subtract_fusion.16), kind=kLoop, calls=%fused_computation.69 | loop fusion | flops 524288 | bytes 3145728 | tf_op jit(solution)/shard_map/sub | solution.py:27
  (38 shorter events, 0.9 us)
Async XLA Ops:
  0.0 18.3 %copy-start = (s32[1,16]{1,0:T(1,128)S(1)}, s32[1,16]{1,0:T(1,128)}, u32[]{:S(2)}) copy-start(s32[1,16]{1,0:T(1,128)} %param.13) | copy-start | bytes 196
  0.0 6.6 %copy-start.4 = (f32[16,1,4096]{2,1,0:T(1,128)S(1)}, f32[16,1,4096]{2,1,0:T(1,128)}, u32[]{:S(2)}) copy-start(f32[16,1,4096]{2,1,0:T(1,128)} %param.15) | copy-start | bytes 786436
  1.7 16.8 %collective-permute-start.4 = (f32[3,32,8]{2,1,0:T(8,128)S(1)}, f32[3,32,8]{2,1,0:T(8,128)S(1)}, u32[]{:S(2)}, u32[]{:S(2)}) collective-permute-start(f32[3,32,8]{2,1,0:T(8,128)S(1)} %get-tuple-element.13), channel_id=1, source_target_pairs={{0,16},{16,32},{32,48},{48,64},{64,80},{80,96},{96,112},{112,128},... | collective-permute-start | bytes 9224 | tf_op jit(solution)/shard_map/ppermute | solution.py:15
  4.7 13.7 %collective-permute-start.5 = (f32[3,32,8]{2,1,0:T(8,128)S(1)}, f32[3,32,8]{2,1,0:T(8,128)S(1)}, u32[]{:S(2)}, u32[]{:S(2)}) collective-permute-start(f32[3,32,8]{2,1,0:T(8,128)S(1)} %get-tuple-element.14), channel_id=1, source_target_pairs={{16,0},{32,16},{48,32},{64,48},{80,64},{96,80},{112,96},{128,112},... | collective-permute-start | bytes 9224 | tf_op jit(solution)/shard_map/ppermute | solution.py:18
  7.4 10.8 %copy-start.5 = (s32[1,4096]{1,0:T(1,128)S(1)}, s32[1,4096]{1,0:T(1,128)}, u32[]{:S(2)}) copy-start(s32[1,4096]{1,0:T(1,128)} %param.12) | copy-start | bytes 49156
  7.4 11.0 %copy-start.2 = (f32[32,256]{1,0:T(8,128)S(1)}, f32[32,256]{1,0:T(8,128)}, u32[]{:S(2)}) copy-start(f32[32,256]{1,0:T(8,128)} %param.10) | copy-start | bytes 98308
  7.4 11.0 %copy-start.3 = (f32[32,256]{1,0:T(8,128)S(1)}, f32[32,256]{1,0:T(8,128)}, u32[]{:S(2)}) copy-start(f32[32,256]{1,0:T(8,128)} %param.9) | copy-start | bytes 98308
  7.4 16.2 %copy-start.1 = (f32[16,32,256]{2,1,0:T(8,128)S(1)}, f32[16,32,256]{2,1,0:T(8,128)}, u32[]{:S(2)}) copy-start(f32[16,32,256]{2,1,0:T(8,128)} %param.8) | copy-start | bytes 1572868
  8.6 34.2 %all-to-all-start = ((f32[16,16,512]{2,0,1:T(8,128)}), f32[16,16,512]{2,0,1:T(8,128)S(1)}, u32[]{:S(2)}, u32[]{:S(2)}) async-start(f32[16,16,512]{2,0,1:T(8,128)} %copy.17), calls=%async_computation | async-start | bytes 1048576 | tf_op jit(solution)/shard_map/all_to_all | solution.py:50
  18.6 24.0 %collective-permute-start.6 = (f32[3,8,272]{2,1,0:T(8,128)S(1)}, f32[3,8,272]{2,1,0:T(8,128)S(1)}, u32[]{:S(2)}, u32[]{:S(2)}) collective-permute-start(f32[3,8,272]{2,1,0:T(8,128)S(1)} %get-tuple-element.11), channel_id=1, source_target_pairs={{0,1},{1,2},{2,3},{3,4},{4,5},{5,6},{6,7},{7,8},{8,9},{9,10},{10,1... | collective-permute-start | bytes 78344 | tf_op jit(solution)/shard_map/ppermute | solution.py:15
  20.0 22.6 %collective-permute-start.7 = (f32[3,8,272]{2,1,0:T(8,128)S(1)}, f32[3,8,272]{2,1,0:T(8,128)S(1)}, u32[]{:S(2)}, u32[]{:S(2)}) collective-permute-start(f32[3,8,272]{2,1,0:T(8,128)S(1)} %get-tuple-element.12), channel_id=1, source_target_pairs={{1,0},{2,1},{3,2},{4,3},{5,4},{6,5},{7,6},{8,7},{9,8},{10,9},{11,1... | collective-permute-start | bytes 78344 | tf_op jit(solution)/shard_map/ppermute | solution.py:18
  78.4 5.3 %collective-permute-start = (f32[16,32,8]{2,1,0:T(8,128)S(1)}, f32[16,32,8]{2,1,0:T(8,128)S(1)}, u32[]{:S(2)}, u32[]{:S(2)}) collective-permute-start(f32[16,32,8]{2,1,0:T(8,128)S(1)} %get-tuple-element.7), channel_id=1, source_target_pairs={{0,16},{16,32},{32,48},{48,64},{64,80},{80,96},{96,112},{112,128},... | collective-permute-start | bytes 49160 | tf_op jit(solution)/shard_map/ppermute | solution.py:15
  80.3 5.8 %collective-permute-start.1 = (f32[16,32,8]{2,1,0:T(8,128)S(1)}, f32[16,32,8]{2,1,0:T(8,128)S(1)}, u32[]{:S(2)}, u32[]{:S(2)}) collective-permute-start(f32[16,32,8]{2,1,0:T(8,128)S(1)} %get-tuple-element.8), channel_id=1, source_target_pairs={{16,0},{32,16},{48,32},{64,48},{80,64},{96,80},{112,96},{128,112},... | collective-permute-start | bytes 49160 | tf_op jit(solution)/shard_map/ppermute | solution.py:18
  86.3 10.2 %collective-permute-start.2 = (f32[16,8,272]{2,1,0:T(8,128)S(1)}, f32[16,8,272]{2,1,0:T(8,128)S(1)}, u32[]{:S(2)}, u32[]{:S(2)}) collective-permute-start(f32[16,8,272]{2,1,0:T(8,128)S(1)} %get-tuple-element.5), channel_id=1, source_target_pairs={{0,1},{1,2},{2,3},{3,4},{4,5},{5,6},{6,7},{7,8},{8,9},{9,10},{10,1... | collective-permute-start | bytes 417800 | tf_op jit(solution)/shard_map/ppermute | solution.py:15
  86.4 10.1 %collective-permute-start.3 = (f32[16,8,272]{2,1,0:T(8,128)S(1)}, f32[16,8,272]{2,1,0:T(8,128)S(1)}, u32[]{:S(2)}, u32[]{:S(2)}) collective-permute-start(f32[16,8,272]{2,1,0:T(8,128)S(1)} %get-tuple-element.6), channel_id=1, source_target_pairs={{1,0},{2,1},{3,2},{4,3},{5,4},{6,5},{7,6},{8,7},{9,8},{10,9},{11,1... | collective-permute-start | bytes 417800 | tf_op jit(solution)/shard_map/ppermute | solution.py:18

commit v4 on v3

--- a/solution.py
+++ b/solution.py
@@ -1,9 +1,90 @@
 import jax
 import jax.numpy as jnp
 from jax import lax
+from jax.experimental import pallas as pl
+from jax.experimental.pallas import tpu as pltpu
 from jax.sharding import PartitionSpec as P
 
 PASSES = 8
+CHUNK = 512
+
+
+def three_parts(x):
+    high = x.astype(jnp.bfloat16)
+    rest = x - high.astype(jnp.float32)
+    middle = rest.astype(jnp.bfloat16)
+    low = (rest - middle.astype(jnp.float32)).astype(jnp.bfloat16)
+    return high, middle, low
+
+
+def scatter_kernel(w_ref, rows_ref, cols_ref, out_ref):
+    levels, slots = w_ref.shape
+    cells, cols_here = out_ref.shape
+    rows_here = cells // levels
+    out_ref[...] = jnp.zeros_like(out_ref)
+
+    def step(k, carry):
+        start = pl.multiple_of(k * CHUNK, CHUNK)
+        w = w_ref[:, pl.ds(start, CHUNK)]
+        row_hit = lax.broadcasted_iota(jnp.int32, (rows_here, CHUNK), 0) == rows_ref[:, pl.ds(start, CHUNK)]
+        col_hit = lax.broadcasted_iota(jnp.int32, (cols_here, CHUNK), 0) == cols_ref[:, pl.ds(start, CHUNK)]
+        col_hit = col_hit.astype(jnp.float32).astype(jnp.bfloat16)
+        for part in three_parts(w):
+            spread = jnp.where(row_hit[None], part.astype(jnp.float32)[:, None, :], 0.0)
+            spread = spread.reshape(cells, CHUNK).astype(jnp.bfloat16)
+            out_ref[...] += lax.dot_general(
+                spread, col_hit, (((1,), (1,)), ((), ())), preferred_element_type=jnp.float32
+            )
+        return carry
+
+    lax.fori_loop(0, slots // CHUNK, step, 0)
+
+
+def gather_kernel(state_ref, rows_ref, cols_ref, out_ref):
+    levels, slots = out_ref.shape
+    cells, cols_here = state_ref.shape
+    rows_here = cells // levels
+    parts = three_parts(state_ref[...])
+
+    def step(k, carry):
+        start = pl.multiple_of(k * CHUNK, CHUNK)
+        col_hit = lax.broadcasted_iota(jnp.int32, (cols_here, CHUNK), 0) == cols_ref[:, pl.ds(start, CHUNK)]
+        col_hit = col_hit.astype(jnp.float32).astype(jnp.bfloat16)
+        picked = None
+        for part in parts:
+            term = jnp.dot(part, col_hit, preferred_element_type=jnp.float32)
+            picked = term if picked is None else picked + term
+        row_hit = lax.broadcasted_iota(jnp.int32, (rows_here, CHUNK), 0) == rows_ref[:, pl.ds(start, CHUNK)]
+        chosen = jnp.where(row_hit[None], picked.reshape(levels, rows_here, CHUNK), 0.0)
+        out_ref[:, pl.ds(start, CHUNK)] = jnp.sum(chosen, axis=1)
+        return carry
+
+    lax.fori_loop(0, slots // CHUNK, step, 0)
+
+
+def vmem_call(kernel, out_shape, flops, nbytes):
+    return pl.pallas_call(
+        kernel,
+        out_shape=out_shape,
+        in_specs=[pl.BlockSpec(memory_space=pltpu.VMEM)] * 3,
+        out_specs=pl.BlockSpec(memory_space=pltpu.VMEM),
+        cost_estimate=pl.CostEstimate(flops=flops, bytes_accessed=nbytes, transcendentals=0),
+    )
+
+
+def onehot_scatter(w, rows, cols, rows_here, cols_here):
+    levels, slots = w.shape
+    shape = jax.ShapeDtypeStruct((levels * rows_here, cols_here), jnp.float32)
+    flops = 6 * levels * rows_here * cols_here * slots
+    return vmem_call(scatter_kernel, shape, flops, 4 * (levels * slots + 2 * slots + levels * rows_here * cols_here))(w, rows, cols)
+
+
+def onehot_gather(state2d, rows, cols, levels):
+    cells, cols_here = state2d.shape
+    slots = rows.shape[1]
+    shape = jax.ShapeDtypeStruct((levels, slots), jnp.float32)
+    flops = 6 * cells * cols_here * slots
+    return vmem_call(gather_kernel, shape, flops, 4 * (levels * slots + 2 * slots + cells * cols_here))(state2d, rows, cols)
 
 
 def with_halo(block, sides, width):
@@ -38,7 +119,6 @@
     lat_count = lax.axis_size("lat")
     slots = send_cols.shape[1]
     capacity = slots // lon_count
-    columns = state.reshape(levels, rows_here * cols_here)
     targets = send_cols[0]
     slot_index = jnp.arange(slots, dtype=jnp.int32)
     limits = jnp.broadcast_to(send_count[0][:, None], (lon_count, capacity)).reshape(slots)
@@ -51,10 +131,12 @@
     at_owner = at_owner.reshape(levels, lon_count, 2 * capacity)
     values = at_owner[:, :, :capacity].reshape(levels, slots)
     weights = at_owner[:, :, capacity:].reshape(levels, slots)
-    at_column = jnp.take(columns, targets, axis=1)
-    weighted = lax.optimization_barrier(weights * (values - at_column) * usable)
+    target_rows = (targets // cols_here)[None, :]
+    target_cols = (targets % cols_here)[None, :]
+    at_column = onehot_gather(state.reshape(levels * rows_here, cols_here), target_rows, target_cols, levels)
+    weighted = weights * (values - at_column) * usable
     sea = land_sea.astype(jnp.float32)
-    gradient = jnp.zeros((levels, rows_here * cols_here), jnp.float32).at[:, targets].add(weighted)
+    gradient = onehot_scatter(weighted, target_rows, target_cols, rows_here, cols_here)
     gradient = gradient.reshape(levels, rows_here, cols_here) * sea[None]
     rim_width = PASSES
     stacked = jnp.stack([sea, coef_lon, coef_lat])

time: 112 us -> 77.3 us (0.69)
  the two profiles are of different devices: /device:TPU:1 before, /device:TPU:30 now
where the time goes in v4:
time: 77.3 us; the launch traced here: 77 us
  other arithmetic  21 us (27%)
  waiting for transfers between devices  19.7 us (25%)
  starting transfers between devices  18.7 us (24%)
  Pallas kernels  13.6 us (18%)
  local copies, waits for them, and re-layouts  3.58 us (5%)
    ppermute x4, waiting for transfers between devices, with_halo(): lax.ppermute(lax.slice_in_dim(block, block.shape[dim] - width, None, axis...  12.6 us
    sub x8, other arithmetic, one_pass(): layer_field[:, 1:-1, 1:-1] + flux_east[:, 1:-1, 1:]  10.6 us
    ppermute x4, starting transfers between devices, with_halo(): lax.ppermute(lax.slice_in_dim(block, 0, width, axis=dim), axis, backward)  9.4 us
    all_to_all x1, starting transfers between devices, body(): lax.all_to_all(held, 'lon', split_axis=1, concat_axis=1, tiled=True)  8.57 us
    ppermute x4, waiting for transfers between devices, with_halo(): lax.ppermute(lax.slice_in_dim(block, 0, width, axis=dim), axis, backward)  7.05 us
    pallas_call x1, Pallas kernels, onehot_scatter(): vmem_call(scatter_kernel, shape, flops, 4 * (levels * slots + 2 * slots +...  6.98 us
    pallas_call x1, Pallas kernels, onehot_gather(): vmem_call(gather_kernel, shape, flops, 4 * (levels * slots + 2 * slots +...  6.64 us
    mul x8, other arithmetic, one_pass(): flux_east = east_face * (layer_field[:, :, 1:] - layer_field[:, :, :-1])  2.79 us
  transfers between devices with their start and end apart: 9, of which 6 were waited for; matrix products, arithmetic and copies ran while one was open for 4% of the time, Pallas kernels for 9%

profile of v4, /device:TPU:30, one launch (start us, length us, event | category | flops | bytes accessed | tf_op | source)
XLA Modules:
  0.0 77.0 jit_solution(14965367699125554788)
XLA Ops:
  0.0 1.6 %reduce = f32[16,4096]{1,0:T(8,128)S(1)} reduce(f32[16,1,4096]{2,1,0:T(1,128)} %param.14, f32[]{:T(128)} %constant.52), dimensions={1}, to_apply=%param.14.reduce_sub_computation | reduce | bytes 524292 | tf_op args[6]
  1.6 0.1 copy.16
  1.7 0.6 reduce.1
  2.4 0.1 copy.17
  2.6 1.1 %copy.11 = f32[16,16,512]{2,0,1:T(8,128)} copy(f32[16,16,512]{2,1,0:T(8,128)S(1)} %pad_maximum_fusion.1) | data formatting | bytes 1048576 | tf_op jit(solution)/shard_map/concatenate | solution.py:127
  3.7 8.6 %all-to-all-start = ((f32[16,16,512]{2,0,1:T(8,128)}), f32[16,16,512]{2,0,1:T(8,128)S(1)}, u32[]{:S(2)}, u32[]{:S(2)}) async-start(f32[16,16,512]{2,0,1:T(8,128)} %copy.11), calls=%async_computation | async-start | bytes 1048576 | tf_op jit(solution)/shard_map/all_to_all | solution.py:130
  12.4 0.4 collective-permute-start.4
  12.8 2.6 %collective-permute-start.5 = (f32[3,32,8]{2,1,0:T(8,128)S(1)}, f32[3,32,8]{2,1,0:T(8,128)S(1)}, u32[]{:S(2)}, u32[]{:S(2)}) collective-permute-start(f32[3,32,8]{2,1,0:T(8,128)S(1)} %get-tuple-element.16), channel_id=1, source_target_pairs={{16,0},{32,16},{48,32},{64,48},{80,64},{96,80},{112,96},{128,112},... | collective-permute-start | bytes 9224 | tf_op jit(solution)/shard_map/ppermute | solution.py:99
  15.4 0.7 and_select_fusion
  16.0 0.7 and_select_fusion.1.rows_ref
  16.8 6.6 %shard_map.82 = f32[16,4096]{1,0:T(8,128)} custom-call(f32[512,256]{1,0:T(8,128)} %bitcast.45, s32[1,4096]{1,0:T(1,128)} %and_select_fusion.1.rows_ref, s32[1,4096]{1,0:T(1,128)} %get-tuple-element.5.cols_ref), custom_call_target="tpu_custom_call" | custom-call | flops 3221225472 | bytes 819200 | tf_op jit(solution)/shard_map/pallas_call | solution.py:87
  23.4 4.3 %collective-permute-done.4 = f32[3,32,8]{2,1,0:T(8,128)S(1)} collective-permute-done((f32[3,32,8]{2,1,0:T(8,128)S(1)}, f32[3,32,8]{2,1,0:T(8,128)S(1)}, u32[]{:S(2)}, u32[]{:S(2)}) %collective-permute-start.4) | collective-permute-done | bytes 3104 | tf_op jit(solution)/shard_map/ppermute | solution.py:96
  27.8 0.1 pad_maximum_fusion.11
  27.9 0.2 collective-permute-start.6
  28.1 1.9 %collective-permute-start.7 = (f32[3,8,272]{2,1,0:T(8,128)S(1)}, f32[3,8,272]{2,1,0:T(8,128)S(1)}, u32[]{:S(2)}, u32[]{:S(2)}) collective-permute-start(f32[3,8,272]{2,1,0:T(8,128)S(1)} %get-tuple-element.14), channel_id=1, source_target_pairs={{1,0},{2,1},{3,2},{4,3},{5,4},{6,5},{7,6},{8,7},{9,8},{10,9},{11,1... | collective-permute-start | bytes 78344 | tf_op jit(solution)/shard_map/ppermute | solution.py:99
  30.0 1.9 %collective-permute-done.6 = f32[3,8,272]{2,1,0:T(8,128)S(1)} collective-permute-done((f32[3,8,272]{2,1,0:T(8,128)S(1)}, f32[3,8,272]{2,1,0:T(8,128)S(1)}, u32[]{:S(2)}, u32[]{:S(2)}) %collective-permute-start.6) | collective-permute-done | bytes 26144 | tf_op jit(solution)/shard_map/ppermute | solution.py:96
  31.9 3.5 %collective-permute-done.7 = f32[3,8,272]{2,1,0:T(8,128)S(1)} collective-permute-done((f32[3,8,272]{2,1,0:T(8,128)S(1)}, f32[3,8,272]{2,1,0:T(8,128)S(1)}, u32[]{:S(2)}, u32[]{:S(2)}) %collective-permute-start.7) | collective-permute-done | bytes 26144 | tf_op jit(solution)/shard_map/ppermute | solution.py:99
  35.3 0.1 pad_maximum_fusion.2
  35.7 0.7 copy-done.4
  36.4 0.8 multiply_multiply_fusion.w_ref
  37.2 7.0 %shard_map.83 = f32[512,256]{1,0:T(8,128)} custom-call(f32[16,4096]{1,0:T(8,128)} %multiply_multiply_fusion.w_ref, s32[1,4096]{1,0:T(1,128)} %and_select_fusion.1.rows_ref, s32[1,4096]{1,0:T(1,128)} %get-tuple-element.5.cols_ref), custom_call_target="tpu_custom_call" | custom-call | flops 3221225472 | bytes 819200 | tf_op jit(solution)/shard_map/pallas_call | solution.py:79
  44.2 1.1 %broadcast_multiply_fusion = f32[16,32,256]{2,1,0:T(8,128)S(1)} fusion(f32[16,32,256]{2,1,0:T(8,128)} %bitcast.37, f32[32,256]{1,0:T(8,128)S(1)} %get-tuple-element.18), kind=kLoop, calls=%fused_computation.68 | loop fusion | flops 131072 | bytes 1081344 | tf_op jit(solution)/shard_map/mul | solution.py:140
  45.3 0.1 fusion.22
  45.4 2.9 %collective-permute-start.1 = (f32[16,32,8]{2,1,0:T(8,128)S(1)}, f32[16,32,8]{2,1,0:T(8,128)S(1)}, u32[]{:S(2)}, u32[]{:S(2)}) collective-permute-start(f32[16,32,8]{2,1,0:T(8,128)S(1)} %get-tuple-element.10), channel_id=1, source_target_pairs={{16,0},{32,16},{48,32},{64,48},{80,64},{96,80},{112,96},{128,112},... | collective-permute-start | bytes 49160 | tf_op jit(solution)/shard_map/ppermute | solution.py:99
  48.5 0.1 slice.446
  48.5 0.1 slice.457
  48.6 3.8 %collective-permute-done = f32[16,32,8]{2,1,0:T(8,128)S(1)} collective-permute-done((f32[16,32,8]{2,1,0:T(8,128)S(1)}, f32[16,32,8]{2,1,0:T(8,128)S(1)}, u32[]{:S(2)}, u32[]{:S(2)}) %collective-permute-start) | collective-permute-done | bytes 16416 | tf_op jit(solution)/shard_map/ppermute | solution.py:96
  52.4 0.2 pad_maximum_fusion.5
  52.6 0.1 collective-permute-start.2
  52.7 2.0 %collective-permute-start.3 = (f32[16,8,272]{2,1,0:T(8,128)S(1)}, f32[16,8,272]{2,1,0:T(8,128)S(1)}, u32[]{:S(2)}, u32[]{:S(2)}) collective-permute-start(f32[16,8,272]{2,1,0:T(8,128)S(1)} %get-tuple-element.8), channel_id=1, source_target_pairs={{1,0},{2,1},{3,2},{4,3},{5,4},{6,5},{7,6},{8,7},{9,8},{10,9},{11,1... | collective-permute-start | bytes 417800 | tf_op jit(solution)/shard_map/ppermute | solution.py:99
  54.7 0.1 slice.451
  54.8 0.1 slice.462
  54.9 0.1 slice.468
  55.0 0.1 slice.473
  55.1 0.1 slice.479
  55.2 0.1 slice.484
  55.5 0.1 slice.501
  55.8 2.6 %collective-permute-done.2 = f32[16,8,272]{2,1,0:T(8,128)S(1)} collective-permute-done((f32[16,8,272]{2,1,0:T(8,128)S(1)}, f32[16,8,272]{2,1,0:T(8,128)S(1)}, u32[]{:S(2)}, u32[]{:S(2)}) %collective-permute-start.2) | collective-permute-done | bytes 139296 | tf_op jit(solution)/shard_map/ppermute | solution.py:96
  58.4 3.6 %collective-permute-done.3 = f32[16,8,272]{2,1,0:T(8,128)S(1)} collective-permute-done((f32[16,8,272]{2,1,0:T(8,128)S(1)}, f32[16,8,272]{2,1,0:T(8,128)S(1)}, u32[]{:S(2)}, u32[]{:S(2)}) %collective-permute-start.3) | collective-permute-done | bytes 139296 | tf_op jit(solution)/shard_map/ppermute | solution.py:99
  62.0 0.3 pad_maximum_fusion
  62.3 0.4 fusion.7
  62.7 0.2 fusion.6
  62.9 1.4 %slice_subtract_fusion.10 = f32[16,46,270]{2,1,0:T(8,128)S(1)} fusion(f32[16,47,272]{2,1,0:T(8,128)S(1)} %fusion.6, f32[16,48,271]{2,1,0:T(8,128)S(1)} %fusion.7, f32[16,48,272]{2,1,0:T(8,128)S(1)} %pad_maximum_fusion), kind=kLoop, calls=%fused_computation.20 | loop fusion | flops 794880 | bytes 4769280 | tf_op jit(solution)/shard_map/sub | solution.py:108
  64.3 0.4 fusion.5
  64.7 0.2 fusion.4
  64.8 1.4 %slice_subtract_fusion.6 = f32[16,44,268]{2,1,0:T(8,128)S(1)} fusion(f32[16,45,270]{2,1,0:T(8,128)S(1)} %fusion.4, f32[16,46,269]{2,1,0:T(8,128)S(1)} %fusion.5, f32[16,46,270]{2,1,0:T(8,128)S(1)} %slice_subtract_fusion.10), kind=kLoop, calls=%fused_computation.12 | loop fusion | flops 754688 | bytes 4528128 | tf_op jit(solution)/shard_map/sub | solution.py:108
  66.3 0.4 fusion.3
  66.7 0.2 fusion.2
  66.8 1.4 %slice_subtract_fusion.2 = f32[16,42,266]{2,1,0:T(8,128)S(1)} fusion(f32[16,43,268]{2,1,0:T(8,128)S(1)} %fusion.2, f32[16,44,267]{2,1,0:T(8,128)S(1)} %fusion.3, f32[16,44,268]{2,1,0:T(8,128)S(1)} %slice_subtract_fusion.6), kind=kLoop, calls=%fused_computation.4 | loop fusion | flops 715008 | bytes 4290048 | tf_op jit(solution)/shard_map/sub | solution.py:108
  68.3 0.4 fusion.1
  68.7 0.2 fusion
  68.8 1.2 %slice_subtract_fusion.28 = f32[16,40,264]{2,1,0:T(8,128)S(1)} fusion(f32[16,41,266]{2,1,0:T(8,128)S(1)} %fusion, f32[16,42,265]{2,1,0:T(8,128)S(1)} %fusion.1, f32[16,42,266]{2,1,0:T(8,128)S(1)} %slice_subtract_fusion.2), kind=kLoop, calls=%fused_computation.57 | loop fusion | flops 675840 | bytes 4055040 | tf_op jit(solution)/shard_map/sub | solution.py:108
  70.0 0.3 fusion.15
  70.4 0.1 fusion.14
  70.5 1.2 %slice_subtract_fusion.24 = f32[16,38,262]{2,1,0:T(8,128)S(1)} fusion(f32[16,39,264]{2,1,0:T(8,128)S(1)} %fusion.14, f32[16,40,263]{2,1,0:T(8,128)S(1)} %fusion.15, f32[16,40,264]{2,1,0:T(8,128)S(1)} %slice_subtract_fusion.28), kind=kLoop, calls=%fused_computation.49 | loop fusion | flops 637184 | bytes 3823104 | tf_op jit(solution)/shard_map/sub | solution.py:108
  71.7 0.3 fusion.13
  72.1 0.1 fusion.12
  72.2 1.2 %slice_subtract_fusion.20 = f32[16,36,260]{2,1,0:T(8,128)S(1)} fusion(f32[16,37,262]{2,1,0:T(8,128)S(1)} %fusion.12, f32[16,38,261]{2,1,0:T(8,128)S(1)} %fusion.13, f32[16,38,262]{2,1,0:T(8,128)S(1)} %slice_subtract_fusion.24), kind=kLoop, calls=%fused_computation.41 | loop fusion | flops 599040 | bytes 3594240 | tf_op jit(solution)/shard_map/sub | solution.py:108
  73.4 0.3 fusion.11
  73.7 0.1 fusion.10
  73.9 1.2 %slice_subtract_fusion.16 = f32[16,34,258]{2,1,0:T(8,128)S(1)} fusion(f32[16,35,260]{2,1,0:T(8,128)S(1)} %fusion.10, f32[16,36,259]{2,1,0:T(8,128)S(1)} %fusion.11, f32[16,36,260]{2,1,0:T(8,128)S(1)} %slice_subtract_fusion.20), kind=kLoop, calls=%fused_computation.33 | loop fusion | flops 561408 | bytes 3368448 | tf_op jit(solution)/shard_map/sub | solution.py:108
  75.1 0.3 fusion.9
  75.4 0.1 fusion.8
  75.6 1.5 %slice_subtract_fusion.30 = f32[16,32,256]{2,1,0:T(8,128)} fusion(f32[16,33,258]{2,1,0:T(8,128)S(1)} %fusion.8, f32[16,34,257]{2,1,0:T(8,128)S(1)} %fusion.9, f32[16,34,258]{2,1,0:T(8,128)S(1)} %slice_subtract_fusion.16), kind=kLoop, calls=%fused_computation.61 | loop fusion | flops 524288 | bytes 3145728 | tf_op jit(solution)/shard_map/sub | solution.py:108
  (37 shorter events, 1.0 us)
Async XLA Ops:
  0.0 16.7 %copy-start = (s32[1,16]{1,0:T(1,128)S(1)}, s32[1,16]{1,0:T(1,128)}, u32[]{:S(2)}) copy-start(s32[1,16]{1,0:T(1,128)} %param.13) | copy-start | bytes 196
  0.0 1.7 %copy-start.3 = (f32[16,1,4096]{2,1,0:T(1,128)S(1)}, f32[16,1,4096]{2,1,0:T(1,128)}, u32[]{:S(2)}) copy-start(f32[16,1,4096]{2,1,0:T(1,128)} %param.15) | copy-start | bytes 786436
  2.5 9.7 %copy-start.6 = (s32[32,256]{1,0:T(8,128)S(1)}, s32[32,256]{1,0:T(8,128)}, u32[]{:S(2)}) copy-start(s32[32,256]{1,0:T(8,128)} %param.11) | copy-start | bytes 98308
  2.6 9.7 %copy-start.1 = (f32[32,256]{1,0:T(8,128)S(1)}, f32[32,256]{1,0:T(8,128)}, u32[]{:S(2)}) copy-start(f32[32,256]{1,0:T(8,128)} %param.10) | copy-start | bytes 98308
  2.6 9.7 %copy-start.2 = (f32[32,256]{1,0:T(8,128)S(1)}, f32[32,256]{1,0:T(8,128)}, u32[]{:S(2)}) copy-start(f32[32,256]{1,0:T(8,128)} %param.9) | copy-start | bytes 98308
  2.6 12.8 %copy-start.5 = (s32[1,4096]{1,0:T(1,128)S(1)}, s32[1,4096]{1,0:T(1,128)}, u32[]{:S(2)}) copy-start(s32[1,4096]{1,0:T(1,128)} %param.12) | copy-start | bytes 49156
  3.7 31.9 %all-to-all-start = ((f32[16,16,512]{2,0,1:T(8,128)}), f32[16,16,512]{2,0,1:T(8,128)S(1)}, u32[]{:S(2)}, u32[]{:S(2)}) async-start(f32[16,16,512]{2,0,1:T(8,128)} %copy.11), calls=%async_computation | async-start | bytes 1048576 | tf_op jit(solution)/shard_map/all_to_all | solution.py:130
  12.4 15.3 %collective-permute-start.4 = (f32[3,32,8]{2,1,0:T(8,128)S(1)}, f32[3,32,8]{2,1,0:T(8,128)S(1)}, u32[]{:S(2)}, u32[]{:S(2)}) collective-permute-start(f32[3,32,8]{2,1,0:T(8,128)S(1)} %get-tuple-element.15), channel_id=1, source_target_pairs={{0,16},{16,32},{32,48},{48,64},{64,80},{80,96},{96,112},{112,128},... | collective-permute-start | bytes 9224 | tf_op jit(solution)/shard_map/ppermute | solution.py:96
  12.8 14.9 %collective-permute-start.5 = (f32[3,32,8]{2,1,0:T(8,128)S(1)}, f32[3,32,8]{2,1,0:T(8,128)S(1)}, u32[]{:S(2)}, u32[]{:S(2)}) collective-permute-start(f32[3,32,8]{2,1,0:T(8,128)S(1)} %get-tuple-element.16), channel_id=1, source_target_pairs={{16,0},{32,16},{48,32},{64,48},{80,64},{96,80},{112,96},{128,112},... | collective-permute-start | bytes 9224 | tf_op jit(solution)/shard_map/ppermute | solution.py:99
  27.9 4.0 %collective-permute-start.6 = (f32[3,8,272]{2,1,0:T(8,128)S(1)}, f32[3,8,272]{2,1,0:T(8,128)S(1)}, u32[]{:S(2)}, u32[]{:S(2)}) collective-permute-start(f32[3,8,272]{2,1,0:T(8,128)S(1)} %get-tuple-element.13), channel_id=1, source_target_pairs={{0,1},{1,2},{2,3},{3,4},{4,5},{5,6},{6,7},{7,8},{8,9},{9,10},{10,1... | collective-permute-start | bytes 78344 | tf_op jit(solution)/shard_map/ppermute | solution.py:96
  28.1 7.3 %collective-permute-start.7 = (f32[3,8,272]{2,1,0:T(8,128)S(1)}, f32[3,8,272]{2,1,0:T(8,128)S(1)}, u32[]{:S(2)}, u32[]{:S(2)}) collective-permute-start(f32[3,8,272]{2,1,0:T(8,128)S(1)} %get-tuple-element.14), channel_id=1, source_target_pairs={{1,0},{2,1},{3,2},{4,3},{5,4},{6,5},{7,6},{8,7},{9,8},{10,9},{11,1... | collective-permute-start | bytes 78344 | tf_op jit(solution)/shard_map/ppermute | solution.py:99
  35.5 1.0 %copy-start.4 = (f32[16,4096]{1,0:T(8,128)S(1)}, f32[16,4096]{1,0:T(8,128)}, u32[]{:S(2)}) copy-start(f32[16,4096]{1,0:T(8,128)} %shard_map.82) | copy-start | bytes 786436
  45.4 7.0 %collective-permute-start = (f32[16,32,8]{2,1,0:T(8,128)S(1)}, f32[16,32,8]{2,1,0:T(8,128)S(1)}, u32[]{:S(2)}, u32[]{:S(2)}) collective-permute-start(f32[16,32,8]{2,1,0:T(8,128)S(1)} %get-tuple-element.9), channel_id=1, source_target_pairs={{0,16},{16,32},{32,48},{48,64},{64,80},{80,96},{96,112},{112,128},... | collective-permute-start | bytes 49160 | tf_op jit(solution)/shard_map/ppermute | solution.py:96
  45.4 7.0 %collective-permute-start.1 = (f32[16,32,8]{2,1,0:T(8,128)S(1)}, f32[16,32,8]{2,1,0:T(8,128)S(1)}, u32[]{:S(2)}, u32[]{:S(2)}) collective-permute-start(f32[16,32,8]{2,1,0:T(8,128)S(1)} %get-tuple-element.10), channel_id=1, source_target_pairs={{16,0},{32,16},{48,32},{64,48},{80,64},{96,80},{112,96},{128,112},... | collective-permute-start | bytes 49160 | tf_op jit(solution)/shard_map/ppermute | solution.py:99
  52.6 5.7 %collective-permute-start.2 = (f32[16,8,272]{2,1,0:T(8,128)S(1)}, f32[16,8,272]{2,1,0:T(8,128)S(1)}, u32[]{:S(2)}, u32[]{:S(2)}) collective-permute-start(f32[16,8,272]{2,1,0:T(8,128)S(1)} %get-tuple-element.7), channel_id=1, source_target_pairs={{0,1},{1,2},{2,3},{3,4},{4,5},{5,6},{6,7},{7,8},{8,9},{9,10},{10,1... | collective-permute-start | bytes 417800 | tf_op jit(solution)/shard_map/ppermute | solution.py:96
  52.7 9.2 %collective-permute-start.3 = (f32[16,8,272]{2,1,0:T(8,128)S(1)}, f32[16,8,272]{2,1,0:T(8,128)S(1)}, u32[]{:S(2)}, u32[]{:S(2)}) collective-permute-start(f32[16,8,272]{2,1,0:T(8,128)S(1)} %get-tuple-element.8), channel_id=1, source_target_pairs={{1,0},{2,1},{3,2},{4,3},{5,4},{6,5},{7,6},{8,7},{9,8},{10,9},{11,1... | collective-permute-start | bytes 417800 | tf_op jit(solution)/shard_map/ppermute | solution.py:99

commit v5 on v4

--- a/solution.py
+++ b/solution.py
@@ -139,8 +139,10 @@
     gradient = onehot_scatter(weighted, target_rows, target_cols, rows_here, cols_here)
     gradient = gradient.reshape(levels, rows_here, cols_here) * sea[None]
     rim_width = PASSES
-    stacked = jnp.stack([sea, coef_lon, coef_lat])
+    stacked = jnp.concatenate([gradient, sea[None], coef_lon[None], coef_lat[None]], axis=0)
     padded = with_halo(stacked, (("lon", 2), ("lat", 1)), rim_width)
+    field = padded[:levels]
+    padded = padded[levels:]
     lat_index = lax.axis_index("lat")
     row_place = jnp.arange(rows_here + 2 * rim_width, dtype=jnp.int32)
     outside = (row_place < rim_width) & (lat_index == 0) | (row_place >= rows_here + rim_width) & (
@@ -150,7 +152,6 @@
     sea_rim = padded[0] * inside
     east_face = padded[1][:, :-1] * sea_rim[:, :-1] * sea_rim[:, 1:]
     north_face = padded[2][:-1, :] * sea_rim[:-1, :] * sea_rim[1:, :]
-    field = with_halo(gradient, (("lon", 2), ("lat", 1)), rim_width)
     for step_number in range(PASSES):
         high, wide = field.shape[1], field.shape[2]
         field = one_pass(

time: 77.3 us -> 74.9 us (0.969)
  the two profiles are of different devices: /device:TPU:30 before, /device:TPU:1 now
where the time goes in v5:
time: 74.9 us; the launch traced here: 74.6 us
  other arithmetic  21.3 us (28%)
  waiting for transfers between devices  20.7 us (28%)
  starting transfers between devices  15.8 us (21%)
  Pallas kernels  13.6 us (18%)
  local copies, waits for them, and re-layouts  2.79 us (4%)
    sub x8, other arithmetic, one_pass(): layer_field[:, 1:-1, 1:-1] + flux_east[:, 1:-1, 1:]  10.8 us
    all_to_all x1, starting transfers between devices, body(): lax.all_to_all(held, 'lon', split_axis=1, concat_axis=1, tiled=True)  9.98 us
    all_to_all x1, waiting for transfers between devices, body(): lax.all_to_all(held, 'lon', split_axis=1, concat_axis=1, tiled=True)  9.24 us
    ppermute x2, waiting for transfers between devices, with_halo(): lax.ppermute(lax.slice_in_dim(block, block.shape[dim] - width, None, axis...  9 us
    pallas_call x1, Pallas kernels, onehot_scatter(): vmem_call(scatter_kernel, shape, flops, 4 * (levels * slots + 2 * slots +...  6.99 us
    pallas_call x1, Pallas kernels, onehot_gather(): vmem_call(gather_kernel, shape, flops, 4 * (levels * slots + 2 * slots +...  6.64 us
    ppermute x2, starting transfers between devices, with_halo(): lax.ppermute(lax.slice_in_dim(block, 0, width, axis=dim), axis, backward)  4.4 us
    mul x8, other arithmetic, one_pass(): flux_east = east_face * (layer_field[:, :, 1:] - layer_field[:, :, :-1])  3.01 us
  transfers between devices with their start and end apart: 5, of which 4 were waited for; matrix products, arithmetic and copies ran while one was open for 2% of the time, Pallas kernels for 9%

profile of v5, /device:TPU:1, one launch (start us, length us, event | category | flops | bytes accessed | tf_op | source)
XLA Modules:
  0.0 74.6 jit_solution(4066068076372313853)
XLA Ops:
  0.0 1.6 %reduce = f32[16,4096]{1,0:T(8,128)S(1)} reduce(f32[16,1,4096]{2,1,0:T(1,128)} %param.14, f32[]{:T(128)} %constant.52), dimensions={1}, to_apply=%param.14.reduce_sub_computation | reduce | bytes 524292 | tf_op args[6]
  1.6 0.1 copy.16
  1.7 0.6 reduce.1
  2.4 0.1 copy.17
  2.5 0.1 pad_maximum_fusion.2
  2.6 1.1 %copy.11 = f32[16,16,512]{2,0,1:T(8,128)} copy(f32[16,16,512]{2,1,0:T(8,128)S(1)} %pad_maximum_fusion.2) | data formatting | bytes 1048576 | tf_op jit(solution)/shard_map/concatenate | solution.py:127
  3.7 10.0 %all-to-all-start = ((f32[16,16,512]{2,0,1:T(8,128)}), f32[16,16,512]{2,0,1:T(8,128)S(1)}, u32[]{:S(2)}, u32[]{:S(2)}) async-start(f32[16,16,512]{2,0,1:T(8,128)} %copy.11), calls=%async_computation | async-start | bytes 1048576 | tf_op jit(solution)/shard_map/all_to_all | solution.py:130
  13.7 0.6 and_select_fusion
  14.3 0.1 broadcast_bitcast_fusion
  14.4 0.7 and_select_fusion.1.rows_ref
  15.1 6.6 %shard_map.82 = f32[16,4096]{1,0:T(8,128)} custom-call(f32[512,256]{1,0:T(8,128)} %bitcast.45, s32[1,4096]{1,0:T(1,128)} %and_select_fusion.1.rows_ref, s32[1,4096]{1,0:T(1,128)} %get-tuple-element.5.cols_ref), custom_call_target="tpu_custom_call" | custom-call | flops 3221225472 | bytes 819200 | tf_op jit(solution)/shard_map/pallas_call | solution.py:87
  21.7 9.2 %all-to-all-done = f32[16,16,512]{2,0,1:T(8,128)S(1)} async-done(((f32[16,16,512]{2,0,1:T(8,128)}), f32[16,16,512]{2,0,1:T(8,128)S(1)}, u32[]{:S(2)}, u32[]{:S(2)}) %all-to-all-start) | async-done | bytes 524320 | tf_op jit(solution)/shard_map/all_to_all | solution.py:130
  31.1 0.8 %multiply_multiply_fusion.w_ref = f32[16,4096]{1,0:T(8,128)} fusion(f32[16,4096]{1,0:T(8,128)S(1)} %bitcast.33, f32[16,4096]{1,0:T(8,128)S(1)} %bitcast.35, f32[16,4096]{1,0:T(8,128)S(1)} %copy-done.4, f32[4096]{0:T(1024)S(1)} %fusion.21), kind=kLoop, calls=%fused_computation.70 | loop fusion | flops 196608 | bytes 1064960 | tf_op jit(solution)/shard_map/mul | solution.py:137
  31.9 7.0 %shard_map.83 = f32[512,256]{1,0:T(8,128)} custom-call(f32[16,4096]{1,0:T(8,128)} %multiply_multiply_fusion.w_ref, s32[1,4096]{1,0:T(1,128)} %and_select_fusion.1.rows_ref, s32[1,4096]{1,0:T(1,128)} %get-tuple-element.5.cols_ref), custom_call_target="tpu_custom_call" | custom-call | flops 3221225472 | bytes 819200 | tf_op jit(solution)/shard_map/pallas_call | solution.py:79
  38.8 1.1 %broadcast_multiply_fusion = f32[16,32,256]{2,1,0:T(8,128)S(1)} fusion(f32[16,32,256]{2,1,0:T(8,128)} %bitcast.37, f32[32,256]{1,0:T(8,128)S(1)} %get-tuple-element.13), kind=kLoop, calls=%fused_computation.69 | loop fusion | flops 131072 | bytes 1081344 | tf_op jit(solution)/shard_map/mul | solution.py:140
  40.0 0.1 fusion.22
  40.2 0.5 collective-permute-start.1
  40.7 3.3 %collective-permute-done = f32[19,32,8]{2,1,0:T(8,128)S(1)} collective-permute-done((f32[19,32,8]{2,1,0:T(8,128)S(1)}, f32[19,32,8]{2,1,0:T(8,128)S(1)}, u32[]{:S(2)}, u32[]{:S(2)}) %collective-permute-start) | collective-permute-done | bytes 19488 | tf_op jit(solution)/shard_map/ppermute | solution.py:96
  44.0 2.5 %collective-permute-done.1 = f32[19,32,8]{2,1,0:T(8,128)S(1)} collective-permute-done((f32[19,32,8]{2,1,0:T(8,128)S(1)}, f32[19,32,8]{2,1,0:T(8,128)S(1)}, u32[]{:S(2)}, u32[]{:S(2)}) %collective-permute-start.1) | collective-permute-done | bytes 19488 | tf_op jit(solution)/shard_map/ppermute | solution.py:99
  46.5 0.2 pad_maximum_fusion.8
  46.8 1.4 %collective-permute-start.2 = (f32[19,8,272]{2,1,0:T(8,128)S(1)}, f32[19,8,272]{2,1,0:T(8,128)S(1)}, u32[]{:S(2)}, u32[]{:S(2)}) collective-permute-start(f32[19,8,272]{2,1,0:T(8,128)S(1)} %get-tuple-element.7), channel_id=1, source_target_pairs={{0,1},{1,2},{2,3},{3,4},{4,5},{5,6},{6,7},{7,8},{8,9},{9,10},{10,1... | collective-permute-start | bytes 496136 | tf_op jit(solution)/shard_map/ppermute | solution.py:96
  48.1 3.9 %collective-permute-start.3 = (f32[19,8,272]{2,1,0:T(8,128)S(1)}, f32[19,8,272]{2,1,0:T(8,128)S(1)}, u32[]{:S(2)}, u32[]{:S(2)}) collective-permute-start(f32[19,8,272]{2,1,0:T(8,128)S(1)} %get-tuple-element.8), channel_id=1, source_target_pairs={{1,0},{2,1},{3,2},{4,3},{5,4},{6,5},{7,6},{8,7},{9,8},{10,9},{11,1... | collective-permute-start | bytes 496136 | tf_op jit(solution)/shard_map/ppermute | solution.py:99
  52.0 5.7 %collective-permute-done.2 = f32[19,8,272]{2,1,0:T(8,128)S(1)} collective-permute-done((f32[19,8,272]{2,1,0:T(8,128)S(1)}, f32[19,8,272]{2,1,0:T(8,128)S(1)}, u32[]{:S(2)}, u32[]{:S(2)}) %collective-permute-start.2) | collective-permute-done | bytes 165408 | tf_op jit(solution)/shard_map/ppermute | solution.py:96
  57.7 0.4 pad_maximum_fusion
  58.1 0.1 fusion.16
  58.2 0.1 slice_multiply_fusion.2
  58.3 0.4 fusion.7
  58.7 0.1 slice.438
  58.8 0.2 fusion.6
  58.9 0.1 slice.443
  59.0 0.1 slice.449
  59.1 0.1 slice.454
  59.2 0.1 slice.460
  59.3 0.1 slice.465
  59.4 0.1 slice.471
  59.5 0.1 slice.476
  59.6 0.1 slice.482
  59.7 0.1 slice.487
  59.8 0.1 slice.493
  59.8 0.1 slice.498
  59.9 0.1 slice.504
  60.0 0.1 slice.509
  60.1 1.5 %slice_subtract_fusion.10 = f32[16,46,270]{2,1,0:T(8,128)S(1)} fusion(f32[16,47,272]{2,1,0:T(8,128)S(1)} %fusion.6, f32[16,48,271]{2,1,0:T(8,128)S(1)} %fusion.7, f32[19,48,272]{2,1,0:T(8,128)S(1)} %pad_maximum_fusion), kind=kLoop, calls=%fused_computation.21 | loop fusion | flops 794880 | bytes 4769280 | tf_op jit(solution)/shard_map/sub | solution.py:108
  61.6 0.4 fusion.5
  62.0 0.2 fusion.4
  62.2 1.4 %slice_subtract_fusion.6 = f32[16,44,268]{2,1,0:T(8,128)S(1)} fusion(f32[16,45,270]{2,1,0:T(8,128)S(1)} %fusion.4, f32[16,46,269]{2,1,0:T(8,128)S(1)} %fusion.5, f32[16,46,270]{2,1,0:T(8,128)S(1)} %slice_subtract_fusion.10), kind=kLoop, calls=%fused_computation.13 | loop fusion | flops 754688 | bytes 4528128 | tf_op jit(solution)/shard_map/sub | solution.py:108
  63.6 0.4 fusion.3
  64.0 0.2 fusion.2
  64.2 1.4 %slice_subtract_fusion.2 = f32[16,42,266]{2,1,0:T(8,128)S(1)} fusion(f32[16,43,268]{2,1,0:T(8,128)S(1)} %fusion.2, f32[16,44,267]{2,1,0:T(8,128)S(1)} %fusion.3, f32[16,44,268]{2,1,0:T(8,128)S(1)} %slice_subtract_fusion.6), kind=kLoop, calls=%fused_computation.5 | loop fusion | flops 715008 | bytes 4290048 | tf_op jit(solution)/shard_map/sub | solution.py:108
  65.6 0.4 fusion.1
  66.0 0.2 fusion
  66.2 1.2 %slice_subtract_fusion.28 = f32[16,40,264]{2,1,0:T(8,128)S(1)} fusion(f32[16,41,266]{2,1,0:T(8,128)S(1)} %fusion, f32[16,42,265]{2,1,0:T(8,128)S(1)} %fusion.1, f32[16,42,266]{2,1,0:T(8,128)S(1)} %slice_subtract_fusion.2), kind=kLoop, calls=%fused_computation.57 | loop fusion | flops 675840 | bytes 4055040 | tf_op jit(solution)/shard_map/sub | solution.py:108
  67.4 0.3 fusion.15
  67.7 0.1 fusion.14
  67.8 1.3 %slice_subtract_fusion.24 = f32[16,38,262]{2,1,0:T(8,128)S(1)} fusion(f32[16,39,264]{2,1,0:T(8,128)S(1)} %fusion.14, f32[16,40,263]{2,1,0:T(8,128)S(1)} %fusion.15, f32[16,40,264]{2,1,0:T(8,128)S(1)} %slice_subtract_fusion.28), kind=kLoop, calls=%fused_computation.49 | loop fusion | flops 637184 | bytes 3823104 | tf_op jit(solution)/shard_map/sub | solution.py:108
  69.1 0.3 fusion.13
  69.5 0.1 fusion.12
  69.6 1.2 %slice_subtract_fusion.20 = f32[16,36,260]{2,1,0:T(8,128)S(1)} fusion(f32[16,37,262]{2,1,0:T(8,128)S(1)} %fusion.12, f32[16,38,261]{2,1,0:T(8,128)S(1)} %fusion.13, f32[16,38,262]{2,1,0:T(8,128)S(1)} %slice_subtract_fusion.24), kind=kLoop, calls=%fused_computation.41 | loop fusion | flops 599040 | bytes 3594240 | tf_op jit(solution)/shard_map/sub | solution.py:108
  70.8 0.5 fusion.11
  71.4 0.1 fusion.10
  71.5 1.2 %slice_subtract_fusion.16 = f32[16,34,258]{2,1,0:T(8,128)S(1)} fusion(f32[16,35,260]{2,1,0:T(8,128)S(1)} %fusion.10, f32[16,36,259]{2,1,0:T(8,128)S(1)} %fusion.11, f32[16,36,260]{2,1,0:T(8,128)S(1)} %slice_subtract_fusion.20), kind=kLoop, calls=%fused_computation.33 | loop fusion | flops 561408 | bytes 3368448 | tf_op jit(solution)/shard_map/sub | solution.py:108
  72.7 0.3 fusion.9
  73.0 0.1 fusion.8
  73.2 1.5 %slice_subtract_fusion.30 = f32[16,32,256]{2,1,0:T(8,128)} fusion(f32[16,33,258]{2,1,0:T(8,128)S(1)} %fusion.8, f32[16,34,257]{2,1,0:T(8,128)S(1)} %fusion.9, f32[16,34,258]{2,1,0:T(8,128)S(1)} %slice_subtract_fusion.16), kind=kLoop, calls=%fused_computation.62 | loop fusion | flops 524288 | bytes 3145728 | tf_op jit(solution)/shard_map/sub | solution.py:108
  (26 shorter events, 0.3 us)
Async XLA Ops:
  0.0 14.3 %copy-start = (s32[1,16]{1,0:T(1,128)S(1)}, s32[1,16]{1,0:T(1,128)}, u32[]{:S(2)}) copy-start(s32[1,16]{1,0:T(1,128)} %param.13) | copy-start | bytes 196
  0.0 1.7 %copy-start.3 = (f32[16,1,4096]{2,1,0:T(1,128)S(1)}, f32[16,1,4096]{2,1,0:T(1,128)}, u32[]{:S(2)}) copy-start(f32[16,1,4096]{2,1,0:T(1,128)} %param.15) | copy-start | bytes 786436
  2.5 11.1 %copy-start.5 = (s32[1,4096]{1,0:T(1,128)S(1)}, s32[1,4096]{1,0:T(1,128)}, u32[]{:S(2)}) copy-start(s32[1,4096]{1,0:T(1,128)} %param.12) | copy-start | bytes 49156
  2.6 11.9 %copy-start.6 = (s32[32,256]{1,0:T(8,128)S(1)}, s32[32,256]{1,0:T(8,128)}, u32[]{:S(2)}) copy-start(s32[32,256]{1,0:T(8,128)} %param.11) | copy-start | bytes 98308
  3.7 27.3 %all-to-all-start = ((f32[16,16,512]{2,0,1:T(8,128)}), f32[16,16,512]{2,0,1:T(8,128)S(1)}, u32[]{:S(2)}, u32[]{:S(2)}) async-start(f32[16,16,512]{2,0,1:T(8,128)} %copy.11), calls=%async_computation | async-start | bytes 1048576 | tf_op jit(solution)/shard_map/all_to_all | solution.py:130
  21.7 9.4 %copy-start.4 = (f32[16,4096]{1,0:T(8,128)S(1)}, f32[16,4096]{1,0:T(8,128)}, u32[]{:S(2)}) copy-start(f32[16,4096]{1,0:T(8,128)} %shard_map.82) | copy-start | bytes 786436
  31.9 8.1 %copy-start.1 = (f32[32,256]{1,0:T(8,128)S(1)}, f32[32,256]{1,0:T(8,128)}, u32[]{:S(2)}) copy-start(f32[32,256]{1,0:T(8,128)} %param.10) | copy-start | bytes 98308
  31.9 8.1 %copy-start.2 = (f32[32,256]{1,0:T(8,128)S(1)}, f32[32,256]{1,0:T(8,128)}, u32[]{:S(2)}) copy-start(f32[32,256]{1,0:T(8,128)} %param.9) | copy-start | bytes 98308
  40.2 3.9 %collective-permute-start = (f32[19,32,8]{2,1,0:T(8,128)S(1)}, f32[19,32,8]{2,1,0:T(8,128)S(1)}, u32[]{:S(2)}, u32[]{:S(2)}) collective-permute-start(f32[19,32,8]{2,1,0:T(8,128)S(1)} %get-tuple-element.9), channel_id=1, source_target_pairs={{0,16},{16,32},{32,48},{48,64},{64,80},{80,96},{96,112},{112,128},... | collective-permute-start | bytes 58376 | tf_op jit(solution)/shard_map/ppermute | solution.py:96
  40.2 6.3 %collective-permute-start.1 = (f32[19,32,8]{2,1,0:T(8,128)S(1)}, f32[19,32,8]{2,1,0:T(8,128)S(1)}, u32[]{:S(2)}, u32[]{:S(2)}) collective-permute-start(f32[19,32,8]{2,1,0:T(8,128)S(1)} %get-tuple-element.10), channel_id=1, source_target_pairs={{16,0},{32,16},{48,32},{64,48},{80,64},{96,80},{112,96},{128,112},... | collective-permute-start | bytes 58376 | tf_op jit(solution)/shard_map/ppermute | solution.py:99
  46.8 10.9 %collective-permute-start.2 = (f32[19,8,272]{2,1,0:T(8,128)S(1)}, f32[19,8,272]{2,1,0:T(8,128)S(1)}, u32[]{:S(2)}, u32[]{:S(2)}) collective-permute-start(f32[19,8,272]{2,1,0:T(8,128)S(1)} %get-tuple-element.7), channel_id=1, source_target_pairs={{0,1},{1,2},{2,3},{3,4},{4,5},{5,6},{6,7},{7,8},{8,9},{9,10},{10,1... | collective-permute-start | bytes 496136 | tf_op jit(solution)/shard_map/ppermute | solution.py:96
  48.1 9.6 %collective-permute-start.3 = (f32[19,8,272]{2,1,0:T(8,128)S(1)}, f32[19,8,272]{2,1,0:T(8,128)S(1)}, u32[]{:S(2)}, u32[]{:S(2)}) collective-permute-start(f32[19,8,272]{2,1,0:T(8,128)S(1)} %get-tuple-element.8), channel_id=1, source_target_pairs={{1,0},{2,1},{3,2},{4,3},{5,4},{6,5},{7,6},{8,7},{9,8},{10,9},{11,1... | collective-permute-start | bytes 496136 | tf_op jit(solution)/shard_map/ppermute | solution.py:99

commit v6 on v5

--- a/solution.py
+++ b/solution.py
@@ -87,30 +87,52 @@
     return vmem_call(gather_kernel, shape, flops, 4 * (levels * slots + 2 * slots + cells * cols_here))(state2d, rows, cols)
 
 
-def with_halo(block, sides, width):
-    for axis, dim in sides:
-        count = lax.axis_size(axis)
-        forward = [(i, i + 1) for i in range(count - 1)]
-        forward.append((count - 1, 0))
-        backward = [(target, source) for source, target in forward]
-        low = lax.ppermute(
-            lax.slice_in_dim(block, block.shape[dim] - width, None, axis=dim), axis, forward
-        )
-        high = lax.ppermute(lax.slice_in_dim(block, 0, width, axis=dim), axis, backward)
-        block = jnp.concatenate([low, block, high], axis=dim)
-    return block
+def passes_kernel(field_ref, east_ref, north_ref, out_ref):
+    levels, rows_out, cols_out = out_ref.shape
+    _, high, wide = field_ref.shape
+    east = east_ref[...]
+    north = north_ref[...]
+
+    def level(l, carry):
+        g = field_ref[l]
+        for step_number in range(PASSES):
+            flux_east = east * (pltpu.roll(g, wide - 1, 1) - g)
+            flux_north = north * (pltpu.roll(g, high - 1, 0) - g)
+            g = g + flux_east - pltpu.roll(flux_east, 1, 1) + flux_north - pltpu.roll(flux_north, 1, 0)
+        out_ref[l] = g[:rows_out, :cols_out]
+        return carry
+
+    lax.fori_loop(0, levels, level, 0)
 
 
-def one_pass(layer_field, east_face, north_face):
-    flux_east = east_face * (layer_field[:, :, 1:] - layer_field[:, :, :-1])
-    flux_north = north_face * (layer_field[:, 1:, :] - layer_field[:, :-1, :])
-    return (
-        layer_field[:, 1:-1, 1:-1]
-        + flux_east[:, 1:-1, 1:]
-        - flux_east[:, 1:-1, :-1]
-        + flux_north[:, 1:, 1:-1]
-        - flux_north[:, :-1, 1:-1]
-    )
+def diffuse(field, east, north, rows_out, cols_out):
+    levels, high, wide = field.shape
+    return pl.pallas_call(
+        passes_kernel,
+        out_shape=jax.ShapeDtypeStruct((levels, rows_out, cols_out), jnp.float32),
+        in_specs=[pl.BlockSpec(memory_space=pltpu.VMEM)] * 3,
+        out_specs=pl.BlockSpec(memory_space=pltpu.VMEM),
+        cost_estimate=pl.CostEstimate(
+            flops=10 * PASSES * levels * high * wide, bytes_accessed=4 * levels * (high * wide + rows_out * cols_out),
+            transcendentals=0,
+        ),
+    )(field, east, north)
+
+
+def wrapped_halo(block, width, extent):
+    lon_count = lax.axis_size("lon")
+    lat_count = lax.axis_size("lat")
+    lon_up = [(i, (i + 1) % lon_count) for i in range(lon_count)]
+    lon_down = [(j, i) for i, j in lon_up]
+    lat_up = [(i, (i + 1) % lat_count) for i in range(lat_count)]
+    lat_down = [(j, i) for i, j in lat_up]
+    west = lax.ppermute(block[..., -width:], "lon", lon_up)
+    east = lax.ppermute(block[..., :width], "lon", lon_down)
+    gap = jnp.zeros(block.shape[:-1] + (extent - block.shape[-1] - 2 * width,), block.dtype)
+    block = jnp.concatenate([block, east, gap, west], axis=-1)
+    south = lax.ppermute(block[..., -width:, :], "lat", lat_up)
+    north = lax.ppermute(block[..., :width, :], "lat", lat_down)
+    return jnp.concatenate([block, north, south], axis=-2)
 
 
 def body(state, coef_lon, coef_lat, land_sea, send_cols, send_count, obs_value, obs_weight):
@@ -139,27 +161,19 @@
     gradient = onehot_scatter(weighted, target_rows, target_cols, rows_here, cols_here)
     gradient = gradient.reshape(levels, rows_here, cols_here) * sea[None]
     rim_width = PASSES
+    lanes_out = 128 * ((cols_here + 2 * rim_width + 127) // 128)
     stacked = jnp.concatenate([gradient, sea[None], coef_lon[None], coef_lat[None]], axis=0)
-    padded = with_halo(stacked, (("lon", 2), ("lat", 1)), rim_width)
-    field = padded[:levels]
-    padded = padded[levels:]
+    padded = wrapped_halo(stacked, rim_width, lanes_out)
     lat_index = lax.axis_index("lat")
     row_place = jnp.arange(rows_here + 2 * rim_width, dtype=jnp.int32)
-    outside = (row_place < rim_width) & (lat_index == 0) | (row_place >= rows_here + rim_width) & (
-        lat_index == lat_count - 1
-    )
+    outside = (row_place >= rows_here + rim_width) & (lat_index == 0) | (
+        row_place >= rows_here
+    ) & (row_place < rows_here + rim_width) & (lat_index == lat_count - 1)
     inside = jnp.where(outside, 0.0, 1.0).astype(jnp.float32)[:, None]
-    sea_rim = padded[0] * inside
-    east_face = padded[1][:, :-1] * sea_rim[:, :-1] * sea_rim[:, 1:]
-    north_face = padded[2][:-1, :] * sea_rim[:-1, :] * sea_rim[1:, :]
-    for step_number in range(PASSES):
-        high, wide = field.shape[1], field.shape[2]
-        field = one_pass(
-            field,
-            east_face[step_number : step_number + high, step_number : step_number + wide - 1],
-            north_face[step_number : step_number + high - 1, step_number : step_number + wide],
-        )
-    gradient = field
+    sea_rim = padded[levels] * inside
+    east_face = padded[levels + 1] * sea_rim * jnp.roll(sea_rim, -1, axis=1)
+    north_face = padded[levels + 2] * sea_rim * jnp.roll(sea_rim, -1, axis=0)
+    gradient = diffuse(padded[:levels], east_face, north_face, rows_here, cols_here)
     return gradient
 
 

time: 74.9 us -> 87.5 us (1.17)
  Pallas kernels: 13.6 us -> 35.5 us
  other arithmetic: 21.3 us -> 7.69 us
  waiting for transfers between devices: 20.7 us -> 24.1 us
  starting transfers between devices: 15.8 us -> 16.7 us
    pallas_call x0 -> x1, Pallas kernels: none -> 21.9 us  [diffuse(): pl.pallas_call(passes_kernel, out_shape=jax.ShapeDtypeStruct((levels, row...]
    sub x8 -> x0, other arithmetic: 10.8 us -> none  [one_pass(): layer_field[:, 1:-1, 1:-1] + flux_east[:, 1:-1, 1:]]
    mul x19 -> x2, other arithmetic: 4.35 us -> 0.83 us  [the longest x1 0.75 us: body(): north_face = padded[levels + 2] * sea_rim * jnp.roll(sea_rim, -1, axis=0)]
    ppermute x4, waiting for transfers between devices: 11.5 us -> 14.9 us  [the longest x1 5.2 us: wrapped_halo(): south = lax.ppermute(block[..., -width:, :], 'lat', lat_up)]
    ppermute x4, starting transfers between devices: 5.79 us -> 6.76 us  [the longest x1 5.01 us: wrapped_halo(): north = lax.ppermute(block[..., :width, :], 'lat', lat_down)]
    unnamed x2, other arithmetic: 2.27 us -> 3.19 us
  transfers between devices with their start and end apart: 5 -> 5, of which waited for: 4 -> 4; matrix products, arithmetic and copies ran while one was open for 2% -> 2% of each run, Pallas kernels for 9% -> 8%
where the time goes in v6:
time: 87.5 us; the launch traced here: 87.1 us
  Pallas kernels  35.5 us (41%)
  waiting for transfers between devices  24.1 us (28%)
  starting transfers between devices  16.7 us (19%)
  other arithmetic  7.69 us (9%)
  local copies, waits for them, and re-layouts  2.86 us (3%)
    pallas_call x1, Pallas kernels, diffuse(): pl.pallas_call(passes_kernel, out_shape=jax.ShapeDtypeStruct((levels, row...  21.9 us
    all_to_all x1, starting transfers between devices, body(): lax.all_to_all(held, 'lon', split_axis=1, concat_axis=1, tiled=True)  9.98 us
    all_to_all x1, waiting for transfers between devices, body(): lax.all_to_all(held, 'lon', split_axis=1, concat_axis=1, tiled=True)  9.24 us
    pallas_call x1, Pallas kernels, onehot_scatter(): vmem_call(scatter_kernel, shape, flops, 4 * (levels * slots + 2 * slots +...  6.99 us
    pallas_call x1, Pallas kernels, onehot_gather(): vmem_call(gather_kernel, shape, flops, 4 * (levels * slots + 2 * slots +...  6.64 us
    ppermute x1, waiting for transfers between devices, wrapped_halo(): south = lax.ppermute(block[..., -width:, :], 'lat', lat_up)  5.2 us
    ppermute x1, waiting for transfers between devices, wrapped_halo(): north = lax.ppermute(block[..., :width, :], 'lat', lat_down)  5.07 us
    ppermute x1, starting transfers between devices, wrapped_halo(): north = lax.ppermute(block[..., :width, :], 'lat', lat_down)  5.01 us
  transfers between devices with their start and end apart: 5, of which 4 were waited for; matrix products, arithmetic and copies ran while one was open for 2% of the time, Pallas kernels for 8%

profile of v6, /device:TPU:1, one launch (start us, length us, event | category | flops | bytes accessed | tf_op | source)
XLA Modules:
  0.0 87.1 jit_solution(17224714673072908797)
XLA Ops:
  0.0 0.0 copy-start
  0.0 1.6 %reduce = f32[16,4096]{1,0:T(8,128)S(1)} reduce(f32[16,1,4096]{2,1,0:T(1,128)} %param.14, f32[]{:T(128)} %constant.54), dimensions={1}, to_apply=%param.14.reduce_sub_computation | reduce | bytes 524292 | tf_op args[6]
  1.6 0.1 copy.16
  1.7 1.6 %reduce.1 = f32[16,4096]{1,0:T(8,128)S(1)} reduce(f32[16,1,4096]{2,1,0:T(1,128)} %param.15, f32[]{:T(128)} %constant.54), dimensions={1}, to_apply=%param.15.reduce_sub_computation | reduce | bytes 524292 | tf_op args[7]
  3.3 0.1 copy.17
  3.4 0.0 copy-start.4
  3.4 0.0 copy-start.5
  3.4 0.1 pad_maximum_fusion.2
  3.5 1.1 %copy.11 = f32[16,16,512]{2,0,1:T(8,128)} copy(f32[16,16,512]{2,1,0:T(8,128)S(1)} %pad_maximum_fusion.2) | data formatting | bytes 1048576 | tf_op jit(solution)/shard_map/concatenate | solution.py:149
  4.6 10.0 %all-to-all-start = ((f32[16,16,512]{2,0,1:T(8,128)}), f32[16,16,512]{2,0,1:T(8,128)S(1)}, u32[]{:S(2)}, u32[]{:S(2)}) async-start(f32[16,16,512]{2,0,1:T(8,128)} %copy.11), calls=%async_computation | async-start | bytes 1048576 | tf_op jit(solution)/shard_map/all_to_all | solution.py:152
  14.6 0.0 copy-done.4
  14.6 0.6 and_select_fusion
  15.2 0.0 copy-done
  15.2 0.1 broadcast_bitcast_fusion
  15.3 0.0 copy-done.5
  15.3 0.7 and_select_fusion.1.rows_ref
  16.0 6.6 %shard_map.82 = f32[16,4096]{1,0:T(8,128)} custom-call(f32[512,256]{1,0:T(8,128)} %bitcast.53, s32[1,4096]{1,0:T(1,128)} %and_select_fusion.1.rows_ref, s32[1,4096]{1,0:T(1,128)} %get-tuple-element.5.cols_ref), custom_call_target="tpu_custom_call" | custom-call | flops 3221225472 | bytes 819200 | tf_op jit(solution)/shard_map/pallas_call | solution.py:87
  22.6 0.0 copy-start.3
  22.6 9.2 %all-to-all-done = f32[16,16,512]{2,0,1:T(8,128)S(1)} async-done(((f32[16,16,512]{2,0,1:T(8,128)}), f32[16,16,512]{2,0,1:T(8,128)S(1)}, u32[]{:S(2)}, u32[]{:S(2)}) %all-to-all-start) | async-done | bytes 524320 | tf_op jit(solution)/shard_map/all_to_all | solution.py:152
  31.9 0.1 slice_bitcast_fusion
  32.0 0.0 copy-done.3
  32.0 0.8 multiply_multiply_fusion.w_ref
  32.8 0.0 copy-start.1
  32.8 0.0 copy-start.2
  32.8 7.0 %shard_map.83 = f32[512,256]{1,0:T(8,128)} custom-call(f32[16,4096]{1,0:T(8,128)} %multiply_multiply_fusion.w_ref, s32[1,4096]{1,0:T(1,128)} %and_select_fusion.1.rows_ref, s32[1,4096]{1,0:T(1,128)} %get-tuple-element.5.cols_ref), custom_call_target="tpu_custom_call" | custom-call | flops 3221225472 | bytes 819200 | tf_op jit(solution)/shard_map/pallas_call | solution.py:79
  39.8 1.1 %broadcast_multiply_fusion = f32[16,32,256]{2,1,0:T(8,128)S(1)} fusion(f32[16,32,256]{2,1,0:T(8,128)} %bitcast.45, f32[32,256]{1,0:T(8,128)S(1)} %get-tuple-element.15), kind=kLoop, calls=%fused_computation.5 | loop fusion | flops 131072 | bytes 1081344 | tf_op jit(solution)/shard_map/mul | solution.py:162
  40.8 0.0 copy-done.1
  40.9 0.0 copy-done.2
  40.9 0.1 pad_maximum_fusion.1
  40.9 0.1 fusion.10
  41.1 0.0 collective-permute-start
  41.1 1.7 %collective-permute-start.1 = (f32[19,32,8]{2,1,0:T(8,128)S(1)}, f32[19,32,8]{2,1,0:T(8,128)S(1)}, u32[]{:S(2)}, u32[]{:S(2)}) collective-permute-start(f32[19,32,8]{2,1,0:T(8,128)S(1)} %get-tuple-element.12), channel_id=1, source_target_pairs={{0,16},{16,32},{32,48},{48,64},{64,80},{80,96},{96,112},{112,128},... | collective-permute-start | bytes 58376 | tf_op jit(solution)/shard_map/ppermute | solution.py:129
  42.8 4.6 %collective-permute-done = f32[19,32,8]{2,1,0:T(8,128)S(1)} collective-permute-done((f32[19,32,8]{2,1,0:T(8,128)S(1)}, f32[19,32,8]{2,1,0:T(8,128)S(1)}, u32[]{:S(2)}, u32[]{:S(2)}) %collective-permute-start) | collective-permute-done | bytes 19488 | tf_op jit(solution)/shard_map/ppermute | solution.py:130
  47.4 0.0 collective-permute-done.1
  47.5 0.2 pad_maximum_fusion.9
  47.6 5.0 %collective-permute-start.2 = (f32[19,8,384]{2,1,0:T(8,128)S(1)}, f32[19,8,384]{2,1,0:T(8,128)S(1)}, u32[]{:S(2)}, u32[]{:S(2)}) collective-permute-start(f32[19,8,384]{2,1,0:T(8,128)S(1)} %get-tuple-element.7), channel_id=1, source_target_pairs={{1,0},{2,1},{3,2},{4,3},{5,4},{6,5},{7,6},{8,7},{9,8},{10,9},{11,1... | collective-permute-start | bytes 700424 | tf_op jit(solution)/shard_map/ppermute | solution.py:134
  52.6 0.0 collective-permute-start.3
  52.6 5.1 %collective-permute-done.2 = f32[19,8,384]{2,1,0:T(8,128)S(1)} collective-permute-done((f32[19,8,384]{2,1,0:T(8,128)S(1)}, f32[19,8,384]{2,1,0:T(8,128)S(1)}, u32[]{:S(2)}, u32[]{:S(2)}) %collective-permute-start.2) | collective-permute-done | bytes 233504 | tf_op jit(solution)/shard_map/ppermute | solution.py:134
  57.7 5.2 %collective-permute-done.3 = f32[19,8,384]{2,1,0:T(8,128)S(1)} collective-permute-done((f32[19,8,384]{2,1,0:T(8,128)S(1)}, f32[19,8,384]{2,1,0:T(8,128)S(1)}, u32[]{:S(2)}, u32[]{:S(2)}) %collective-permute-start.3) | collective-permute-done | bytes 233504 | tf_op jit(solution)/shard_map/ppermute | solution.py:133
  62.9 0.2 pad_maximum_fusion
  63.2 0.1 fusion.2
  63.2 0.1 slice.67
  63.4 1.1 %slice.64.field_ref = f32[16,48,384]{2,1,0:T(8,128)} slice(f32[19,48,384]{2,1,0:T(8,128)S(1)} %pad_maximum_fusion), slice={[0:16], [0:48], [0:384]} | slice | bytes 2359296 | tf_op jit(solution)/shard_map/slice | solution.py:176
  64.5 0.8 fusion.1
  65.2 21.9 %shard_map.84 = f32[16,32,256]{2,1,0:T(8,128)} custom-call(f32[16,48,384]{2,1,0:T(8,128)} %slice.64.field_ref, f32[48,384]{1,0:T(8,128)} %get-tuple-element.10.east_ref, f32[48,384]{1,0:T(8,128)} %get-tuple-element.9.north_ref), custom_call_target="tpu_custom_call" | custom-call | flops 23592960 | bytes 1703936 | tf_op jit(solution)/shard_map/pallas_call | solution.py:110
  (10 shorter events, 0.1 us)
Async XLA Ops:
  0.0 15.2 %copy-start = (s32[1,16]{1,0:T(1,128)S(1)}, s32[1,16]{1,0:T(1,128)}, u32[]{:S(2)}) copy-start(s32[1,16]{1,0:T(1,128)} %param.13) | copy-start | bytes 196
  3.4 11.2 %copy-start.4 = (s32[1,4096]{1,0:T(1,128)S(1)}, s32[1,4096]{1,0:T(1,128)}, u32[]{:S(2)}) copy-start(s32[1,4096]{1,0:T(1,128)} %param.12) | copy-start | bytes 49156
  3.4 11.9 %copy-start.5 = (s32[32,256]{1,0:T(8,128)S(1)}, s32[32,256]{1,0:T(8,128)}, u32[]{:S(2)}) copy-start(s32[32,256]{1,0:T(8,128)} %param.11) | copy-start | bytes 98308
  4.6 27.3 %all-to-all-start = ((f32[16,16,512]{2,0,1:T(8,128)}), f32[16,16,512]{2,0,1:T(8,128)S(1)}, u32[]{:S(2)}, u32[]{:S(2)}) async-start(f32[16,16,512]{2,0,1:T(8,128)} %copy.11), calls=%async_computation | async-start | bytes 1048576 | tf_op jit(solution)/shard_map/all_to_all | solution.py:152
  22.6 9.4 %copy-start.3 = (f32[16,4096]{1,0:T(8,128)S(1)}, f32[16,4096]{1,0:T(8,128)}, u32[]{:S(2)}) copy-start(f32[16,4096]{1,0:T(8,128)} %shard_map.82) | copy-start | bytes 786436
  32.8 8.1 %copy-start.1 = (f32[32,256]{1,0:T(8,128)S(1)}, f32[32,256]{1,0:T(8,128)}, u32[]{:S(2)}) copy-start(f32[32,256]{1,0:T(8,128)} %param.10) | copy-start | bytes 98308
  32.8 8.1 %copy-start.2 = (f32[32,256]{1,0:T(8,128)S(1)}, f32[32,256]{1,0:T(8,128)}, u32[]{:S(2)}) copy-start(f32[32,256]{1,0:T(8,128)} %param.9) | copy-start | bytes 98308
  41.1 6.3 %collective-permute-start = (f32[19,32,8]{2,1,0:T(8,128)S(1)}, f32[19,32,8]{2,1,0:T(8,128)S(1)}, u32[]{:S(2)}, u32[]{:S(2)}) collective-permute-start(f32[19,32,8]{2,1,0:T(8,128)S(1)} %get-tuple-element.11), channel_id=1, source_target_pairs={{16,0},{32,16},{48,32},{64,48},{80,64},{96,80},{112,96},{128,112},... | collective-permute-start | bytes 58376 | tf_op jit(solution)/shard_map/ppermute | solution.py:130
  41.1 6.3 %collective-permute-start.1 = (f32[19,32,8]{2,1,0:T(8,128)S(1)}, f32[19,32,8]{2,1,0:T(8,128)S(1)}, u32[]{:S(2)}, u32[]{:S(2)}) collective-permute-start(f32[19,32,8]{2,1,0:T(8,128)S(1)} %get-tuple-element.12), channel_id=1, source_target_pairs={{0,16},{16,32},{32,48},{48,64},{64,80},{80,96},{96,112},{112,128},... | collective-permute-start | bytes 58376 | tf_op jit(solution)/shard_map/ppermute | solution.py:129
  47.6 10.1 %collective-permute-start.2 = (f32[19,8,384]{2,1,0:T(8,128)S(1)}, f32[19,8,384]{2,1,0:T(8,128)S(1)}, u32[]{:S(2)}, u32[]{:S(2)}) collective-permute-start(f32[19,8,384]{2,1,0:T(8,128)S(1)} %get-tuple-element.7), channel_id=1, source_target_pairs={{1,0},{2,1},{3,2},{4,3},{5,4},{6,5},{7,6},{8,7},{9,8},{10,9},{11,1... | collective-permute-start | bytes 700424 | tf_op jit(solution)/shard_map/ppermute | solution.py:134
  52.6 10.3 %collective-permute-start.3 = (f32[19,8,384]{2,1,0:T(8,128)S(1)}, f32[19,8,384]{2,1,0:T(8,128)S(1)}, u32[]{:S(2)}, u32[]{:S(2)}) collective-permute-start(f32[19,8,384]{2,1,0:T(8,128)S(1)} %get-tuple-element.8), channel_id=1, source_target_pairs={{0,1},{1,2},{2,3},{3,4},{4,5},{5,6},{6,7},{7,8},{8,9},{9,10},{10,1... | collective-permute-start | bytes 700424 | tf_op jit(solution)/shard_map/ppermute | solution.py:133

commit v7 on v5

--- a/solution.py
+++ b/solution.py
@@ -93,10 +93,15 @@
         forward = [(i, i + 1) for i in range(count - 1)]
         forward.append((count - 1, 0))
         backward = [(target, source) for source, target in forward]
-        low = lax.ppermute(
-            lax.slice_in_dim(block, block.shape[dim] - width, None, axis=dim), axis, forward
-        )
-        high = lax.ppermute(lax.slice_in_dim(block, 0, width, axis=dim), axis, backward)
+        low = lax.slice_in_dim(block, block.shape[dim] - width, None, axis=dim)
+        high = lax.slice_in_dim(block, 0, width, axis=dim)
+        if dim == block.ndim - 1:
+            flat = block.shape[:-2] + (-1,)
+            low = lax.ppermute(low.reshape(flat), axis, forward).reshape(low.shape)
+            high = lax.ppermute(high.reshape(flat), axis, backward).reshape(high.shape)
+        else:
+            low = lax.ppermute(low, axis, forward)
+            high = lax.ppermute(high, axis, backward)
         block = jnp.concatenate([low, block, high], axis=dim)
     return block
 

time: 74.9 us -> 73.8 us (0.985)
  waiting for transfers between devices: 20.7 us -> 18.3 us
  local copies, waits for them, and re-layouts: 2.79 us -> 4.14 us
    ppermute x4, waiting for transfers between devices: 11.5 us -> 9.06 us  [the longest x1 5.57 us: with_halo(): low = lax.ppermute(low, axis, forward)]
    reshape x0 -> x2, local copies, waits for them, and re-layouts: none -> 0.8 us  [the longest x1 0.4 us: with_halo(): high = lax.ppermute(high.reshape(flat), axis, backward).reshape(high.shape)]
  transfers between devices with their start and end apart: 5 -> 5, of which waited for: 4 -> 4; matrix products, arithmetic and copies ran while one was open for 2% -> 3% of each run, Pallas kernels for 9% -> 9%
where the time goes in v7:
time: 73.8 us; the launch traced here: 73.5 us
  other arithmetic  21.3 us (29%)
  waiting for transfers between devices  18.3 us (25%)
  starting transfers between devices  15.8 us (21%)
  Pallas kernels  13.6 us (18%)
  local copies, waits for them, and re-layouts  4.14 us (6%)
    sub x8, other arithmetic, one_pass(): layer_field[:, 1:-1, 1:-1] + flux_east[:, 1:-1, 1:]  10.8 us
    all_to_all x1, starting transfers between devices, body(): lax.all_to_all(held, 'lon', split_axis=1, concat_axis=1, tiled=True)  9.98 us
    all_to_all x1, waiting for transfers between devices, body(): lax.all_to_all(held, 'lon', split_axis=1, concat_axis=1, tiled=True)  9.24 us
    pallas_call x1, Pallas kernels, onehot_scatter(): vmem_call(scatter_kernel, shape, flops, 4 * (levels * slots + 2 * slots +...  6.99 us
    pallas_call x1, Pallas kernels, onehot_gather(): vmem_call(gather_kernel, shape, flops, 4 * (levels * slots + 2 * slots +...  6.64 us
    ppermute x1, waiting for transfers between devices, with_halo(): low = lax.ppermute(low, axis, forward)  5.57 us
    ppermute x1, starting transfers between devices, with_halo(): high = lax.ppermute(high, axis, backward)  3.9 us
    mul x8, other arithmetic, one_pass(): flux_east = east_face * (layer_field[:, :, 1:] - layer_field[:, :, :-1])  3.01 us
  transfers between devices with their start and end apart: 5, of which 4 were waited for; matrix products, arithmetic and copies ran while one was open for 3% of the time, Pallas kernels for 9%

profile of v7, /device:TPU:1, one launch (start us, length us, event | category | flops | bytes accessed | tf_op | source)
XLA Modules:
  0.0 73.5 jit_solution(10603090049233856422)
XLA Ops:
  0.0 1.6 %reduce = f32[16,4096]{1,0:T(8,128)S(1)} reduce(f32[16,1,4096]{2,1,0:T(1,128)} %param.14, f32[]{:T(128)} %constant.52), dimensions={1}, to_apply=%param.14.reduce_sub_computation | reduce | bytes 524292 | tf_op args[6]
  1.6 0.1 copy.28
  1.7 0.6 reduce.1
  2.4 0.1 copy.29
  2.6 1.1 %copy.19 = f32[16,16,512]{2,0,1:T(8,128)} copy(f32[16,16,512]{2,1,0:T(8,128)S(1)} %pad_maximum_fusion.2) | data formatting | bytes 1048576 | tf_op jit(solution)/shard_map/concatenate | solution.py:132
  3.7 10.0 %all-to-all-start = ((f32[16,16,512]{2,0,1:T(8,128)}), f32[16,16,512]{2,0,1:T(8,128)S(1)}, u32[]{:S(2)}, u32[]{:S(2)}) async-start(f32[16,16,512]{2,0,1:T(8,128)} %copy.19), calls=%async_computation | async-start | bytes 1048576 | tf_op jit(solution)/shard_map/all_to_all | solution.py:135
  13.7 0.6 and_select_fusion
  14.4 0.7 and_select_fusion.1.rows_ref
  15.1 6.6 %shard_map.82 = f32[16,4096]{1,0:T(8,128)} custom-call(f32[512,256]{1,0:T(8,128)} %bitcast.53, s32[1,4096]{1,0:T(1,128)} %and_select_fusion.1.rows_ref, s32[1,4096]{1,0:T(1,128)} %get-tuple-element.5.cols_ref), custom_call_target="tpu_custom_call" | custom-call | flops 3221225472 | bytes 819200 | tf_op jit(solution)/shard_map/pallas_call | solution.py:87
  21.7 9.2 %all-to-all-done = f32[16,16,512]{2,0,1:T(8,128)S(1)} async-done(((f32[16,16,512]{2,0,1:T(8,128)}), f32[16,16,512]{2,0,1:T(8,128)S(1)}, u32[]{:S(2)}, u32[]{:S(2)}) %all-to-all-start) | async-done | bytes 524320 | tf_op jit(solution)/shard_map/all_to_all | solution.py:135
  31.1 0.8 %multiply_multiply_fusion.w_ref = f32[16,4096]{1,0:T(8,128)} fusion(f32[16,4096]{1,0:T(8,128)S(1)} %bitcast.37, f32[16,4096]{1,0:T(8,128)S(1)} %bitcast.39, f32[16,4096]{1,0:T(8,128)S(1)} %copy-done.4, f32[4096]{0:T(1024)S(1)} %fusion.21), kind=kLoop, calls=%fused_computation.70 | loop fusion | flops 196608 | bytes 1064960 | tf_op jit(solution)/shard_map/mul | solution.py:142
  31.9 7.0 %shard_map.83 = f32[512,256]{1,0:T(8,128)} custom-call(f32[16,4096]{1,0:T(8,128)} %multiply_multiply_fusion.w_ref, s32[1,4096]{1,0:T(1,128)} %and_select_fusion.1.rows_ref, s32[1,4096]{1,0:T(1,128)} %get-tuple-element.5.cols_ref), custom_call_target="tpu_custom_call" | custom-call | flops 3221225472 | bytes 819200 | tf_op jit(solution)/shard_map/pallas_call | solution.py:79
  38.8 1.1 %broadcast_multiply_fusion = f32[16,32,256]{2,1,0:T(8,128)S(1)} fusion(f32[16,32,256]{2,1,0:T(8,128)} %bitcast.41, f32[32,256]{1,0:T(8,128)S(1)} %get-tuple-element.13), kind=kLoop, calls=%fused_computation.69 | loop fusion | flops 131072 | bytes 1081344 | tf_op jit(solution)/shard_map/mul | solution.py:145
  40.0 0.1 fusion.22
  40.2 0.3 copy.22
  40.4 0.3 copy.23
  40.7 0.5 collective-permute-start.1
  41.2 1.2 %collective-permute-done = f32[19,256]{0,1:T(8,128)S(1)} collective-permute-done((f32[19,256]{0,1:T(8,128)S(1)}, f32[19,256]{0,1:T(8,128)S(1)}, u32[]{:S(2)}, u32[]{:S(2)}) %collective-permute-start) | collective-permute-done | bytes 19488 | tf_op jit(solution)/shard_map/ppermute | solution.py:100
  42.4 0.4 copy.24
  42.8 2.3 %collective-permute-done.1 = f32[19,256]{0,1:T(8,128)S(1)} collective-permute-done((f32[19,256]{0,1:T(8,128)S(1)}, f32[19,256]{0,1:T(8,128)S(1)}, u32[]{:S(2)}, u32[]{:S(2)}) %collective-permute-start.1) | collective-permute-done | bytes 19488 | tf_op jit(solution)/shard_map/ppermute | solution.py:101
  45.1 0.4 copy.25
  45.5 0.2 pad_maximum_fusion.8
  45.8 1.4 %collective-permute-start.2 = (f32[19,8,272]{2,1,0:T(8,128)S(1)}, f32[19,8,272]{2,1,0:T(8,128)S(1)}, u32[]{:S(2)}, u32[]{:S(2)}) collective-permute-start(f32[19,8,272]{2,1,0:T(8,128)S(1)} %get-tuple-element.7), channel_id=1, source_target_pairs={{0,1},{1,2},{2,3},{3,4},{4,5},{5,6},{6,7},{7,8},{8,9},{9,10},{10,1... | collective-permute-start | bytes 496136 | tf_op jit(solution)/shard_map/ppermute | solution.py:103
  47.1 3.9 %collective-permute-start.3 = (f32[19,8,272]{2,1,0:T(8,128)S(1)}, f32[19,8,272]{2,1,0:T(8,128)S(1)}, u32[]{:S(2)}, u32[]{:S(2)}) collective-permute-start(f32[19,8,272]{2,1,0:T(8,128)S(1)} %get-tuple-element.8), channel_id=1, source_target_pairs={{1,0},{2,1},{3,2},{4,3},{5,4},{6,5},{7,6},{8,7},{9,8},{10,9},{11,1... | collective-permute-start | bytes 496136 | tf_op jit(solution)/shard_map/ppermute | solution.py:104
  51.0 5.6 %collective-permute-done.2 = f32[19,8,272]{2,1,0:T(8,128)S(1)} collective-permute-done((f32[19,8,272]{2,1,0:T(8,128)S(1)}, f32[19,8,272]{2,1,0:T(8,128)S(1)}, u32[]{:S(2)}, u32[]{:S(2)}) %collective-permute-start.2) | collective-permute-done | bytes 165408 | tf_op jit(solution)/shard_map/ppermute | solution.py:103
  56.6 0.4 pad_maximum_fusion
  57.1 0.1 slice_multiply_fusion.2
  57.2 0.4 fusion.7
  57.6 0.1 slice.438
  57.7 0.2 fusion.6
  57.9 0.1 slice.443
  57.9 0.1 slice.449
  58.0 0.1 slice.454
  58.1 0.1 slice.460
  58.2 0.1 slice.465
  58.3 0.1 slice.471
  58.4 0.1 slice.476
  58.5 0.1 slice.482
  58.6 0.1 slice.487
  58.7 0.1 slice.493
  58.7 0.1 slice.498
  58.8 0.1 slice.504
  59.0 1.5 %slice_subtract_fusion.10 = f32[16,46,270]{2,1,0:T(8,128)S(1)} fusion(f32[16,47,272]{2,1,0:T(8,128)S(1)} %fusion.6, f32[16,48,271]{2,1,0:T(8,128)S(1)} %fusion.7, f32[19,48,272]{2,1,0:T(8,128)S(1)} %pad_maximum_fusion), kind=kLoop, calls=%fused_computation.21 | loop fusion | flops 794880 | bytes 4769280 | tf_op jit(solution)/shard_map/sub | solution.py:113
  60.5 0.4 fusion.5
  60.9 0.2 fusion.4
  61.1 1.4 %slice_subtract_fusion.6 = f32[16,44,268]{2,1,0:T(8,128)S(1)} fusion(f32[16,45,270]{2,1,0:T(8,128)S(1)} %fusion.4, f32[16,46,269]{2,1,0:T(8,128)S(1)} %fusion.5, f32[16,46,270]{2,1,0:T(8,128)S(1)} %slice_subtract_fusion.10), kind=kLoop, calls=%fused_computation.13 | loop fusion | flops 754688 | bytes 4528128 | tf_op jit(solution)/shard_map/sub | solution.py:113
  62.5 0.4 fusion.3
  62.9 0.2 fusion.2
  63.1 1.4 %slice_subtract_fusion.2 = f32[16,42,266]{2,1,0:T(8,128)S(1)} fusion(f32[16,43,268]{2,1,0:T(8,128)S(1)} %fusion.2, f32[16,44,267]{2,1,0:T(8,128)S(1)} %fusion.3, f32[16,44,268]{2,1,0:T(8,128)S(1)} %slice_subtract_fusion.6), kind=kLoop, calls=%fused_computation.5 | loop fusion | flops 715008 | bytes 4290048 | tf_op jit(solution)/shard_map/sub | solution.py:113
  64.5 0.4 fusion.1
  64.9 0.2 fusion
  65.1 1.2 %slice_subtract_fusion.28 = f32[16,40,264]{2,1,0:T(8,128)S(1)} fusion(f32[16,41,266]{2,1,0:T(8,128)S(1)} %fusion, f32[16,42,265]{2,1,0:T(8,128)S(1)} %fusion.1, f32[16,42,266]{2,1,0:T(8,128)S(1)} %slice_subtract_fusion.2), kind=kLoop, calls=%fused_computation.57 | loop fusion | flops 675840 | bytes 4055040 | tf_op jit(solution)/shard_map/sub | solution.py:113
  66.3 0.3 fusion.15
  66.6 0.1 fusion.14
  66.7 1.3 %slice_subtract_fusion.24 = f32[16,38,262]{2,1,0:T(8,128)S(1)} fusion(f32[16,39,264]{2,1,0:T(8,128)S(1)} %fusion.14, f32[16,40,263]{2,1,0:T(8,128)S(1)} %fusion.15, f32[16,40,264]{2,1,0:T(8,128)S(1)} %slice_subtract_fusion.28), kind=kLoop, calls=%fused_computation.49 | loop fusion | flops 637184 | bytes 3823104 | tf_op jit(solution)/shard_map/sub | solution.py:113
  68.0 0.3 fusion.13
  68.4 0.1 fusion.12
  68.5 1.2 %slice_subtract_fusion.20 = f32[16,36,260]{2,1,0:T(8,128)S(1)} fusion(f32[16,37,262]{2,1,0:T(8,128)S(1)} %fusion.12, f32[16,38,261]{2,1,0:T(8,128)S(1)} %fusion.13, f32[16,38,262]{2,1,0:T(8,128)S(1)} %slice_subtract_fusion.24), kind=kLoop, calls=%fused_computation.41 | loop fusion | flops 599040 | bytes 3594240 | tf_op jit(solution)/shard_map/sub | solution.py:113
  69.7 0.5 fusion.11
  70.3 0.1 fusion.10
  70.4 1.2 %slice_subtract_fusion.16 = f32[16,34,258]{2,1,0:T(8,128)S(1)} fusion(f32[16,35,260]{2,1,0:T(8,128)S(1)} %fusion.10, f32[16,36,259]{2,1,0:T(8,128)S(1)} %fusion.11, f32[16,36,260]{2,1,0:T(8,128)S(1)} %slice_subtract_fusion.20), kind=kLoop, calls=%fused_computation.33 | loop fusion | flops 561408 | bytes 3368448 | tf_op jit(solution)/shard_map/sub | solution.py:113
  71.6 0.3 fusion.9
  71.9 0.1 fusion.8
  72.1 1.5 %slice_subtract_fusion.30 = f32[16,32,256]{2,1,0:T(8,128)} fusion(f32[16,33,258]{2,1,0:T(8,128)S(1)} %fusion.8, f32[16,34,257]{2,1,0:T(8,128)S(1)} %fusion.9, f32[16,34,258]{2,1,0:T(8,128)S(1)} %slice_subtract_fusion.16), kind=kLoop, calls=%fused_computation.62 | loop fusion | flops 524288 | bytes 3145728 | tf_op jit(solution)/shard_map/sub | solution.py:113
  (30 shorter events, 0.5 us)
Async XLA Ops:
  0.0 14.3 %copy-start = (s32[1,16]{1,0:T(1,128)S(1)}, s32[1,16]{1,0:T(1,128)}, u32[]{:S(2)}) copy-start(s32[1,16]{1,0:T(1,128)} %param.13) | copy-start | bytes 196
  0.0 1.7 %copy-start.3 = (f32[16,1,4096]{2,1,0:T(1,128)S(1)}, f32[16,1,4096]{2,1,0:T(1,128)}, u32[]{:S(2)}) copy-start(f32[16,1,4096]{2,1,0:T(1,128)} %param.15) | copy-start | bytes 786436
  2.5 11.1 %copy-start.5 = (s32[1,4096]{1,0:T(1,128)S(1)}, s32[1,4096]{1,0:T(1,128)}, u32[]{:S(2)}) copy-start(s32[1,4096]{1,0:T(1,128)} %param.12) | copy-start | bytes 49156
  2.6 11.9 %copy-start.6 = (s32[32,256]{1,0:T(8,128)S(1)}, s32[32,256]{1,0:T(8,128)}, u32[]{:S(2)}) copy-start(s32[32,256]{1,0:T(8,128)} %param.11) | copy-start | bytes 98308
  3.7 27.3 %all-to-all-start = ((f32[16,16,512]{2,0,1:T(8,128)}), f32[16,16,512]{2,0,1:T(8,128)S(1)}, u32[]{:S(2)}, u32[]{:S(2)}) async-start(f32[16,16,512]{2,0,1:T(8,128)} %copy.19), calls=%async_computation | async-start | bytes 1048576 | tf_op jit(solution)/shard_map/all_to_all | solution.py:135
  21.7 9.4 %copy-start.4 = (f32[16,4096]{1,0:T(8,128)S(1)}, f32[16,4096]{1,0:T(8,128)}, u32[]{:S(2)}) copy-start(f32[16,4096]{1,0:T(8,128)} %shard_map.82) | copy-start | bytes 786436
  31.9 8.1 %copy-start.1 = (f32[32,256]{1,0:T(8,128)S(1)}, f32[32,256]{1,0:T(8,128)}, u32[]{:S(2)}) copy-start(f32[32,256]{1,0:T(8,128)} %param.10) | copy-start | bytes 98308
  31.9 8.1 %copy-start.2 = (f32[32,256]{1,0:T(8,128)S(1)}, f32[32,256]{1,0:T(8,128)}, u32[]{:S(2)}) copy-start(f32[32,256]{1,0:T(8,128)} %param.9) | copy-start | bytes 98308
  40.4 2.0 %collective-permute-start = (f32[19,256]{0,1:T(8,128)S(1)}, f32[19,256]{0,1:T(8,128)S(1)}, u32[]{:S(2)}, u32[]{:S(2)}) collective-permute-start(f32[19,256]{0,1:T(8,128)S(1)} %bitcast.48), channel_id=1, source_target_pairs={{0,16},{16,32},{32,48},{48,64},{64,80},{80,96},{96,112},{112,128},... | collective-permute-start | bytes 58376 | tf_op jit(solution)/shard_map/ppermute | solution.py:100
  40.7 4.4 %collective-permute-start.1 = (f32[19,256]{0,1:T(8,128)S(1)}, f32[19,256]{0,1:T(8,128)S(1)}, u32[]{:S(2)}, u32[]{:S(2)}) collective-permute-start(f32[19,256]{0,1:T(8,128)S(1)} %bitcast.50), channel_id=1, source_target_pairs={{16,0},{32,16},{48,32},{64,48},{80,64},{96,80},{112,96},{128,112},... | collective-permute-start | bytes 58376 | tf_op jit(solution)/shard_map/ppermute | solution.py:101
  45.8 10.9 %collective-permute-start.2 = (f32[19,8,272]{2,1,0:T(8,128)S(1)}, f32[19,8,272]{2,1,0:T(8,128)S(1)}, u32[]{:S(2)}, u32[]{:S(2)}) collective-permute-start(f32[19,8,272]{2,1,0:T(8,128)S(1)} %get-tuple-element.7), channel_id=1, source_target_pairs={{0,1},{1,2},{2,3},{3,4},{4,5},{5,6},{6,7},{7,8},{8,9},{9,10},{10,1... | collective-permute-start | bytes 496136 | tf_op jit(solution)/shard_map/ppermute | solution.py:103
  47.1 9.5 %collective-permute-start.3 = (f32[19,8,272]{2,1,0:T(8,128)S(1)}, f32[19,8,272]{2,1,0:T(8,128)S(1)}, u32[]{:S(2)}, u32[]{:S(2)}) collective-permute-start(f32[19,8,272]{2,1,0:T(8,128)S(1)} %get-tuple-element.8), channel_id=1, source_target_pairs={{1,0},{2,1},{3,2},{4,3},{5,4},{6,5},{7,6},{8,7},{9,8},{10,9},{11,1... | collective-permute-start | bytes 496136 | tf_op jit(solution)/shard_map/ppermute | solution.py:104

commit v8 on v7

--- a/solution.py
+++ b/solution.py
@@ -106,15 +106,21 @@
     return block
 
 
-def one_pass(layer_field, east_face, north_face):
-    flux_east = east_face * (layer_field[:, :, 1:] - layer_field[:, :, :-1])
-    flux_north = north_face * (layer_field[:, 1:, :] - layer_field[:, :-1, :])
+def one_pass(field, east_face, north_face, offset):
+    high, wide = field.shape[1], field.shape[2]
+    rows = slice(offset + 1, offset + high - 1)
+    cols = slice(offset + 1, offset + wide - 1)
+    centre = field[:, 1:-1, 1:-1]
+    east_here = east_face[rows, cols]
+    east_west = east_face[rows, offset : offset + wide - 2]
+    north_here = north_face[rows, cols]
+    north_south = north_face[offset : offset + high - 2, cols]
     return (
-        layer_field[:, 1:-1, 1:-1]
-        + flux_east[:, 1:-1, 1:]
-        - flux_east[:, 1:-1, :-1]
-        + flux_north[:, 1:, 1:-1]
-        - flux_north[:, :-1, 1:-1]
+        centre
+        + east_here * (field[:, 1:-1, 2:] - centre)
+        - east_west * (centre - field[:, 1:-1, :-2])
+        + north_here * (field[:, 2:, 1:-1] - centre)
+        - north_south * (centre - field[:, :-2, 1:-1])
     )
 
 
@@ -158,12 +164,7 @@
     east_face = padded[1][:, :-1] * sea_rim[:, :-1] * sea_rim[:, 1:]
     north_face = padded[2][:-1, :] * sea_rim[:-1, :] * sea_rim[1:, :]
     for step_number in range(PASSES):
-        high, wide = field.shape[1], field.shape[2]
-        field = one_pass(
-            field,
-            east_face[step_number : step_number + high, step_number : step_number + wide - 1],
-            north_face[step_number : step_number + high - 1, step_number : step_number + wide],
-        )
+        field = one_pass(field, east_face, north_face, step_number)
     gradient = field
     return gradient
 

time: 73.8 us -> 73.1 us (level)
  other arithmetic: 21.3 us -> 16.1 us
  waiting for transfers between devices: 18.3 us -> 22 us
  starting transfers between devices: 15.8 us -> 16.7 us
    ppermute x1, waiting for transfers between devices: 0.01 us -> 5.24 us  [with_halo(): high = lax.ppermute(high, axis, backward)]
    mul x16 -> x0, other arithmetic: 4.18 us -> none  [the longest x8 3.01 us: one_pass(): flux_east = east_face * (layer_field[:, :, 1:] - layer_field[:, :, :-1])]
    ppermute x1, starting transfers between devices: 0.01 us -> 1.75 us  [with_halo(): low = lax.ppermute(low.reshape(flat), axis, forward).reshape(low.shape)]
    ppermute x1, starting transfers between devices: 1.37 us -> 0.01 us  [with_halo(): low = lax.ppermute(low, axis, forward)]
    ppermute x1, waiting for transfers between devices: 1.16 us -> 0.01 us  [with_halo(): low = lax.ppermute(low.reshape(flat), axis, forward).reshape(low.shape)]
    ppermute x1, starting transfers between devices: 3.9 us -> 5.01 us  [with_halo(): high = lax.ppermute(high, axis, backward)]
    sub x8, other arithmetic: 10.8 us -> 9.72 us  [one_pass(): centre + east_here * (field[:, 1:-1, 2:] - centre)]
where the time goes in v8:
time: 73.1 us; the launch traced here: 72.8 us
  waiting for transfers between devices  22 us (30%)
  starting transfers between devices  16.7 us (23%)
  other arithmetic  16.1 us (22%)
  Pallas kernels  13.6 us (19%)
  local copies, waits for them, and re-layouts  4.04 us (6%)
    all_to_all x1, starting transfers between devices, body(): lax.all_to_all(held, 'lon', split_axis=1, concat_axis=1, tiled=True)  9.98 us
    sub x8, other arithmetic, one_pass(): centre + east_here * (field[:, 1:-1, 2:] - centre)  9.72 us
    all_to_all x1, waiting for transfers between devices, body(): lax.all_to_all(held, 'lon', split_axis=1, concat_axis=1, tiled=True)  9.23 us
    pallas_call x1, Pallas kernels, onehot_scatter(): vmem_call(scatter_kernel, shape, flops, 4 * (levels * slots + 2 * slots +...  6.99 us
    pallas_call x1, Pallas kernels, onehot_gather(): vmem_call(gather_kernel, shape, flops, 4 * (levels * slots + 2 * slots +...  6.64 us
    ppermute x1, waiting for transfers between devices, with_halo(): high = lax.ppermute(high, axis, backward)  5.24 us
    ppermute x1, waiting for transfers between devices, with_halo(): low = lax.ppermute(low, axis, forward)  5.2 us
    ppermute x1, starting transfers between devices, with_halo(): high = lax.ppermute(high, axis, backward)  5.01 us
  transfers between devices with their start and end apart: 5, of which 4 were waited for; matrix products, arithmetic and copies ran while one was open for 3% of the time, Pallas kernels for 9%

profile of v8, /device:TPU:1, one launch (start us, length us, event | category | flops | bytes accessed | tf_op | source)
XLA Modules:
  0.0 72.8 jit_solution(17600269518384186700)
XLA Ops:
  0.0 0.0 copy-start
  0.0 0.0 copy-start.3
  0.0 1.6 %reduce.1 = f32[16,4096]{1,0:T(8,128)S(1)} reduce(f32[16,1,4096]{2,1,0:T(1,128)} %param.15, f32[]{:T(128)} %constant.52), dimensions={1}, to_apply=%param.15.reduce_sub_computation | reduce | bytes 524292 | tf_op args[7]
  1.6 0.1 copy.29
  1.7 0.0 copy-done.3
  1.7 0.6 reduce
  2.4 0.1 copy.28
  2.5 0.1 pad_maximum_fusion.2
  2.5 0.0 copy-start.6
  2.6 0.0 copy-start.5
  2.6 1.1 %copy.19 = f32[16,16,512]{2,0,1:T(8,128)} copy(f32[16,16,512]{2,1,0:T(8,128)S(1)} %pad_maximum_fusion.2) | data formatting | bytes 1048576 | tf_op jit(solution)/shard_map/concatenate | solution.py:138
  3.7 10.0 %all-to-all-start = ((f32[16,16,512]{2,0,1:T(8,128)}), f32[16,16,512]{2,0,1:T(8,128)S(1)}, u32[]{:S(2)}, u32[]{:S(2)}) async-start(f32[16,16,512]{2,0,1:T(8,128)} %copy.19), calls=%async_computation | async-start | bytes 1048576 | tf_op jit(solution)/shard_map/all_to_all | solution.py:141
  13.6 0.0 copy-done.6
  13.7 0.0 copy-done.5
  13.7 0.7 and_select_fusion
  14.3 0.0 copy-done
  14.3 0.1 broadcast_bitcast_fusion
  14.4 0.7 and_select_fusion.1.rows_ref
  15.1 6.6 %shard_map.82 = f32[16,4096]{1,0:T(8,128)} custom-call(f32[512,256]{1,0:T(8,128)} %bitcast.53, s32[1,4096]{1,0:T(1,128)} %and_select_fusion.1.rows_ref, s32[1,4096]{1,0:T(1,128)} %get-tuple-element.5.cols_ref), custom_call_target="tpu_custom_call" | custom-call | flops 3221225472 | bytes 819200 | tf_op jit(solution)/shard_map/pallas_call | solution.py:87
  21.7 0.0 copy-start.4
  21.7 9.2 %all-to-all-done = f32[16,16,512]{2,0,1:T(8,128)S(1)} async-done(((f32[16,16,512]{2,0,1:T(8,128)}), f32[16,16,512]{2,0,1:T(8,128)S(1)}, u32[]{:S(2)}, u32[]{:S(2)}) %all-to-all-start) | async-done | bytes 524320 | tf_op jit(solution)/shard_map/all_to_all | solution.py:141
  31.0 0.1 slice_bitcast_fusion
  31.1 0.0 copy-done.4
  31.1 0.7 %multiply_multiply_fusion.w_ref = f32[16,4096]{1,0:T(8,128)} fusion(f32[16,4096]{1,0:T(8,128)S(1)} %bitcast.37, f32[16,4096]{1,0:T(8,128)S(1)} %bitcast.39, f32[16,4096]{1,0:T(8,128)S(1)} %copy-done.4, f32[4096]{0:T(1024)S(1)} %fusion.69), kind=kLoop, calls=%fused_computation.102 | loop fusion | flops 196608 | bytes 1064960 | tf_op jit(solution)/shard_map/mul | solution.py:148
  31.8 0.0 copy-start.1
  31.8 0.0 copy-start.2
  31.9 7.0 %shard_map.83 = f32[512,256]{1,0:T(8,128)} custom-call(f32[16,4096]{1,0:T(8,128)} %multiply_multiply_fusion.w_ref, s32[1,4096]{1,0:T(1,128)} %and_select_fusion.1.rows_ref, s32[1,4096]{1,0:T(1,128)} %get-tuple-element.5.cols_ref), custom_call_target="tpu_custom_call" | custom-call | flops 3221225472 | bytes 819200 | tf_op jit(solution)/shard_map/pallas_call | solution.py:79
  38.8 1.1 %broadcast_multiply_fusion = f32[16,32,256]{2,1,0:T(8,128)S(1)} fusion(f32[16,32,256]{2,1,0:T(8,128)} %bitcast.41, f32[32,256]{1,0:T(8,128)S(1)} %get-tuple-element.45), kind=kLoop, calls=%fused_computation.101 | loop fusion | flops 131072 | bytes 1081344 | tf_op jit(solution)/shard_map/mul | solution.py:151
  39.9 0.0 copy-done.1
  39.9 0.0 copy-done.2
  40.0 0.1 fusion.70
  40.2 0.3 copy.23
  40.4 0.0 collective-permute-start.1
  40.4 0.3 copy.22
  40.7 1.7 %collective-permute-start = (f32[19,256]{0,1:T(8,128)S(1)}, f32[19,256]{0,1:T(8,128)S(1)}, u32[]{:S(2)}, u32[]{:S(2)}) collective-permute-start(f32[19,256]{0,1:T(8,128)S(1)} %bitcast.50), channel_id=1, source_target_pairs={{0,16},{16,32},{32,48},{48,64},{64,80},{80,96},{96,112},{112,128},... | collective-permute-start | bytes 58376 | tf_op jit(solution)/shard_map/ppermute | solution.py:100
  42.5 2.4 %collective-permute-done.1 = f32[19,256]{0,1:T(8,128)S(1)} collective-permute-done((f32[19,256]{0,1:T(8,128)S(1)}, f32[19,256]{0,1:T(8,128)S(1)}, u32[]{:S(2)}, u32[]{:S(2)}) %collective-permute-start.1) | collective-permute-done | bytes 19488 | tf_op jit(solution)/shard_map/ppermute | solution.py:101
  44.8 0.4 copy.25
  45.2 0.0 collective-permute-done
  45.2 0.4 copy.24
  45.6 0.2 pad_maximum_fusion.8
  45.9 5.0 %collective-permute-start.3 = (f32[19,8,272]{2,1,0:T(8,128)S(1)}, f32[19,8,272]{2,1,0:T(8,128)S(1)}, u32[]{:S(2)}, u32[]{:S(2)}) collective-permute-start(f32[19,8,272]{2,1,0:T(8,128)S(1)} %get-tuple-element.8), channel_id=1, source_target_pairs={{1,0},{2,1},{3,2},{4,3},{5,4},{6,5},{7,6},{8,7},{9,8},{10,9},{11,1... | collective-permute-start | bytes 496136 | tf_op jit(solution)/shard_map/ppermute | solution.py:104
  50.9 0.0 collective-permute-start.2
  50.9 5.2 %collective-permute-done.3 = f32[19,8,272]{2,1,0:T(8,128)S(1)} collective-permute-done((f32[19,8,272]{2,1,0:T(8,128)S(1)}, f32[19,8,272]{2,1,0:T(8,128)S(1)}, u32[]{:S(2)}, u32[]{:S(2)}) %collective-permute-start.3) | collective-permute-done | bytes 165408 | tf_op jit(solution)/shard_map/ppermute | solution.py:104
  56.1 5.2 %collective-permute-done.2 = f32[19,8,272]{2,1,0:T(8,128)S(1)} collective-permute-done((f32[19,8,272]{2,1,0:T(8,128)S(1)}, f32[19,8,272]{2,1,0:T(8,128)S(1)}, u32[]{:S(2)}, u32[]{:S(2)}) %collective-permute-start.2) | collective-permute-done | bytes 165408 | tf_op jit(solution)/shard_map/ppermute | solution.py:103
  61.3 0.4 pad_maximum_fusion
  61.8 0.1 fusion.64
  61.9 0.1 slice_multiply_fusion.2
  62.0 0.1 fusion.85
  62.1 0.1 fusion.83
  62.2 0.1 fusion.81
  62.4 0.1 fusion.79
  62.5 0.1 fusion.77
  62.7 0.1 fusion.75
  62.8 0.1 fusion.73
  63.0 0.1 fusion.71
  63.1 1.3 %fusion.17 = f32[16,46,270]{2,1,0:T(8,128)S(1)} fusion(f32[19,48,272]{2,1,0:T(8,128)S(1)} %pad_maximum_fusion, f32[46,270]{1,0:T(8,128)S(1)} %get-tuple-element.47, f32[46,270]{1,0:T(8,128)S(1)} %get-tuple-element.48, f32[46,270]{1,0:T(8,128)S(1)} %get-tuple-element.42, f32[46,270]{1,0:T(8,128)S(1)} %get-tuple-element.41), kind=kLoop, calls=%fused_computation.27 | loop fusion | flops 2384640 | bytes 4968000 | tf_op jit(solution)/shard_map/sub | solution.py:119
  64.4 1.3 %fusion.9 = f32[16,44,268]{2,1,0:T(8,128)S(1)} fusion(f32[16,46,270]{2,1,0:T(8,128)S(1)} %fusion.17, f32[44,268]{1,0:T(8,128)S(1)} %get-tuple-element.49, f32[44,268]{1,0:T(8,128)S(1)} %get-tuple-element.50, f32[44,268]{1,0:T(8,128)S(1)} %get-tuple-element.38, f32[44,268]{1,0:T(8,128)S(1)} %get-tuple-element.37), kind=kLoop, calls=%fused_computation.15 | loop fusion | flops 2264064 | bytes 4716800 | tf_op jit(solution)/shard_map/sub | solution.py:119
  65.7 1.3 %fusion.1 = f32[16,42,266]{2,1,0:T(8,128)S(1)} fusion(f32[16,44,268]{2,1,0:T(8,128)S(1)} %fusion.9, f32[42,266]{1,0:T(8,128)S(1)} %get-tuple-element.51, f32[42,266]{1,0:T(8,128)S(1)} %get-tuple-element.52, f32[42,266]{1,0:T(8,128)S(1)} %get-tuple-element.34, f32[42,266]{1,0:T(8,128)S(1)} %get-tuple-element.33), kind=kLoop, calls=%fused_computation.3 | loop fusion | flops 2145024 | bytes 4468800 | tf_op jit(solution)/shard_map/sub | solution.py:119
  67.0 1.1 %fusion.49 = f32[16,40,264]{2,1,0:T(8,128)S(1)} fusion(f32[16,42,266]{2,1,0:T(8,128)S(1)} %fusion.1, f32[40,264]{1,0:T(8,128)S(1)} %get-tuple-element.53, f32[40,264]{1,0:T(8,128)S(1)} %get-tuple-element.54, f32[40,264]{1,0:T(8,128)S(1)} %get-tuple-element.30, f32[40,264]{1,0:T(8,128)S(1)} %get-tuple-element.29), kind=kLoop, calls=%fused_computation.75 | loop fusion | flops 2027520 | bytes 4224000 | tf_op jit(solution)/shard_map/sub | solution.py:119
  68.1 1.1 %fusion.41 = f32[16,38,262]{2,1,0:T(8,128)S(1)} fusion(f32[16,40,264]{2,1,0:T(8,128)S(1)} %fusion.49, f32[38,262]{1,0:T(8,128)S(1)} %get-tuple-element.55, f32[38,262]{1,0:T(8,128)S(1)} %get-tuple-element.56, f32[38,262]{1,0:T(8,128)S(1)} %get-tuple-element.26, f32[38,262]{1,0:T(8,128)S(1)} %get-tuple-element.25), kind=kLoop, calls=%fused_computation.63 | loop fusion | flops 1911552 | bytes 3982400 | tf_op jit(solution)/shard_map/sub | solution.py:119
  69.2 1.1 %fusion.33 = f32[16,36,260]{2,1,0:T(8,128)S(1)} fusion(f32[16,38,262]{2,1,0:T(8,128)S(1)} %fusion.41, f32[36,260]{1,0:T(8,128)S(1)} %get-tuple-element.57, f32[36,260]{1,0:T(8,128)S(1)} %get-tuple-element.58, f32[36,260]{1,0:T(8,128)S(1)} %get-tuple-element.22, f32[36,260]{1,0:T(8,128)S(1)} %get-tuple-element.21), kind=kLoop, calls=%fused_computation.51 | loop fusion | flops 1797120 | bytes 3744000 | tf_op jit(solution)/shard_map/sub | solution.py:119
  70.3 1.1 %fusion.25 = f32[16,34,258]{2,1,0:T(8,128)S(1)} fusion(f32[16,36,260]{2,1,0:T(8,128)S(1)} %fusion.33, f32[34,258]{1,0:T(8,128)S(1)} %get-tuple-element.59, f32[34,258]{1,0:T(8,128)S(1)} %get-tuple-element.60, f32[34,258]{1,0:T(8,128)S(1)} %get-tuple-element.18, f32[34,258]{1,0:T(8,128)S(1)} %get-tuple-element.17), kind=kLoop, calls=%fused_computation.39 | loop fusion | flops 1684224 | bytes 3508800 | tf_op jit(solution)/shard_map/sub | solution.py:119
  71.4 1.4 %fusion.57 = f32[16,32,256]{2,1,0:T(8,128)} fusion(f32[16,34,258]{2,1,0:T(8,128)S(1)} %fusion.25, f32[32,256]{1,0:T(8,128)S(1)} %get-tuple-element.61, f32[32,256]{1,0:T(8,128)S(1)} %get-tuple-element.62, f32[32,256]{1,0:T(8,128)S(1)} %get-tuple-element.14, f32[32,256]{1,0:T(8,128)S(1)} %get-tuple-element.13), kind=kLoop, calls=%fused_computation.88 | loop fusion | flops 1572864 | bytes 3276800 | tf_op jit(solution)/shard_map/sub | solution.py:119
  (9 shorter events, 0.1 us)
Async XLA Ops:
  0.0 14.3 %copy-start = (s32[1,16]{1,0:T(1,128)S(1)}, s32[1,16]{1,0:T(1,128)}, u32[]{:S(2)}) copy-start(s32[1,16]{1,0:T(1,128)} %param.13) | copy-start | bytes 196
  0.0 1.7 %copy-start.3 = (f32[16,1,4096]{2,1,0:T(1,128)S(1)}, f32[16,1,4096]{2,1,0:T(1,128)}, u32[]{:S(2)}) copy-start(f32[16,1,4096]{2,1,0:T(1,128)} %param.14) | copy-start | bytes 786436
  2.5 11.1 %copy-start.6 = (s32[32,256]{1,0:T(8,128)S(1)}, s32[32,256]{1,0:T(8,128)}, u32[]{:S(2)}) copy-start(s32[32,256]{1,0:T(8,128)} %param.11) | copy-start | bytes 98308
  2.6 11.1 %copy-start.5 = (s32[1,4096]{1,0:T(1,128)S(1)}, s32[1,4096]{1,0:T(1,128)}, u32[]{:S(2)}) copy-start(s32[1,4096]{1,0:T(1,128)} %param.12) | copy-start | bytes 49156
  3.7 27.3 %all-to-all-start = ((f32[16,16,512]{2,0,1:T(8,128)}), f32[16,16,512]{2,0,1:T(8,128)S(1)}, u32[]{:S(2)}, u32[]{:S(2)}) async-start(f32[16,16,512]{2,0,1:T(8,128)} %copy.19), calls=%async_computation | async-start | bytes 1048576 | tf_op jit(solution)/shard_map/all_to_all | solution.py:141
  21.7 9.4 %copy-start.4 = (f32[16,4096]{1,0:T(8,128)S(1)}, f32[16,4096]{1,0:T(8,128)}, u32[]{:S(2)}) copy-start(f32[16,4096]{1,0:T(8,128)} %shard_map.82) | copy-start | bytes 786436
  31.8 8.1 %copy-start.1 = (f32[32,256]{1,0:T(8,128)S(1)}, f32[32,256]{1,0:T(8,128)}, u32[]{:S(2)}) copy-start(f32[32,256]{1,0:T(8,128)} %param.10) | copy-start | bytes 98308
  31.8 8.1 %copy-start.2 = (f32[32,256]{1,0:T(8,128)S(1)}, f32[32,256]{1,0:T(8,128)}, u32[]{:S(2)}) copy-start(f32[32,256]{1,0:T(8,128)} %param.9) | copy-start | bytes 98308
  40.4 4.4 %collective-permute-start.1 = (f32[19,256]{0,1:T(8,128)S(1)}, f32[19,256]{0,1:T(8,128)S(1)}, u32[]{:S(2)}, u32[]{:S(2)}) collective-permute-start(f32[19,256]{0,1:T(8,128)S(1)} %bitcast.48), channel_id=1, source_target_pairs={{16,0},{32,16},{48,32},{64,48},{80,64},{96,80},{112,96},{128,112},... | collective-permute-start | bytes 58376 | tf_op jit(solution)/shard_map/ppermute | solution.py:101
  40.7 4.5 %collective-permute-start = (f32[19,256]{0,1:T(8,128)S(1)}, f32[19,256]{0,1:T(8,128)S(1)}, u32[]{:S(2)}, u32[]{:S(2)}) collective-permute-start(f32[19,256]{0,1:T(8,128)S(1)} %bitcast.50), channel_id=1, source_target_pairs={{0,16},{16,32},{32,48},{48,64},{64,80},{80,96},{96,112},{112,128},... | collective-permute-start | bytes 58376 | tf_op jit(solution)/shard_map/ppermute | solution.py:100
  45.9 10.3 %collective-permute-start.3 = (f32[19,8,272]{2,1,0:T(8,128)S(1)}, f32[19,8,272]{2,1,0:T(8,128)S(1)}, u32[]{:S(2)}, u32[]{:S(2)}) collective-permute-start(f32[19,8,272]{2,1,0:T(8,128)S(1)} %get-tuple-element.8), channel_id=1, source_target_pairs={{1,0},{2,1},{3,2},{4,3},{5,4},{6,5},{7,6},{8,7},{9,8},{10,9},{11,1... | collective-permute-start | bytes 496136 | tf_op jit(solution)/shard_map/ppermute | solution.py:104
  50.9 10.5 %collective-permute-start.2 = (f32[19,8,272]{2,1,0:T(8,128)S(1)}, f32[19,8,272]{2,1,0:T(8,128)S(1)}, u32[]{:S(2)}, u32[]{:S(2)}) collective-permute-start(f32[19,8,272]{2,1,0:T(8,128)S(1)} %get-tuple-element.7), channel_id=1, source_target_pairs={{0,1},{1,2},{2,3},{3,4},{4,5},{5,6},{6,7},{7,8},{8,9},{9,10},{10,1... | collective-permute-start | bytes 496136 | tf_op jit(solution)/shard_map/ppermute | solution.py:103

commit v9 on v8

--- a/solution.py
+++ b/solution.py
@@ -7,6 +7,7 @@
 
 PASSES = 8
 CHUNK = 512
+SCATTER_CHUNK = 1024
 
 
 def three_parts(x):
@@ -17,27 +18,35 @@
     return high, middle, low
 
 
-def scatter_kernel(w_ref, rows_ref, cols_ref, out_ref):
-    levels, slots = w_ref.shape
-    cells, cols_here = out_ref.shape
-    rows_here = cells // levels
-    out_ref[...] = jnp.zeros_like(out_ref)
+def scatter_kernel(values_ref, weights_ref, seen_ref, usable_ref, rows_ref, cols_ref, sea_ref, out_ref, acc_ref):
+    levels, slots = values_ref.shape
+    _, rows_here, cols_here = out_ref.shape
+    cells = levels * rows_here
+    acc_ref[...] = jnp.zeros_like(acc_ref)
 
     def step(k, carry):
-        start = pl.multiple_of(k * CHUNK, CHUNK)
-        w = w_ref[:, pl.ds(start, CHUNK)]
-        row_hit = lax.broadcasted_iota(jnp.int32, (rows_here, CHUNK), 0) == rows_ref[:, pl.ds(start, CHUNK)]
-        col_hit = lax.broadcasted_iota(jnp.int32, (cols_here, CHUNK), 0) == cols_ref[:, pl.ds(start, CHUNK)]
+        start = pl.multiple_of(k * SCATTER_CHUNK, SCATTER_CHUNK)
+        here = pl.ds(start, SCATTER_CHUNK)
+        w = weights_ref[:, here] * (values_ref[:, here] - seen_ref[:, here]) * usable_ref[:, here]
+        row_hit = lax.broadcasted_iota(jnp.int32, (rows_here, SCATTER_CHUNK), 0) == rows_ref[:, here]
+        col_hit = lax.broadcasted_iota(jnp.int32, (cols_here, SCATTER_CHUNK), 0) == cols_ref[:, here]
         col_hit = col_hit.astype(jnp.float32).astype(jnp.bfloat16)
-        for part in three_parts(w):
-            spread = jnp.where(row_hit[None], part.astype(jnp.float32)[:, None, :], 0.0)
-            spread = spread.reshape(cells, CHUNK).astype(jnp.bfloat16)
-            out_ref[...] += lax.dot_general(
-                spread, col_hit, (((1,), (1,)), ((), ())), preferred_element_type=jnp.float32
-            )
+        spread = [
+            jnp.where(row_hit[None], part.astype(jnp.float32)[:, None, :], 0.0)
+            .reshape(cells, SCATTER_CHUNK)
+            .astype(jnp.bfloat16)
+            for part in three_parts(w)
+        ]
+        acc_ref[...] += lax.dot_general(
+            jnp.concatenate(spread, axis=1),
+            jnp.concatenate([col_hit] * 3, axis=1),
+            (((1,), (1,)), ((), ())),
+            preferred_element_type=jnp.float32,
+        )
         return carry
 
-    lax.fori_loop(0, slots // CHUNK, step, 0)
+    lax.fori_loop(0, slots // SCATTER_CHUNK, step, 0)
+    out_ref[...] = acc_ref[...].reshape(levels, rows_here, cols_here) * sea_ref[...][None]
 
 
 def gather_kernel(state_ref, rows_ref, cols_ref, out_ref):
@@ -72,11 +81,22 @@
     )
 
 
-def onehot_scatter(w, rows, cols, rows_here, cols_here):
-    levels, slots = w.shape
-    shape = jax.ShapeDtypeStruct((levels * rows_here, cols_here), jnp.float32)
+def onehot_scatter(values, weights, seen, usable, rows, cols, sea):
+    levels, slots = values.shape
+    rows_here, cols_here = sea.shape
+    shape = jax.ShapeDtypeStruct((levels, rows_here, cols_here), jnp.float32)
     flops = 6 * levels * rows_here * cols_here * slots
-    return vmem_call(scatter_kernel, shape, flops, 4 * (levels * slots + 2 * slots + levels * rows_here * cols_here))(w, rows, cols)
+    return pl.pallas_call(
+        scatter_kernel,
+        out_shape=shape,
+        in_specs=[pl.BlockSpec(memory_space=pltpu.VMEM)] * 7,
+        out_specs=pl.BlockSpec(memory_space=pltpu.VMEM),
+        scratch_shapes=[pltpu.VMEM((levels * rows_here, cols_here), jnp.float32)],
+        cost_estimate=pl.CostEstimate(
+            flops=flops, bytes_accessed=4 * (3 * levels * slots + 3 * slots + levels * rows_here * cols_here),
+            transcendentals=0,
+        ),
+    )(values, weights, seen, usable, rows, cols, sea)
 
 
 def onehot_gather(state2d, rows, cols, levels):
@@ -145,10 +165,8 @@
     target_rows = (targets // cols_here)[None, :]
     target_cols = (targets % cols_here)[None, :]
     at_column = onehot_gather(state.reshape(levels * rows_here, cols_here), target_rows, target_cols, levels)
-    weighted = weights * (values - at_column) * usable
     sea = land_sea.astype(jnp.float32)
-    gradient = onehot_scatter(weighted, target_rows, target_cols, rows_here, cols_here)
-    gradient = gradient.reshape(levels, rows_here, cols_here) * sea[None]
+    gradient = onehot_scatter(values, weights, at_column, usable[None, :], target_rows, target_cols, sea)
     rim_width = PASSES
     stacked = jnp.concatenate([gradient, sea[None], coef_lon[None], coef_lat[None]], axis=0)
     padded = with_halo(stacked, (("lon", 2), ("lat", 1)), rim_width)

time: 73.1 us -> 72.8 us (level)
  local copies, waits for them, and re-layouts: 4.04 us -> 5.44 us
  waiting for transfers between devices: 22 us -> 20.8 us
  Pallas kernels: 13.6 us -> 12.8 us
    mul x2 -> x0, other arithmetic: 1.83 us -> none  [the longest x1 1.08 us: body(): gradient = gradient.reshape(levels, rows_here, cols_here) * sea[None]]
    all_to_all x1, waiting for transfers between devices: 9.23 us -> 8.03 us  [body(): lax.all_to_all(held, 'lon', split_axis=1, concat_axis=1, tiled=True)]
    concatenate x1, other arithmetic: 0.05 us -> 1.08 us  [body(): jnp.concatenate([gradient, sea[None], coef_lon[None], coef_lat[None]], ax...]
    pallas_call x1, Pallas kernels: 6.99 us -> 6.14 us  [onehot_scatter(): pl.pallas_call(scatter_kernel, out_shape=shape, in_specs=[pl.BlockSpec(me...]
  transfers between devices with their start and end apart: 5 -> 5, of which waited for: 4 -> 4; matrix products, arithmetic and copies ran while one was open for 3% -> 5% of each run, Pallas kernels for 9% -> 9%
where the time goes in v9:
time: 72.8 us; the launch traced here: 72.5 us
  waiting for transfers between devices  20.8 us (29%)
  starting transfers between devices  16.7 us (23%)
  other arithmetic  16.5 us (23%)
  Pallas kernels  12.8 us (18%)
  local copies, waits for them, and re-layouts  5.44 us (7%)
    all_to_all x1, starting transfers between devices, body(): lax.all_to_all(held, 'lon', split_axis=1, concat_axis=1, tiled=True)  9.98 us
    sub x8, other arithmetic, one_pass(): centre + east_here * (field[:, 1:-1, 2:] - centre)  9.72 us
    all_to_all x1, waiting for transfers between devices, body(): lax.all_to_all(held, 'lon', split_axis=1, concat_axis=1, tiled=True)  8.03 us
    pallas_call x1, Pallas kernels, onehot_gather(): vmem_call(gather_kernel, shape, flops, 4 * (levels * slots + 2 * slots +...  6.64 us
    pallas_call x1, Pallas kernels, onehot_scatter(): pl.pallas_call(scatter_kernel, out_shape=shape, in_specs=[pl.BlockSpec(me...  6.14 us
    ppermute x1, waiting for transfers between devices, with_halo(): high = lax.ppermute(high, axis, backward)  5.24 us
    ppermute x1, waiting for transfers between devices, with_halo(): low = lax.ppermute(low, axis, forward)  5.2 us
    ppermute x1, starting transfers between devices, with_halo(): high = lax.ppermute(high, axis, backward)  5 us
  transfers between devices with their start and end apart: 5, of which 4 were waited for; matrix products, arithmetic and copies ran while one was open for 5% of the time, Pallas kernels for 9%

profile of v9, /device:TPU:1, one launch (start us, length us, event | category | flops | bytes accessed | tf_op | source)
XLA Modules:
  0.0 72.5 jit_solution(4402037119313576375)
XLA Ops:
  0.0 0.0 copy-start
  0.0 0.0 copy-start.4
  0.0 1.6 %reduce.1 = f32[16,4096]{1,0:T(8,128)S(1)} reduce(f32[16,1,4096]{2,1,0:T(1,128)} %param.15, f32[]{:T(128)} %constant.52), dimensions={1}, to_apply=%param.15.reduce_sub_computation | reduce | bytes 524292 | tf_op args[7]
  1.6 0.1 copy.29
  1.7 0.0 copy-done.4
  1.7 0.6 reduce
  2.4 0.1 copy.28
  2.5 0.1 pad_maximum_fusion.2
  2.5 0.0 copy-start.6
  2.6 0.0 copy-start.5
  2.6 1.1 %copy.19 = f32[16,16,512]{2,0,1:T(8,128)} copy(f32[16,16,512]{2,1,0:T(8,128)S(1)} %pad_maximum_fusion.2) | data formatting | bytes 1048576 | tf_op jit(solution)/shard_map/concatenate | solution.py:158
  3.7 10.0 %all-to-all-start = ((f32[16,16,512]{2,0,1:T(8,128)}), f32[16,16,512]{2,0,1:T(8,128)S(1)}, u32[]{:S(2)}, u32[]{:S(2)}) async-start(f32[16,16,512]{2,0,1:T(8,128)} %copy.19), calls=%async_computation | async-start | bytes 1048576 | tf_op jit(solution)/shard_map/all_to_all | solution.py:161
  13.6 0.0 copy-done.6
  13.7 0.6 fusion.82
  14.3 0.0 copy-done.5
  14.3 0.7 and_select_fusion.1
  14.9 0.7 and_select_fusion.2.rows_ref
  15.6 6.6 %shard_map.82.seen_ref = f32[16,4096]{1,0:T(8,128)} custom-call(f32[512,256]{1,0:T(8,128)} %bitcast.52, s32[1,4096]{1,0:T(1,128)} %and_select_fusion.2.rows_ref, s32[1,4096]{1,0:T(1,128)} %get-tuple-element.5.cols_ref), custom_call_target="tpu_custom_call" | custom-call | flops 3221225472 | bytes 819200 | tf_op jit(solution)/shard_map/pallas_call | solution.py:107
  22.2 0.0 copy-done
  22.2 0.1 broadcast_bitcast_fusion
  22.3 0.6 compare_select_fusion.usable_ref
  22.9 8.0 %all-to-all-done = f32[16,16,512]{2,0,1:T(8,128)S(1)} async-done(((f32[16,16,512]{2,0,1:T(8,128)}), f32[16,16,512]{2,0,1:T(8,128)S(1)}, u32[]{:S(2)}, u32[]{:S(2)}) %all-to-all-start) | async-done | bytes 524320 | tf_op jit(solution)/shard_map/all_to_all | solution.py:161
  31.0 0.1 slice_bitcast_fusion
  31.0 0.7 copy.26
  31.8 0.7 copy.27
  32.5 6.1 %shard_map.83 = f32[16,32,256]{2,1,0:T(8,128)} custom-call(f32[16,4096]{1,0:T(8,128)} %bitcast.45, f32[16,4096]{1,0:T(8,128)} %bitcast.46, f32[16,4096]{1,0:T(8,128)} %shard_map.82.seen_ref, f32[1,4096]{1,0:T(1,128)} %compare_select_fusion.usable_ref, s32[1,4096]{1,0:T(1,128)} %and_select_fusion.2.rows_ref, s32[1,4096]{1,0:T(1,128)} %get-tuple-element.5.cols_ref, ...), custom_call_target="tpu_custom_call" | custom-call | flops 3221225472 | bytes 1359872 | tf_op jit(solution)/shard_map/pallas_call | solution.py:89
  38.6 0.0 copy-done.2
  38.6 0.0 copy-done.3
  38.6 1.1 %pad_maximum_fusion.1 = f32[19,32,256]{2,1,0:T(8,128)S(1)} fusion(f32[1,32,256]{2,1,0:T(8,128)S(1)} %bitcast.39, f32[1,32,256]{2,1,0:T(8,128)S(1)} %bitcast.42, f32[1,32,256]{2,1,0:T(8,128)S(1)} %get-tuple-element.46, f32[16,32,256]{2,1,0:T(8,128)} %shard_map.83), kind=kLoop, calls=%fused_computation.85 | loop fusion | flops 466944 | bytes 1245184 | tf_op jit(solution)/shard_map/concatenate | solution.py:171
  39.7 0.1 fusion.65
  39.9 0.0 copy-start.1
  39.9 0.3 copy.23
  40.1 0.0 collective-permute-start.1
  40.1 0.3 copy.22
  40.4 1.7 %collective-permute-start = (f32[19,256]{0,1:T(8,128)S(1)}, f32[19,256]{0,1:T(8,128)S(1)}, u32[]{:S(2)}, u32[]{:S(2)}) collective-permute-start(f32[19,256]{0,1:T(8,128)S(1)} %bitcast.49), channel_id=1, source_target_pairs={{0,16},{16,32},{32,48},{48,64},{64,80},{80,96},{96,112},{112,128},... | collective-permute-start | bytes 58376 | tf_op jit(solution)/shard_map/ppermute | solution.py:120
  42.2 2.4 %collective-permute-done.1 = f32[19,256]{0,1:T(8,128)S(1)} collective-permute-done((f32[19,256]{0,1:T(8,128)S(1)}, f32[19,256]{0,1:T(8,128)S(1)}, u32[]{:S(2)}, u32[]{:S(2)}) %collective-permute-start.1) | collective-permute-done | bytes 19488 | tf_op jit(solution)/shard_map/ppermute | solution.py:121
  44.5 0.4 copy.25
  44.9 0.0 collective-permute-done
  44.9 0.4 copy.24
  45.4 0.0 copy-done.1
  45.4 0.2 pad_maximum_fusion.8
  45.6 5.0 %collective-permute-start.3 = (f32[19,8,272]{2,1,0:T(8,128)S(1)}, f32[19,8,272]{2,1,0:T(8,128)S(1)}, u32[]{:S(2)}, u32[]{:S(2)}) collective-permute-start(f32[19,8,272]{2,1,0:T(8,128)S(1)} %get-tuple-element.8), channel_id=1, source_target_pairs={{1,0},{2,1},{3,2},{4,3},{5,4},{6,5},{7,6},{8,7},{9,8},{10,9},{11,1... | collective-permute-start | bytes 496136 | tf_op jit(solution)/shard_map/ppermute | solution.py:124
  50.6 0.0 collective-permute-start.2
  50.6 5.2 %collective-permute-done.3 = f32[19,8,272]{2,1,0:T(8,128)S(1)} collective-permute-done((f32[19,8,272]{2,1,0:T(8,128)S(1)}, f32[19,8,272]{2,1,0:T(8,128)S(1)}, u32[]{:S(2)}, u32[]{:S(2)}) %collective-permute-start.3) | collective-permute-done | bytes 165408 | tf_op jit(solution)/shard_map/ppermute | solution.py:124
  55.9 5.2 %collective-permute-done.2 = f32[19,8,272]{2,1,0:T(8,128)S(1)} collective-permute-done((f32[19,8,272]{2,1,0:T(8,128)S(1)}, f32[19,8,272]{2,1,0:T(8,128)S(1)}, u32[]{:S(2)}, u32[]{:S(2)}) %collective-permute-start.2) | collective-permute-done | bytes 165408 | tf_op jit(solution)/shard_map/ppermute | solution.py:123
  61.1 0.4 pad_maximum_fusion
  61.5 0.1 fusion.64
  61.6 0.1 slice_multiply_fusion.2
  61.7 0.1 fusion.80
  61.8 0.1 fusion.78
  61.9 0.1 fusion.76
  62.1 0.1 fusion.74
  62.2 0.1 fusion.72
  62.4 0.1 fusion.70
  62.5 0.1 fusion.68
  62.7 0.1 fusion.66
  62.8 1.3 %fusion.17 = f32[16,46,270]{2,1,0:T(8,128)S(1)} fusion(f32[19,48,272]{2,1,0:T(8,128)S(1)} %pad_maximum_fusion, f32[46,270]{1,0:T(8,128)S(1)} %get-tuple-element.47, f32[46,270]{1,0:T(8,128)S(1)} %get-tuple-element.48, f32[46,270]{1,0:T(8,128)S(1)} %get-tuple-element.42, f32[46,270]{1,0:T(8,128)S(1)} %get-tuple-element.41), kind=kLoop, calls=%fused_computation.27 | loop fusion | flops 2384640 | bytes 4968000 | tf_op jit(solution)/shard_map/sub | solution.py:139
  64.1 1.3 %fusion.9 = f32[16,44,268]{2,1,0:T(8,128)S(1)} fusion(f32[16,46,270]{2,1,0:T(8,128)S(1)} %fusion.17, f32[44,268]{1,0:T(8,128)S(1)} %get-tuple-element.49, f32[44,268]{1,0:T(8,128)S(1)} %get-tuple-element.50, f32[44,268]{1,0:T(8,128)S(1)} %get-tuple-element.38, f32[44,268]{1,0:T(8,128)S(1)} %get-tuple-element.37), kind=kLoop, calls=%fused_computation.15 | loop fusion | flops 2264064 | bytes 4716800 | tf_op jit(solution)/shard_map/sub | solution.py:139
  65.4 1.3 %fusion.1 = f32[16,42,266]{2,1,0:T(8,128)S(1)} fusion(f32[16,44,268]{2,1,0:T(8,128)S(1)} %fusion.9, f32[42,266]{1,0:T(8,128)S(1)} %get-tuple-element.51, f32[42,266]{1,0:T(8,128)S(1)} %get-tuple-element.52, f32[42,266]{1,0:T(8,128)S(1)} %get-tuple-element.34, f32[42,266]{1,0:T(8,128)S(1)} %get-tuple-element.33), kind=kLoop, calls=%fused_computation.3 | loop fusion | flops 2145024 | bytes 4468800 | tf_op jit(solution)/shard_map/sub | solution.py:139
  66.7 1.1 %fusion.49 = f32[16,40,264]{2,1,0:T(8,128)S(1)} fusion(f32[16,42,266]{2,1,0:T(8,128)S(1)} %fusion.1, f32[40,264]{1,0:T(8,128)S(1)} %get-tuple-element.53, f32[40,264]{1,0:T(8,128)S(1)} %get-tuple-element.54, f32[40,264]{1,0:T(8,128)S(1)} %get-tuple-element.30, f32[40,264]{1,0:T(8,128)S(1)} %get-tuple-element.29), kind=kLoop, calls=%fused_computation.75 | loop fusion | flops 2027520 | bytes 4224000 | tf_op jit(solution)/shard_map/sub | solution.py:139
  67.8 1.1 %fusion.41 = f32[16,38,262]{2,1,0:T(8,128)S(1)} fusion(f32[16,40,264]{2,1,0:T(8,128)S(1)} %fusion.49, f32[38,262]{1,0:T(8,128)S(1)} %get-tuple-element.55, f32[38,262]{1,0:T(8,128)S(1)} %get-tuple-element.56, f32[38,262]{1,0:T(8,128)S(1)} %get-tuple-element.26, f32[38,262]{1,0:T(8,128)S(1)} %get-tuple-element.25), kind=kLoop, calls=%fused_computation.63 | loop fusion | flops 1911552 | bytes 3982400 | tf_op jit(solution)/shard_map/sub | solution.py:139
  68.9 1.1 %fusion.33 = f32[16,36,260]{2,1,0:T(8,128)S(1)} fusion(f32[16,38,262]{2,1,0:T(8,128)S(1)} %fusion.41, f32[36,260]{1,0:T(8,128)S(1)} %get-tuple-element.57, f32[36,260]{1,0:T(8,128)S(1)} %get-tuple-element.58, f32[36,260]{1,0:T(8,128)S(1)} %get-tuple-element.22, f32[36,260]{1,0:T(8,128)S(1)} %get-tuple-element.21), kind=kLoop, calls=%fused_computation.51 | loop fusion | flops 1797120 | bytes 3744000 | tf_op jit(solution)/shard_map/sub | solution.py:139
  70.0 1.1 %fusion.25 = f32[16,34,258]{2,1,0:T(8,128)S(1)} fusion(f32[16,36,260]{2,1,0:T(8,128)S(1)} %fusion.33, f32[34,258]{1,0:T(8,128)S(1)} %get-tuple-element.59, f32[34,258]{1,0:T(8,128)S(1)} %get-tuple-element.60, f32[34,258]{1,0:T(8,128)S(1)} %get-tuple-element.18, f32[34,258]{1,0:T(8,128)S(1)} %get-tuple-element.17), kind=kLoop, calls=%fused_computation.39 | loop fusion | flops 1684224 | bytes 3508800 | tf_op jit(solution)/shard_map/sub | solution.py:139
  71.1 1.4 %fusion.57 = f32[16,32,256]{2,1,0:T(8,128)} fusion(f32[16,34,258]{2,1,0:T(8,128)S(1)} %fusion.25, f32[32,256]{1,0:T(8,128)S(1)} %get-tuple-element.61, f32[32,256]{1,0:T(8,128)S(1)} %get-tuple-element.62, f32[32,256]{1,0:T(8,128)S(1)} %get-tuple-element.14, f32[32,256]{1,0:T(8,128)S(1)} %get-tuple-element.13), kind=kLoop, calls=%fused_computation.88 | loop fusion | flops 1572864 | bytes 3276800 | tf_op jit(solution)/shard_map/sub | solution.py:139
  (6 shorter events, 0.1 us)
Async XLA Ops:
  0.0 22.2 %copy-start = (s32[1,16]{1,0:T(1,128)S(1)}, s32[1,16]{1,0:T(1,128)}, u32[]{:S(2)}) copy-start(s32[1,16]{1,0:T(1,128)} %param.13) | copy-start | bytes 196
  0.0 1.7 %copy-start.4 = (f32[16,1,4096]{2,1,0:T(1,128)S(1)}, f32[16,1,4096]{2,1,0:T(1,128)}, u32[]{:S(2)}) copy-start(f32[16,1,4096]{2,1,0:T(1,128)} %param.14) | copy-start | bytes 786436
  2.5 11.1 %copy-start.6 = (s32[32,256]{1,0:T(8,128)S(1)}, s32[32,256]{1,0:T(8,128)}, u32[]{:S(2)}) copy-start(s32[32,256]{1,0:T(8,128)} %param.11) | copy-start | bytes 98308
  2.6 11.7 %copy-start.5 = (s32[1,4096]{1,0:T(1,128)S(1)}, s32[1,4096]{1,0:T(1,128)}, u32[]{:S(2)}) copy-start(s32[1,4096]{1,0:T(1,128)} %param.12) | copy-start | bytes 49156
  3.7 27.3 %all-to-all-start = ((f32[16,16,512]{2,0,1:T(8,128)}), f32[16,16,512]{2,0,1:T(8,128)S(1)}, u32[]{:S(2)}, u32[]{:S(2)}) async-start(f32[16,16,512]{2,0,1:T(8,128)} %copy.19), calls=%async_computation | async-start | bytes 1048576 | tf_op jit(solution)/shard_map/all_to_all | solution.py:161
  32.5 6.1 %copy-start.2 = (f32[32,256]{1,0:T(8,128)S(1)}, f32[32,256]{1,0:T(8,128)}, u32[]{:S(2)}) copy-start(f32[32,256]{1,0:T(8,128)} %param.10) | copy-start | bytes 98308
  32.5 6.1 %copy-start.3 = (f32[32,256]{1,0:T(8,128)S(1)}, f32[32,256]{1,0:T(8,128)}, u32[]{:S(2)}) copy-start(f32[32,256]{1,0:T(8,128)} %param.9) | copy-start | bytes 98308
  39.9 5.5 %copy-start.1 = (f32[16,32,256]{2,1,0:T(8,128)S(1)}, f32[16,32,256]{2,1,0:T(8,128)}, u32[]{:S(2)}) copy-start(f32[16,32,256]{2,1,0:T(8,128)} %shard_map.83) | copy-start | bytes 1572868
  40.1 4.4 %collective-permute-start.1 = (f32[19,256]{0,1:T(8,128)S(1)}, f32[19,256]{0,1:T(8,128)S(1)}, u32[]{:S(2)}, u32[]{:S(2)}) collective-permute-start(f32[19,256]{0,1:T(8,128)S(1)} %bitcast.47), channel_id=1, source_target_pairs={{16,0},{32,16},{48,32},{64,48},{80,64},{96,80},{112,96},{128,112},... | collective-permute-start | bytes 58376 | tf_op jit(solution)/shard_map/ppermute | solution.py:121
  40.4 4.5 %collective-permute-start = (f32[19,256]{0,1:T(8,128)S(1)}, f32[19,256]{0,1:T(8,128)S(1)}, u32[]{:S(2)}, u32[]{:S(2)}) collective-permute-start(f32[19,256]{0,1:T(8,128)S(1)} %bitcast.49), channel_id=1, source_target_pairs={{0,16},{16,32},{32,48},{48,64},{64,80},{80,96},{96,112},{112,128},... | collective-permute-start | bytes 58376 | tf_op jit(solution)/shard_map/ppermute | solution.py:120
  45.6 10.3 %collective-permute-start.3 = (f32[19,8,272]{2,1,0:T(8,128)S(1)}, f32[19,8,272]{2,1,0:T(8,128)S(1)}, u32[]{:S(2)}, u32[]{:S(2)}) collective-permute-start(f32[19,8,272]{2,1,0:T(8,128)S(1)} %get-tuple-element.8), channel_id=1, source_target_pairs={{1,0},{2,1},{3,2},{4,3},{5,4},{6,5},{7,6},{8,7},{9,8},{10,9},{11,1... | collective-permute-start | bytes 496136 | tf_op jit(solution)/shard_map/ppermute | solution.py:124
  50.6 10.5 %collective-permute-start.2 = (f32[19,8,272]{2,1,0:T(8,128)S(1)}, f32[19,8,272]{2,1,0:T(8,128)S(1)}, u32[]{:S(2)}, u32[]{:S(2)}) collective-permute-start(f32[19,8,272]{2,1,0:T(8,128)S(1)} %get-tuple-element.7), channel_id=1, source_target_pairs={{0,1},{1,2},{2,3},{3,4},{4,5},{5,6},{6,7},{7,8},{8,9},{9,10},{10,1... | collective-permute-start | bytes 496136 | tf_op jit(solution)/shard_map/ppermute | solution.py:123

commit v10 on v9

--- a/solution.py
+++ b/solution.py
@@ -107,23 +107,38 @@
     return vmem_call(gather_kernel, shape, flops, 4 * (levels * slots + 2 * slots + cells * cols_here))(state2d, rows, cols)
 
 
-def with_halo(block, sides, width):
-    for axis, dim in sides:
-        count = lax.axis_size(axis)
-        forward = [(i, i + 1) for i in range(count - 1)]
-        forward.append((count - 1, 0))
-        backward = [(target, source) for source, target in forward]
-        low = lax.slice_in_dim(block, block.shape[dim] - width, None, axis=dim)
-        high = lax.slice_in_dim(block, 0, width, axis=dim)
-        if dim == block.ndim - 1:
-            flat = block.shape[:-2] + (-1,)
-            low = lax.ppermute(low.reshape(flat), axis, forward).reshape(low.shape)
-            high = lax.ppermute(high.reshape(flat), axis, backward).reshape(high.shape)
-        else:
-            low = lax.ppermute(low, axis, forward)
-            high = lax.ppermute(high, axis, backward)
-        block = jnp.concatenate([low, block, high], axis=dim)
-    return block
+def full_halo(block, width):
+    lon_count = lax.axis_size("lon")
+    lat_count = lax.axis_size("lat")
+
+    def shift(piece, lon_step, lat_step):
+        flat = piece.shape[:-2] + (-1,)
+        pairs = [
+            (i * lat_count + j, ((i + lon_step) % lon_count) * lat_count + (j + lat_step) % lat_count)
+            for i in range(lon_count)
+            for j in range(lat_count)
+        ]
+        moved = lax.ppermute(piece.reshape(flat) if piece.shape[-1] == width else piece, ("lon", "lat"), pairs)
+        return moved.reshape(piece.shape)
+
+    low_rows = block[..., -width:, :]
+    high_rows = block[..., :width, :]
+    south = shift(low_rows, 0, 1)
+    north = shift(high_rows, 0, -1)
+    west = shift(block[..., -width:], 1, 0)
+    east = shift(block[..., :width], -1, 0)
+    south_west = shift(low_rows[..., -width:], 1, 1)
+    south_east = shift(low_rows[..., :width], -1, 1)
+    north_west = shift(high_rows[..., -width:], 1, -1)
+    north_east = shift(high_rows[..., :width], -1, -1)
+    return jnp.concatenate(
+        [
+            jnp.concatenate([south_west, south, south_east], axis=-1),
+            jnp.concatenate([west, block, east], axis=-1),
+            jnp.concatenate([north_west, north, north_east], axis=-1),
+        ],
+        axis=-2,
+    )
 
 
 def one_pass(field, east_face, north_face, offset):
@@ -169,7 +184,7 @@
     gradient = onehot_scatter(values, weights, at_column, usable[None, :], target_rows, target_cols, sea)
     rim_width = PASSES
     stacked = jnp.concatenate([gradient, sea[None], coef_lon[None], coef_lat[None]], axis=0)
-    padded = with_halo(stacked, (("lon", 2), ("lat", 1)), rim_width)
+    padded = full_halo(stacked, rim_width)
     field = padded[:levels]
     padded = padded[levels:]
     lat_index = lax.axis_index("lat")

time: 72.8 us -> 74.6 us (1.025)
  starting transfers between devices: 16.7 us -> 21.2 us
  waiting for transfers between devices: 20.8 us -> 17 us
  local copies, waits for them, and re-layouts: 5.44 us -> 6.58 us
    ppermute x4 -> x8, starting transfers between devices: 6.75 us -> 11.2 us  [shift(): lax.ppermute(piece.reshape(flat) if piece.shape[-1] == width else piece,...]
    ppermute x4 -> x8, waiting for transfers between devices: 12.8 us -> 9.01 us  [shift(): lax.ppermute(piece.reshape(flat) if piece.shape[-1] == width else piece,...]
  transfers between devices with their start and end apart: 5 -> 9, of which waited for: 4 -> 3; matrix products, arithmetic and copies ran while one was open for 5% -> 7% of each run, Pallas kernels for 9% -> 9%
where the time goes in v10:
time: 74.6 us; the launch traced here: 74.3 us
  starting transfers between devices  21.2 us (28%)
  waiting for transfers between devices  17 us (23%)
  other arithmetic  16.4 us (22%)
  Pallas kernels  12.8 us (17%)
  local copies, waits for them, and re-layouts  6.58 us (9%)
    ppermute x8, starting transfers between devices, shift(): lax.ppermute(piece.reshape(flat) if piece.shape[-1] == width else piece,...  11.2 us
    all_to_all x1, starting transfers between devices, body(): lax.all_to_all(held, 'lon', split_axis=1, concat_axis=1, tiled=True)  9.98 us
    sub x8, other arithmetic, one_pass(): centre + east_here * (field[:, 1:-1, 2:] - centre)  9.72 us
    ppermute x8, waiting for transfers between devices, shift(): lax.ppermute(piece.reshape(flat) if piece.shape[-1] == width else piece,...  9.01 us
    all_to_all x1, waiting for transfers between devices, body(): lax.all_to_all(held, 'lon', split_axis=1, concat_axis=1, tiled=True)  8.02 us
    pallas_call x1, Pallas kernels, onehot_gather(): vmem_call(gather_kernel, shape, flops, 4 * (levels * slots + 2 * slots +...  6.63 us
    pallas_call x1, Pallas kernels, onehot_scatter(): pl.pallas_call(scatter_kernel, out_shape=shape, in_specs=[pl.BlockSpec(me...  6.14 us
    unnamed x2, other arithmetic  2.27 us
  transfers between devices with their start and end apart: 9, of which 3 were waited for; matrix products, arithmetic and copies ran while one was open for 7% of the time, Pallas kernels for 9%

profile of v10, /device:TPU:1, one launch (start us, length us, event | category | flops | bytes accessed | tf_op | source)
XLA Modules:
  0.0 74.3 jit_solution(960917610634829967)
XLA Ops:
  0.0 1.6 %reduce.1 = f32[16,4096]{1,0:T(8,128)S(1)} reduce(f32[16,1,4096]{2,1,0:T(1,128)} %param.15, f32[]{:T(128)} %constant.52), dimensions={1}, to_apply=%param.15.reduce_sub_computation | reduce | bytes 524292 | tf_op args[7]
  1.6 0.1 copy.53
  1.7 0.6 reduce
  2.4 0.1 copy.52
  2.5 0.1 pad_maximum_fusion.1
  2.5 0.0 copy-start.6
  2.6 0.0 copy-start.5
  2.6 1.1 %copy.35 = f32[16,16,512]{2,0,1:T(8,128)} copy(f32[16,16,512]{2,1,0:T(8,128)S(1)} %pad_maximum_fusion.1) | data formatting | bytes 1048576 | tf_op jit(solution)/shard_map/concatenate | solution.py:173
  3.7 10.0 %all-to-all-start = ((f32[16,16,512]{2,0,1:T(8,128)}), f32[16,16,512]{2,0,1:T(8,128)S(1)}, u32[]{:S(2)}, u32[]{:S(2)}) async-start(f32[16,16,512]{2,0,1:T(8,128)} %copy.35), calls=%async_computation | async-start | bytes 1048576 | tf_op jit(solution)/shard_map/all_to_all | solution.py:176
  13.7 0.6 fusion.84
  14.3 0.6 and_select_fusion.1
  14.9 0.7 and_select_fusion.2.rows_ref
  15.6 6.6 %shard_map.82.seen_ref = f32[16,4096]{1,0:T(8,128)} custom-call(f32[512,256]{1,0:T(8,128)} %bitcast.66, s32[1,4096]{1,0:T(1,128)} %and_select_fusion.2.rows_ref, s32[1,4096]{1,0:T(1,128)} %get-tuple-element.5.cols_ref), custom_call_target="tpu_custom_call" | custom-call | flops 3221225472 | bytes 819200 | tf_op jit(solution)/shard_map/pallas_call | solution.py:107
  22.2 0.1 broadcast_bitcast_fusion
  22.3 0.6 compare_select_fusion.usable_ref
  22.9 8.0 %all-to-all-done = f32[16,16,512]{2,0,1:T(8,128)S(1)} async-done(((f32[16,16,512]{2,0,1:T(8,128)}), f32[16,16,512]{2,0,1:T(8,128)S(1)}, u32[]{:S(2)}, u32[]{:S(2)}) %all-to-all-start) | async-done | bytes 524320 | tf_op jit(solution)/shard_map/all_to_all | solution.py:176
  31.0 0.1 slice_bitcast_fusion
  31.0 0.7 copy.50
  31.8 0.7 copy.51
  32.5 6.1 %shard_map.83 = f32[16,32,256]{2,1,0:T(8,128)} custom-call(f32[16,4096]{1,0:T(8,128)} %bitcast.47, f32[16,4096]{1,0:T(8,128)} %bitcast.48, f32[16,4096]{1,0:T(8,128)} %shard_map.82.seen_ref, f32[1,4096]{1,0:T(1,128)} %compare_select_fusion.usable_ref, s32[1,4096]{1,0:T(1,128)} %and_select_fusion.2.rows_ref, s32[1,4096]{1,0:T(1,128)} %get-tuple-element.5.cols_ref, ...), custom_call_target="tpu_custom_call" | custom-call | flops 3221225472 | bytes 1359872 | tf_op jit(solution)/shard_map/pallas_call | solution.py:89
  38.6 1.1 %pad_maximum_fusion = f32[19,32,256]{2,1,0:T(8,128)S(1)} fusion(f32[1,32,256]{2,1,0:T(8,128)S(1)} %bitcast.49, f32[1,32,256]{2,1,0:T(8,128)S(1)} %bitcast.51, f32[1,32,256]{2,1,0:T(8,128)S(1)} %get-tuple-element.50, f32[16,32,256]{2,1,0:T(8,128)} %shard_map.83), kind=kLoop, calls=%fused_computation.85 | loop fusion | flops 466944 | bytes 1245184 | tf_op jit(solution)/shard_map/concatenate | solution.py:186
  39.7 0.1 fusion.65
  39.9 0.1 copy.47
  40.0 3.6 %collective-permute-start.7 = (f32[19,64]{0,1:T(8,128)S(1)}, f32[19,64]{0,1:T(8,128)S(1)}, u32[]{:S(2)}, u32[]{:S(2)}) collective-permute-start(f32[19,64]{0,1:T(8,128)S(1)} %bitcast.61), channel_id=1, source_target_pairs={{0,255},{1,240},{2,241},{3,242},{4,243},{5,244},{6,245},{7,246},{8... | collective-permute-start | bytes 14600 | tf_op jit(solution)/shard_map/ppermute | solution.py:121
  43.6 1.4 %collective-permute-start.6 = (f32[19,8,256]{2,1,0:T(8,128)S(1)}, f32[19,8,256]{2,1,0:T(8,128)S(1)}, u32[]{:S(2)}, u32[]{:S(2)}) collective-permute-start(f32[19,8,256]{2,1,0:T(8,128)S(1)} %get-tuple-element.12), channel_id=1, source_target_pairs={{0,15},{1,0},{2,1},{3,2},{4,3},{5,4},{6,5},{7,6},{8,7},{9,8},{10,9... | collective-permute-start | bytes 466952 | tf_op jit(solution)/shard_map/ppermute | solution.py:121
  45.0 0.1 copy.46
  45.2 2.0 %collective-permute-start.5 = (f32[19,64]{0,1:T(8,128)S(1)}, f32[19,64]{0,1:T(8,128)S(1)}, u32[]{:S(2)}, u32[]{:S(2)}) collective-permute-start(f32[19,64]{0,1:T(8,128)S(1)} %bitcast.63), channel_id=1, source_target_pairs={{0,31},{1,16},{2,17},{3,18},{4,19},{5,20},{6,21},{7,22},{8,23},{9,... | collective-permute-start | bytes 14600 | tf_op jit(solution)/shard_map/ppermute | solution.py:121
  47.2 0.1 copy.39
  47.3 0.0 collective-permute-start.2
  47.3 1.4 %collective-permute-start.1 = (f32[19,8,256]{2,1,0:T(8,128)S(1)}, f32[19,8,256]{2,1,0:T(8,128)S(1)}, u32[]{:S(2)}, u32[]{:S(2)}) collective-permute-start(f32[19,8,256]{2,1,0:T(8,128)S(1)} %get-tuple-element.11), channel_id=1, source_target_pairs={{0,1},{1,2},{2,3},{3,4},{4,5},{5,6},{6,7},{7,8},{8,9},{9,10},{10,1... | collective-permute-start | bytes 466952 | tf_op jit(solution)/shard_map/ppermute | solution.py:121
  48.7 0.1 fusion.67
  48.9 0.0 copy-start.1
  48.9 0.3 copy.43
  49.2 0.3 copy.42
  49.4 0.1 copy.38
  49.6 0.9 %collective-permute-start.4 = (f32[19,256]{0,1:T(8,128)S(1)}, f32[19,256]{0,1:T(8,128)S(1)}, u32[]{:S(2)}, u32[]{:S(2)}) collective-permute-start(f32[19,256]{0,1:T(8,128)S(1)} %bitcast.54), channel_id=1, source_target_pairs={{0,240},{1,241},{2,242},{3,243},{4,244},{5,245},{6,246},{7,247},{8... | collective-permute-start | bytes 58376 | tf_op jit(solution)/shard_map/ppermute | solution.py:121
  50.5 1.7 %collective-permute-start.3 = (f32[19,256]{0,1:T(8,128)S(1)}, f32[19,256]{0,1:T(8,128)S(1)}, u32[]{:S(2)}, u32[]{:S(2)}) collective-permute-start(f32[19,256]{0,1:T(8,128)S(1)} %bitcast.53), channel_id=1, source_target_pairs={{0,16},{1,17},{2,18},{3,19},{4,20},{5,21},{6,22},{7,23},{8,24},{9,... | collective-permute-start | bytes 58376 | tf_op jit(solution)/shard_map/ppermute | solution.py:121
  52.3 2.7 %collective-permute-done.2 = f32[19,64]{0,1:T(8,128)S(1)} collective-permute-done((f32[19,64]{0,1:T(8,128)S(1)}, f32[19,64]{0,1:T(8,128)S(1)}, u32[]{:S(2)}, u32[]{:S(2)}) %collective-permute-start.2) | collective-permute-done | bytes 4896 | tf_op jit(solution)/shard_map/ppermute | solution.py:121
  55.0 0.1 copy.49
  55.1 0.1 copy.48
  55.3 0.1 copy.41
  55.4 6.3 %collective-permute-done = f32[19,64]{0,1:T(8,128)S(1)} collective-permute-done((f32[19,64]{0,1:T(8,128)S(1)}, f32[19,64]{0,1:T(8,128)S(1)}, u32[]{:S(2)}, u32[]{:S(2)}) %collective-permute-start) | collective-permute-done | bytes 4896 | tf_op jit(solution)/shard_map/ppermute | solution.py:121
  61.7 0.1 copy.40
  61.8 0.4 copy.45
  62.2 0.4 copy.44
  62.6 0.6 maximum_maximum_fusion
  63.2 0.1 fusion.64
  63.3 0.1 slice_multiply_fusion.2
  63.4 0.1 fusion.82
  63.5 0.1 fusion.80
  63.7 0.1 fusion.78
  63.8 0.1 fusion.76
  64.0 0.1 fusion.74
  64.1 0.1 fusion.72
  64.3 0.1 fusion.70
  64.4 0.1 fusion.68
  64.5 1.3 %fusion.17 = f32[16,46,270]{2,1,0:T(8,128)S(1)} fusion(f32[19,48,272]{2,1,0:T(8,128)S(1)} %maximum_maximum_fusion, f32[46,270]{1,0:T(8,128)S(1)} %get-tuple-element.51, f32[46,270]{1,0:T(8,128)S(1)} %get-tuple-element.52, f32[46,270]{1,0:T(8,128)S(1)} %get-tuple-element.46, f32[46,270]{1,0:T(8,128)S(1)} %get-tuple-element.45), kind=kLoop, calls=%fused_computation.27 | loop fusion | flops 2384640 | bytes 4968000 | tf_op jit(solution)/shard_map/sub | solution.py:154
  65.8 1.3 %fusion.9 = f32[16,44,268]{2,1,0:T(8,128)S(1)} fusion(f32[16,46,270]{2,1,0:T(8,128)S(1)} %fusion.17, f32[44,268]{1,0:T(8,128)S(1)} %get-tuple-element.53, f32[44,268]{1,0:T(8,128)S(1)} %get-tuple-element.54, f32[44,268]{1,0:T(8,128)S(1)} %get-tuple-element.42, f32[44,268]{1,0:T(8,128)S(1)} %get-tuple-element.41), kind=kLoop, calls=%fused_computation.15 | loop fusion | flops 2264064 | bytes 4716800 | tf_op jit(solution)/shard_map/sub | solution.py:154
  67.1 1.3 %fusion.1 = f32[16,42,266]{2,1,0:T(8,128)S(1)} fusion(f32[16,44,268]{2,1,0:T(8,128)S(1)} %fusion.9, f32[42,266]{1,0:T(8,128)S(1)} %get-tuple-element.55, f32[42,266]{1,0:T(8,128)S(1)} %get-tuple-element.56, f32[42,266]{1,0:T(8,128)S(1)} %get-tuple-element.38, f32[42,266]{1,0:T(8,128)S(1)} %get-tuple-element.37), kind=kLoop, calls=%fused_computation.3 | loop fusion | flops 2145024 | bytes 4468800 | tf_op jit(solution)/shard_map/sub | solution.py:154
  68.4 1.1 %fusion.49 = f32[16,40,264]{2,1,0:T(8,128)S(1)} fusion(f32[16,42,266]{2,1,0:T(8,128)S(1)} %fusion.1, f32[40,264]{1,0:T(8,128)S(1)} %get-tuple-element.57, f32[40,264]{1,0:T(8,128)S(1)} %get-tuple-element.58, f32[40,264]{1,0:T(8,128)S(1)} %get-tuple-element.34, f32[40,264]{1,0:T(8,128)S(1)} %get-tuple-element.33), kind=kLoop, calls=%fused_computation.75 | loop fusion | flops 2027520 | bytes 4224000 | tf_op jit(solution)/shard_map/sub | solution.py:154
  69.5 1.1 %fusion.41 = f32[16,38,262]{2,1,0:T(8,128)S(1)} fusion(f32[16,40,264]{2,1,0:T(8,128)S(1)} %fusion.49, f32[38,262]{1,0:T(8,128)S(1)} %get-tuple-element.59, f32[38,262]{1,0:T(8,128)S(1)} %get-tuple-element.60, f32[38,262]{1,0:T(8,128)S(1)} %get-tuple-element.30, f32[38,262]{1,0:T(8,128)S(1)} %get-tuple-element.29), kind=kLoop, calls=%fused_computation.63 | loop fusion | flops 1911552 | bytes 3982400 | tf_op jit(solution)/shard_map/sub | solution.py:154
  70.6 1.1 %fusion.33 = f32[16,36,260]{2,1,0:T(8,128)S(1)} fusion(f32[16,38,262]{2,1,0:T(8,128)S(1)} %fusion.41, f32[36,260]{1,0:T(8,128)S(1)} %get-tuple-element.61, f32[36,260]{1,0:T(8,128)S(1)} %get-tuple-element.62, f32[36,260]{1,0:T(8,128)S(1)} %get-tuple-element.26, f32[36,260]{1,0:T(8,128)S(1)} %get-tuple-element.25), kind=kLoop, calls=%fused_computation.51 | loop fusion | flops 1797120 | bytes 3744000 | tf_op jit(solution)/shard_map/sub | solution.py:154
  71.7 1.1 %fusion.25 = f32[16,34,258]{2,1,0:T(8,128)S(1)} fusion(f32[16,36,260]{2,1,0:T(8,128)S(1)} %fusion.33, f32[34,258]{1,0:T(8,128)S(1)} %get-tuple-element.63, f32[34,258]{1,0:T(8,128)S(1)} %get-tuple-element.64, f32[34,258]{1,0:T(8,128)S(1)} %get-tuple-element.22, f32[34,258]{1,0:T(8,128)S(1)} %get-tuple-element.21), kind=kLoop, calls=%fused_computation.39 | loop fusion | flops 1684224 | bytes 3508800 | tf_op jit(solution)/shard_map/sub | solution.py:154
  72.9 1.4 %fusion.57 = f32[16,32,256]{2,1,0:T(8,128)} fusion(f32[16,34,258]{2,1,0:T(8,128)S(1)} %fusion.25, f32[32,256]{1,0:T(8,128)S(1)} %get-tuple-element.65, f32[32,256]{1,0:T(8,128)S(1)} %get-tuple-element.66, f32[32,256]{1,0:T(8,128)S(1)} %get-tuple-element.18, f32[32,256]{1,0:T(8,128)S(1)} %get-tuple-element.17), kind=kLoop, calls=%fused_computation.88 | loop fusion | flops 1572864 | bytes 3276800 | tf_op jit(solution)/shard_map/sub | solution.py:154
  (23 shorter events, 0.1 us)
Async XLA Ops:
  0.0 22.2 %copy-start = (s32[1,16]{1,0:T(1,128)S(1)}, s32[1,16]{1,0:T(1,128)}, u32[]{:S(2)}) copy-start(s32[1,16]{1,0:T(1,128)} %param.13) | copy-start | bytes 196
  0.0 1.7 %copy-start.2 = (f32[16,1,4096]{2,1,0:T(1,128)S(1)}, f32[16,1,4096]{2,1,0:T(1,128)}, u32[]{:S(2)}) copy-start(f32[16,1,4096]{2,1,0:T(1,128)} %param.14) | copy-start | bytes 786436
  2.5 11.1 %copy-start.6 = (s32[32,256]{1,0:T(8,128)S(1)}, s32[32,256]{1,0:T(8,128)}, u32[]{:S(2)}) copy-start(s32[32,256]{1,0:T(8,128)} %param.11) | copy-start | bytes 98308
  2.6 11.7 %copy-start.5 = (s32[1,4096]{1,0:T(1,128)S(1)}, s32[1,4096]{1,0:T(1,128)}, u32[]{:S(2)}) copy-start(s32[1,4096]{1,0:T(1,128)} %param.12) | copy-start | bytes 49156
  3.7 27.3 %all-to-all-start = ((f32[16,16,512]{2,0,1:T(8,128)}), f32[16,16,512]{2,0,1:T(8,128)S(1)}, u32[]{:S(2)}, u32[]{:S(2)}) async-start(f32[16,16,512]{2,0,1:T(8,128)} %copy.35), calls=%async_computation | async-start | bytes 1048576 | tf_op jit(solution)/shard_map/all_to_all | solution.py:176
  32.5 6.1 %copy-start.3 = (f32[32,256]{1,0:T(8,128)S(1)}, f32[32,256]{1,0:T(8,128)}, u32[]{:S(2)}) copy-start(f32[32,256]{1,0:T(8,128)} %param.10) | copy-start | bytes 98308
  32.5 6.1 %copy-start.4 = (f32[32,256]{1,0:T(8,128)S(1)}, f32[32,256]{1,0:T(8,128)}, u32[]{:S(2)}) copy-start(f32[32,256]{1,0:T(8,128)} %param.9) | copy-start | bytes 98308
  40.0 9.6 %collective-permute-start.7 = (f32[19,64]{0,1:T(8,128)S(1)}, f32[19,64]{0,1:T(8,128)S(1)}, u32[]{:S(2)}, u32[]{:S(2)}) collective-permute-start(f32[19,64]{0,1:T(8,128)S(1)} %bitcast.61), channel_id=1, source_target_pairs={{0,255},{1,240},{2,241},{3,242},{4,243},{5,244},{6,245},{7,246},{8... | collective-permute-start | bytes 14600 | tf_op jit(solution)/shard_map/ppermute | solution.py:121
  43.6 19.0 %collective-permute-start.6 = (f32[19,8,256]{2,1,0:T(8,128)S(1)}, f32[19,8,256]{2,1,0:T(8,128)S(1)}, u32[]{:S(2)}, u32[]{:S(2)}) collective-permute-start(f32[19,8,256]{2,1,0:T(8,128)S(1)} %get-tuple-element.12), channel_id=1, source_target_pairs={{0,15},{1,0},{2,1},{3,2},{4,3},{5,4},{6,5},{7,6},{8,7},{9,8},{10,9... | collective-permute-start | bytes 466952 | tf_op jit(solution)/shard_map/ppermute | solution.py:121
  45.2 5.3 %collective-permute-start.5 = (f32[19,64]{0,1:T(8,128)S(1)}, f32[19,64]{0,1:T(8,128)S(1)}, u32[]{:S(2)}, u32[]{:S(2)}) collective-permute-start(f32[19,64]{0,1:T(8,128)S(1)} %bitcast.63), channel_id=1, source_target_pairs={{0,31},{1,16},{2,17},{3,18},{4,19},{5,20},{6,21},{7,22},{8,23},{9,... | collective-permute-start | bytes 14600 | tf_op jit(solution)/shard_map/ppermute | solution.py:121
  47.3 7.7 %collective-permute-start.2 = (f32[19,64]{0,1:T(8,128)S(1)}, f32[19,64]{0,1:T(8,128)S(1)}, u32[]{:S(2)}, u32[]{:S(2)}) collective-permute-start(f32[19,64]{0,1:T(8,128)S(1)} %bitcast.62), channel_id=1, source_target_pairs={{0,241},{1,242},{2,243},{3,244},{4,245},{5,246},{6,247},{7,248},{8... | collective-permute-start | bytes 14600 | tf_op jit(solution)/shard_map/ppermute | solution.py:121
  47.3 15.3 %collective-permute-start.1 = (f32[19,8,256]{2,1,0:T(8,128)S(1)}, f32[19,8,256]{2,1,0:T(8,128)S(1)}, u32[]{:S(2)}, u32[]{:S(2)}) collective-permute-start(f32[19,8,256]{2,1,0:T(8,128)S(1)} %get-tuple-element.11), channel_id=1, source_target_pairs={{0,1},{1,2},{2,3},{3,4},{4,5},{5,6},{6,7},{7,8},{8,9},{9,10},{10,1... | collective-permute-start | bytes 466952 | tf_op jit(solution)/shard_map/ppermute | solution.py:121
  48.9 13.7 %copy-start.1 = (f32[16,32,256]{2,1,0:T(8,128)S(1)}, f32[16,32,256]{2,1,0:T(8,128)}, u32[]{:S(2)}) copy-start(f32[16,32,256]{2,1,0:T(8,128)} %shard_map.83) | copy-start | bytes 1572868
  49.6 12.2 %collective-permute-start.4 = (f32[19,256]{0,1:T(8,128)S(1)}, f32[19,256]{0,1:T(8,128)S(1)}, u32[]{:S(2)}, u32[]{:S(2)}) collective-permute-start(f32[19,256]{0,1:T(8,128)S(1)} %bitcast.54), channel_id=1, source_target_pairs={{0,240},{1,241},{2,242},{3,243},{4,244},{5,245},{6,246},{7,247},{8... | collective-permute-start | bytes 58376 | tf_op jit(solution)/shard_map/ppermute | solution.py:121
  50.5 11.7 %collective-permute-start.3 = (f32[19,256]{0,1:T(8,128)S(1)}, f32[19,256]{0,1:T(8,128)S(1)}, u32[]{:S(2)}, u32[]{:S(2)}) collective-permute-start(f32[19,256]{0,1:T(8,128)S(1)} %bitcast.53), channel_id=1, source_target_pairs={{0,16},{1,17},{2,18},{3,19},{4,20},{5,21},{6,22},{7,23},{8,24},{9,... | collective-permute-start | bytes 58376 | tf_op jit(solution)/shard_map/ppermute | solution.py:121
  55.0 6.7 %collective-permute-start = (f32[19,64]{0,1:T(8,128)S(1)}, f32[19,64]{0,1:T(8,128)S(1)}, u32[]{:S(2)}, u32[]{:S(2)}) collective-permute-start(f32[19,64]{0,1:T(8,128)S(1)} %bitcast.64), channel_id=1, source_target_pairs={{0,17},{1,18},{2,19},{3,20},{4,21},{5,22},{6,23},{7,24},{8,25},{9,... | collective-permute-start | bytes 14600 | tf_op jit(solution)/shard_map/ppermute | solution.py:121

commit v11 on v9

--- a/solution.py
+++ b/solution.py
@@ -18,8 +18,11 @@
     return high, middle, low
 
 
-def scatter_kernel(values_ref, weights_ref, seen_ref, usable_ref, rows_ref, cols_ref, sea_ref, out_ref, acc_ref):
-    levels, slots = values_ref.shape
+def scatter_kernel(held_ref, seen_ref, usable_ref, rows_ref, cols_ref, sea_ref, out_ref, acc_ref):
+    levels, slots = seen_ref.shape
+    peers, _, pair = held_ref.shape
+    capacity = pair // 2
+    per_chunk = SCATTER_CHUNK // capacity
     _, rows_here, cols_here = out_ref.shape
     cells = levels * rows_here
     acc_ref[...] = jnp.zeros_like(acc_ref)
@@ -27,7 +30,10 @@
     def step(k, carry):
         start = pl.multiple_of(k * SCATTER_CHUNK, SCATTER_CHUNK)
         here = pl.ds(start, SCATTER_CHUNK)
-        w = weights_ref[:, here] * (values_ref[:, here] - seen_ref[:, here]) * usable_ref[:, here]
+        held = [held_ref[k * per_chunk + i] for i in range(per_chunk)]
+        values = jnp.concatenate([h[:, :capacity] for h in held], axis=1)
+        weights = jnp.concatenate([h[:, capacity:] for h in held], axis=1)
+        w = weights * (values - seen_ref[:, here]) * usable_ref[:, here]
         row_hit = lax.broadcasted_iota(jnp.int32, (rows_here, SCATTER_CHUNK), 0) == rows_ref[:, here]
         col_hit = lax.broadcasted_iota(jnp.int32, (cols_here, SCATTER_CHUNK), 0) == cols_ref[:, here]
         col_hit = col_hit.astype(jnp.float32).astype(jnp.bfloat16)
@@ -81,22 +87,22 @@
     )
 
 
-def onehot_scatter(values, weights, seen, usable, rows, cols, sea):
-    levels, slots = values.shape
+def onehot_scatter(held, seen, usable, rows, cols, sea):
+    levels, slots = seen.shape
     rows_here, cols_here = sea.shape
     shape = jax.ShapeDtypeStruct((levels, rows_here, cols_here), jnp.float32)
     flops = 6 * levels * rows_here * cols_here * slots
     return pl.pallas_call(
         scatter_kernel,
         out_shape=shape,
-        in_specs=[pl.BlockSpec(memory_space=pltpu.VMEM)] * 7,
+        in_specs=[pl.BlockSpec(memory_space=pltpu.VMEM)] * 6,
         out_specs=pl.BlockSpec(memory_space=pltpu.VMEM),
         scratch_shapes=[pltpu.VMEM((levels * rows_here, cols_here), jnp.float32)],
         cost_estimate=pl.CostEstimate(
             flops=flops, bytes_accessed=4 * (3 * levels * slots + 3 * slots + levels * rows_here * cols_here),
             transcendentals=0,
         ),
-    )(values, weights, seen, usable, rows, cols, sea)
+    )(held, seen, usable, rows, cols, sea)
 
 
 def onehot_gather(state2d, rows, cols, levels):
@@ -155,18 +161,14 @@
     limits = jnp.broadcast_to(send_count[0][:, None], (lon_count, capacity)).reshape(slots)
     usable = jnp.where(slot_index % capacity < limits, 1.0, 0.0).astype(jnp.float32)
     chunked = (levels, lon_count, capacity)
-    held = jnp.concatenate(
-        [obs_value[:, 0, :].reshape(chunked), obs_weight[:, 0, :].reshape(chunked)], axis=2
-    ).reshape(levels, 2 * slots)
-    at_owner = lax.all_to_all(held, "lon", split_axis=1, concat_axis=1, tiled=True)
-    at_owner = at_owner.reshape(levels, lon_count, 2 * capacity)
-    values = at_owner[:, :, :capacity].reshape(levels, slots)
-    weights = at_owner[:, :, capacity:].reshape(levels, slots)
+    held = jnp.concatenate([obs_value.reshape(chunked), obs_weight.reshape(chunked)], axis=2)
+    held = jnp.transpose(held, (1, 0, 2))
+    at_owner = lax.all_to_all(held, "lon", split_axis=0, concat_axis=0, tiled=True)
     target_rows = (targets // cols_here)[None, :]
     target_cols = (targets % cols_here)[None, :]
     at_column = onehot_gather(state.reshape(levels * rows_here, cols_here), target_rows, target_cols, levels)
     sea = land_sea.astype(jnp.float32)
-    gradient = onehot_scatter(values, weights, at_column, usable[None, :], target_rows, target_cols, sea)
+    gradient = onehot_scatter(at_owner, at_column, usable[None, :], target_rows, target_cols, sea)
     rim_width = PASSES
     stacked = jnp.concatenate([gradient, sea[None], coef_lon[None], coef_lat[None]], axis=0)
     padded = with_halo(stacked, (("lon", 2), ("lat", 1)), rim_width)

time: 72.8 us -> 68.4 us (0.940)
  waiting for transfers between devices: 20.8 us -> 17.1 us
  other arithmetic: 16.5 us -> 18.2 us
  local copies, waits for them, and re-layouts: 5.44 us -> 3.97 us
  starting transfers between devices: 16.7 us -> 15.8 us
    ppermute x1, waiting for transfers between devices: 5.24 us -> 0.01 us  [with_halo(): high = lax.ppermute(high, axis, backward)]
    ppermute x1, starting transfers between devices: 1.75 us -> 0.01 us  [with_halo(): low = lax.ppermute(low.reshape(flat), axis, forward).reshape(low.shape)]
    reshape x2 -> x1, local copies, waits for them, and re-layouts: 1.43 us -> 0.06 us  [body(): obs_weight.reshape(chunked)]
    ppermute x1, starting transfers between devices: 0.01 us -> 1.37 us  [with_halo(): low = lax.ppermute(low, axis, forward)]
    ppermute x1, waiting for transfers between devices: 0.01 us -> 1.16 us  [with_halo(): low = lax.ppermute(low.reshape(flat), axis, forward).reshape(low.shape)]
    ppermute x1, starting transfers between devices: 5 us -> 3.9 us  [with_halo(): high = lax.ppermute(high, axis, backward)]
    concatenate x1 -> x0, local copies, waits for them, and re-layouts: 1.1 us -> none  [body(): jnp.concatenate([obs_value[:, 0, :].reshape(chunked), obs_weight[:, 0, :]...]
    unnamed x2, other arithmetic: 2.27 us -> 3.19 us
  transfers between devices with their start and end apart: 5 -> 5, of which waited for: 4 -> 4; matrix products, arithmetic and copies ran while one was open for 5% -> 5% of each run, Pallas kernels for 9% -> 10%
where the time goes in v11:
time: 68.4 us; the launch traced here: 68.1 us
  other arithmetic  18.2 us (27%)
  waiting for transfers between devices  17.1 us (25%)
  starting transfers between devices  15.8 us (23%)
  Pallas kernels  12.8 us (19%)
  local copies, waits for them, and re-layouts  3.97 us (6%)
    all_to_all x1, starting transfers between devices, body(): lax.all_to_all(held, 'lon', split_axis=0, concat_axis=0, tiled=True)  9.98 us
    sub x8, other arithmetic, one_pass(): centre + east_here * (field[:, 1:-1, 2:] - centre)  9.73 us
    all_to_all x1, waiting for transfers between devices, body(): lax.all_to_all(held, 'lon', split_axis=0, concat_axis=0, tiled=True)  8.01 us
    pallas_call x1, Pallas kernels, onehot_gather(): vmem_call(gather_kernel, shape, flops, 4 * (levels * slots + 2 * slots +...  6.65 us
    pallas_call x1, Pallas kernels, onehot_scatter(): pl.pallas_call(scatter_kernel, out_shape=shape, in_specs=[pl.BlockSpec(me...  6.16 us
    ppermute x1, waiting for transfers between devices, with_halo(): low = lax.ppermute(low, axis, forward)  5.57 us
    ppermute x1, starting transfers between devices, with_halo(): high = lax.ppermute(high, axis, backward)  3.9 us
    unnamed x2, other arithmetic  3.19 us
  transfers between devices with their start and end apart: 5, of which 4 were waited for; matrix products, arithmetic and copies ran while one was open for 5% of the time, Pallas kernels for 10%

profile of v11, /device:TPU:1, one launch (start us, length us, event | category | flops | bytes accessed | tf_op | source)
XLA Modules:
  0.0 68.1 jit_solution(851252155988009029)
XLA Ops:
  0.0 0.0 copy-start
  0.0 1.6 %reduce = f32[16,4096]{1,0:T(8,128)S(1)} reduce(f32[16,1,4096]{2,1,0:T(1,128)} %param.14, f32[]{:T(128)} %constant.52), dimensions={1}, to_apply=%param.14.reduce_sub_computation | reduce | bytes 524292 | tf_op args[6]
  1.6 1.6 %reduce.1 = f32[16,4096]{1,0:T(8,128)S(1)} reduce(f32[16,1,4096]{2,1,0:T(1,128)} %param.15, f32[]{:T(128)} %constant.52), dimensions={1}, to_apply=%param.15.reduce_sub_computation | reduce | bytes 524292 | tf_op args[7]
  3.2 0.1 copy_bitcast_fusion
  3.3 0.0 copy-start.5
  3.3 0.0 copy-start.6
  3.3 0.9 %maximum_bitcast_fusion = f32[16,16,512]{2,1,0:T(8,128)} fusion(f32[16,16,256]{2,0,1:T(8,128)S(1)} %get-tuple-element.45, f32[16,16,256]{2,0,1:T(8,128)S(1)} %get-tuple-element.46), kind=kLoop, calls=%fused_computation.98 | loop fusion | flops 131072 | bytes 1048576 | tf_op jit(solution)/shard_map/transpose | solution.py:165
  4.1 10.0 %all-to-all-start = ((f32[16,16,512]{2,1,0:T(8,128)}), f32[16,16,512]{2,1,0:T(8,128)S(1)}, u32[]{:S(2)}, u32[]{:S(2)}) async-start(f32[16,16,512]{2,1,0:T(8,128)} %maximum_bitcast_fusion), calls=%async_computation | async-start | bytes 1048576 | tf_op jit(solution)/shard_map/all_to_all | solution.py:166
  14.1 0.0 copy-done.5
  14.1 0.7 and_select_fusion.1
  14.8 0.7 and_select_fusion.2.rows_ref
  15.4 0.0 copy-done.6
  15.4 0.6 fusion.82
  16.1 6.6 %shard_map.82.seen_ref = f32[16,4096]{1,0:T(8,128)} custom-call(f32[512,256]{1,0:T(8,128)} %bitcast.46, s32[1,4096]{1,0:T(1,128)} %and_select_fusion.2.rows_ref, s32[1,4096]{1,0:T(1,128)} %get-tuple-element.5.cols_ref), custom_call_target="tpu_custom_call" | custom-call | flops 3221225472 | bytes 819200 | tf_op jit(solution)/shard_map/pallas_call | solution.py:113
  22.7 0.0 copy-done
  22.7 0.1 broadcast_bitcast_fusion
  22.8 0.6 compare_select_fusion.usable_ref
  23.4 8.0 %all-to-all-done.held_ref = f32[16,16,512]{2,1,0:T(8,128)S(1)} async-done(((f32[16,16,512]{2,1,0:T(8,128)}), f32[16,16,512]{2,1,0:T(8,128)S(1)}, u32[]{:S(2)}, u32[]{:S(2)}) %all-to-all-start) | async-done | bytes 524320 | tf_op jit(solution)/shard_map/all_to_all | solution.py:166
  31.5 0.8 %copy-done.2 = f32[16,16,512]{2,1,0:T(8,128)} copy-done((f32[16,16,512]{2,1,0:T(8,128)}, f32[16,16,512]{2,1,0:T(8,128)S(1)}, u32[]{:S(2)}) %copy-start.2) | copy-done | bytes 524312
  32.2 6.2 %shard_map.83 = f32[16,32,256]{2,1,0:T(8,128)} custom-call(f32[16,16,512]{2,1,0:T(8,128)} %copy-done.2, f32[16,4096]{1,0:T(8,128)} %shard_map.82.seen_ref, f32[1,4096]{1,0:T(1,128)} %compare_select_fusion.usable_ref, s32[1,4096]{1,0:T(1,128)} %and_select_fusion.2.rows_ref, s32[1,4096]{1,0:T(1,128)} %get-tuple-element.5.cols_ref, ...), custom_call_target="tpu_custom_call" | custom-call | flops 3221225472 | bytes 1359872 | tf_op jit(solution)/shard_map/pallas_call | solution.py:95
  38.4 0.0 copy-done.3
  38.4 1.1 %pad_maximum_fusion.1 = f32[19,32,256]{2,1,0:T(8,128)S(1)} fusion(f32[1,32,256]{2,1,0:T(8,128)S(1)} %bitcast.35, f32[1,32,256]{2,1,0:T(8,128)S(1)} %bitcast.38, f32[1,32,256]{2,1,0:T(8,128)S(1)} %get-tuple-element.44, f32[16,32,256]{2,1,0:T(8,128)} %shard_map.83), kind=kLoop, calls=%fused_computation.85 | loop fusion | flops 466944 | bytes 1245184 | tf_op jit(solution)/shard_map/concatenate | solution.py:173
  39.5 0.1 fusion.65
  39.6 0.0 copy-start.1
  39.7 0.3 copy.11
  39.9 0.0 collective-permute-start
  39.9 0.3 copy.12
  40.2 0.5 collective-permute-start.1
  40.7 1.2 %collective-permute-done = f32[19,256]{0,1:T(8,128)S(1)} collective-permute-done((f32[19,256]{0,1:T(8,128)S(1)}, f32[19,256]{0,1:T(8,128)S(1)}, u32[]{:S(2)}, u32[]{:S(2)}) %collective-permute-start) | collective-permute-done | bytes 19488 | tf_op jit(solution)/shard_map/ppermute | solution.py:126
  41.9 0.4 copy.13
  42.3 2.3 %collective-permute-done.1 = f32[19,256]{0,1:T(8,128)S(1)} collective-permute-done((f32[19,256]{0,1:T(8,128)S(1)}, f32[19,256]{0,1:T(8,128)S(1)}, u32[]{:S(2)}, u32[]{:S(2)}) %collective-permute-start.1) | collective-permute-done | bytes 19488 | tf_op jit(solution)/shard_map/ppermute | solution.py:127
  44.6 0.4 copy.14
  45.0 0.2 pad_maximum_fusion.7
  45.3 1.4 %collective-permute-start.2 = (f32[19,8,272]{2,1,0:T(8,128)S(1)}, f32[19,8,272]{2,1,0:T(8,128)S(1)}, u32[]{:S(2)}, u32[]{:S(2)}) collective-permute-start(f32[19,8,272]{2,1,0:T(8,128)S(1)} %get-tuple-element.7), channel_id=1, source_target_pairs={{0,1},{1,2},{2,3},{3,4},{4,5},{5,6},{6,7},{7,8},{8,9},{9,10},{10,1... | collective-permute-start | bytes 496136 | tf_op jit(solution)/shard_map/ppermute | solution.py:129
  46.6 3.9 %collective-permute-start.3 = (f32[19,8,272]{2,1,0:T(8,128)S(1)}, f32[19,8,272]{2,1,0:T(8,128)S(1)}, u32[]{:S(2)}, u32[]{:S(2)}) collective-permute-start(f32[19,8,272]{2,1,0:T(8,128)S(1)} %get-tuple-element.8), channel_id=1, source_target_pairs={{1,0},{2,1},{3,2},{4,3},{5,4},{6,5},{7,6},{8,7},{9,8},{10,9},{11,1... | collective-permute-start | bytes 496136 | tf_op jit(solution)/shard_map/ppermute | solution.py:130
  50.5 5.6 %collective-permute-done.2 = f32[19,8,272]{2,1,0:T(8,128)S(1)} collective-permute-done((f32[19,8,272]{2,1,0:T(8,128)S(1)}, f32[19,8,272]{2,1,0:T(8,128)S(1)}, u32[]{:S(2)}, u32[]{:S(2)}) %collective-permute-start.2) | collective-permute-done | bytes 165408 | tf_op jit(solution)/shard_map/ppermute | solution.py:129
  56.1 0.0 collective-permute-done.3
  56.1 0.4 pad_maximum_fusion
  56.5 0.1 fusion.64
  56.6 0.1 slice_multiply_fusion.2
  56.7 0.1 fusion.80
  56.8 0.1 fusion.78
  56.9 0.1 fusion.81
  57.0 0.1 fusion.79
  57.1 0.1 fusion.76
  57.2 0.1 fusion.77
  57.3 0.1 fusion.74
  57.4 0.1 fusion.75
  57.5 0.1 fusion.72
  57.6 0.1 fusion.73
  57.7 0.1 fusion.70
  57.8 0.1 fusion.71
  57.9 0.1 fusion.68
  58.0 0.1 fusion.69
  58.1 0.1 fusion.66
  58.2 0.1 fusion.67
  58.3 1.3 %fusion.17 = f32[16,46,270]{2,1,0:T(8,128)S(1)} fusion(f32[19,48,272]{2,1,0:T(8,128)S(1)} %pad_maximum_fusion, f32[46,270]{1,0:T(8,128)S(1)} %get-tuple-element.42, f32[46,270]{1,0:T(8,128)S(1)} %get-tuple-element.41, f32[46,270]{1,0:T(8,128)S(1)} %get-tuple-element.40, f32[46,270]{1,0:T(8,128)S(1)} %get-tuple-element.39), kind=kLoop, calls=%fused_computation.27 | loop fusion | flops 2384640 | bytes 4968000 | tf_op jit(solution)/shard_map/sub | solution.py:145
  59.6 1.3 %fusion.9 = f32[16,44,268]{2,1,0:T(8,128)S(1)} fusion(f32[16,46,270]{2,1,0:T(8,128)S(1)} %fusion.17, f32[44,268]{1,0:T(8,128)S(1)} %get-tuple-element.38, f32[44,268]{1,0:T(8,128)S(1)} %get-tuple-element.37, f32[44,268]{1,0:T(8,128)S(1)} %get-tuple-element.36, f32[44,268]{1,0:T(8,128)S(1)} %get-tuple-element.35), kind=kLoop, calls=%fused_computation.15 | loop fusion | flops 2264064 | bytes 4716800 | tf_op jit(solution)/shard_map/sub | solution.py:145
  60.9 1.3 %fusion.1 = f32[16,42,266]{2,1,0:T(8,128)S(1)} fusion(f32[16,44,268]{2,1,0:T(8,128)S(1)} %fusion.9, f32[42,266]{1,0:T(8,128)S(1)} %get-tuple-element.34, f32[42,266]{1,0:T(8,128)S(1)} %get-tuple-element.33, f32[42,266]{1,0:T(8,128)S(1)} %get-tuple-element.32, f32[42,266]{1,0:T(8,128)S(1)} %get-tuple-element.31), kind=kLoop, calls=%fused_computation.3 | loop fusion | flops 2145024 | bytes 4468800 | tf_op jit(solution)/shard_map/sub | solution.py:145
  62.3 1.1 %fusion.49 = f32[16,40,264]{2,1,0:T(8,128)S(1)} fusion(f32[16,42,266]{2,1,0:T(8,128)S(1)} %fusion.1, f32[40,264]{1,0:T(8,128)S(1)} %get-tuple-element.30, f32[40,264]{1,0:T(8,128)S(1)} %get-tuple-element.29, f32[40,264]{1,0:T(8,128)S(1)} %get-tuple-element.28, f32[40,264]{1,0:T(8,128)S(1)} %get-tuple-element.27), kind=kLoop, calls=%fused_computation.75 | loop fusion | flops 2027520 | bytes 4224000 | tf_op jit(solution)/shard_map/sub | solution.py:145
  63.4 1.1 %fusion.41 = f32[16,38,262]{2,1,0:T(8,128)S(1)} fusion(f32[16,40,264]{2,1,0:T(8,128)S(1)} %fusion.49, f32[38,262]{1,0:T(8,128)S(1)} %get-tuple-element.26, f32[38,262]{1,0:T(8,128)S(1)} %get-tuple-element.25, f32[38,262]{1,0:T(8,128)S(1)} %get-tuple-element.24, f32[38,262]{1,0:T(8,128)S(1)} %get-tuple-element.23), kind=kLoop, calls=%fused_computation.63 | loop fusion | flops 1911552 | bytes 3982400 | tf_op jit(solution)/shard_map/sub | solution.py:145
  64.5 1.1 %fusion.33 = f32[16,36,260]{2,1,0:T(8,128)S(1)} fusion(f32[16,38,262]{2,1,0:T(8,128)S(1)} %fusion.41, f32[36,260]{1,0:T(8,128)S(1)} %get-tuple-element.22, f32[36,260]{1,0:T(8,128)S(1)} %get-tuple-element.21, f32[36,260]{1,0:T(8,128)S(1)} %get-tuple-element.20, f32[36,260]{1,0:T(8,128)S(1)} %get-tuple-element.19), kind=kLoop, calls=%fused_computation.51 | loop fusion | flops 1797120 | bytes 3744000 | tf_op jit(solution)/shard_map/sub | solution.py:145
  65.6 1.1 %fusion.25 = f32[16,34,258]{2,1,0:T(8,128)S(1)} fusion(f32[16,36,260]{2,1,0:T(8,128)S(1)} %fusion.33, f32[34,258]{1,0:T(8,128)S(1)} %get-tuple-element.18, f32[34,258]{1,0:T(8,128)S(1)} %get-tuple-element.17, f32[34,258]{1,0:T(8,128)S(1)} %get-tuple-element.16, f32[34,258]{1,0:T(8,128)S(1)} %get-tuple-element.15), kind=kLoop, calls=%fused_computation.39 | loop fusion | flops 1684224 | bytes 3508800 | tf_op jit(solution)/shard_map/sub | solution.py:145
  66.7 1.4 %fusion.57 = f32[16,32,256]{2,1,0:T(8,128)} fusion(f32[16,34,258]{2,1,0:T(8,128)S(1)} %fusion.25, f32[32,256]{1,0:T(8,128)S(1)} %get-tuple-element.14, f32[32,256]{1,0:T(8,128)S(1)} %get-tuple-element.13, f32[32,256]{1,0:T(8,128)S(1)} %get-tuple-element.12, f32[32,256]{1,0:T(8,128)S(1)} %get-tuple-element.11), kind=kLoop, calls=%fused_computation.88 | loop fusion | flops 1572864 | bytes 3276800 | tf_op jit(solution)/shard_map/sub | solution.py:145
  (9 shorter events, 0.1 us)
Async XLA Ops:
  0.0 22.7 %copy-start = (s32[1,16]{1,0:T(1,128)S(1)}, s32[1,16]{1,0:T(1,128)}, u32[]{:S(2)}) copy-start(s32[1,16]{1,0:T(1,128)} %param.13) | copy-start | bytes 196
  3.3 10.9 %copy-start.5 = (s32[1,4096]{1,0:T(1,128)S(1)}, s32[1,4096]{1,0:T(1,128)}, u32[]{:S(2)}) copy-start(s32[1,4096]{1,0:T(1,128)} %param.12) | copy-start | bytes 49156
  3.3 12.2 %copy-start.6 = (s32[32,256]{1,0:T(8,128)S(1)}, s32[32,256]{1,0:T(8,128)}, u32[]{:S(2)}) copy-start(s32[32,256]{1,0:T(8,128)} %param.11) | copy-start | bytes 98308
  4.1 27.3 %all-to-all-start = ((f32[16,16,512]{2,1,0:T(8,128)}), f32[16,16,512]{2,1,0:T(8,128)S(1)}, u32[]{:S(2)}, u32[]{:S(2)}) async-start(f32[16,16,512]{2,1,0:T(8,128)} %maximum_bitcast_fusion), calls=%async_computation | async-start | bytes 1048576 | tf_op jit(solution)/shard_map/all_to_all | solution.py:166
  31.4 0.8 %copy-start.2 = (f32[16,16,512]{2,1,0:T(8,128)}, f32[16,16,512]{2,1,0:T(8,128)S(1)}, u32[]{:S(2)}) copy-start(f32[16,16,512]{2,1,0:T(8,128)S(1)} %all-to-all-done.held_ref) | copy-start | bytes 1572868
  32.2 6.2 %copy-start.3 = (f32[32,256]{1,0:T(8,128)S(1)}, f32[32,256]{1,0:T(8,128)}, u32[]{:S(2)}) copy-start(f32[32,256]{1,0:T(8,128)} %param.10) | copy-start | bytes 98308
  32.2 6.2 %copy-start.4 = (f32[32,256]{1,0:T(8,128)S(1)}, f32[32,256]{1,0:T(8,128)}, u32[]{:S(2)}) copy-start(f32[32,256]{1,0:T(8,128)} %param.9) | copy-start | bytes 98308
  39.6 5.4 %copy-start.1 = (f32[16,32,256]{2,1,0:T(8,128)S(1)}, f32[16,32,256]{2,1,0:T(8,128)}, u32[]{:S(2)}) copy-start(f32[16,32,256]{2,1,0:T(8,128)} %shard_map.83) | copy-start | bytes 1572868
  39.9 2.0 %collective-permute-start = (f32[19,256]{0,1:T(8,128)S(1)}, f32[19,256]{0,1:T(8,128)S(1)}, u32[]{:S(2)}, u32[]{:S(2)}) collective-permute-start(f32[19,256]{0,1:T(8,128)S(1)} %bitcast.41), channel_id=1, source_target_pairs={{0,16},{16,32},{32,48},{48,64},{64,80},{80,96},{96,112},{112,128},... | collective-permute-start | bytes 58376 | tf_op jit(solution)/shard_map/ppermute | solution.py:126
  40.2 4.4 %collective-permute-start.1 = (f32[19,256]{0,1:T(8,128)S(1)}, f32[19,256]{0,1:T(8,128)S(1)}, u32[]{:S(2)}, u32[]{:S(2)}) collective-permute-start(f32[19,256]{0,1:T(8,128)S(1)} %bitcast.43), channel_id=1, source_target_pairs={{16,0},{32,16},{48,32},{64,48},{80,64},{96,80},{112,96},{128,112},... | collective-permute-start | bytes 58376 | tf_op jit(solution)/shard_map/ppermute | solution.py:127
  45.3 10.8 %collective-permute-start.2 = (f32[19,8,272]{2,1,0:T(8,128)S(1)}, f32[19,8,272]{2,1,0:T(8,128)S(1)}, u32[]{:S(2)}, u32[]{:S(2)}) collective-permute-start(f32[19,8,272]{2,1,0:T(8,128)S(1)} %get-tuple-element.7), channel_id=1, source_target_pairs={{0,1},{1,2},{2,3},{3,4},{4,5},{5,6},{6,7},{7,8},{8,9},{9,10},{10,1... | collective-permute-start | bytes 496136 | tf_op jit(solution)/shard_map/ppermute | solution.py:129
  46.6 9.5 %collective-permute-start.3 = (f32[19,8,272]{2,1,0:T(8,128)S(1)}, f32[19,8,272]{2,1,0:T(8,128)S(1)}, u32[]{:S(2)}, u32[]{:S(2)}) collective-permute-start(f32[19,8,272]{2,1,0:T(8,128)S(1)} %get-tuple-element.8), channel_id=1, source_target_pairs={{1,0},{2,1},{3,2},{4,3},{5,4},{6,5},{7,6},{8,7},{9,8},{10,9},{11,1... | collective-permute-start | bytes 496136 | tf_op jit(solution)/shard_map/ppermute | solution.py:130

commit v12 on v11

--- a/solution.py
+++ b/solution.py
@@ -113,6 +113,27 @@
     return vmem_call(gather_kernel, shape, flops, 4 * (levels * slots + 2 * slots + cells * cols_here))(state2d, rows, cols)
 
 
+def pack_kernel(values_ref, weights_ref, out_ref):
+    peers, _, pair = out_ref.shape
+    capacity = pair // 2
+    for peer in range(peers):
+        here = slice(peer * capacity, (peer + 1) * capacity)
+        out_ref[peer, :, :capacity] = values_ref[:, 0, here]
+        out_ref[peer, :, capacity:] = weights_ref[:, 0, here]
+
+
+def pack_for_owners(values, weights, peers):
+    levels, _, slots = values.shape
+    capacity = slots // peers
+    return pl.pallas_call(
+        pack_kernel,
+        out_shape=jax.ShapeDtypeStruct((peers, levels, 2 * capacity), jnp.float32),
+        in_specs=[pl.BlockSpec(memory_space=pltpu.VMEM)] * 2,
+        out_specs=pl.BlockSpec(memory_space=pltpu.VMEM),
+        cost_estimate=pl.CostEstimate(flops=0, bytes_accessed=16 * levels * slots, transcendentals=0),
+    )(values, weights)
+
+
 def with_halo(block, sides, width):
     for axis, dim in sides:
         count = lax.axis_size(axis)
@@ -160,9 +181,7 @@
     slot_index = jnp.arange(slots, dtype=jnp.int32)
     limits = jnp.broadcast_to(send_count[0][:, None], (lon_count, capacity)).reshape(slots)
     usable = jnp.where(slot_index % capacity < limits, 1.0, 0.0).astype(jnp.float32)
-    chunked = (levels, lon_count, capacity)
-    held = jnp.concatenate([obs_value.reshape(chunked), obs_weight.reshape(chunked)], axis=2)
-    held = jnp.transpose(held, (1, 0, 2))
+    held = pack_for_owners(obs_value, obs_weight, lon_count)
     at_owner = lax.all_to_all(held, "lon", split_axis=0, concat_axis=0, tiled=True)
     target_rows = (targets // cols_here)[None, :]
     target_cols = (targets % cols_here)[None, :]

time: 68.4 us -> 70.5 us (1.031)
  other arithmetic: 18.2 us -> 14.2 us
  waiting for transfers between devices: 17.1 us -> 20.8 us
  Pallas kernels: 12.8 us -> 14.8 us
  starting transfers between devices: 15.8 us -> 16.7 us
    ppermute x1, waiting for transfers between devices: 0.01 us -> 5.2 us  [with_halo(): high = lax.ppermute(high, axis, backward)]
    unnamed x2 -> x0, other arithmetic: 3.19 us -> none
    pallas_call x0 -> x1, Pallas kernels: none -> 2.03 us  [pack_for_owners(): pl.pallas_call(pack_kernel, out_shape=jax.ShapeDtypeStruct((peers, levels...]
    ppermute x1, starting transfers between devices: 0.01 us -> 1.75 us  [with_halo(): low = lax.ppermute(low.reshape(flat), axis, forward).reshape(low.shape)]
    ppermute x1, starting transfers between devices: 1.37 us -> 0.01 us  [with_halo(): low = lax.ppermute(low, axis, forward)]
    ppermute x1, waiting for transfers between devices: 1.16 us -> 0.01 us  [with_halo(): low = lax.ppermute(low.reshape(flat), axis, forward).reshape(low.shape)]
    ppermute x1, starting transfers between devices: 3.9 us -> 5 us  [with_halo(): high = lax.ppermute(high, axis, backward)]
    transpose x1 -> x0, other arithmetic: 0.85 us -> none  [body(): held = jnp.transpose(held, (1, 0, 2))]
  transfers between devices with their start and end apart: 5 -> 5, of which waited for: 4 -> 4; matrix products, arithmetic and copies ran while one was open for 5% -> 5% of each run, Pallas kernels for 10% -> 9%
where the time goes in v12:
time: 70.5 us; the launch traced here: 70.2 us
  waiting for transfers between devices  20.8 us (30%)
  starting transfers between devices  16.7 us (24%)
  Pallas kernels  14.8 us (21%)
  other arithmetic  14.2 us (20%)
  local copies, waits for them, and re-layouts  3.49 us (5%)
    all_to_all x1, starting transfers between devices, body(): lax.all_to_all(held, 'lon', split_axis=0, concat_axis=0, tiled=True)  9.98 us
    sub x8, other arithmetic, one_pass(): centre + east_here * (field[:, 1:-1, 2:] - centre)  9.71 us
    all_to_all x1, waiting for transfers between devices, body(): lax.all_to_all(held, 'lon', split_axis=0, concat_axis=0, tiled=True)  8.03 us
    pallas_call x1, Pallas kernels, onehot_gather(): vmem_call(gather_kernel, shape, flops, 4 * (levels * slots + 2 * slots +...  6.64 us
    pallas_call x1, Pallas kernels, onehot_scatter(): pl.pallas_call(scatter_kernel, out_shape=shape, in_specs=[pl.BlockSpec(me...  6.15 us
    ppermute x1, waiting for transfers between devices, with_halo(): low = lax.ppermute(low, axis, forward)  5.2 us
    ppermute x1, waiting for transfers between devices, with_halo(): high = lax.ppermute(high, axis, backward)  5.2 us
    ppermute x1, starting transfers between devices, with_halo(): high = lax.ppermute(high, axis, backward)  5 us
  transfers between devices with their start and end apart: 5, of which 4 were waited for; matrix products, arithmetic and copies ran while one was open for 5% of the time, Pallas kernels for 9%

profile of v12, /device:TPU:1, one launch (start us, length us, event | category | flops | bytes accessed | tf_op | source)
XLA Modules:
  0.0 70.2 jit_solution(14721575117402754384)
XLA Ops:
  0.0 0.0 copy-start
  0.0 0.0 copy-start.6
  0.0 0.0 copy-start.5
  0.0 2.0 %shard_map.82 = f32[16,16,512]{2,1,0:T(8,128)} custom-call(f32[16,1,4096]{2,1,0:T(1,128)} %values_ref.1, f32[16,1,4096]{2,1,0:T(1,128)} %weights_ref.1), custom_call_target="tpu_custom_call" | custom-call | bytes 1048576 | tf_op jit(solution)/shard_map/pallas_call | solution.py:128
  2.0 10.0 %all-to-all-start = ((f32[16,16,512]{2,1,0:T(8,128)}), f32[16,16,512]{2,1,0:T(8,128)S(1)}, u32[]{:S(2)}, u32[]{:S(2)}) async-start(f32[16,16,512]{2,1,0:T(8,128)} %shard_map.82), calls=%async_computation | async-start | bytes 1048576 | tf_op jit(solution)/shard_map/all_to_all | solution.py:185
  12.0 0.0 copy-done.6
  12.0 0.6 fusion.82
  12.6 0.0 copy-done.5
  12.6 0.7 and_select_fusion.1
  13.3 0.7 and_select_fusion.2.rows_ref
  14.0 6.6 %shard_map.83.seen_ref = f32[16,4096]{1,0:T(8,128)} custom-call(f32[512,256]{1,0:T(8,128)} %bitcast.36, s32[1,4096]{1,0:T(1,128)} %and_select_fusion.2.rows_ref, s32[1,4096]{1,0:T(1,128)} %get-tuple-element.5.cols_ref), custom_call_target="tpu_custom_call" | custom-call | flops 3221225472 | bytes 819200 | tf_op jit(solution)/shard_map/pallas_call | solution.py:113
  20.6 0.0 copy-done
  20.6 0.1 broadcast_bitcast_fusion
  20.7 0.6 compare_select_fusion.usable_ref
  21.3 8.0 %all-to-all-done.held_ref = f32[16,16,512]{2,1,0:T(8,128)S(1)} async-done(((f32[16,16,512]{2,1,0:T(8,128)}), f32[16,16,512]{2,1,0:T(8,128)S(1)}, u32[]{:S(2)}, u32[]{:S(2)}) %all-to-all-start) | async-done | bytes 524320 | tf_op jit(solution)/shard_map/all_to_all | solution.py:185
  29.3 0.0 copy-start.2
  29.3 0.8 %copy-done.2 = f32[16,16,512]{2,1,0:T(8,128)} copy-done((f32[16,16,512]{2,1,0:T(8,128)}, f32[16,16,512]{2,1,0:T(8,128)S(1)}, u32[]{:S(2)}) %copy-start.2) | copy-done | bytes 524312
  30.1 0.0 copy-start.3
  30.1 0.0 copy-start.4
  30.1 6.2 %shard_map.84 = f32[16,32,256]{2,1,0:T(8,128)} custom-call(f32[16,16,512]{2,1,0:T(8,128)} %copy-done.2, f32[16,4096]{1,0:T(8,128)} %shard_map.83.seen_ref, f32[1,4096]{1,0:T(1,128)} %compare_select_fusion.usable_ref, s32[1,4096]{1,0:T(1,128)} %and_select_fusion.2.rows_ref, s32[1,4096]{1,0:T(1,128)} %get-tuple-element.5.cols_ref, ...), custom_call_target="tpu_custom_call" | custom-call | flops 3221225472 | bytes 1359872 | tf_op jit(solution)/shard_map/pallas_call | solution.py:95
  36.3 0.0 copy-done.3
  36.3 0.0 copy-done.4
  36.3 1.1 %pad_maximum_fusion.1 = f32[19,32,256]{2,1,0:T(8,128)S(1)} fusion(f32[1,32,256]{2,1,0:T(8,128)S(1)} %bitcast.25, f32[1,32,256]{2,1,0:T(8,128)S(1)} %bitcast.28, f32[1,32,256]{2,1,0:T(8,128)S(1)} %get-tuple-element.44, f32[16,32,256]{2,1,0:T(8,128)} %shard_map.84), kind=kLoop, calls=%fused_computation.85 | loop fusion | flops 466944 | bytes 1245184 | tf_op jit(solution)/shard_map/concatenate | solution.py:192
  37.4 0.1 fusion.65
  37.5 0.0 copy-start.1
  37.6 0.3 copy.10
  37.9 0.0 collective-permute-start.1
  37.9 0.3 copy.9
  38.2 1.7 %collective-permute-start = (f32[19,256]{0,1:T(8,128)S(1)}, f32[19,256]{0,1:T(8,128)S(1)}, u32[]{:S(2)}, u32[]{:S(2)}) collective-permute-start(f32[19,256]{0,1:T(8,128)S(1)} %bitcast.33), channel_id=1, source_target_pairs={{0,16},{16,32},{32,48},{48,64},{64,80},{80,96},{96,112},{112,128},... | collective-permute-start | bytes 58376 | tf_op jit(solution)/shard_map/ppermute | solution.py:147
  39.9 2.3 %collective-permute-done.1 = f32[19,256]{0,1:T(8,128)S(1)} collective-permute-done((f32[19,256]{0,1:T(8,128)S(1)}, f32[19,256]{0,1:T(8,128)S(1)}, u32[]{:S(2)}, u32[]{:S(2)}) %collective-permute-start.1) | collective-permute-done | bytes 19488 | tf_op jit(solution)/shard_map/ppermute | solution.py:148
  42.3 0.4 copy.12
  42.6 0.0 collective-permute-done
  42.6 0.4 copy.11
  43.0 0.0 copy-done.1
  43.0 0.2 pad_maximum_fusion.7
  43.3 5.0 %collective-permute-start.3 = (f32[19,8,272]{2,1,0:T(8,128)S(1)}, f32[19,8,272]{2,1,0:T(8,128)S(1)}, u32[]{:S(2)}, u32[]{:S(2)}) collective-permute-start(f32[19,8,272]{2,1,0:T(8,128)S(1)} %get-tuple-element.8), channel_id=1, source_target_pairs={{1,0},{2,1},{3,2},{4,3},{5,4},{6,5},{7,6},{8,7},{9,8},{10,9},{11,1... | collective-permute-start | bytes 496136 | tf_op jit(solution)/shard_map/ppermute | solution.py:151
  48.3 0.0 collective-permute-start.2
  48.3 5.2 %collective-permute-done.3 = f32[19,8,272]{2,1,0:T(8,128)S(1)} collective-permute-done((f32[19,8,272]{2,1,0:T(8,128)S(1)}, f32[19,8,272]{2,1,0:T(8,128)S(1)}, u32[]{:S(2)}, u32[]{:S(2)}) %collective-permute-start.3) | collective-permute-done | bytes 165408 | tf_op jit(solution)/shard_map/ppermute | solution.py:151
  53.5 5.2 %collective-permute-done.2 = f32[19,8,272]{2,1,0:T(8,128)S(1)} collective-permute-done((f32[19,8,272]{2,1,0:T(8,128)S(1)}, f32[19,8,272]{2,1,0:T(8,128)S(1)}, u32[]{:S(2)}, u32[]{:S(2)}) %collective-permute-start.2) | collective-permute-done | bytes 165408 | tf_op jit(solution)/shard_map/ppermute | solution.py:150
  58.7 0.4 pad_maximum_fusion
  59.1 0.1 fusion.64
  59.2 0.1 slice_multiply_fusion.2
  59.3 0.1 fusion.80
  59.4 0.1 fusion.78
  59.6 0.1 fusion.76
  59.7 0.1 fusion.74
  59.9 0.1 fusion.72
  60.0 0.1 fusion.70
  60.2 0.1 fusion.68
  60.3 0.1 fusion.66
  60.4 1.3 %fusion.17 = f32[16,46,270]{2,1,0:T(8,128)S(1)} fusion(f32[19,48,272]{2,1,0:T(8,128)S(1)} %pad_maximum_fusion, f32[46,270]{1,0:T(8,128)S(1)} %get-tuple-element.45, f32[46,270]{1,0:T(8,128)S(1)} %get-tuple-element.46, f32[46,270]{1,0:T(8,128)S(1)} %get-tuple-element.40, f32[46,270]{1,0:T(8,128)S(1)} %get-tuple-element.39), kind=kLoop, calls=%fused_computation.27 | loop fusion | flops 2384640 | bytes 4968000 | tf_op jit(solution)/shard_map/sub | solution.py:166
  61.7 1.3 %fusion.9 = f32[16,44,268]{2,1,0:T(8,128)S(1)} fusion(f32[16,46,270]{2,1,0:T(8,128)S(1)} %fusion.17, f32[44,268]{1,0:T(8,128)S(1)} %get-tuple-element.47, f32[44,268]{1,0:T(8,128)S(1)} %get-tuple-element.48, f32[44,268]{1,0:T(8,128)S(1)} %get-tuple-element.36, f32[44,268]{1,0:T(8,128)S(1)} %get-tuple-element.35), kind=kLoop, calls=%fused_computation.15 | loop fusion | flops 2264064 | bytes 4716800 | tf_op jit(solution)/shard_map/sub | solution.py:166
  63.0 1.3 %fusion.1 = f32[16,42,266]{2,1,0:T(8,128)S(1)} fusion(f32[16,44,268]{2,1,0:T(8,128)S(1)} %fusion.9, f32[42,266]{1,0:T(8,128)S(1)} %get-tuple-element.49, f32[42,266]{1,0:T(8,128)S(1)} %get-tuple-element.50, f32[42,266]{1,0:T(8,128)S(1)} %get-tuple-element.32, f32[42,266]{1,0:T(8,128)S(1)} %get-tuple-element.31), kind=kLoop, calls=%fused_computation.3 | loop fusion | flops 2145024 | bytes 4468800 | tf_op jit(solution)/shard_map/sub | solution.py:166
  64.3 1.1 %fusion.49 = f32[16,40,264]{2,1,0:T(8,128)S(1)} fusion(f32[16,42,266]{2,1,0:T(8,128)S(1)} %fusion.1, f32[40,264]{1,0:T(8,128)S(1)} %get-tuple-element.51, f32[40,264]{1,0:T(8,128)S(1)} %get-tuple-element.52, f32[40,264]{1,0:T(8,128)S(1)} %get-tuple-element.28, f32[40,264]{1,0:T(8,128)S(1)} %get-tuple-element.27), kind=kLoop, calls=%fused_computation.75 | loop fusion | flops 2027520 | bytes 4224000 | tf_op jit(solution)/shard_map/sub | solution.py:166
  65.4 1.1 %fusion.41 = f32[16,38,262]{2,1,0:T(8,128)S(1)} fusion(f32[16,40,264]{2,1,0:T(8,128)S(1)} %fusion.49, f32[38,262]{1,0:T(8,128)S(1)} %get-tuple-element.53, f32[38,262]{1,0:T(8,128)S(1)} %get-tuple-element.54, f32[38,262]{1,0:T(8,128)S(1)} %get-tuple-element.24, f32[38,262]{1,0:T(8,128)S(1)} %get-tuple-element.23), kind=kLoop, calls=%fused_computation.63 | loop fusion | flops 1911552 | bytes 3982400 | tf_op jit(solution)/shard_map/sub | solution.py:166
  66.5 1.1 %fusion.33 = f32[16,36,260]{2,1,0:T(8,128)S(1)} fusion(f32[16,38,262]{2,1,0:T(8,128)S(1)} %fusion.41, f32[36,260]{1,0:T(8,128)S(1)} %get-tuple-element.55, f32[36,260]{1,0:T(8,128)S(1)} %get-tuple-element.56, f32[36,260]{1,0:T(8,128)S(1)} %get-tuple-element.20, f32[36,260]{1,0:T(8,128)S(1)} %get-tuple-element.19), kind=kLoop, calls=%fused_computation.51 | loop fusion | flops 1797120 | bytes 3744000 | tf_op jit(solution)/shard_map/sub | solution.py:166
  67.7 1.1 %fusion.25 = f32[16,34,258]{2,1,0:T(8,128)S(1)} fusion(f32[16,36,260]{2,1,0:T(8,128)S(1)} %fusion.33, f32[34,258]{1,0:T(8,128)S(1)} %get-tuple-element.57, f32[34,258]{1,0:T(8,128)S(1)} %get-tuple-element.58, f32[34,258]{1,0:T(8,128)S(1)} %get-tuple-element.16, f32[34,258]{1,0:T(8,128)S(1)} %get-tuple-element.15), kind=kLoop, calls=%fused_computation.39 | loop fusion | flops 1684224 | bytes 3508800 | tf_op jit(solution)/shard_map/sub | solution.py:166
  68.8 1.4 %fusion.57 = f32[16,32,256]{2,1,0:T(8,128)} fusion(f32[16,34,258]{2,1,0:T(8,128)S(1)} %fusion.25, f32[32,256]{1,0:T(8,128)S(1)} %get-tuple-element.59, f32[32,256]{1,0:T(8,128)S(1)} %get-tuple-element.60, f32[32,256]{1,0:T(8,128)S(1)} %get-tuple-element.12, f32[32,256]{1,0:T(8,128)S(1)} %get-tuple-element.11), kind=kLoop, calls=%fused_computation.88 | loop fusion | flops 1572864 | bytes 3276800 | tf_op jit(solution)/shard_map/sub | solution.py:166
  (4 shorter events, 0.0 us)
Async XLA Ops:
  0.0 20.6 %copy-start = (s32[1,16]{1,0:T(1,128)S(1)}, s32[1,16]{1,0:T(1,128)}, u32[]{:S(2)}) copy-start(s32[1,16]{1,0:T(1,128)} %param.13) | copy-start | bytes 196
  0.0 12.0 %copy-start.6 = (s32[32,256]{1,0:T(8,128)S(1)}, s32[32,256]{1,0:T(8,128)}, u32[]{:S(2)}) copy-start(s32[32,256]{1,0:T(8,128)} %param.11) | copy-start | bytes 98308
  0.0 12.6 %copy-start.5 = (s32[1,4096]{1,0:T(1,128)S(1)}, s32[1,4096]{1,0:T(1,128)}, u32[]{:S(2)}) copy-start(s32[1,4096]{1,0:T(1,128)} %param.12) | copy-start | bytes 49156
  2.0 27.3 %all-to-all-start = ((f32[16,16,512]{2,1,0:T(8,128)}), f32[16,16,512]{2,1,0:T(8,128)S(1)}, u32[]{:S(2)}, u32[]{:S(2)}) async-start(f32[16,16,512]{2,1,0:T(8,128)} %shard_map.82), calls=%async_computation | async-start | bytes 1048576 | tf_op jit(solution)/shard_map/all_to_all | solution.py:185
  29.3 0.8 %copy-start.2 = (f32[16,16,512]{2,1,0:T(8,128)}, f32[16,16,512]{2,1,0:T(8,128)S(1)}, u32[]{:S(2)}) copy-start(f32[16,16,512]{2,1,0:T(8,128)S(1)} %all-to-all-done.held_ref) | copy-start | bytes 1572868
  30.1 6.2 %copy-start.3 = (f32[32,256]{1,0:T(8,128)S(1)}, f32[32,256]{1,0:T(8,128)}, u32[]{:S(2)}) copy-start(f32[32,256]{1,0:T(8,128)} %param.10) | copy-start | bytes 98308
  30.1 6.2 %copy-start.4 = (f32[32,256]{1,0:T(8,128)S(1)}, f32[32,256]{1,0:T(8,128)}, u32[]{:S(2)}) copy-start(f32[32,256]{1,0:T(8,128)} %param.9) | copy-start | bytes 98308
  37.5 5.5 %copy-start.1 = (f32[16,32,256]{2,1,0:T(8,128)S(1)}, f32[16,32,256]{2,1,0:T(8,128)}, u32[]{:S(2)}) copy-start(f32[16,32,256]{2,1,0:T(8,128)} %shard_map.84) | copy-start | bytes 1572868
  37.9 4.4 %collective-permute-start.1 = (f32[19,256]{0,1:T(8,128)S(1)}, f32[19,256]{0,1:T(8,128)S(1)}, u32[]{:S(2)}, u32[]{:S(2)}) collective-permute-start(f32[19,256]{0,1:T(8,128)S(1)} %bitcast.31), channel_id=1, source_target_pairs={{16,0},{32,16},{48,32},{64,48},{80,64},{96,80},{112,96},{128,112},... | collective-permute-start | bytes 58376 | tf_op jit(solution)/shard_map/ppermute | solution.py:148
  38.2 4.5 %collective-permute-start = (f32[19,256]{0,1:T(8,128)S(1)}, f32[19,256]{0,1:T(8,128)S(1)}, u32[]{:S(2)}, u32[]{:S(2)}) collective-permute-start(f32[19,256]{0,1:T(8,128)S(1)} %bitcast.33), channel_id=1, source_target_pairs={{0,16},{16,32},{32,48},{48,64},{64,80},{80,96},{96,112},{112,128},... | collective-permute-start | bytes 58376 | tf_op jit(solution)/shard_map/ppermute | solution.py:147
  43.3 10.2 %collective-permute-start.3 = (f32[19,8,272]{2,1,0:T(8,128)S(1)}, f32[19,8,272]{2,1,0:T(8,128)S(1)}, u32[]{:S(2)}, u32[]{:S(2)}) collective-permute-start(f32[19,8,272]{2,1,0:T(8,128)S(1)} %get-tuple-element.8), channel_id=1, source_target_pairs={{1,0},{2,1},{3,2},{4,3},{5,4},{6,5},{7,6},{8,7},{9,8},{10,9},{11,1... | collective-permute-start | bytes 496136 | tf_op jit(solution)/shard_map/ppermute | solution.py:151
  48.3 10.4 %collective-permute-start.2 = (f32[19,8,272]{2,1,0:T(8,128)S(1)}, f32[19,8,272]{2,1,0:T(8,128)S(1)}, u32[]{:S(2)}, u32[]{:S(2)}) collective-permute-start(f32[19,8,272]{2,1,0:T(8,128)S(1)} %get-tuple-element.7), channel_id=1, source_target_pairs={{0,1},{1,2},{2,3},{3,4},{4,5},{5,6},{6,7},{7,8},{8,9},{9,10},{10,1... | collective-permute-start | bytes 496136 | tf_op jit(solution)/shard_map/ppermute | solution.py:150

commit v13 on v11

--- a/solution.py
+++ b/solution.py
@@ -18,7 +18,9 @@
     return high, middle, low
 
 
-def scatter_kernel(held_ref, seen_ref, usable_ref, rows_ref, cols_ref, sea_ref, out_ref, acc_ref):
+def scatter_kernel(
+    held_ref, seen_ref, usable_ref, rows_ref, cols_ref, sea_ref, coef_lon_ref, coef_lat_ref, out_ref, acc_ref
+):
     levels, slots = seen_ref.shape
     peers, _, pair = held_ref.shape
     capacity = pair // 2
@@ -52,7 +54,10 @@
         return carry
 
     lax.fori_loop(0, slots // SCATTER_CHUNK, step, 0)
-    out_ref[...] = acc_ref[...].reshape(levels, rows_here, cols_here) * sea_ref[...][None]
+    out_ref[:levels] = acc_ref[...].reshape(levels, rows_here, cols_here) * sea_ref[...][None]
+    out_ref[levels] = sea_ref[...]
+    out_ref[levels + 1] = coef_lon_ref[...]
+    out_ref[levels + 2] = coef_lat_ref[...]
 
 
 def gather_kernel(state_ref, rows_ref, cols_ref, out_ref):
@@ -87,22 +92,22 @@
     )
 
 
-def onehot_scatter(held, seen, usable, rows, cols, sea):
+def onehot_scatter(held, seen, usable, rows, cols, sea, coef_lon, coef_lat):
     levels, slots = seen.shape
     rows_here, cols_here = sea.shape
-    shape = jax.ShapeDtypeStruct((levels, rows_here, cols_here), jnp.float32)
+    shape = jax.ShapeDtypeStruct((levels + 3, rows_here, cols_here), jnp.float32)
     flops = 6 * levels * rows_here * cols_here * slots
     return pl.pallas_call(
         scatter_kernel,
         out_shape=shape,
-        in_specs=[pl.BlockSpec(memory_space=pltpu.VMEM)] * 6,
+        in_specs=[pl.BlockSpec(memory_space=pltpu.VMEM)] * 8,
         out_specs=pl.BlockSpec(memory_space=pltpu.VMEM),
         scratch_shapes=[pltpu.VMEM((levels * rows_here, cols_here), jnp.float32)],
         cost_estimate=pl.CostEstimate(
             flops=flops, bytes_accessed=4 * (3 * levels * slots + 3 * slots + levels * rows_here * cols_here),
             transcendentals=0,
         ),
-    )(held, seen, usable, rows, cols, sea)
+    )(held, seen, usable, rows, cols, sea, coef_lon, coef_lat)
 
 
 def onehot_gather(state2d, rows, cols, levels):
@@ -168,9 +173,8 @@
     target_cols = (targets % cols_here)[None, :]
     at_column = onehot_gather(state.reshape(levels * rows_here, cols_here), target_rows, target_cols, levels)
     sea = land_sea.astype(jnp.float32)
-    gradient = onehot_scatter(at_owner, at_column, usable[None, :], target_rows, target_cols, sea)
+    stacked = onehot_scatter(at_owner, at_column, usable[None, :], target_rows, target_cols, sea, coef_lon, coef_lat)
     rim_width = PASSES
-    stacked = jnp.concatenate([gradient, sea[None], coef_lon[None], coef_lat[None]], axis=0)
     padded = with_halo(stacked, (("lon", 2), ("lat", 1)), rim_width)
     field = padded[:levels]
     padded = padded[levels:]

time: 68.4 us -> 73.3 us (1.072)
  waiting for transfers between devices: 17.1 us -> 20.7 us
  local copies, waits for them, and re-layouts: 3.97 us -> 5.04 us
  other arithmetic: 18.2 us -> 17.3 us
  starting transfers between devices: 15.8 us -> 16.7 us
    ppermute x1, waiting for transfers between devices: 0.01 us -> 5.19 us  [with_halo(): high = lax.ppermute(high, axis, backward)]
    ppermute x1, starting transfers between devices: 0.01 us -> 1.75 us  [with_halo(): low = lax.ppermute(low.reshape(flat), axis, forward).reshape(low.shape)]
    ppermute x1, starting transfers between devices: 1.37 us -> 0.01 us  [with_halo(): low = lax.ppermute(low, axis, forward)]
    ppermute x1, waiting for transfers between devices: 1.16 us -> 0.01 us  [with_halo(): low = lax.ppermute(low.reshape(flat), axis, forward).reshape(low.shape)]
    ppermute x1, starting transfers between devices: 3.9 us -> 4.99 us  [with_halo(): high = lax.ppermute(high, axis, backward)]
    slice x2, local copies, waits for them, and re-layouts: 0.42 us -> 1.51 us  [with_halo(): low = lax.slice_in_dim(block, block.shape[dim] - width, None, axis=dim)]
    concatenate x1 -> x0, other arithmetic: 1.08 us -> none  [body(): jnp.concatenate([gradient, sea[None], coef_lon[None], coef_lat[None]], ax...]
  transfers between devices with their start and end apart: 5 -> 5, of which waited for: 4 -> 4; matrix products, arithmetic and copies ran while one was open for 5% -> 5% of each run, Pallas kernels for 10% -> 9%
where the time goes in v13:
time: 73.3 us; the launch traced here: 73 us
  waiting for transfers between devices  20.7 us (28%)
  other arithmetic  17.3 us (24%)
  starting transfers between devices  16.7 us (23%)
  Pallas kernels  12.9 us (18%)
  local copies, waits for them, and re-layouts  5.04 us (7%)
    all_to_all x1, starting transfers between devices, body(): lax.all_to_all(held, 'lon', split_axis=0, concat_axis=0, tiled=True)  9.98 us
    sub x8, other arithmetic, one_pass(): centre + east_here * (field[:, 1:-1, 2:] - centre)  9.72 us
    all_to_all x1, waiting for transfers between devices, body(): lax.all_to_all(held, 'lon', split_axis=0, concat_axis=0, tiled=True)  8.01 us
    pallas_call x1, Pallas kernels, onehot_gather(): vmem_call(gather_kernel, shape, flops, 4 * (levels * slots + 2 * slots +...  6.66 us
    pallas_call x1, Pallas kernels, onehot_scatter(): pl.pallas_call(scatter_kernel, out_shape=shape, in_specs=[pl.BlockSpec(me...  6.23 us
    ppermute x1, waiting for transfers between devices, with_halo(): low = lax.ppermute(low, axis, forward)  5.2 us
    ppermute x1, waiting for transfers between devices, with_halo(): high = lax.ppermute(high, axis, backward)  5.19 us
    ppermute x1, starting transfers between devices, with_halo(): high = lax.ppermute(high, axis, backward)  4.99 us
  transfers between devices with their start and end apart: 5, of which 4 were waited for; matrix products, arithmetic and copies ran while one was open for 5% of the time, Pallas kernels for 9%

profile of v13, /device:TPU:1, one launch (start us, length us, event | category | flops | bytes accessed | tf_op | source)
XLA Modules:
  0.0 73.0 jit_solution(5401146475216622701)
XLA Ops:
  0.0 0.0 copy-start
  0.0 1.6 %reduce.1 = f32[16,4096]{1,0:T(8,128)S(1)} reduce(f32[16,1,4096]{2,1,0:T(1,128)} %param.15, f32[]{:T(128)} %constant.52), dimensions={1}, to_apply=%param.15.reduce_sub_computation | reduce | bytes 524292 | tf_op args[7]
  1.6 1.6 %reduce = f32[16,4096]{1,0:T(8,128)S(1)} reduce(f32[16,1,4096]{2,1,0:T(1,128)} %param.14, f32[]{:T(128)} %constant.52), dimensions={1}, to_apply=%param.14.reduce_sub_computation | reduce | bytes 524292 | tf_op args[6]
  3.2 0.1 copy_bitcast_fusion
  3.3 0.0 copy-start.3
  3.3 0.9 %maximum_bitcast_fusion = f32[16,16,512]{2,1,0:T(8,128)} fusion(f32[16,16,256]{2,0,1:T(8,128)S(1)} %get-tuple-element.43, f32[16,16,256]{2,0,1:T(8,128)S(1)} %get-tuple-element.44), kind=kLoop, calls=%fused_computation.97 | loop fusion | flops 131072 | bytes 1048576 | tf_op jit(solution)/shard_map/transpose | solution.py:170
  4.1 10.0 %all-to-all-start = ((f32[16,16,512]{2,1,0:T(8,128)}), f32[16,16,512]{2,1,0:T(8,128)S(1)}, u32[]{:S(2)}, u32[]{:S(2)}) async-start(f32[16,16,512]{2,1,0:T(8,128)} %maximum_bitcast_fusion), calls=%async_computation | async-start | bytes 1048576 | tf_op jit(solution)/shard_map/all_to_all | solution.py:171
  14.1 0.0 copy-done.3
  14.1 0.7 and_select_fusion.1
  14.8 0.7 and_select_fusion.2.rows_ref
  15.4 0.0 copy-start.4
  15.4 6.7 %shard_map.82.seen_ref = f32[16,4096]{1,0:T(8,128)} custom-call(f32[512,256]{1,0:T(8,128)} %bitcast.36, s32[1,4096]{1,0:T(1,128)} %and_select_fusion.2.rows_ref, s32[1,4096]{1,0:T(1,128)} %get-tuple-element.5.cols_ref), custom_call_target="tpu_custom_call" | custom-call | flops 3221225472 | bytes 819200 | tf_op jit(solution)/shard_map/pallas_call | solution.py:118
  22.1 0.0 copy-done
  22.1 0.1 broadcast_bitcast_fusion
  22.2 0.0 copy-done.4
  22.2 0.6 convert_element_type.3.sea_ref
  22.8 0.6 compare_select_fusion.usable_ref
  23.4 8.0 %all-to-all-done.held_ref = f32[16,16,512]{2,1,0:T(8,128)S(1)} async-done(((f32[16,16,512]{2,1,0:T(8,128)}), f32[16,16,512]{2,1,0:T(8,128)S(1)}, u32[]{:S(2)}, u32[]{:S(2)}) %all-to-all-start) | async-done | bytes 524320 | tf_op jit(solution)/shard_map/all_to_all | solution.py:171
  31.4 0.8 %copy-done.2 = f32[16,16,512]{2,1,0:T(8,128)} copy-done((f32[16,16,512]{2,1,0:T(8,128)}, f32[16,16,512]{2,1,0:T(8,128)S(1)}, u32[]{:S(2)}) %copy-start.2) | copy-done | bytes 524312
  32.2 6.2 %shard_map.83 = f32[19,32,256]{2,1,0:T(8,128)} custom-call(f32[16,16,512]{2,1,0:T(8,128)} %copy-done.2, f32[16,4096]{1,0:T(8,128)} %shard_map.82.seen_ref, f32[1,4096]{1,0:T(1,128)} %compare_select_fusion.usable_ref, s32[1,4096]{1,0:T(1,128)} %and_select_fusion.2.rows_ref, s32[1,4096]{1,0:T(1,128)} %get-tuple-element.5.cols_ref, ...), custom_call_target="tpu_custom_call" | custom-call | flops 3221225472 | bytes 1359872 | tf_op jit(solution)/shard_map/pallas_call | solution.py:100
  38.5 1.2 %fusion.65 = (f32[19,32,8]{2,1,0:T(8,128)S(1)}, f32[19,32,8]{2,1,0:T(8,128)S(1)}) fusion(f32[19,32,256]{2,1,0:T(8,128)} %shard_map.83), kind=kLoop, calls=%fused_computation.120 | loop fusion | bytes 77824 | tf_op jit(solution)/shard_map/slice | solution.py:127
  39.7 0.3 copy.12
  40.0 0.0 collective-permute-start.1
  40.0 0.3 copy.11
  40.3 1.7 %collective-permute-start = (f32[19,256]{0,1:T(8,128)S(1)}, f32[19,256]{0,1:T(8,128)S(1)}, u32[]{:S(2)}, u32[]{:S(2)}) collective-permute-start(f32[19,256]{0,1:T(8,128)S(1)} %bitcast.33), channel_id=1, source_target_pairs={{0,16},{16,32},{32,48},{48,64},{64,80},{80,96},{96,112},{112,128},... | collective-permute-start | bytes 58376 | tf_op jit(solution)/shard_map/ppermute | solution.py:131
  42.0 2.3 %collective-permute-done.1 = f32[19,256]{0,1:T(8,128)S(1)} collective-permute-done((f32[19,256]{0,1:T(8,128)S(1)}, f32[19,256]{0,1:T(8,128)S(1)}, u32[]{:S(2)}, u32[]{:S(2)}) %collective-permute-start.1) | collective-permute-done | bytes 19488 | tf_op jit(solution)/shard_map/ppermute | solution.py:132
  44.4 0.4 copy.14
  44.8 0.0 collective-permute-done
  44.8 0.4 copy.13
  45.2 0.0 copy-done.1
  45.2 0.2 pad_maximum_fusion.3
  45.4 5.0 %collective-permute-start.3 = (f32[19,8,272]{2,1,0:T(8,128)S(1)}, f32[19,8,272]{2,1,0:T(8,128)S(1)}, u32[]{:S(2)}, u32[]{:S(2)}) collective-permute-start(f32[19,8,272]{2,1,0:T(8,128)S(1)} %get-tuple-element.8), channel_id=1, source_target_pairs={{1,0},{2,1},{3,2},{4,3},{5,4},{6,5},{7,6},{8,7},{9,8},{10,9},{11,1... | collective-permute-start | bytes 496136 | tf_op jit(solution)/shard_map/ppermute | solution.py:135
  50.4 0.0 collective-permute-start.2
  50.4 5.2 %collective-permute-done.3 = f32[19,8,272]{2,1,0:T(8,128)S(1)} collective-permute-done((f32[19,8,272]{2,1,0:T(8,128)S(1)}, f32[19,8,272]{2,1,0:T(8,128)S(1)}, u32[]{:S(2)}, u32[]{:S(2)}) %collective-permute-start.3) | collective-permute-done | bytes 165408 | tf_op jit(solution)/shard_map/ppermute | solution.py:135
  55.6 5.2 %collective-permute-done.2 = f32[19,8,272]{2,1,0:T(8,128)S(1)} collective-permute-done((f32[19,8,272]{2,1,0:T(8,128)S(1)}, f32[19,8,272]{2,1,0:T(8,128)S(1)}, u32[]{:S(2)}, u32[]{:S(2)}) %collective-permute-start.2) | collective-permute-done | bytes 165408 | tf_op jit(solution)/shard_map/ppermute | solution.py:134
  60.8 0.1 fusion.64
  60.9 0.1 slice_multiply_fusion
  61.0 0.1 fusion.81
  61.1 0.1 fusion.79
  61.2 0.1 maximum_bitcast_fusion.3
  61.3 0.1 slice_multiply_fusion.2
  61.4 0.1 fusion.80
  61.5 0.1 fusion.78
  61.6 0.1 fusion.77
  61.7 0.1 fusion.76
  61.8 0.1 fusion.75
  61.9 0.1 fusion.74
  62.0 0.1 fusion.73
  62.1 0.1 fusion.72
  62.2 0.1 fusion.71
  62.3 0.1 fusion.70
  62.4 0.1 fusion.69
  62.5 0.1 fusion.68
  62.6 0.1 fusion.67
  62.7 0.1 fusion.66
  62.8 0.4 pad_maximum_fusion
  63.2 1.3 %fusion.17 = f32[16,46,270]{2,1,0:T(8,128)S(1)} fusion(f32[19,48,272]{2,1,0:T(8,128)S(1)} %pad_maximum_fusion, f32[46,270]{1,0:T(8,128)S(1)} %get-tuple-element.42, f32[46,270]{1,0:T(8,128)S(1)} %get-tuple-element.41, f32[46,270]{1,0:T(8,128)S(1)} %get-tuple-element.40, f32[46,270]{1,0:T(8,128)S(1)} %get-tuple-element.39), kind=kLoop, calls=%fused_computation.27 | loop fusion | flops 2384640 | bytes 4968000 | tf_op jit(solution)/shard_map/sub | solution.py:150
  64.5 1.3 %fusion.9 = f32[16,44,268]{2,1,0:T(8,128)S(1)} fusion(f32[16,46,270]{2,1,0:T(8,128)S(1)} %fusion.17, f32[44,268]{1,0:T(8,128)S(1)} %get-tuple-element.38, f32[44,268]{1,0:T(8,128)S(1)} %get-tuple-element.37, f32[44,268]{1,0:T(8,128)S(1)} %get-tuple-element.36, f32[44,268]{1,0:T(8,128)S(1)} %get-tuple-element.35), kind=kLoop, calls=%fused_computation.15 | loop fusion | flops 2264064 | bytes 4716800 | tf_op jit(solution)/shard_map/sub | solution.py:150
  65.8 1.3 %fusion.1 = f32[16,42,266]{2,1,0:T(8,128)S(1)} fusion(f32[16,44,268]{2,1,0:T(8,128)S(1)} %fusion.9, f32[42,266]{1,0:T(8,128)S(1)} %get-tuple-element.34, f32[42,266]{1,0:T(8,128)S(1)} %get-tuple-element.33, f32[42,266]{1,0:T(8,128)S(1)} %get-tuple-element.32, f32[42,266]{1,0:T(8,128)S(1)} %get-tuple-element.31), kind=kLoop, calls=%fused_computation.3 | loop fusion | flops 2145024 | bytes 4468800 | tf_op jit(solution)/shard_map/sub | solution.py:150
  67.1 1.1 %fusion.49 = f32[16,40,264]{2,1,0:T(8,128)S(1)} fusion(f32[16,42,266]{2,1,0:T(8,128)S(1)} %fusion.1, f32[40,264]{1,0:T(8,128)S(1)} %get-tuple-element.30, f32[40,264]{1,0:T(8,128)S(1)} %get-tuple-element.29, f32[40,264]{1,0:T(8,128)S(1)} %get-tuple-element.28, f32[40,264]{1,0:T(8,128)S(1)} %get-tuple-element.27), kind=kLoop, calls=%fused_computation.75 | loop fusion | flops 2027520 | bytes 4224000 | tf_op jit(solution)/shard_map/sub | solution.py:150
  68.2 1.1 %fusion.41 = f32[16,38,262]{2,1,0:T(8,128)S(1)} fusion(f32[16,40,264]{2,1,0:T(8,128)S(1)} %fusion.49, f32[38,262]{1,0:T(8,128)S(1)} %get-tuple-element.26, f32[38,262]{1,0:T(8,128)S(1)} %get-tuple-element.25, f32[38,262]{1,0:T(8,128)S(1)} %get-tuple-element.24, f32[38,262]{1,0:T(8,128)S(1)} %get-tuple-element.23), kind=kLoop, calls=%fused_computation.63 | loop fusion | flops 1911552 | bytes 3982400 | tf_op jit(solution)/shard_map/sub | solution.py:150
  69.3 1.1 %fusion.33 = f32[16,36,260]{2,1,0:T(8,128)S(1)} fusion(f32[16,38,262]{2,1,0:T(8,128)S(1)} %fusion.41, f32[36,260]{1,0:T(8,128)S(1)} %get-tuple-element.22, f32[36,260]{1,0:T(8,128)S(1)} %get-tuple-element.21, f32[36,260]{1,0:T(8,128)S(1)} %get-tuple-element.20, f32[36,260]{1,0:T(8,128)S(1)} %get-tuple-element.19), kind=kLoop, calls=%fused_computation.51 | loop fusion | flops 1797120 | bytes 3744000 | tf_op jit(solution)/shard_map/sub | solution.py:150
  70.4 1.1 %fusion.25 = f32[16,34,258]{2,1,0:T(8,128)S(1)} fusion(f32[16,36,260]{2,1,0:T(8,128)S(1)} %fusion.33, f32[34,258]{1,0:T(8,128)S(1)} %get-tuple-element.18, f32[34,258]{1,0:T(8,128)S(1)} %get-tuple-element.17, f32[34,258]{1,0:T(8,128)S(1)} %get-tuple-element.16, f32[34,258]{1,0:T(8,128)S(1)} %get-tuple-element.15), kind=kLoop, calls=%fused_computation.39 | loop fusion | flops 1684224 | bytes 3508800 | tf_op jit(solution)/shard_map/sub | solution.py:150
  71.5 1.4 %fusion.57 = f32[16,32,256]{2,1,0:T(8,128)} fusion(f32[16,34,258]{2,1,0:T(8,128)S(1)} %fusion.25, f32[32,256]{1,0:T(8,128)S(1)} %get-tuple-element.14, f32[32,256]{1,0:T(8,128)S(1)} %get-tuple-element.13, f32[32,256]{1,0:T(8,128)S(1)} %get-tuple-element.12, f32[32,256]{1,0:T(8,128)S(1)} %get-tuple-element.11), kind=kLoop, calls=%fused_computation.87 | loop fusion | flops 1572864 | bytes 3276800 | tf_op jit(solution)/shard_map/sub | solution.py:150
  (4 shorter events, 0.0 us)
Async XLA Ops:
  0.0 22.1 %copy-start = (s32[1,16]{1,0:T(1,128)S(1)}, s32[1,16]{1,0:T(1,128)}, u32[]{:S(2)}) copy-start(s32[1,16]{1,0:T(1,128)} %param.13) | copy-start | bytes 196
  3.3 10.9 %copy-start.3 = (s32[1,4096]{1,0:T(1,128)S(1)}, s32[1,4096]{1,0:T(1,128)}, u32[]{:S(2)}) copy-start(s32[1,4096]{1,0:T(1,128)} %param.12) | copy-start | bytes 49156
  4.1 27.3 %all-to-all-start = ((f32[16,16,512]{2,1,0:T(8,128)}), f32[16,16,512]{2,1,0:T(8,128)S(1)}, u32[]{:S(2)}, u32[]{:S(2)}) async-start(f32[16,16,512]{2,1,0:T(8,128)} %maximum_bitcast_fusion), calls=%async_computation | async-start | bytes 1048576 | tf_op jit(solution)/shard_map/all_to_all | solution.py:171
  15.4 6.8 %copy-start.4 = (s32[32,256]{1,0:T(8,128)S(1)}, s32[32,256]{1,0:T(8,128)}, u32[]{:S(2)}) copy-start(s32[32,256]{1,0:T(8,128)} %param.11) | copy-start | bytes 98308
  31.4 0.8 %copy-start.2 = (f32[16,16,512]{2,1,0:T(8,128)}, f32[16,16,512]{2,1,0:T(8,128)S(1)}, u32[]{:S(2)}) copy-start(f32[16,16,512]{2,1,0:T(8,128)S(1)} %all-to-all-done.held_ref) | copy-start | bytes 1572868
  39.7 5.5 %copy-start.1 = (f32[19,32,256]{2,1,0:T(8,128)S(1)}, f32[19,32,256]{2,1,0:T(8,128)}, u32[]{:S(2)}) copy-start(f32[19,32,256]{2,1,0:T(8,128)} %shard_map.83) | copy-start | bytes 1867780
  40.0 4.4 %collective-permute-start.1 = (f32[19,256]{0,1:T(8,128)S(1)}, f32[19,256]{0,1:T(8,128)S(1)}, u32[]{:S(2)}, u32[]{:S(2)}) collective-permute-start(f32[19,256]{0,1:T(8,128)S(1)} %bitcast.31), channel_id=1, source_target_pairs={{16,0},{32,16},{48,32},{64,48},{80,64},{96,80},{112,96},{128,112},... | collective-permute-start | bytes 58376 | tf_op jit(solution)/shard_map/ppermute | solution.py:132
  40.3 4.5 %collective-permute-start = (f32[19,256]{0,1:T(8,128)S(1)}, f32[19,256]{0,1:T(8,128)S(1)}, u32[]{:S(2)}, u32[]{:S(2)}) collective-permute-start(f32[19,256]{0,1:T(8,128)S(1)} %bitcast.33), channel_id=1, source_target_pairs={{0,16},{16,32},{32,48},{48,64},{64,80},{80,96},{96,112},{112,128},... | collective-permute-start | bytes 58376 | tf_op jit(solution)/shard_map/ppermute | solution.py:131
  45.4 10.2 %collective-permute-start.3 = (f32[19,8,272]{2,1,0:T(8,128)S(1)}, f32[19,8,272]{2,1,0:T(8,128)S(1)}, u32[]{:S(2)}, u32[]{:S(2)}) collective-permute-start(f32[19,8,272]{2,1,0:T(8,128)S(1)} %get-tuple-element.8), channel_id=1, source_target_pairs={{1,0},{2,1},{3,2},{4,3},{5,4},{6,5},{7,6},{8,7},{9,8},{10,9},{11,1... | collective-permute-start | bytes 496136 | tf_op jit(solution)/shard_map/ppermute | solution.py:135
  50.4 10.4 %collective-permute-start.2 = (f32[19,8,272]{2,1,0:T(8,128)S(1)}, f32[19,8,272]{2,1,0:T(8,128)S(1)}, u32[]{:S(2)}, u32[]{:S(2)}) collective-permute-start(f32[19,8,272]{2,1,0:T(8,128)S(1)} %get-tuple-element.7), channel_id=1, source_target_pairs={{0,1},{1,2},{2,3},{3,4},{4,5},{5,6},{6,7},{7,8},{8,9},{9,10},{10,1... | collective-permute-start | bytes 496136 | tf_op jit(solution)/shard_map/ppermute | solution.py:134

commit v14 on v11

--- a/solution.py
+++ b/solution.py
@@ -171,7 +171,7 @@
     gradient = onehot_scatter(at_owner, at_column, usable[None, :], target_rows, target_cols, sea)
     rim_width = PASSES
     stacked = jnp.concatenate([gradient, sea[None], coef_lon[None], coef_lat[None]], axis=0)
-    padded = with_halo(stacked, (("lon", 2), ("lat", 1)), rim_width)
+    padded = with_halo(stacked, (("lat", 1), ("lon", 2)), rim_width)
     field = padded[:levels]
     padded = padded[levels:]
     lat_index = lax.axis_index("lat")

time: 68.4 us -> 67.1 us (0.981)
  waiting for transfers between devices: 17.1 us -> 15.6 us
    ppermute x1, waiting for transfers between devices: 5.57 us -> 3.15 us  [with_halo(): low = lax.ppermute(low, axis, forward)]
    concatenate x1 -> x0, other arithmetic: 1.08 us -> none  [body(): jnp.concatenate([gradient, sea[None], coef_lon[None], coef_lat[None]], ax...]
    slice x1, other arithmetic: 0.24 us -> 1.05 us  [with_halo(): low = lax.slice_in_dim(block, block.shape[dim] - width, None, axis=dim)]
where the time goes in v14:
time: 67.1 us; the launch traced here: 66.9 us
  other arithmetic  18.2 us (27%)
  starting transfers between devices  15.8 us (24%)
  waiting for transfers between devices  15.6 us (23%)
  Pallas kernels  12.8 us (19%)
  local copies, waits for them, and re-layouts  4.2 us (6%)
    all_to_all x1, starting transfers between devices, body(): lax.all_to_all(held, 'lon', split_axis=0, concat_axis=0, tiled=True)  9.98 us
    sub x8, other arithmetic, one_pass(): centre + east_here * (field[:, 1:-1, 2:] - centre)  9.73 us
    all_to_all x1, waiting for transfers between devices, body(): lax.all_to_all(held, 'lon', split_axis=0, concat_axis=0, tiled=True)  8.01 us
    pallas_call x1, Pallas kernels, onehot_gather(): vmem_call(gather_kernel, shape, flops, 4 * (levels * slots + 2 * slots +...  6.65 us
    pallas_call x1, Pallas kernels, onehot_scatter(): pl.pallas_call(scatter_kernel, out_shape=shape, in_specs=[pl.BlockSpec(me...  6.16 us
    ppermute x1, starting transfers between devices, with_halo(): high = lax.ppermute(high, axis, backward)  3.9 us
    unnamed x2, other arithmetic  3.19 us
    ppermute x1, waiting for transfers between devices, with_halo(): low = lax.ppermute(low, axis, forward)  3.15 us
  transfers between devices with their start and end apart: 5, of which 4 were waited for; matrix products, arithmetic and copies ran while one was open for 5% of the time, Pallas kernels for 10%

profile of v14, /device:TPU:1, one launch (start us, length us, event | category | flops | bytes accessed | tf_op | source)
XLA Modules:
  0.0 66.9 jit_solution(5620272048173787568)
XLA Ops:
  0.0 0.0 copy-start
  0.0 1.6 %reduce = f32[16,4096]{1,0:T(8,128)S(1)} reduce(f32[16,1,4096]{2,1,0:T(1,128)} %param.14, f32[]{:T(128)} %constant.52), dimensions={1}, to_apply=%param.14.reduce_sub_computation | reduce | bytes 524292 | tf_op args[6]
  1.6 1.6 %reduce.1 = f32[16,4096]{1,0:T(8,128)S(1)} reduce(f32[16,1,4096]{2,1,0:T(1,128)} %param.15, f32[]{:T(128)} %constant.52), dimensions={1}, to_apply=%param.15.reduce_sub_computation | reduce | bytes 524292 | tf_op args[7]
  3.2 0.1 copy_bitcast_fusion
  3.3 0.0 copy-start.5
  3.3 0.0 copy-start.6
  3.3 0.9 %maximum_bitcast_fusion = f32[16,16,512]{2,1,0:T(8,128)} fusion(f32[16,16,256]{2,0,1:T(8,128)S(1)} %get-tuple-element.45, f32[16,16,256]{2,0,1:T(8,128)S(1)} %get-tuple-element.46), kind=kLoop, calls=%fused_computation.98 | loop fusion | flops 131072 | bytes 1048576 | tf_op jit(solution)/shard_map/transpose | solution.py:165
  4.1 10.0 %all-to-all-start = ((f32[16,16,512]{2,1,0:T(8,128)}), f32[16,16,512]{2,1,0:T(8,128)S(1)}, u32[]{:S(2)}, u32[]{:S(2)}) async-start(f32[16,16,512]{2,1,0:T(8,128)} %maximum_bitcast_fusion), calls=%async_computation | async-start | bytes 1048576 | tf_op jit(solution)/shard_map/all_to_all | solution.py:166
  14.1 0.0 copy-done.5
  14.1 0.7 and_select_fusion.1
  14.8 0.7 and_select_fusion.2.rows_ref
  15.4 0.0 copy-done.6
  15.4 0.6 fusion.82
  16.1 6.6 %shard_map.82.seen_ref = f32[16,4096]{1,0:T(8,128)} custom-call(f32[512,256]{1,0:T(8,128)} %bitcast.46, s32[1,4096]{1,0:T(1,128)} %and_select_fusion.2.rows_ref, s32[1,4096]{1,0:T(1,128)} %get-tuple-element.5.cols_ref), custom_call_target="tpu_custom_call" | custom-call | flops 3221225472 | bytes 819200 | tf_op jit(solution)/shard_map/pallas_call | solution.py:113
  22.7 0.0 copy-done
  22.7 0.1 broadcast_bitcast_fusion
  22.8 0.6 compare_select_fusion.usable_ref
  23.4 8.0 %all-to-all-done.held_ref = f32[16,16,512]{2,1,0:T(8,128)S(1)} async-done(((f32[16,16,512]{2,1,0:T(8,128)}), f32[16,16,512]{2,1,0:T(8,128)S(1)}, u32[]{:S(2)}, u32[]{:S(2)}) %all-to-all-start) | async-done | bytes 524320 | tf_op jit(solution)/shard_map/all_to_all | solution.py:166
  31.5 0.8 %copy-done.2 = f32[16,16,512]{2,1,0:T(8,128)} copy-done((f32[16,16,512]{2,1,0:T(8,128)}, f32[16,16,512]{2,1,0:T(8,128)S(1)}, u32[]{:S(2)}) %copy-start.2) | copy-done | bytes 524312
  32.2 6.2 %shard_map.83 = f32[16,32,256]{2,1,0:T(8,128)} custom-call(f32[16,16,512]{2,1,0:T(8,128)} %copy-done.2, f32[16,4096]{1,0:T(8,128)} %shard_map.82.seen_ref, f32[1,4096]{1,0:T(1,128)} %compare_select_fusion.usable_ref, s32[1,4096]{1,0:T(1,128)} %and_select_fusion.2.rows_ref, s32[1,4096]{1,0:T(1,128)} %get-tuple-element.5.cols_ref, ...), custom_call_target="tpu_custom_call" | custom-call | flops 3221225472 | bytes 1359872 | tf_op jit(solution)/shard_map/pallas_call | solution.py:95
  38.4 0.0 copy-done.3
  38.4 0.0 copy-done.4
  38.4 1.0 %pad_maximum_fusion.5 = (f32[19,8,256]{2,1,0:T(8,128)S(1)}, f32[19,8,256]{2,1,0:T(8,128)S(1)}) fusion(f32[1,32,256]{2,1,0:T(8,128)S(1)} %bitcast.35, f32[1,32,256]{2,1,0:T(8,128)S(1)} %bitcast.38, f32[1,32,256]{2,1,0:T(8,128)S(1)} %get-tuple-element.44, f32[16,32,256]{2,1,0:T(8,128)} %shard_map.83), kind=kLoop, calls=%fused_computation.104 | loop fusion | flops 233472 | bytes 933888 | tf_op jit(solution)/shard_map/slice | solution.py:122
  39.5 1.4 %collective-permute-start = (f32[19,8,256]{2,1,0:T(8,128)S(1)}, f32[19,8,256]{2,1,0:T(8,128)S(1)}, u32[]{:S(2)}, u32[]{:S(2)}) collective-permute-start(f32[19,8,256]{2,1,0:T(8,128)S(1)} %get-tuple-element.9), channel_id=1, source_target_pairs={{0,1},{1,2},{2,3},{3,4},{4,5},{5,6},{6,7},{7,8},{8,9},{9,10},{10,1... | collective-permute-start | bytes 466952 | tf_op jit(solution)/shard_map/ppermute | solution.py:129
  40.8 3.9 %collective-permute-start.1 = (f32[19,8,256]{2,1,0:T(8,128)S(1)}, f32[19,8,256]{2,1,0:T(8,128)S(1)}, u32[]{:S(2)}, u32[]{:S(2)}) collective-permute-start(f32[19,8,256]{2,1,0:T(8,128)S(1)} %get-tuple-element.10), channel_id=1, source_target_pairs={{1,0},{2,1},{3,2},{4,3},{5,4},{6,5},{7,6},{8,7},{9,8},{10,9},{11,1... | collective-permute-start | bytes 466952 | tf_op jit(solution)/shard_map/ppermute | solution.py:130
  44.7 3.2 %collective-permute-done = f32[19,8,256]{2,1,0:T(8,128)S(1)} collective-permute-done((f32[19,8,256]{2,1,0:T(8,128)S(1)}, f32[19,8,256]{2,1,0:T(8,128)S(1)}, u32[]{:S(2)}, u32[]{:S(2)}) %collective-permute-start) | collective-permute-done | bytes 155680 | tf_op jit(solution)/shard_map/ppermute | solution.py:129
  47.9 0.0 collective-permute-done.1
  47.9 0.1 pad_maximum_fusion.1
  48.0 0.2 fusion.65
  48.2 0.4 copy.11
  48.5 0.0 collective-permute-start.2
  48.5 0.4 copy.12
  48.9 0.5 collective-permute-start.3
  49.4 1.7 %collective-permute-done.2 = f32[19,384]{0,1:T(8,128)S(1)} collective-permute-done((f32[19,384]{0,1:T(8,128)S(1)}, f32[19,384]{0,1:T(8,128)S(1)}, u32[]{:S(2)}, u32[]{:S(2)}) %collective-permute-start.2) | collective-permute-done | bytes 29216 | tf_op jit(solution)/shard_map/ppermute | solution.py:126
  51.1 0.4 copy.13
  51.6 2.7 %collective-permute-done.3 = f32[19,384]{0,1:T(8,128)S(1)} collective-permute-done((f32[19,384]{0,1:T(8,128)S(1)}, f32[19,384]{0,1:T(8,128)S(1)}, u32[]{:S(2)}, u32[]{:S(2)}) %collective-permute-start.3) | collective-permute-done | bytes 29216 | tf_op jit(solution)/shard_map/ppermute | solution.py:127
  54.3 0.4 copy.14
  54.7 0.6 pad_maximum_fusion
  55.3 0.1 fusion.64
  55.4 0.1 slice_multiply_fusion.2
  55.5 0.1 fusion.80
  55.6 0.1 fusion.78
  55.7 0.1 fusion.81
  55.8 0.1 fusion.79
  55.9 0.1 fusion.76
  56.0 0.1 fusion.77
  56.1 0.1 fusion.74
  56.2 0.1 fusion.75
  56.3 0.1 fusion.72
  56.4 0.1 fusion.73
  56.5 0.1 fusion.70
  56.6 0.1 fusion.71
  56.7 0.1 fusion.68
  56.8 0.1 fusion.69
  56.9 0.1 fusion.66
  57.0 0.1 fusion.67
  57.1 1.3 %fusion.17 = f32[16,46,270]{2,1,0:T(8,128)S(1)} fusion(f32[19,48,272]{2,1,0:T(8,128)S(1)} %pad_maximum_fusion, f32[46,270]{1,0:T(8,128)S(1)} %get-tuple-element.42, f32[46,270]{1,0:T(8,128)S(1)} %get-tuple-element.41, f32[46,270]{1,0:T(8,128)S(1)} %get-tuple-element.40, f32[46,270]{1,0:T(8,128)S(1)} %get-tuple-element.39), kind=kLoop, calls=%fused_computation.27 | loop fusion | flops 2384640 | bytes 4968000 | tf_op jit(solution)/shard_map/sub | solution.py:145
  58.4 1.3 %fusion.9 = f32[16,44,268]{2,1,0:T(8,128)S(1)} fusion(f32[16,46,270]{2,1,0:T(8,128)S(1)} %fusion.17, f32[44,268]{1,0:T(8,128)S(1)} %get-tuple-element.38, f32[44,268]{1,0:T(8,128)S(1)} %get-tuple-element.37, f32[44,268]{1,0:T(8,128)S(1)} %get-tuple-element.36, f32[44,268]{1,0:T(8,128)S(1)} %get-tuple-element.35), kind=kLoop, calls=%fused_computation.15 | loop fusion | flops 2264064 | bytes 4716800 | tf_op jit(solution)/shard_map/sub | solution.py:145
  59.7 1.3 %fusion.1 = f32[16,42,266]{2,1,0:T(8,128)S(1)} fusion(f32[16,44,268]{2,1,0:T(8,128)S(1)} %fusion.9, f32[42,266]{1,0:T(8,128)S(1)} %get-tuple-element.34, f32[42,266]{1,0:T(8,128)S(1)} %get-tuple-element.33, f32[42,266]{1,0:T(8,128)S(1)} %get-tuple-element.32, f32[42,266]{1,0:T(8,128)S(1)} %get-tuple-element.31), kind=kLoop, calls=%fused_computation.3 | loop fusion | flops 2145024 | bytes 4468800 | tf_op jit(solution)/shard_map/sub | solution.py:145
  61.0 1.1 %fusion.49 = f32[16,40,264]{2,1,0:T(8,128)S(1)} fusion(f32[16,42,266]{2,1,0:T(8,128)S(1)} %fusion.1, f32[40,264]{1,0:T(8,128)S(1)} %get-tuple-element.30, f32[40,264]{1,0:T(8,128)S(1)} %get-tuple-element.29, f32[40,264]{1,0:T(8,128)S(1)} %get-tuple-element.28, f32[40,264]{1,0:T(8,128)S(1)} %get-tuple-element.27), kind=kLoop, calls=%fused_computation.75 | loop fusion | flops 2027520 | bytes 4224000 | tf_op jit(solution)/shard_map/sub | solution.py:145
  62.1 1.1 %fusion.41 = f32[16,38,262]{2,1,0:T(8,128)S(1)} fusion(f32[16,40,264]{2,1,0:T(8,128)S(1)} %fusion.49, f32[38,262]{1,0:T(8,128)S(1)} %get-tuple-element.26, f32[38,262]{1,0:T(8,128)S(1)} %get-tuple-element.25, f32[38,262]{1,0:T(8,128)S(1)} %get-tuple-element.24, f32[38,262]{1,0:T(8,128)S(1)} %get-tuple-element.23), kind=kLoop, calls=%fused_computation.63 | loop fusion | flops 1911552 | bytes 3982400 | tf_op jit(solution)/shard_map/sub | solution.py:145
  63.2 1.1 %fusion.33 = f32[16,36,260]{2,1,0:T(8,128)S(1)} fusion(f32[16,38,262]{2,1,0:T(8,128)S(1)} %fusion.41, f32[36,260]{1,0:T(8,128)S(1)} %get-tuple-element.22, f32[36,260]{1,0:T(8,128)S(1)} %get-tuple-element.21, f32[36,260]{1,0:T(8,128)S(1)} %get-tuple-element.20, f32[36,260]{1,0:T(8,128)S(1)} %get-tuple-element.19), kind=kLoop, calls=%fused_computation.51 | loop fusion | flops 1797120 | bytes 3744000 | tf_op jit(solution)/shard_map/sub | solution.py:145
  64.3 1.1 %fusion.25 = f32[16,34,258]{2,1,0:T(8,128)S(1)} fusion(f32[16,36,260]{2,1,0:T(8,128)S(1)} %fusion.33, f32[34,258]{1,0:T(8,128)S(1)} %get-tuple-element.18, f32[34,258]{1,0:T(8,128)S(1)} %get-tuple-element.17, f32[34,258]{1,0:T(8,128)S(1)} %get-tuple-element.16, f32[34,258]{1,0:T(8,128)S(1)} %get-tuple-element.15), kind=kLoop, calls=%fused_computation.39 | loop fusion | flops 1684224 | bytes 3508800 | tf_op jit(solution)/shard_map/sub | solution.py:145
  65.4 1.4 %fusion.57 = f32[16,32,256]{2,1,0:T(8,128)} fusion(f32[16,34,258]{2,1,0:T(8,128)S(1)} %fusion.25, f32[32,256]{1,0:T(8,128)S(1)} %get-tuple-element.14, f32[32,256]{1,0:T(8,128)S(1)} %get-tuple-element.13, f32[32,256]{1,0:T(8,128)S(1)} %get-tuple-element.12, f32[32,256]{1,0:T(8,128)S(1)} %get-tuple-element.11), kind=kLoop, calls=%fused_computation.88 | loop fusion | flops 1572864 | bytes 3276800 | tf_op jit(solution)/shard_map/sub | solution.py:145
  (9 shorter events, 0.1 us)
Async XLA Ops:
  0.0 22.7 %copy-start = (s32[1,16]{1,0:T(1,128)S(1)}, s32[1,16]{1,0:T(1,128)}, u32[]{:S(2)}) copy-start(s32[1,16]{1,0:T(1,128)} %param.13) | copy-start | bytes 196
  3.3 10.9 %copy-start.5 = (s32[1,4096]{1,0:T(1,128)S(1)}, s32[1,4096]{1,0:T(1,128)}, u32[]{:S(2)}) copy-start(s32[1,4096]{1,0:T(1,128)} %param.12) | copy-start | bytes 49156
  3.3 12.2 %copy-start.6 = (s32[32,256]{1,0:T(8,128)S(1)}, s32[32,256]{1,0:T(8,128)}, u32[]{:S(2)}) copy-start(s32[32,256]{1,0:T(8,128)} %param.11) | copy-start | bytes 98308
  4.1 27.3 %all-to-all-start = ((f32[16,16,512]{2,1,0:T(8,128)}), f32[16,16,512]{2,1,0:T(8,128)S(1)}, u32[]{:S(2)}, u32[]{:S(2)}) async-start(f32[16,16,512]{2,1,0:T(8,128)} %maximum_bitcast_fusion), calls=%async_computation | async-start | bytes 1048576 | tf_op jit(solution)/shard_map/all_to_all | solution.py:166
  31.4 0.8 %copy-start.2 = (f32[16,16,512]{2,1,0:T(8,128)}, f32[16,16,512]{2,1,0:T(8,128)S(1)}, u32[]{:S(2)}) copy-start(f32[16,16,512]{2,1,0:T(8,128)S(1)} %all-to-all-done.held_ref) | copy-start | bytes 1572868
  32.2 6.2 %copy-start.3 = (f32[32,256]{1,0:T(8,128)S(1)}, f32[32,256]{1,0:T(8,128)}, u32[]{:S(2)}) copy-start(f32[32,256]{1,0:T(8,128)} %param.10) | copy-start | bytes 98308
  32.2 6.2 %copy-start.4 = (f32[32,256]{1,0:T(8,128)S(1)}, f32[32,256]{1,0:T(8,128)}, u32[]{:S(2)}) copy-start(f32[32,256]{1,0:T(8,128)} %param.9) | copy-start | bytes 98308
  38.4 9.5 %copy-start.1 = (f32[16,32,256]{2,1,0:T(8,128)S(1)}, f32[16,32,256]{2,1,0:T(8,128)}, u32[]{:S(2)}) copy-start(f32[16,32,256]{2,1,0:T(8,128)} %shard_map.83) | copy-start | bytes 1572868
  39.5 8.4 %collective-permute-start = (f32[19,8,256]{2,1,0:T(8,128)S(1)}, f32[19,8,256]{2,1,0:T(8,128)S(1)}, u32[]{:S(2)}, u32[]{:S(2)}) collective-permute-start(f32[19,8,256]{2,1,0:T(8,128)S(1)} %get-tuple-element.9), channel_id=1, source_target_pairs={{0,1},{1,2},{2,3},{3,4},{4,5},{5,6},{6,7},{7,8},{8,9},{9,10},{10,1... | collective-permute-start | bytes 466952 | tf_op jit(solution)/shard_map/ppermute | solution.py:129
  40.8 7.1 %collective-permute-start.1 = (f32[19,8,256]{2,1,0:T(8,128)S(1)}, f32[19,8,256]{2,1,0:T(8,128)S(1)}, u32[]{:S(2)}, u32[]{:S(2)}) collective-permute-start(f32[19,8,256]{2,1,0:T(8,128)S(1)} %get-tuple-element.10), channel_id=1, source_target_pairs={{1,0},{2,1},{3,2},{4,3},{5,4},{6,5},{7,6},{8,7},{9,8},{10,9},{11,1... | collective-permute-start | bytes 466952 | tf_op jit(solution)/shard_map/ppermute | solution.py:130
  48.5 2.6 %collective-permute-start.2 = (f32[19,384]{0,1:T(8,128)S(1)}, f32[19,384]{0,1:T(8,128)S(1)}, u32[]{:S(2)}, u32[]{:S(2)}) collective-permute-start(f32[19,384]{0,1:T(8,128)S(1)} %bitcast.41), channel_id=1, source_target_pairs={{0,16},{16,32},{32,48},{48,64},{64,80},{80,96},{96,112},{112,128},... | collective-permute-start | bytes 87560 | tf_op jit(solution)/shard_map/ppermute | solution.py:126
  48.9 5.4 %collective-permute-start.3 = (f32[19,384]{0,1:T(8,128)S(1)}, f32[19,384]{0,1:T(8,128)S(1)}, u32[]{:S(2)}, u32[]{:S(2)}) collective-permute-start(f32[19,384]{0,1:T(8,128)S(1)} %bitcast.43), channel_id=1, source_target_pairs={{16,0},{32,16},{48,32},{64,48},{80,64},{96,80},{112,96},{128,112},... | collective-permute-start | bytes 87560 | tf_op jit(solution)/shard_map/ppermute | solution.py:127

commit v15 on v14

--- a/solution.py
+++ b/solution.py
@@ -122,7 +122,7 @@
         low = lax.slice_in_dim(block, block.shape[dim] - width, None, axis=dim)
         high = lax.slice_in_dim(block, 0, width, axis=dim)
         if dim == block.ndim - 1:
-            flat = block.shape[:-2] + (-1,)
+            flat = (-1, 128) if low.size % 128 == 0 else block.shape[:-2] + (-1,)
             low = lax.ppermute(low.reshape(flat), axis, forward).reshape(low.shape)
             high = lax.ppermute(high.reshape(flat), axis, backward).reshape(high.shape)
         else:

time: 67.1 us -> 65 us (0.969)
  waiting for transfers between devices: 15.6 us -> 14 us
    ppermute x1, waiting for transfers between devices: 1.74 us -> 0.45 us  [with_halo(): low = lax.ppermute(low.reshape(flat), axis, forward).reshape(low.shape)]
where the time goes in v15:
time: 65 us; the launch traced here: 64.7 us
  other arithmetic  18.2 us (28%)
  starting transfers between devices  15.8 us (24%)
  waiting for transfers between devices  14 us (22%)
  Pallas kernels  12.8 us (20%)
  local copies, waits for them, and re-layouts  3.67 us (6%)
    all_to_all x1, starting transfers between devices, body(): lax.all_to_all(held, 'lon', split_axis=0, concat_axis=0, tiled=True)  9.98 us
    sub x8, other arithmetic, one_pass(): centre + east_here * (field[:, 1:-1, 2:] - centre)  9.73 us
    all_to_all x1, waiting for transfers between devices, body(): lax.all_to_all(held, 'lon', split_axis=0, concat_axis=0, tiled=True)  8.01 us
    pallas_call x1, Pallas kernels, onehot_gather(): vmem_call(gather_kernel, shape, flops, 4 * (levels * slots + 2 * slots +...  6.65 us
    pallas_call x1, Pallas kernels, onehot_scatter(): pl.pallas_call(scatter_kernel, out_shape=shape, in_specs=[pl.BlockSpec(me...  6.16 us
    ppermute x1, starting transfers between devices, with_halo(): high = lax.ppermute(high, axis, backward)  3.9 us
    unnamed x2, other arithmetic  3.19 us
    ppermute x1, waiting for transfers between devices, with_halo(): low = lax.ppermute(low, axis, forward)  3.15 us
  transfers between devices with their start and end apart: 5, of which 4 were waited for; matrix products, arithmetic and copies ran while one was open for 5% of the time, Pallas kernels for 10%

profile of v15, /device:TPU:1, one launch (start us, length us, event | category | flops | bytes accessed | tf_op | source)
XLA Modules:
  0.0 64.7 jit_solution(12338833477518608110)
XLA Ops:
  0.0 0.0 copy-start
  0.0 1.6 %reduce.1 = f32[16,4096]{1,0:T(8,128)S(1)} reduce(f32[16,1,4096]{2,1,0:T(1,128)} %param.15, f32[]{:T(128)} %constant.52), dimensions={1}, to_apply=%param.15.reduce_sub_computation | reduce | bytes 524292 | tf_op args[7]
  1.6 1.6 %reduce = f32[16,4096]{1,0:T(8,128)S(1)} reduce(f32[16,1,4096]{2,1,0:T(1,128)} %param.14, f32[]{:T(128)} %constant.52), dimensions={1}, to_apply=%param.14.reduce_sub_computation | reduce | bytes 524292 | tf_op args[6]
  3.2 0.1 copy_bitcast_fusion
  3.3 0.0 copy-start.5
  3.3 0.0 copy-start.6
  3.3 0.9 %maximum_bitcast_fusion = f32[16,16,512]{2,1,0:T(8,128)} fusion(f32[16,16,256]{2,0,1:T(8,128)S(1)} %get-tuple-element.45, f32[16,16,256]{2,0,1:T(8,128)S(1)} %get-tuple-element.46), kind=kLoop, calls=%fused_computation.98 | loop fusion | flops 131072 | bytes 1048576 | tf_op jit(solution)/shard_map/transpose | solution.py:165
  4.1 10.0 %all-to-all-start = ((f32[16,16,512]{2,1,0:T(8,128)}), f32[16,16,512]{2,1,0:T(8,128)S(1)}, u32[]{:S(2)}, u32[]{:S(2)}) async-start(f32[16,16,512]{2,1,0:T(8,128)} %maximum_bitcast_fusion), calls=%async_computation | async-start | bytes 1048576 | tf_op jit(solution)/shard_map/all_to_all | solution.py:166
  14.1 0.0 copy-done.5
  14.1 0.7 %and_select_fusion.1 = (s32[1,4096]{1,0:T(1,128)}, s32[1,4096]{1,0:T(1,128)S(1)}) fusion(s32[1,4096]{1,0:T(1,128)S(1)} %copy-done.5), kind=kLoop, calls=%fused_computation.115 | loop fusion | flops 45056 | bytes 49152 | tf_op jit(solution)/shard_map/jit(remainder)/select_n | solution.py:168
  14.8 0.7 %and_select_fusion.2.rows_ref = s32[1,4096]{1,0:T(1,128)} fusion(s32[1,4096]{1,0:T(1,128)S(1)} %get-tuple-element.6, s32[1,4096]{1,0:T(1,128)S(1)} %copy-done.5), kind=kLoop, calls=%fused_computation.116 | loop fusion | flops 49152 | bytes 49152 | tf_op jit(solution)/shard_map/jit(floor_divide)/jit(_where)/select_n | solution.py:167
  15.4 0.0 copy-done.6
  15.4 0.6 fusion.82
  16.1 6.6 %shard_map.82.seen_ref = f32[16,4096]{1,0:T(8,128)} custom-call(f32[512,256]{1,0:T(8,128)} %bitcast.38, s32[1,4096]{1,0:T(1,128)} %and_select_fusion.2.rows_ref, s32[1,4096]{1,0:T(1,128)} %get-tuple-element.5.cols_ref), custom_call_target="tpu_custom_call" | custom-call | flops 3221225472 | bytes 819200 | tf_op jit(solution)/shard_map/pallas_call | solution.py:113
  22.7 0.0 copy-done
  22.7 0.1 broadcast_bitcast_fusion
  22.8 0.6 compare_select_fusion.usable_ref
  23.4 8.0 %all-to-all-done.held_ref = f32[16,16,512]{2,1,0:T(8,128)S(1)} async-done(((f32[16,16,512]{2,1,0:T(8,128)}), f32[16,16,512]{2,1,0:T(8,128)S(1)}, u32[]{:S(2)}, u32[]{:S(2)}) %all-to-all-start) | async-done | bytes 524320 | tf_op jit(solution)/shard_map/all_to_all | solution.py:166
  31.5 0.8 %copy-done.2 = f32[16,16,512]{2,1,0:T(8,128)} copy-done((f32[16,16,512]{2,1,0:T(8,128)}, f32[16,16,512]{2,1,0:T(8,128)S(1)}, u32[]{:S(2)}) %copy-start.2) | copy-done | bytes 524312
  32.2 6.2 %shard_map.83 = f32[16,32,256]{2,1,0:T(8,128)} custom-call(f32[16,16,512]{2,1,0:T(8,128)} %copy-done.2, f32[16,4096]{1,0:T(8,128)} %shard_map.82.seen_ref, f32[1,4096]{1,0:T(1,128)} %compare_select_fusion.usable_ref, s32[1,4096]{1,0:T(1,128)} %and_select_fusion.2.rows_ref, s32[1,4096]{1,0:T(1,128)} %get-tuple-element.5.cols_ref, ...), custom_call_target="tpu_custom_call" | custom-call | flops 3221225472 | bytes 1359872 | tf_op jit(solution)/shard_map/pallas_call | solution.py:95
  38.4 0.0 copy-done.3
  38.4 0.0 copy-done.4
  38.4 1.0 %pad_maximum_fusion.5 = (f32[19,8,256]{2,1,0:T(8,128)S(1)}, f32[19,8,256]{2,1,0:T(8,128)S(1)}) fusion(f32[1,32,256]{2,1,0:T(8,128)S(1)} %bitcast.31, f32[1,32,256]{2,1,0:T(8,128)S(1)} %bitcast.34, f32[1,32,256]{2,1,0:T(8,128)S(1)} %get-tuple-element.44, f32[16,32,256]{2,1,0:T(8,128)} %shard_map.83), kind=kLoop, calls=%fused_computation.104 | loop fusion | flops 233472 | bytes 933888 | tf_op jit(solution)/shard_map/slice | solution.py:122
  39.5 1.4 %collective-permute-start = (f32[19,8,256]{2,1,0:T(8,128)S(1)}, f32[19,8,256]{2,1,0:T(8,128)S(1)}, u32[]{:S(2)}, u32[]{:S(2)}) collective-permute-start(f32[19,8,256]{2,1,0:T(8,128)S(1)} %get-tuple-element.9), channel_id=1, source_target_pairs={{0,1},{1,2},{2,3},{3,4},{4,5},{5,6},{6,7},{7,8},{8,9},{9,10},{10,1... | collective-permute-start | bytes 466952 | tf_op jit(solution)/shard_map/ppermute | solution.py:129
  40.8 3.9 %collective-permute-start.1 = (f32[19,8,256]{2,1,0:T(8,128)S(1)}, f32[19,8,256]{2,1,0:T(8,128)S(1)}, u32[]{:S(2)}, u32[]{:S(2)}) collective-permute-start(f32[19,8,256]{2,1,0:T(8,128)S(1)} %get-tuple-element.10), channel_id=1, source_target_pairs={{1,0},{2,1},{3,2},{4,3},{5,4},{6,5},{7,6},{8,7},{9,8},{10,9},{11,1... | collective-permute-start | bytes 466952 | tf_op jit(solution)/shard_map/ppermute | solution.py:130
  44.7 3.2 %collective-permute-done = f32[19,8,256]{2,1,0:T(8,128)S(1)} collective-permute-done((f32[19,8,256]{2,1,0:T(8,128)S(1)}, f32[19,8,256]{2,1,0:T(8,128)S(1)}, u32[]{:S(2)}, u32[]{:S(2)}) %collective-permute-start) | collective-permute-done | bytes 155680 | tf_op jit(solution)/shard_map/ppermute | solution.py:129
  47.9 0.0 collective-permute-done.1
  47.9 0.1 pad_maximum_fusion.1
  48.0 0.2 fusion.65
  48.2 0.2 reshape.107
  48.4 0.0 collective-permute-start.2
  48.4 0.2 reshape.109
  48.6 0.5 collective-permute-start.3
  49.2 0.5 collective-permute-done.2
  49.6 0.3 reshape.108
  49.9 2.4 %collective-permute-done.3 = f32[57,128]{1,0:T(8,128)S(1)} collective-permute-done((f32[57,128]{1,0:T(8,128)S(1)}, f32[57,128]{1,0:T(8,128)S(1)}, u32[]{:S(2)}, u32[]{:S(2)}) %collective-permute-start.3) | collective-permute-done | bytes 29216 | tf_op jit(solution)/shard_map/ppermute | solution.py:127
  52.3 0.3 reshape.110
  52.6 0.6 pad_maximum_fusion
  53.1 0.1 fusion.64
  53.2 0.1 slice_multiply_fusion.2
  53.3 0.1 fusion.80
  53.4 0.1 fusion.78
  53.5 0.1 fusion.81
  53.6 0.1 fusion.79
  53.7 0.1 fusion.76
  53.9 0.1 fusion.77
  54.0 0.1 fusion.74
  54.1 0.1 fusion.75
  54.2 0.1 fusion.72
  54.3 0.1 fusion.73
  54.4 0.1 fusion.70
  54.5 0.1 fusion.71
  54.6 0.1 fusion.68
  54.7 0.1 fusion.69
  54.8 0.1 fusion.66
  54.9 0.1 fusion.67
  54.9 1.3 %fusion.17 = f32[16,46,270]{2,1,0:T(8,128)S(1)} fusion(f32[19,48,272]{2,1,0:T(8,128)S(1)} %pad_maximum_fusion, f32[46,270]{1,0:T(8,128)S(1)} %get-tuple-element.42, f32[46,270]{1,0:T(8,128)S(1)} %get-tuple-element.41, f32[46,270]{1,0:T(8,128)S(1)} %get-tuple-element.40, f32[46,270]{1,0:T(8,128)S(1)} %get-tuple-element.39), kind=kLoop, calls=%fused_computation.27 | loop fusion | flops 2384640 | bytes 4968000 | tf_op jit(solution)/shard_map/sub | solution.py:145
  56.3 1.3 %fusion.9 = f32[16,44,268]{2,1,0:T(8,128)S(1)} fusion(f32[16,46,270]{2,1,0:T(8,128)S(1)} %fusion.17, f32[44,268]{1,0:T(8,128)S(1)} %get-tuple-element.38, f32[44,268]{1,0:T(8,128)S(1)} %get-tuple-element.37, f32[44,268]{1,0:T(8,128)S(1)} %get-tuple-element.36, f32[44,268]{1,0:T(8,128)S(1)} %get-tuple-element.35), kind=kLoop, calls=%fused_computation.15 | loop fusion | flops 2264064 | bytes 4716800 | tf_op jit(solution)/shard_map/sub | solution.py:145
  57.6 1.3 %fusion.1 = f32[16,42,266]{2,1,0:T(8,128)S(1)} fusion(f32[16,44,268]{2,1,0:T(8,128)S(1)} %fusion.9, f32[42,266]{1,0:T(8,128)S(1)} %get-tuple-element.34, f32[42,266]{1,0:T(8,128)S(1)} %get-tuple-element.33, f32[42,266]{1,0:T(8,128)S(1)} %get-tuple-element.32, f32[42,266]{1,0:T(8,128)S(1)} %get-tuple-element.31), kind=kLoop, calls=%fused_computation.3 | loop fusion | flops 2145024 | bytes 4468800 | tf_op jit(solution)/shard_map/sub | solution.py:145
  58.9 1.1 %fusion.49 = f32[16,40,264]{2,1,0:T(8,128)S(1)} fusion(f32[16,42,266]{2,1,0:T(8,128)S(1)} %fusion.1, f32[40,264]{1,0:T(8,128)S(1)} %get-tuple-element.30, f32[40,264]{1,0:T(8,128)S(1)} %get-tuple-element.29, f32[40,264]{1,0:T(8,128)S(1)} %get-tuple-element.28, f32[40,264]{1,0:T(8,128)S(1)} %get-tuple-element.27), kind=kLoop, calls=%fused_computation.75 | loop fusion | flops 2027520 | bytes 4224000 | tf_op jit(solution)/shard_map/sub | solution.py:145
  60.0 1.1 %fusion.41 = f32[16,38,262]{2,1,0:T(8,128)S(1)} fusion(f32[16,40,264]{2,1,0:T(8,128)S(1)} %fusion.49, f32[38,262]{1,0:T(8,128)S(1)} %get-tuple-element.26, f32[38,262]{1,0:T(8,128)S(1)} %get-tuple-element.25, f32[38,262]{1,0:T(8,128)S(1)} %get-tuple-element.24, f32[38,262]{1,0:T(8,128)S(1)} %get-tuple-element.23), kind=kLoop, calls=%fused_computation.63 | loop fusion | flops 1911552 | bytes 3982400 | tf_op jit(solution)/shard_map/sub | solution.py:145
  61.1 1.1 %fusion.33 = f32[16,36,260]{2,1,0:T(8,128)S(1)} fusion(f32[16,38,262]{2,1,0:T(8,128)S(1)} %fusion.41, f32[36,260]{1,0:T(8,128)S(1)} %get-tuple-element.22, f32[36,260]{1,0:T(8,128)S(1)} %get-tuple-element.21, f32[36,260]{1,0:T(8,128)S(1)} %get-tuple-element.20, f32[36,260]{1,0:T(8,128)S(1)} %get-tuple-element.19), kind=kLoop, calls=%fused_computation.51 | loop fusion | flops 1797120 | bytes 3744000 | tf_op jit(solution)/shard_map/sub | solution.py:145
  62.2 1.1 %fusion.25 = f32[16,34,258]{2,1,0:T(8,128)S(1)} fusion(f32[16,36,260]{2,1,0:T(8,128)S(1)} %fusion.33, f32[34,258]{1,0:T(8,128)S(1)} %get-tuple-element.18, f32[34,258]{1,0:T(8,128)S(1)} %get-tuple-element.17, f32[34,258]{1,0:T(8,128)S(1)} %get-tuple-element.16, f32[34,258]{1,0:T(8,128)S(1)} %get-tuple-element.15), kind=kLoop, calls=%fused_computation.39 | loop fusion | flops 1684224 | bytes 3508800 | tf_op jit(solution)/shard_map/sub | solution.py:145
  63.3 1.4 %fusion.57 = f32[16,32,256]{2,1,0:T(8,128)} fusion(f32[16,34,258]{2,1,0:T(8,128)S(1)} %fusion.25, f32[32,256]{1,0:T(8,128)S(1)} %get-tuple-element.14, f32[32,256]{1,0:T(8,128)S(1)} %get-tuple-element.13, f32[32,256]{1,0:T(8,128)S(1)} %get-tuple-element.12, f32[32,256]{1,0:T(8,128)S(1)} %get-tuple-element.11), kind=kLoop, calls=%fused_computation.88 | loop fusion | flops 1572864 | bytes 3276800 | tf_op jit(solution)/shard_map/sub | solution.py:145
  (9 shorter events, 0.1 us)
Async XLA Ops:
  0.0 22.7 %copy-start = (s32[1,16]{1,0:T(1,128)S(1)}, s32[1,16]{1,0:T(1,128)}, u32[]{:S(2)}) copy-start(s32[1,16]{1,0:T(1,128)} %param.13) | copy-start | bytes 196
  3.3 10.9 %copy-start.5 = (s32[1,4096]{1,0:T(1,128)S(1)}, s32[1,4096]{1,0:T(1,128)}, u32[]{:S(2)}) copy-start(s32[1,4096]{1,0:T(1,128)} %param.12) | copy-start | bytes 49156
  3.3 12.2 %copy-start.6 = (s32[32,256]{1,0:T(8,128)S(1)}, s32[32,256]{1,0:T(8,128)}, u32[]{:S(2)}) copy-start(s32[32,256]{1,0:T(8,128)} %param.11) | copy-start | bytes 98308
  4.1 27.3 %all-to-all-start = ((f32[16,16,512]{2,1,0:T(8,128)}), f32[16,16,512]{2,1,0:T(8,128)S(1)}, u32[]{:S(2)}, u32[]{:S(2)}) async-start(f32[16,16,512]{2,1,0:T(8,128)} %maximum_bitcast_fusion), calls=%async_computation | async-start | bytes 1048576 | tf_op jit(solution)/shard_map/all_to_all | solution.py:166
  31.4 0.8 %copy-start.2 = (f32[16,16,512]{2,1,0:T(8,128)}, f32[16,16,512]{2,1,0:T(8,128)S(1)}, u32[]{:S(2)}) copy-start(f32[16,16,512]{2,1,0:T(8,128)S(1)} %all-to-all-done.held_ref) | copy-start | bytes 1572868
  32.2 6.2 %copy-start.3 = (f32[32,256]{1,0:T(8,128)S(1)}, f32[32,256]{1,0:T(8,128)}, u32[]{:S(2)}) copy-start(f32[32,256]{1,0:T(8,128)} %param.10) | copy-start | bytes 98308
  32.2 6.2 %copy-start.4 = (f32[32,256]{1,0:T(8,128)S(1)}, f32[32,256]{1,0:T(8,128)}, u32[]{:S(2)}) copy-start(f32[32,256]{1,0:T(8,128)} %param.9) | copy-start | bytes 98308
  38.4 9.5 %copy-start.1 = (f32[16,32,256]{2,1,0:T(8,128)S(1)}, f32[16,32,256]{2,1,0:T(8,128)}, u32[]{:S(2)}) copy-start(f32[16,32,256]{2,1,0:T(8,128)} %shard_map.83) | copy-start | bytes 1572868
  39.5 8.4 %collective-permute-start = (f32[19,8,256]{2,1,0:T(8,128)S(1)}, f32[19,8,256]{2,1,0:T(8,128)S(1)}, u32[]{:S(2)}, u32[]{:S(2)}) collective-permute-start(f32[19,8,256]{2,1,0:T(8,128)S(1)} %get-tuple-element.9), channel_id=1, source_target_pairs={{0,1},{1,2},{2,3},{3,4},{4,5},{5,6},{6,7},{7,8},{8,9},{9,10},{10,1... | collective-permute-start | bytes 466952 | tf_op jit(solution)/shard_map/ppermute | solution.py:129
  40.8 7.1 %collective-permute-start.1 = (f32[19,8,256]{2,1,0:T(8,128)S(1)}, f32[19,8,256]{2,1,0:T(8,128)S(1)}, u32[]{:S(2)}, u32[]{:S(2)}) collective-permute-start(f32[19,8,256]{2,1,0:T(8,128)S(1)} %get-tuple-element.10), channel_id=1, source_target_pairs={{1,0},{2,1},{3,2},{4,3},{5,4},{6,5},{7,6},{8,7},{9,8},{10,9},{11,1... | collective-permute-start | bytes 466952 | tf_op jit(solution)/shard_map/ppermute | solution.py:130
  48.4 1.2 %collective-permute-start.2 = (f32[57,128]{1,0:T(8,128)S(1)}, f32[57,128]{1,0:T(8,128)S(1)}, u32[]{:S(2)}, u32[]{:S(2)}) collective-permute-start(f32[57,128]{1,0:T(8,128)S(1)} %reshape.107), channel_id=1, source_target_pairs={{0,16},{16,32},{32,48},{48,64},{64,80},{80,96},{96,112},{112,128},... | collective-permute-start | bytes 87560 | tf_op jit(solution)/shard_map/ppermute | solution.py:126
  48.6 3.6 %collective-permute-start.3 = (f32[57,128]{1,0:T(8,128)S(1)}, f32[57,128]{1,0:T(8,128)S(1)}, u32[]{:S(2)}, u32[]{:S(2)}) collective-permute-start(f32[57,128]{1,0:T(8,128)S(1)} %reshape.109), channel_id=1, source_target_pairs={{16,0},{32,16},{48,32},{64,48},{80,64},{96,80},{112,96},{128,112},... | collective-permute-start | bytes 87560 | tf_op jit(solution)/shard_map/ppermute | solution.py:127

commit v16 on v15

--- a/solution.py
+++ b/solution.py
@@ -113,14 +113,20 @@
     return vmem_call(gather_kernel, shape, flops, 4 * (levels * slots + 2 * slots + cells * cols_here))(state2d, rows, cols)
 
 
-def with_halo(block, sides, width):
+def with_halo(planes, sides, width):
+    block = None
     for axis, dim in sides:
         count = lax.axis_size(axis)
         forward = [(i, i + 1) for i in range(count - 1)]
         forward.append((count - 1, 0))
         backward = [(target, source) for source, target in forward]
-        low = lax.slice_in_dim(block, block.shape[dim] - width, None, axis=dim)
-        high = lax.slice_in_dim(block, 0, width, axis=dim)
+        if block is None:
+            low = jnp.concatenate([lax.slice_in_dim(p, p.shape[dim] - width, None, axis=dim) for p in planes])
+            high = jnp.concatenate([lax.slice_in_dim(p, 0, width, axis=dim) for p in planes])
+            block = jnp.concatenate(planes)
+        else:
+            low = lax.slice_in_dim(block, block.shape[dim] - width, None, axis=dim)
+            high = lax.slice_in_dim(block, 0, width, axis=dim)
         if dim == block.ndim - 1:
             flat = (-1, 128) if low.size % 128 == 0 else block.shape[:-2] + (-1,)
             low = lax.ppermute(low.reshape(flat), axis, forward).reshape(low.shape)
@@ -170,8 +176,7 @@
     sea = land_sea.astype(jnp.float32)
     gradient = onehot_scatter(at_owner, at_column, usable[None, :], target_rows, target_cols, sea)
     rim_width = PASSES
-    stacked = jnp.concatenate([gradient, sea[None], coef_lon[None], coef_lat[None]], axis=0)
-    padded = with_halo(stacked, (("lat", 1), ("lon", 2)), rim_width)
+    padded = with_halo([gradient, sea[None], coef_lon[None], coef_lat[None]], (("lat", 1), ("lon", 2)), rim_width)
     field = padded[:levels]
     padded = padded[levels:]
     lat_index = lax.axis_index("lat")

time: 65 us -> 65.2 us (level)
  local copies, waits for them, and re-layouts: 3.67 us -> 4.72 us
  other arithmetic: 18.2 us -> 17.2 us
    slice x0 -> x3, local copies, waits for them, and re-layouts: none -> 1.05 us  [with_halo(): lax.slice_in_dim(p, p.shape[dim] - width, None, axis=dim)]
    slice x1 -> x0, other arithmetic: 1.05 us -> none  [with_halo(): low = lax.slice_in_dim(block, block.shape[dim] - width, None, axis=dim)]
  transfers between devices with their start and end apart: 5 -> 5, of which waited for: 4 -> 5; matrix products, arithmetic and copies ran while one was open for 5% -> 5% of each run, Pallas kernels for 10% -> 10%
where the time goes in v16:
time: 65.2 us; the launch traced here: 64.9 us
  other arithmetic  17.2 us (26%)
  starting transfers between devices  15.8 us (24%)
  waiting for transfers between devices  14.1 us (22%)
  Pallas kernels  12.8 us (20%)
  local copies, waits for them, and re-layouts  4.72 us (7%)
    all_to_all x1, starting transfers between devices, body(): lax.all_to_all(held, 'lon', split_axis=0, concat_axis=0, tiled=True)  9.98 us
    sub x8, other arithmetic, one_pass(): centre + east_here * (field[:, 1:-1, 2:] - centre)  9.72 us
    all_to_all x1, waiting for transfers between devices, body(): lax.all_to_all(held, 'lon', split_axis=0, concat_axis=0, tiled=True)  8 us
    pallas_call x1, Pallas kernels, onehot_gather(): vmem_call(gather_kernel, shape, flops, 4 * (levels * slots + 2 * slots +...  6.66 us
    pallas_call x1, Pallas kernels, onehot_scatter(): pl.pallas_call(scatter_kernel, out_shape=shape, in_specs=[pl.BlockSpec(me...  6.15 us
    ppermute x1, starting transfers between devices, with_halo(): high = lax.ppermute(high, axis, backward)  3.93 us
    unnamed x2, other arithmetic  3.19 us
    ppermute x1, waiting for transfers between devices, with_halo(): low = lax.ppermute(low, axis, forward)  3.1 us
  transfers between devices with their start and end apart: 5, of which 5 were waited for; matrix products, arithmetic and copies ran while one was open for 5% of the time, Pallas kernels for 10%

profile of v16, /device:TPU:1, one launch (start us, length us, event | category | flops | bytes accessed | tf_op | source)
XLA Modules:
  0.0 64.9 jit_solution(10096276259154167611)
XLA Ops:
  0.0 0.0 copy-start
  0.0 1.6 %reduce.1 = f32[16,4096]{1,0:T(8,128)S(1)} reduce(f32[16,1,4096]{2,1,0:T(1,128)} %param.15, f32[]{:T(128)} %constant.52), dimensions={1}, to_apply=%param.15.reduce_sub_computation | reduce | bytes 524292 | tf_op args[7]
  1.6 1.6 %reduce = f32[16,4096]{1,0:T(8,128)S(1)} reduce(f32[16,1,4096]{2,1,0:T(1,128)} %param.14, f32[]{:T(128)} %constant.52), dimensions={1}, to_apply=%param.14.reduce_sub_computation | reduce | bytes 524292 | tf_op args[6]
  3.2 0.1 copy_bitcast_fusion
  3.3 0.0 copy-start.5
  3.3 0.0 copy-start.6
  3.3 0.0 copy-start.3
  3.3 0.0 copy-start.4
  3.3 0.9 %maximum_bitcast_fusion = f32[16,16,512]{2,1,0:T(8,128)} fusion(f32[16,16,256]{2,0,1:T(8,128)S(1)} %get-tuple-element.51, f32[16,16,256]{2,0,1:T(8,128)S(1)} %get-tuple-element.52), kind=kLoop, calls=%fused_computation.98 | loop fusion | flops 131072 | bytes 1048576 | tf_op jit(solution)/shard_map/transpose | solution.py:171
  4.2 10.0 %all-to-all-start = ((f32[16,16,512]{2,1,0:T(8,128)}), f32[16,16,512]{2,1,0:T(8,128)S(1)}, u32[]{:S(2)}, u32[]{:S(2)}) async-start(f32[16,16,512]{2,1,0:T(8,128)} %maximum_bitcast_fusion), calls=%async_computation | async-start | bytes 1048576 | tf_op jit(solution)/shard_map/all_to_all | solution.py:172
  14.1 0.0 copy-done.5
  14.2 0.7 %and_select_fusion.1 = (s32[1,4096]{1,0:T(1,128)}, s32[1,4096]{1,0:T(1,128)S(1)}) fusion(s32[1,4096]{1,0:T(1,128)S(1)} %copy-done.5), kind=kLoop, calls=%fused_computation.113 | loop fusion | flops 45056 | bytes 49152 | tf_op jit(solution)/shard_map/jit(remainder)/select_n | solution.py:174
  14.8 0.7 %and_select_fusion.2.rows_ref = s32[1,4096]{1,0:T(1,128)} fusion(s32[1,4096]{1,0:T(1,128)S(1)} %get-tuple-element.6, s32[1,4096]{1,0:T(1,128)S(1)} %copy-done.5), kind=kLoop, calls=%fused_computation.114 | loop fusion | flops 49152 | bytes 49152 | tf_op jit(solution)/shard_map/jit(floor_divide)/jit(_where)/select_n | solution.py:173
  15.5 0.0 copy-done.6
  15.5 0.6 fusion.86
  16.1 0.0 copy-done.3
  16.1 6.7 %shard_map.82.seen_ref = f32[16,4096]{1,0:T(8,128)} custom-call(f32[512,256]{1,0:T(8,128)} %bitcast.38, s32[1,4096]{1,0:T(1,128)} %and_select_fusion.2.rows_ref, s32[1,4096]{1,0:T(1,128)} %get-tuple-element.5.cols_ref), custom_call_target="tpu_custom_call" | custom-call | flops 3221225472 | bytes 819200 | tf_op jit(solution)/shard_map/pallas_call | solution.py:113
  22.8 0.1 broadcast_bitcast_fusion
  22.8 0.6 compare_select_fusion.usable_ref
  23.5 8.0 %all-to-all-done.held_ref = f32[16,16,512]{2,1,0:T(8,128)S(1)} async-done(((f32[16,16,512]{2,1,0:T(8,128)}), f32[16,16,512]{2,1,0:T(8,128)S(1)}, u32[]{:S(2)}, u32[]{:S(2)}) %all-to-all-start) | async-done | bytes 524320 | tf_op jit(solution)/shard_map/all_to_all | solution.py:172
  31.5 0.8 %copy-done.2 = f32[16,16,512]{2,1,0:T(8,128)} copy-done((f32[16,16,512]{2,1,0:T(8,128)}, f32[16,16,512]{2,1,0:T(8,128)S(1)}, u32[]{:S(2)}) %copy-start.2) | copy-done | bytes 524312
  32.3 6.2 %shard_map.83 = f32[16,32,256]{2,1,0:T(8,128)} custom-call(f32[16,16,512]{2,1,0:T(8,128)} %copy-done.2, f32[16,4096]{1,0:T(8,128)} %shard_map.82.seen_ref, f32[1,4096]{1,0:T(1,128)} %compare_select_fusion.usable_ref, s32[1,4096]{1,0:T(1,128)} %and_select_fusion.2.rows_ref, s32[1,4096]{1,0:T(1,128)} %get-tuple-element.5.cols_ref, ...), custom_call_target="tpu_custom_call" | custom-call | flops 3221225472 | bytes 1359872 | tf_op jit(solution)/shard_map/pallas_call | solution.py:95
  38.4 1.0 %fusion.66 = (f32[16,8,256]{2,1,0:T(8,128)S(1)}, f32[16,8,256]{2,1,0:T(8,128)S(1)}) fusion(f32[16,32,256]{2,1,0:T(8,128)} %shard_map.83), kind=kLoop, calls=%fused_computation.122 | loop fusion | bytes 524288 | tf_op jit(solution)/shard_map/slice | solution.py:124
  39.5 1.4 %collective-permute-start = (f32[19,8,256]{2,1,0:T(8,128)S(1)}, f32[19,8,256]{2,1,0:T(8,128)S(1)}, u32[]{:S(2)}, u32[]{:S(2)}) collective-permute-start(f32[19,8,256]{2,1,0:T(8,128)S(1)} %pad_maximum_fusion.2), channel_id=1, source_target_pairs={{0,1},{1,2},{2,3},{3,4},{4,5},{5,6},{6,7},{7,8},{8,9},{9,10},{10,1... | collective-permute-start | bytes 466952 | tf_op jit(solution)/shard_map/ppermute | solution.py:135
  40.9 3.9 %collective-permute-start.1 = (f32[19,8,256]{2,1,0:T(8,128)S(1)}, f32[19,8,256]{2,1,0:T(8,128)S(1)}, u32[]{:S(2)}, u32[]{:S(2)}) collective-permute-start(f32[19,8,256]{2,1,0:T(8,128)S(1)} %pad_maximum_fusion.3), channel_id=1, source_target_pairs={{1,0},{2,1},{3,2},{4,3},{5,4},{6,5},{7,6},{8,7},{9,8},{10,9},{11,1... | collective-permute-start | bytes 466952 | tf_op jit(solution)/shard_map/ppermute | solution.py:136
  44.8 3.1 %collective-permute-done = f32[19,8,256]{2,1,0:T(8,128)S(1)} collective-permute-done((f32[19,8,256]{2,1,0:T(8,128)S(1)}, f32[19,8,256]{2,1,0:T(8,128)S(1)}, u32[]{:S(2)}, u32[]{:S(2)}) %collective-permute-start) | collective-permute-done | bytes 155680 | tf_op jit(solution)/shard_map/ppermute | solution.py:135
  47.9 0.1 collective-permute-done.1
  48.0 0.1 pad_maximum_fusion.1
  48.1 0.2 fusion.65
  48.3 0.2 reshape.107
  48.5 0.0 collective-permute-start.2
  48.6 0.2 reshape.109
  48.8 0.5 collective-permute-start.3
  49.3 0.5 collective-permute-done.2
  49.8 0.3 reshape.108
  50.0 2.4 %collective-permute-done.3 = f32[57,128]{1,0:T(8,128)S(1)} collective-permute-done((f32[57,128]{1,0:T(8,128)S(1)}, f32[57,128]{1,0:T(8,128)S(1)}, u32[]{:S(2)}, u32[]{:S(2)}) %collective-permute-start.3) | collective-permute-done | bytes 29216 | tf_op jit(solution)/shard_map/ppermute | solution.py:133
  52.4 0.3 reshape.110
  52.7 0.6 pad_maximum_fusion
  53.3 0.1 fusion.64
  53.4 0.1 slice_multiply_fusion.2
  53.5 0.1 fusion.81
  53.6 0.1 fusion.79
  53.7 0.1 fusion.82
  53.8 0.1 fusion.80
  53.9 0.1 fusion.77
  54.0 0.1 fusion.78
  54.1 0.1 fusion.75
  54.2 0.1 fusion.76
  54.3 0.1 fusion.73
  54.4 0.1 fusion.74
  54.5 0.1 fusion.71
  54.6 0.1 fusion.72
  54.7 0.1 fusion.69
  54.8 0.1 fusion.70
  54.9 0.1 fusion.67
  55.0 0.1 fusion.68
  55.1 1.3 %fusion.17 = f32[16,46,270]{2,1,0:T(8,128)S(1)} fusion(f32[19,48,272]{2,1,0:T(8,128)S(1)} %pad_maximum_fusion, f32[46,270]{1,0:T(8,128)S(1)} %get-tuple-element.42, f32[46,270]{1,0:T(8,128)S(1)} %get-tuple-element.41, f32[46,270]{1,0:T(8,128)S(1)} %get-tuple-element.40, f32[46,270]{1,0:T(8,128)S(1)} %get-tuple-element.39), kind=kLoop, calls=%fused_computation.27 | loop fusion | flops 2384640 | bytes 4968000 | tf_op jit(solution)/shard_map/sub | solution.py:151
  56.4 1.3 %fusion.9 = f32[16,44,268]{2,1,0:T(8,128)S(1)} fusion(f32[16,46,270]{2,1,0:T(8,128)S(1)} %fusion.17, f32[44,268]{1,0:T(8,128)S(1)} %get-tuple-element.38, f32[44,268]{1,0:T(8,128)S(1)} %get-tuple-element.37, f32[44,268]{1,0:T(8,128)S(1)} %get-tuple-element.36, f32[44,268]{1,0:T(8,128)S(1)} %get-tuple-element.35), kind=kLoop, calls=%fused_computation.15 | loop fusion | flops 2264064 | bytes 4716800 | tf_op jit(solution)/shard_map/sub | solution.py:151
  57.7 1.3 %fusion.1 = f32[16,42,266]{2,1,0:T(8,128)S(1)} fusion(f32[16,44,268]{2,1,0:T(8,128)S(1)} %fusion.9, f32[42,266]{1,0:T(8,128)S(1)} %get-tuple-element.34, f32[42,266]{1,0:T(8,128)S(1)} %get-tuple-element.33, f32[42,266]{1,0:T(8,128)S(1)} %get-tuple-element.32, f32[42,266]{1,0:T(8,128)S(1)} %get-tuple-element.31), kind=kLoop, calls=%fused_computation.3 | loop fusion | flops 2145024 | bytes 4468800 | tf_op jit(solution)/shard_map/sub | solution.py:151
  59.0 1.1 %fusion.49 = f32[16,40,264]{2,1,0:T(8,128)S(1)} fusion(f32[16,42,266]{2,1,0:T(8,128)S(1)} %fusion.1, f32[40,264]{1,0:T(8,128)S(1)} %get-tuple-element.30, f32[40,264]{1,0:T(8,128)S(1)} %get-tuple-element.29, f32[40,264]{1,0:T(8,128)S(1)} %get-tuple-element.28, f32[40,264]{1,0:T(8,128)S(1)} %get-tuple-element.27), kind=kLoop, calls=%fused_computation.75 | loop fusion | flops 2027520 | bytes 4224000 | tf_op jit(solution)/shard_map/sub | solution.py:151
  60.1 1.1 %fusion.41 = f32[16,38,262]{2,1,0:T(8,128)S(1)} fusion(f32[16,40,264]{2,1,0:T(8,128)S(1)} %fusion.49, f32[38,262]{1,0:T(8,128)S(1)} %get-tuple-element.26, f32[38,262]{1,0:T(8,128)S(1)} %get-tuple-element.25, f32[38,262]{1,0:T(8,128)S(1)} %get-tuple-element.24, f32[38,262]{1,0:T(8,128)S(1)} %get-tuple-element.23), kind=kLoop, calls=%fused_computation.63 | loop fusion | flops 1911552 | bytes 3982400 | tf_op jit(solution)/shard_map/sub | solution.py:151
  61.2 1.1 %fusion.33 = f32[16,36,260]{2,1,0:T(8,128)S(1)} fusion(f32[16,38,262]{2,1,0:T(8,128)S(1)} %fusion.41, f32[36,260]{1,0:T(8,128)S(1)} %get-tuple-element.22, f32[36,260]{1,0:T(8,128)S(1)} %get-tuple-element.21, f32[36,260]{1,0:T(8,128)S(1)} %get-tuple-element.20, f32[36,260]{1,0:T(8,128)S(1)} %get-tuple-element.19), kind=kLoop, calls=%fused_computation.51 | loop fusion | flops 1797120 | bytes 3744000 | tf_op jit(solution)/shard_map/sub | solution.py:151
  62.3 1.1 %fusion.25 = f32[16,34,258]{2,1,0:T(8,128)S(1)} fusion(f32[16,36,260]{2,1,0:T(8,128)S(1)} %fusion.33, f32[34,258]{1,0:T(8,128)S(1)} %get-tuple-element.18, f32[34,258]{1,0:T(8,128)S(1)} %get-tuple-element.17, f32[34,258]{1,0:T(8,128)S(1)} %get-tuple-element.16, f32[34,258]{1,0:T(8,128)S(1)} %get-tuple-element.15), kind=kLoop, calls=%fused_computation.39 | loop fusion | flops 1684224 | bytes 3508800 | tf_op jit(solution)/shard_map/sub | solution.py:151
  63.4 1.4 %fusion.57 = f32[16,32,256]{2,1,0:T(8,128)} fusion(f32[16,34,258]{2,1,0:T(8,128)S(1)} %fusion.25, f32[32,256]{1,0:T(8,128)S(1)} %get-tuple-element.14, f32[32,256]{1,0:T(8,128)S(1)} %get-tuple-element.13, f32[32,256]{1,0:T(8,128)S(1)} %get-tuple-element.12, f32[32,256]{1,0:T(8,128)S(1)} %get-tuple-element.11), kind=kLoop, calls=%fused_computation.88 | loop fusion | flops 1572864 | bytes 3276800 | tf_op jit(solution)/shard_map/sub | solution.py:151
  (13 shorter events, 0.1 us)
Async XLA Ops:
  0.0 22.8 %copy-start = (s32[1,16]{1,0:T(1,128)S(1)}, s32[1,16]{1,0:T(1,128)}, u32[]{:S(2)}) copy-start(s32[1,16]{1,0:T(1,128)} %param.13) | copy-start | bytes 196
  3.3 10.9 %copy-start.5 = (s32[1,4096]{1,0:T(1,128)S(1)}, s32[1,4096]{1,0:T(1,128)}, u32[]{:S(2)}) copy-start(s32[1,4096]{1,0:T(1,128)} %param.12) | copy-start | bytes 49156
  3.3 12.2 %copy-start.6 = (s32[32,256]{1,0:T(8,128)S(1)}, s32[32,256]{1,0:T(8,128)}, u32[]{:S(2)}) copy-start(s32[32,256]{1,0:T(8,128)} %param.11) | copy-start | bytes 98308
  3.3 12.8 %copy-start.3 = (f32[32,256]{1,0:T(8,128)S(1)}, f32[32,256]{1,0:T(8,128)}, u32[]{:S(2)}) copy-start(f32[32,256]{1,0:T(8,128)} %param.10) | copy-start | bytes 98308
  3.3 12.8 %copy-start.4 = (f32[32,256]{1,0:T(8,128)S(1)}, f32[32,256]{1,0:T(8,128)}, u32[]{:S(2)}) copy-start(f32[32,256]{1,0:T(8,128)} %param.9) | copy-start | bytes 98308
  4.2 27.3 %all-to-all-start = ((f32[16,16,512]{2,1,0:T(8,128)}), f32[16,16,512]{2,1,0:T(8,128)S(1)}, u32[]{:S(2)}, u32[]{:S(2)}) async-start(f32[16,16,512]{2,1,0:T(8,128)} %maximum_bitcast_fusion), calls=%async_computation | async-start | bytes 1048576 | tf_op jit(solution)/shard_map/all_to_all | solution.py:172
  31.5 0.8 %copy-start.2 = (f32[16,16,512]{2,1,0:T(8,128)}, f32[16,16,512]{2,1,0:T(8,128)S(1)}, u32[]{:S(2)}) copy-start(f32[16,16,512]{2,1,0:T(8,128)S(1)} %all-to-all-done.held_ref) | copy-start | bytes 1572868
  38.4 9.6 %copy-start.1 = (f32[16,32,256]{2,1,0:T(8,128)S(1)}, f32[16,32,256]{2,1,0:T(8,128)}, u32[]{:S(2)}) copy-start(f32[16,32,256]{2,1,0:T(8,128)} %shard_map.83) | copy-start | bytes 1572868
  39.5 8.4 %collective-permute-start = (f32[19,8,256]{2,1,0:T(8,128)S(1)}, f32[19,8,256]{2,1,0:T(8,128)S(1)}, u32[]{:S(2)}, u32[]{:S(2)}) collective-permute-start(f32[19,8,256]{2,1,0:T(8,128)S(1)} %pad_maximum_fusion.2), channel_id=1, source_target_pairs={{0,1},{1,2},{2,3},{3,4},{4,5},{5,6},{6,7},{7,8},{8,9},{9,10},{10,1... | collective-permute-start | bytes 466952 | tf_op jit(solution)/shard_map/ppermute | solution.py:135
  40.9 7.1 %collective-permute-start.1 = (f32[19,8,256]{2,1,0:T(8,128)S(1)}, f32[19,8,256]{2,1,0:T(8,128)S(1)}, u32[]{:S(2)}, u32[]{:S(2)}) collective-permute-start(f32[19,8,256]{2,1,0:T(8,128)S(1)} %pad_maximum_fusion.3), channel_id=1, source_target_pairs={{1,0},{2,1},{3,2},{4,3},{5,4},{6,5},{7,6},{8,7},{9,8},{10,9},{11,1... | collective-permute-start | bytes 466952 | tf_op jit(solution)/shard_map/ppermute | solution.py:136
  48.5 1.2 %collective-permute-start.2 = (f32[57,128]{1,0:T(8,128)S(1)}, f32[57,128]{1,0:T(8,128)S(1)}, u32[]{:S(2)}, u32[]{:S(2)}) collective-permute-start(f32[57,128]{1,0:T(8,128)S(1)} %reshape.107), channel_id=1, source_target_pairs={{0,16},{16,32},{32,48},{48,64},{64,80},{80,96},{96,112},{112,128},... | collective-permute-start | bytes 87560 | tf_op jit(solution)/shard_map/ppermute | solution.py:132
  48.8 3.6 %collective-permute-start.3 = (f32[57,128]{1,0:T(8,128)S(1)}, f32[57,128]{1,0:T(8,128)S(1)}, u32[]{:S(2)}, u32[]{:S(2)}) collective-permute-start(f32[57,128]{1,0:T(8,128)S(1)} %reshape.109), channel_id=1, source_target_pairs={{16,0},{32,16},{48,32},{64,48},{80,64},{96,80},{112,96},{128,112},... | collective-permute-start | bytes 87560 | tf_op jit(solution)/shard_map/ppermute | solution.py:133

commit v17 on v16

--- a/solution.py
+++ b/solution.py
@@ -1,3 +1,5 @@
+import functools
+
 import jax
 import jax.numpy as jnp
 from jax import lax
@@ -18,7 +20,7 @@
     return high, middle, low
 
 
-def scatter_kernel(held_ref, seen_ref, usable_ref, rows_ref, cols_ref, sea_ref, out_ref, acc_ref):
+def scatter_kernel(row_starts, block_rows, held_ref, seen_ref, usable_ref, rows_ref, cols_ref, sea_ref, out_ref, acc_ref):
     levels, slots = seen_ref.shape
     peers, _, pair = held_ref.shape
     capacity = pair // 2
@@ -34,7 +36,11 @@
         values = jnp.concatenate([h[:, :capacity] for h in held], axis=1)
         weights = jnp.concatenate([h[:, capacity:] for h in held], axis=1)
         w = weights * (values - seen_ref[:, here]) * usable_ref[:, here]
-        row_hit = lax.broadcasted_iota(jnp.int32, (rows_here, SCATTER_CHUNK), 0) == rows_ref[:, here]
+        place = lax.broadcasted_iota(jnp.int32, (rows_here, SCATTER_CHUNK), 0)
+        row_index = place + row_starts[0]
+        for block, start_row in enumerate(row_starts[1:], 1):
+            row_index = jnp.where(place >= block * block_rows, place - block * block_rows + start_row, row_index)
+        row_hit = row_index == rows_ref[:, here]
         col_hit = lax.broadcasted_iota(jnp.int32, (cols_here, SCATTER_CHUNK), 0) == cols_ref[:, here]
         col_hit = col_hit.astype(jnp.float32).astype(jnp.bfloat16)
         spread = [
@@ -87,13 +93,13 @@
     )
 
 
-def onehot_scatter(held, seen, usable, rows, cols, sea):
+def onehot_scatter(held, seen, usable, rows, cols, sea, row_starts, block_rows):
     levels, slots = seen.shape
     rows_here, cols_here = sea.shape
     shape = jax.ShapeDtypeStruct((levels, rows_here, cols_here), jnp.float32)
     flops = 6 * levels * rows_here * cols_here * slots
     return pl.pallas_call(
-        scatter_kernel,
+        functools.partial(scatter_kernel, row_starts, block_rows),
         out_shape=shape,
         in_specs=[pl.BlockSpec(memory_space=pltpu.VMEM)] * 6,
         out_specs=pl.BlockSpec(memory_space=pltpu.VMEM),
@@ -174,9 +180,25 @@
     target_cols = (targets % cols_here)[None, :]
     at_column = onehot_gather(state.reshape(levels * rows_here, cols_here), target_rows, target_cols, levels)
     sea = land_sea.astype(jnp.float32)
-    gradient = onehot_scatter(at_owner, at_column, usable[None, :], target_rows, target_cols, sea)
     rim_width = PASSES
-    padded = with_halo([gradient, sea[None], coef_lon[None], coef_lat[None]], (("lat", 1), ("lon", 2)), rim_width)
+    scatter_args = (at_owner, at_column, usable[None, :], target_rows, target_cols)
+    edge_sea = jnp.concatenate([sea[:rim_width], sea[rows_here - rim_width :]])
+    edge = onehot_scatter(*scatter_args, edge_sea, (0, rows_here - rim_width), rim_width)
+    inner = onehot_scatter(
+        *scatter_args, sea[rim_width : rows_here - rim_width], (rim_width,), rows_here - 2 * rim_width
+    )
+    lat_count_ = lax.axis_size("lat")
+    up = [(i, (i + 1) % lat_count_) for i in range(lat_count_)]
+    down = [(j, i) for i, j in up]
+    extra = [sea[None], coef_lon[None], coef_lat[None]]
+    low = jnp.concatenate([edge[:, rim_width:]] + [p[:, rows_here - rim_width :] for p in extra])
+    high = jnp.concatenate([edge[:, :rim_width]] + [p[:, :rim_width] for p in extra])
+    low = lax.ppermute(low, "lat", up)
+    high = lax.ppermute(high, "lat", down)
+    gradient = jnp.concatenate([edge[:, :rim_width], inner, edge[:, rim_width:]], axis=1)
+    block = jnp.concatenate([gradient] + extra)
+    block = jnp.concatenate([low, block, high], axis=1)
+    padded = with_halo([block], (("lon", 2),), rim_width)
     field = padded[:levels]
     padded = padded[levels:]
     lat_index = lax.axis_index("lat")

time: 65.2 us -> 65.9 us (1.011)
  waiting for transfers between devices: 14.1 us -> 10.5 us
  Pallas kernels: 12.8 us -> 15.5 us
  other arithmetic: 17.2 us -> 18.1 us
    ppermute x2, waiting for transfers between devices: 3.22 us -> 0.01 us  [the longest x1 0.01 us: body(): high = lax.ppermute(high, 'lat', down)]
    pallas_call x1 -> x2, Pallas kernels: 6.15 us -> 8.91 us  [onehot_scatter(): pl.pallas_call(functools.partial(scatter_kernel, row_starts, block_rows),...]
    concatenate x2 -> x4, other arithmetic: 0.03 us -> 1.67 us  [the longest x1 1.04 us: body(): block = jnp.concatenate([low, block, high], axis=1)]
    slice x1 -> x5, local copies, waits for them, and re-layouts: 0.19 us -> 1.6 us  [the longest x1 0.99 us: body(): edge[:, rim_width:]]
    slice x3 -> x1, local copies, waits for them, and re-layouts: 1.05 us -> 0.19 us  [with_halo(): lax.slice_in_dim(p, p.shape[dim] - width, None, axis=dim)]
  transfers between devices with their start and end apart: 5 -> 5, of which waited for: 5 -> 3; matrix products, arithmetic and copies ran while one was open for 5% -> 6% of each run, Pallas kernels for 10% -> 17%
where the time goes in v17:
time: 65.9 us; the launch traced here: 65.6 us
  other arithmetic  18.1 us (27%)
  starting transfers between devices  15.8 us (24%)
  Pallas kernels  15.5 us (24%)
  waiting for transfers between devices  10.5 us (16%)
  local copies, waits for them, and re-layouts  5.27 us (8%)
    all_to_all x1, starting transfers between devices, body(): lax.all_to_all(held, 'lon', split_axis=0, concat_axis=0, tiled=True)  9.98 us
    sub x8, other arithmetic, one_pass(): centre + east_here * (field[:, 1:-1, 2:] - centre)  9.72 us
    pallas_call x2, Pallas kernels, onehot_scatter(): pl.pallas_call(functools.partial(scatter_kernel, row_starts, block_rows),...  8.91 us
    all_to_all x1, waiting for transfers between devices, body(): lax.all_to_all(held, 'lon', split_axis=0, concat_axis=0, tiled=True)  7.97 us
    pallas_call x1, Pallas kernels, onehot_gather(): vmem_call(gather_kernel, shape, flops, 4 * (levels * slots + 2 * slots +...  6.64 us
    ppermute x1, starting transfers between devices, body(): high = lax.ppermute(high, 'lat', down)  3.91 us
    unnamed x2, other arithmetic  3.19 us
    ppermute x1, waiting for transfers between devices, with_halo(): high = lax.ppermute(high.reshape(flat), axis, backward).reshape(high.shape)  2.1 us
  transfers between devices with their start and end apart: 5, of which 3 were waited for; matrix products, arithmetic and copies ran while one was open for 6% of the time, Pallas kernels for 17%

profile of v17, /device:TPU:1, one launch (start us, length us, event | category | flops | bytes accessed | tf_op | source)
XLA Modules:
  0.0 65.6 jit_solution(5896728294771135138)
XLA Ops:
  0.0 1.6 %reduce.1 = f32[16,4096]{1,0:T(8,128)S(1)} reduce(f32[16,1,4096]{2,1,0:T(1,128)} %param.15, f32[]{:T(128)} %constant.52), dimensions={1}, to_apply=%param.15.reduce_sub_computation | reduce | bytes 524292 | tf_op args[7]
  1.6 1.6 %reduce = f32[16,4096]{1,0:T(8,128)S(1)} reduce(f32[16,1,4096]{2,1,0:T(1,128)} %param.14, f32[]{:T(128)} %constant.52), dimensions={1}, to_apply=%param.14.reduce_sub_computation | reduce | bytes 524292 | tf_op args[6]
  3.2 0.1 copy_bitcast_fusion
  3.3 0.0 copy-start.5
  3.3 0.0 copy-start.6
  3.3 0.0 copy-start.3
  3.3 0.0 copy-start.4
  3.3 0.9 %maximum_bitcast_fusion = f32[16,16,512]{2,1,0:T(8,128)} fusion(f32[16,16,256]{2,0,1:T(8,128)S(1)} %get-tuple-element.53, f32[16,16,256]{2,0,1:T(8,128)S(1)} %get-tuple-element.54), kind=kLoop, calls=%fused_computation.98 | loop fusion | flops 131072 | bytes 1048576 | tf_op jit(solution)/shard_map/transpose | solution.py:177
  4.2 10.0 %all-to-all-start = ((f32[16,16,512]{2,1,0:T(8,128)}), f32[16,16,512]{2,1,0:T(8,128)S(1)}, u32[]{:S(2)}, u32[]{:S(2)}) async-start(f32[16,16,512]{2,1,0:T(8,128)} %maximum_bitcast_fusion), calls=%async_computation | async-start | bytes 1048576 | tf_op jit(solution)/shard_map/all_to_all | solution.py:178
  14.1 0.0 copy-done.5
  14.2 0.7 and_select_fusion.1
  14.8 0.7 %and_select_fusion.2.rows_ref = s32[1,4096]{1,0:T(1,128)} fusion(s32[1,4096]{1,0:T(1,128)S(1)} %get-tuple-element.6, s32[1,4096]{1,0:T(1,128)S(1)} %copy-done.5), kind=kLoop, calls=%fused_computation.114 | loop fusion | flops 49152 | bytes 49152 | tf_op jit(solution)/shard_map/jit(floor_divide)/jit(_where)/select_n | solution.py:179
  15.5 0.1 broadcast_bitcast_fusion
  15.6 6.6 %shard_map.82.seen_ref = f32[16,4096]{1,0:T(8,128)} custom-call(f32[512,256]{1,0:T(8,128)} %bitcast.38, s32[1,4096]{1,0:T(1,128)} %and_select_fusion.2.rows_ref, s32[1,4096]{1,0:T(1,128)} %get-tuple-element.5.cols_ref), custom_call_target="tpu_custom_call" | custom-call | flops 3221225472 | bytes 819200 | tf_op jit(solution)/shard_map/pallas_call | solution.py:119
  22.3 0.6 pad_maximum_fusion.4.sea_ref
  22.9 0.6 compare_select_fusion.usable_ref
  23.5 8.0 %all-to-all-done.held_ref = f32[16,16,512]{2,1,0:T(8,128)S(1)} async-done(((f32[16,16,512]{2,1,0:T(8,128)}), f32[16,16,512]{2,1,0:T(8,128)S(1)}, u32[]{:S(2)}, u32[]{:S(2)}) %all-to-all-start) | async-done | bytes 524320 | tf_op jit(solution)/shard_map/all_to_all | solution.py:178
  31.5 0.8 %copy-done.2 = f32[16,16,512]{2,1,0:T(8,128)} copy-done((f32[16,16,512]{2,1,0:T(8,128)}, f32[16,16,512]{2,1,0:T(8,128)S(1)}, u32[]{:S(2)}) %copy-start.2) | copy-done | bytes 524312
  32.3 4.5 %shard_map.83 = f32[16,16,256]{2,1,0:T(8,128)} custom-call(f32[16,16,512]{2,1,0:T(8,128)} %copy-done.2, f32[16,4096]{1,0:T(8,128)} %shard_map.82.seen_ref, f32[1,4096]{1,0:T(1,128)} %compare_select_fusion.usable_ref, s32[1,4096]{1,0:T(1,128)} %and_select_fusion.2.rows_ref, s32[1,4096]{1,0:T(1,128)} %get-tuple-element.5.cols_ref, ...), custom_call_target="tpu_custom_call" | custom-call | flops 1610612736 | bytes 1097728 | tf_op jit(solution)/shard_map/pallas_call | solution.py:101
  36.7 1.0 %fusion.66 = (f32[16,8,256]{2,1,0:T(8,128)S(1)}, f32[16,8,256]{2,1,0:T(8,128)S(1)}) fusion(f32[16,16,256]{2,1,0:T(8,128)} %shard_map.83), kind=kLoop, calls=%fused_computation.123 | loop fusion | bytes 524288 | tf_op jit(solution)/shard_map/slice | solution.py:194
  37.7 1.4 %collective-permute-start = (f32[19,8,256]{2,1,0:T(8,128)S(1)}, f32[19,8,256]{2,1,0:T(8,128)S(1)}, u32[]{:S(2)}, u32[]{:S(2)}) collective-permute-start(f32[19,8,256]{2,1,0:T(8,128)S(1)} %pad_maximum_fusion.2), channel_id=1, source_target_pairs={{0,1},{1,2},{2,3},{3,4},{4,5},{5,6},{6,7},{7,8},{8,9},{9,10},{10,1... | collective-permute-start | bytes 466952 | tf_op jit(solution)/shard_map/ppermute | solution.py:196
  39.1 3.9 %collective-permute-start.1 = (f32[19,8,256]{2,1,0:T(8,128)S(1)}, f32[19,8,256]{2,1,0:T(8,128)S(1)}, u32[]{:S(2)}, u32[]{:S(2)}) collective-permute-start(f32[19,8,256]{2,1,0:T(8,128)S(1)} %pad_maximum_fusion.3), channel_id=1, source_target_pairs={{1,0},{2,1},{3,2},{4,3},{5,4},{6,5},{7,6},{8,7},{9,8},{10,9},{11,1... | collective-permute-start | bytes 466952 | tf_op jit(solution)/shard_map/ppermute | solution.py:197
  43.0 0.6 slice.397.sea_ref
  43.6 4.5 %shard_map.84 = f32[16,16,256]{2,1,0:T(8,128)} custom-call(f32[16,16,512]{2,1,0:T(8,128)} %copy-done.2, f32[16,4096]{1,0:T(8,128)} %shard_map.82.seen_ref, f32[1,4096]{1,0:T(1,128)} %compare_select_fusion.usable_ref, s32[1,4096]{1,0:T(1,128)} %and_select_fusion.2.rows_ref, s32[1,4096]{1,0:T(1,128)} %get-tuple-element.5.cols_ref, f32[16,256]{1,0:T(8,128)} %slice.397.sea_ref), custom_call_target="tpu_custom_call" | custom-call | flops 1610612736 | bytes 1097728 | tf_op jit(solution)/shard_map/pallas_call | solution.py:101
  48.1 0.0 collective-permute-done
  48.1 0.0 collective-permute-done.1
  48.1 1.0 %pad_maximum_fusion.1 = f32[19,48,256]{2,1,0:T(8,128)S(1)} fusion(f32[19,8,256]{2,1,0:T(8,128)S(1)} %collective-permute-done.1, f32[1,32,256]{2,1,0:T(8,128)S(1)} %bitcast.32, f32[1,32,256]{2,1,0:T(8,128)S(1)} %bitcast.35, f32[1,32,256]{2,1,0:T(8,128)S(1)} %get-tuple-element.52, f32[16,8,256]{2,1,0:T(8,128)S(1)} %get-tuple-element.9, ...), kind=kLoop, calls=%fused_computation.85 | loop fusion | flops 1634304 | bytes 1867776 | tf_op jit(solution)/shard_map/concatenate | solution.py:200
  49.1 0.2 fusion.65
  49.3 0.2 reshape.107
  49.6 0.0 collective-permute-start.2
  49.6 0.2 reshape.109
  49.8 0.5 collective-permute-start.3
  50.3 0.5 collective-permute-done.2
  50.8 0.3 reshape.108
  51.1 2.1 %collective-permute-done.3 = f32[57,128]{1,0:T(8,128)S(1)} collective-permute-done((f32[57,128]{1,0:T(8,128)S(1)}, f32[57,128]{1,0:T(8,128)S(1)}, u32[]{:S(2)}, u32[]{:S(2)}) %collective-permute-start.3) | collective-permute-done | bytes 29216 | tf_op jit(solution)/shard_map/ppermute | solution.py:139
  53.2 0.3 reshape.110
  53.4 0.0 copy-done.1
  53.5 0.6 pad_maximum_fusion
  54.0 0.1 fusion.64
  54.1 0.1 slice_multiply_fusion.2
  54.2 0.1 fusion.81
  54.3 0.1 fusion.79
  54.4 0.1 fusion.82
  54.5 0.1 fusion.80
  54.6 0.1 fusion.77
  54.7 0.1 fusion.78
  54.8 0.1 fusion.75
  55.0 0.1 fusion.76
  55.1 0.1 fusion.73
  55.2 0.1 fusion.74
  55.3 0.1 fusion.71
  55.4 0.1 fusion.72
  55.5 0.1 fusion.69
  55.6 0.1 fusion.70
  55.7 0.1 fusion.67
  55.7 0.1 fusion.68
  55.8 1.3 %fusion.17 = f32[16,46,270]{2,1,0:T(8,128)S(1)} fusion(f32[19,48,272]{2,1,0:T(8,128)S(1)} %pad_maximum_fusion, f32[46,270]{1,0:T(8,128)S(1)} %get-tuple-element.42, f32[46,270]{1,0:T(8,128)S(1)} %get-tuple-element.41, f32[46,270]{1,0:T(8,128)S(1)} %get-tuple-element.40, f32[46,270]{1,0:T(8,128)S(1)} %get-tuple-element.39), kind=kLoop, calls=%fused_computation.27 | loop fusion | flops 2384640 | bytes 4968000 | tf_op jit(solution)/shard_map/sub | solution.py:157
  57.2 1.3 %fusion.9 = f32[16,44,268]{2,1,0:T(8,128)S(1)} fusion(f32[16,46,270]{2,1,0:T(8,128)S(1)} %fusion.17, f32[44,268]{1,0:T(8,128)S(1)} %get-tuple-element.38, f32[44,268]{1,0:T(8,128)S(1)} %get-tuple-element.37, f32[44,268]{1,0:T(8,128)S(1)} %get-tuple-element.36, f32[44,268]{1,0:T(8,128)S(1)} %get-tuple-element.35), kind=kLoop, calls=%fused_computation.15 | loop fusion | flops 2264064 | bytes 4716800 | tf_op jit(solution)/shard_map/sub | solution.py:157
  58.5 1.3 %fusion.1 = f32[16,42,266]{2,1,0:T(8,128)S(1)} fusion(f32[16,44,268]{2,1,0:T(8,128)S(1)} %fusion.9, f32[42,266]{1,0:T(8,128)S(1)} %get-tuple-element.34, f32[42,266]{1,0:T(8,128)S(1)} %get-tuple-element.33, f32[42,266]{1,0:T(8,128)S(1)} %get-tuple-element.32, f32[42,266]{1,0:T(8,128)S(1)} %get-tuple-element.31), kind=kLoop, calls=%fused_computation.3 | loop fusion | flops 2145024 | bytes 4468800 | tf_op jit(solution)/shard_map/sub | solution.py:157
  59.8 1.1 %fusion.49 = f32[16,40,264]{2,1,0:T(8,128)S(1)} fusion(f32[16,42,266]{2,1,0:T(8,128)S(1)} %fusion.1, f32[40,264]{1,0:T(8,128)S(1)} %get-tuple-element.30, f32[40,264]{1,0:T(8,128)S(1)} %get-tuple-element.29, f32[40,264]{1,0:T(8,128)S(1)} %get-tuple-element.28, f32[40,264]{1,0:T(8,128)S(1)} %get-tuple-element.27), kind=kLoop, calls=%fused_computation.75 | loop fusion | flops 2027520 | bytes 4224000 | tf_op jit(solution)/shard_map/sub | solution.py:157
  60.9 1.1 %fusion.41 = f32[16,38,262]{2,1,0:T(8,128)S(1)} fusion(f32[16,40,264]{2,1,0:T(8,128)S(1)} %fusion.49, f32[38,262]{1,0:T(8,128)S(1)} %get-tuple-element.26, f32[38,262]{1,0:T(8,128)S(1)} %get-tuple-element.25, f32[38,262]{1,0:T(8,128)S(1)} %get-tuple-element.24, f32[38,262]{1,0:T(8,128)S(1)} %get-tuple-element.23), kind=kLoop, calls=%fused_computation.63 | loop fusion | flops 1911552 | bytes 3982400 | tf_op jit(solution)/shard_map/sub | solution.py:157
  62.0 1.1 %fusion.33 = f32[16,36,260]{2,1,0:T(8,128)S(1)} fusion(f32[16,38,262]{2,1,0:T(8,128)S(1)} %fusion.41, f32[36,260]{1,0:T(8,128)S(1)} %get-tuple-element.22, f32[36,260]{1,0:T(8,128)S(1)} %get-tuple-element.21, f32[36,260]{1,0:T(8,128)S(1)} %get-tuple-element.20, f32[36,260]{1,0:T(8,128)S(1)} %get-tuple-element.19), kind=kLoop, calls=%fused_computation.51 | loop fusion | flops 1797120 | bytes 3744000 | tf_op jit(solution)/shard_map/sub | solution.py:157
  63.1 1.1 %fusion.25 = f32[16,34,258]{2,1,0:T(8,128)S(1)} fusion(f32[16,36,260]{2,1,0:T(8,128)S(1)} %fusion.33, f32[34,258]{1,0:T(8,128)S(1)} %get-tuple-element.18, f32[34,258]{1,0:T(8,128)S(1)} %get-tuple-element.17, f32[34,258]{1,0:T(8,128)S(1)} %get-tuple-element.16, f32[34,258]{1,0:T(8,128)S(1)} %get-tuple-element.15), kind=kLoop, calls=%fused_computation.39 | loop fusion | flops 1684224 | bytes 3508800 | tf_op jit(solution)/shard_map/sub | solution.py:157
  64.2 1.4 %fusion.57 = f32[16,32,256]{2,1,0:T(8,128)} fusion(f32[16,34,258]{2,1,0:T(8,128)S(1)} %fusion.25, f32[32,256]{1,0:T(8,128)S(1)} %get-tuple-element.14, f32[32,256]{1,0:T(8,128)S(1)} %get-tuple-element.13, f32[32,256]{1,0:T(8,128)S(1)} %get-tuple-element.12, f32[32,256]{1,0:T(8,128)S(1)} %get-tuple-element.11), kind=kLoop, calls=%fused_computation.88 | loop fusion | flops 1572864 | bytes 3276800 | tf_op jit(solution)/shard_map/sub | solution.py:157
  (17 shorter events, 0.1 us)
Async XLA Ops:
  0.0 15.5 %copy-start = (s32[1,16]{1,0:T(1,128)S(1)}, s32[1,16]{1,0:T(1,128)}, u32[]{:S(2)}) copy-start(s32[1,16]{1,0:T(1,128)} %param.13) | copy-start | bytes 196
  3.3 10.9 %copy-start.5 = (s32[1,4096]{1,0:T(1,128)S(1)}, s32[1,4096]{1,0:T(1,128)}, u32[]{:S(2)}) copy-start(s32[1,4096]{1,0:T(1,128)} %param.12) | copy-start | bytes 49156
  3.3 12.2 %copy-start.6 = (s32[32,256]{1,0:T(8,128)S(1)}, s32[32,256]{1,0:T(8,128)}, u32[]{:S(2)}) copy-start(s32[32,256]{1,0:T(8,128)} %param.11) | copy-start | bytes 98308
  3.3 12.3 %copy-start.3 = (f32[32,256]{1,0:T(8,128)S(1)}, f32[32,256]{1,0:T(8,128)}, u32[]{:S(2)}) copy-start(f32[32,256]{1,0:T(8,128)} %param.10) | copy-start | bytes 98308
  3.3 12.3 %copy-start.4 = (f32[32,256]{1,0:T(8,128)S(1)}, f32[32,256]{1,0:T(8,128)}, u32[]{:S(2)}) copy-start(f32[32,256]{1,0:T(8,128)} %param.9) | copy-start | bytes 98308
  4.2 27.3 %all-to-all-start = ((f32[16,16,512]{2,1,0:T(8,128)}), f32[16,16,512]{2,1,0:T(8,128)S(1)}, u32[]{:S(2)}, u32[]{:S(2)}) async-start(f32[16,16,512]{2,1,0:T(8,128)} %maximum_bitcast_fusion), calls=%async_computation | async-start | bytes 1048576 | tf_op jit(solution)/shard_map/all_to_all | solution.py:178
  31.5 0.8 %copy-start.2 = (f32[16,16,512]{2,1,0:T(8,128)}, f32[16,16,512]{2,1,0:T(8,128)S(1)}, u32[]{:S(2)}) copy-start(f32[16,16,512]{2,1,0:T(8,128)S(1)} %all-to-all-done.held_ref) | copy-start | bytes 1572868
  37.7 10.4 %collective-permute-start = (f32[19,8,256]{2,1,0:T(8,128)S(1)}, f32[19,8,256]{2,1,0:T(8,128)S(1)}, u32[]{:S(2)}, u32[]{:S(2)}) collective-permute-start(f32[19,8,256]{2,1,0:T(8,128)S(1)} %pad_maximum_fusion.2), channel_id=1, source_target_pairs={{0,1},{1,2},{2,3},{3,4},{4,5},{5,6},{6,7},{7,8},{8,9},{9,10},{10,1... | collective-permute-start | bytes 466952 | tf_op jit(solution)/shard_map/ppermute | solution.py:196
  39.1 9.0 %collective-permute-start.1 = (f32[19,8,256]{2,1,0:T(8,128)S(1)}, f32[19,8,256]{2,1,0:T(8,128)S(1)}, u32[]{:S(2)}, u32[]{:S(2)}) collective-permute-start(f32[19,8,256]{2,1,0:T(8,128)S(1)} %pad_maximum_fusion.3), channel_id=1, source_target_pairs={{1,0},{2,1},{3,2},{4,3},{5,4},{6,5},{7,6},{8,7},{9,8},{10,9},{11,1... | collective-permute-start | bytes 466952 | tf_op jit(solution)/shard_map/ppermute | solution.py:197
  49.3 4.1 %copy-start.1 = (f32[16,16,256]{2,1,0:T(8,128)S(1)}, f32[16,16,256]{2,1,0:T(8,128)}, u32[]{:S(2)}) copy-start(f32[16,16,256]{2,1,0:T(8,128)} %shard_map.84) | copy-start | bytes 786436
  49.6 1.2 %collective-permute-start.2 = (f32[57,128]{1,0:T(8,128)S(1)}, f32[57,128]{1,0:T(8,128)S(1)}, u32[]{:S(2)}, u32[]{:S(2)}) collective-permute-start(f32[57,128]{1,0:T(8,128)S(1)} %reshape.107), channel_id=1, source_target_pairs={{0,16},{16,32},{32,48},{48,64},{64,80},{80,96},{96,112},{112,128},... | collective-permute-start | bytes 87560 | tf_op jit(solution)/shard_map/ppermute | solution.py:138
  49.8 3.3 %collective-permute-start.3 = (f32[57,128]{1,0:T(8,128)S(1)}, f32[57,128]{1,0:T(8,128)S(1)}, u32[]{:S(2)}, u32[]{:S(2)}) collective-permute-start(f32[57,128]{1,0:T(8,128)S(1)} %reshape.109), channel_id=1, source_target_pairs={{16,0},{32,16},{48,32},{64,48},{80,64},{96,80},{112,96},{128,112},... | collective-permute-start | bytes 87560 | tf_op jit(solution)/shard_map/ppermute | solution.py:139

commit v18 on v15

--- a/solution.py
+++ b/solution.py
@@ -7,7 +7,7 @@
 
 PASSES = 8
 CHUNK = 512
-SCATTER_CHUNK = 1024
+SCATTER_CHUNK = 2048
 
 
 def three_parts(x):

time: 65 us -> 64.6 us (level)
  no operation moved by 1% of the time
where the time goes in v18:
time: 64.6 us; the launch traced here: 64.3 us
  other arithmetic  18.2 us (28%)
  starting transfers between devices  15.8 us (24%)
  waiting for transfers between devices  14 us (22%)
  Pallas kernels  12.4 us (19%)
  local copies, waits for them, and re-layouts  3.67 us (6%)
    all_to_all x1, starting transfers between devices, body(): lax.all_to_all(held, 'lon', split_axis=0, concat_axis=0, tiled=True)  9.98 us
    sub x8, other arithmetic, one_pass(): centre + east_here * (field[:, 1:-1, 2:] - centre)  9.73 us
    all_to_all x1, waiting for transfers between devices, body(): lax.all_to_all(held, 'lon', split_axis=0, concat_axis=0, tiled=True)  8.01 us
    pallas_call x1, Pallas kernels, onehot_gather(): vmem_call(gather_kernel, shape, flops, 4 * (levels * slots + 2 * slots +...  6.65 us
    pallas_call x1, Pallas kernels, onehot_scatter(): pl.pallas_call(scatter_kernel, out_shape=shape, in_specs=[pl.BlockSpec(me...  5.74 us
    ppermute x1, starting transfers between devices, with_halo(): high = lax.ppermute(high, axis, backward)  3.9 us
    unnamed x2, other arithmetic  3.19 us
    ppermute x1, waiting for transfers between devices, with_halo(): low = lax.ppermute(low, axis, forward)  3.14 us
  transfers between devices with their start and end apart: 5, of which 4 were waited for; matrix products, arithmetic and copies ran while one was open for 5% of the time, Pallas kernels for 10%

profile of v18, /device:TPU:1, one launch (start us, length us, event | category | flops | bytes accessed | tf_op | source)
XLA Modules:
  0.0 64.3 jit_solution(11079720310607352361)
XLA Ops:
  0.0 0.0 copy-start
  0.0 1.6 %reduce.1 = f32[16,4096]{1,0:T(8,128)S(1)} reduce(f32[16,1,4096]{2,1,0:T(1,128)} %param.15, f32[]{:T(128)} %constant.52), dimensions={1}, to_apply=%param.15.reduce_sub_computation | reduce | bytes 524292 | tf_op args[7]
  1.6 1.6 %reduce = f32[16,4096]{1,0:T(8,128)S(1)} reduce(f32[16,1,4096]{2,1,0:T(1,128)} %param.14, f32[]{:T(128)} %constant.52), dimensions={1}, to_apply=%param.14.reduce_sub_computation | reduce | bytes 524292 | tf_op args[6]
  3.2 0.1 copy_bitcast_fusion
  3.3 0.0 copy-start.5
  3.3 0.0 copy-start.6
  3.3 0.9 %maximum_bitcast_fusion = f32[16,16,512]{2,1,0:T(8,128)} fusion(f32[16,16,256]{2,0,1:T(8,128)S(1)} %get-tuple-element.45, f32[16,16,256]{2,0,1:T(8,128)S(1)} %get-tuple-element.46), kind=kLoop, calls=%fused_computation.98 | loop fusion | flops 131072 | bytes 1048576 | tf_op jit(solution)/shard_map/transpose | solution.py:165
  4.1 10.0 %all-to-all-start = ((f32[16,16,512]{2,1,0:T(8,128)}), f32[16,16,512]{2,1,0:T(8,128)S(1)}, u32[]{:S(2)}, u32[]{:S(2)}) async-start(f32[16,16,512]{2,1,0:T(8,128)} %maximum_bitcast_fusion), calls=%async_computation | async-start | bytes 1048576 | tf_op jit(solution)/shard_map/all_to_all | solution.py:166
  14.1 0.0 copy-done.5
  14.1 0.7 %and_select_fusion.1 = (s32[1,4096]{1,0:T(1,128)}, s32[1,4096]{1,0:T(1,128)S(1)}) fusion(s32[1,4096]{1,0:T(1,128)S(1)} %copy-done.5), kind=kLoop, calls=%fused_computation.115 | loop fusion | flops 45056 | bytes 49152 | tf_op jit(solution)/shard_map/jit(remainder)/select_n | solution.py:168
  14.8 0.7 %and_select_fusion.2.rows_ref = s32[1,4096]{1,0:T(1,128)} fusion(s32[1,4096]{1,0:T(1,128)S(1)} %get-tuple-element.6, s32[1,4096]{1,0:T(1,128)S(1)} %copy-done.5), kind=kLoop, calls=%fused_computation.116 | loop fusion | flops 49152 | bytes 49152 | tf_op jit(solution)/shard_map/jit(floor_divide)/jit(_where)/select_n | solution.py:167
  15.4 0.0 copy-done.6
  15.4 0.6 fusion.82
  16.1 6.6 %shard_map.82.seen_ref = f32[16,4096]{1,0:T(8,128)} custom-call(f32[512,256]{1,0:T(8,128)} %bitcast.38, s32[1,4096]{1,0:T(1,128)} %and_select_fusion.2.rows_ref, s32[1,4096]{1,0:T(1,128)} %get-tuple-element.5.cols_ref), custom_call_target="tpu_custom_call" | custom-call | flops 3221225472 | bytes 819200 | tf_op jit(solution)/shard_map/pallas_call | solution.py:113
  22.7 0.0 copy-done
  22.7 0.1 broadcast_bitcast_fusion
  22.8 0.6 compare_select_fusion.usable_ref
  23.4 8.0 %all-to-all-done.held_ref = f32[16,16,512]{2,1,0:T(8,128)S(1)} async-done(((f32[16,16,512]{2,1,0:T(8,128)}), f32[16,16,512]{2,1,0:T(8,128)S(1)}, u32[]{:S(2)}, u32[]{:S(2)}) %all-to-all-start) | async-done | bytes 524320 | tf_op jit(solution)/shard_map/all_to_all | solution.py:166
  31.5 0.8 %copy-done.2 = f32[16,16,512]{2,1,0:T(8,128)} copy-done((f32[16,16,512]{2,1,0:T(8,128)}, f32[16,16,512]{2,1,0:T(8,128)S(1)}, u32[]{:S(2)}) %copy-start.2) | copy-done | bytes 524312
  32.2 5.7 %shard_map.83 = f32[16,32,256]{2,1,0:T(8,128)} custom-call(f32[16,16,512]{2,1,0:T(8,128)} %copy-done.2, f32[16,4096]{1,0:T(8,128)} %shard_map.82.seen_ref, f32[1,4096]{1,0:T(1,128)} %compare_select_fusion.usable_ref, s32[1,4096]{1,0:T(1,128)} %and_select_fusion.2.rows_ref, s32[1,4096]{1,0:T(1,128)} %get-tuple-element.5.cols_ref, ...), custom_call_target="tpu_custom_call" | custom-call | flops 3221225472 | bytes 1359872 | tf_op jit(solution)/shard_map/pallas_call | solution.py:95
  38.0 0.0 copy-done.3
  38.0 0.0 copy-done.4
  38.0 1.0 %pad_maximum_fusion.5 = (f32[19,8,256]{2,1,0:T(8,128)S(1)}, f32[19,8,256]{2,1,0:T(8,128)S(1)}) fusion(f32[1,32,256]{2,1,0:T(8,128)S(1)} %bitcast.31, f32[1,32,256]{2,1,0:T(8,128)S(1)} %bitcast.34, f32[1,32,256]{2,1,0:T(8,128)S(1)} %get-tuple-element.44, f32[16,32,256]{2,1,0:T(8,128)} %shard_map.83), kind=kLoop, calls=%fused_computation.104 | loop fusion | flops 233472 | bytes 933888 | tf_op jit(solution)/shard_map/slice | solution.py:122
  39.1 1.4 %collective-permute-start = (f32[19,8,256]{2,1,0:T(8,128)S(1)}, f32[19,8,256]{2,1,0:T(8,128)S(1)}, u32[]{:S(2)}, u32[]{:S(2)}) collective-permute-start(f32[19,8,256]{2,1,0:T(8,128)S(1)} %get-tuple-element.9), channel_id=1, source_target_pairs={{0,1},{1,2},{2,3},{3,4},{4,5},{5,6},{6,7},{7,8},{8,9},{9,10},{10,1... | collective-permute-start | bytes 466952 | tf_op jit(solution)/shard_map/ppermute | solution.py:129
  40.4 3.9 %collective-permute-start.1 = (f32[19,8,256]{2,1,0:T(8,128)S(1)}, f32[19,8,256]{2,1,0:T(8,128)S(1)}, u32[]{:S(2)}, u32[]{:S(2)}) collective-permute-start(f32[19,8,256]{2,1,0:T(8,128)S(1)} %get-tuple-element.10), channel_id=1, source_target_pairs={{1,0},{2,1},{3,2},{4,3},{5,4},{6,5},{7,6},{8,7},{9,8},{10,9},{11,1... | collective-permute-start | bytes 466952 | tf_op jit(solution)/shard_map/ppermute | solution.py:130
  44.3 3.1 %collective-permute-done = f32[19,8,256]{2,1,0:T(8,128)S(1)} collective-permute-done((f32[19,8,256]{2,1,0:T(8,128)S(1)}, f32[19,8,256]{2,1,0:T(8,128)S(1)}, u32[]{:S(2)}, u32[]{:S(2)}) %collective-permute-start) | collective-permute-done | bytes 155680 | tf_op jit(solution)/shard_map/ppermute | solution.py:129
  47.5 0.0 collective-permute-done.1
  47.5 0.1 pad_maximum_fusion.1
  47.5 0.2 fusion.65
  47.7 0.2 reshape.107
  48.0 0.0 collective-permute-start.2
  48.0 0.2 reshape.109
  48.2 0.5 collective-permute-start.3
  48.7 0.5 collective-permute-done.2
  49.2 0.3 reshape.108
  49.5 2.4 %collective-permute-done.3 = f32[57,128]{1,0:T(8,128)S(1)} collective-permute-done((f32[57,128]{1,0:T(8,128)S(1)}, f32[57,128]{1,0:T(8,128)S(1)}, u32[]{:S(2)}, u32[]{:S(2)}) %collective-permute-start.3) | collective-permute-done | bytes 29216 | tf_op jit(solution)/shard_map/ppermute | solution.py:127
  51.9 0.3 reshape.110
  52.1 0.6 pad_maximum_fusion
  52.7 0.1 fusion.64
  52.8 0.1 slice_multiply_fusion.2
  52.9 0.1 fusion.80
  53.0 0.1 fusion.78
  53.1 0.1 fusion.81
  53.2 0.1 fusion.79
  53.3 0.1 fusion.76
  53.4 0.1 fusion.77
  53.5 0.1 fusion.74
  53.6 0.1 fusion.75
  53.7 0.1 fusion.72
  53.8 0.1 fusion.73
  53.9 0.1 fusion.70
  54.0 0.1 fusion.71
  54.2 0.1 fusion.68
  54.3 0.1 fusion.69
  54.4 0.1 fusion.66
  54.4 0.1 fusion.67
  54.5 1.3 %fusion.17 = f32[16,46,270]{2,1,0:T(8,128)S(1)} fusion(f32[19,48,272]{2,1,0:T(8,128)S(1)} %pad_maximum_fusion, f32[46,270]{1,0:T(8,128)S(1)} %get-tuple-element.42, f32[46,270]{1,0:T(8,128)S(1)} %get-tuple-element.41, f32[46,270]{1,0:T(8,128)S(1)} %get-tuple-element.40, f32[46,270]{1,0:T(8,128)S(1)} %get-tuple-element.39), kind=kLoop, calls=%fused_computation.27 | loop fusion | flops 2384640 | bytes 4968000 | tf_op jit(solution)/shard_map/sub | solution.py:145
  55.8 1.3 %fusion.9 = f32[16,44,268]{2,1,0:T(8,128)S(1)} fusion(f32[16,46,270]{2,1,0:T(8,128)S(1)} %fusion.17, f32[44,268]{1,0:T(8,128)S(1)} %get-tuple-element.38, f32[44,268]{1,0:T(8,128)S(1)} %get-tuple-element.37, f32[44,268]{1,0:T(8,128)S(1)} %get-tuple-element.36, f32[44,268]{1,0:T(8,128)S(1)} %get-tuple-element.35), kind=kLoop, calls=%fused_computation.15 | loop fusion | flops 2264064 | bytes 4716800 | tf_op jit(solution)/shard_map/sub | solution.py:145
  57.2 1.3 %fusion.1 = f32[16,42,266]{2,1,0:T(8,128)S(1)} fusion(f32[16,44,268]{2,1,0:T(8,128)S(1)} %fusion.9, f32[42,266]{1,0:T(8,128)S(1)} %get-tuple-element.34, f32[42,266]{1,0:T(8,128)S(1)} %get-tuple-element.33, f32[42,266]{1,0:T(8,128)S(1)} %get-tuple-element.32, f32[42,266]{1,0:T(8,128)S(1)} %get-tuple-element.31), kind=kLoop, calls=%fused_computation.3 | loop fusion | flops 2145024 | bytes 4468800 | tf_op jit(solution)/shard_map/sub | solution.py:145
  58.5 1.1 %fusion.49 = f32[16,40,264]{2,1,0:T(8,128)S(1)} fusion(f32[16,42,266]{2,1,0:T(8,128)S(1)} %fusion.1, f32[40,264]{1,0:T(8,128)S(1)} %get-tuple-element.30, f32[40,264]{1,0:T(8,128)S(1)} %get-tuple-element.29, f32[40,264]{1,0:T(8,128)S(1)} %get-tuple-element.28, f32[40,264]{1,0:T(8,128)S(1)} %get-tuple-element.27), kind=kLoop, calls=%fused_computation.75 | loop fusion | flops 2027520 | bytes 4224000 | tf_op jit(solution)/shard_map/sub | solution.py:145
  59.6 1.1 %fusion.41 = f32[16,38,262]{2,1,0:T(8,128)S(1)} fusion(f32[16,40,264]{2,1,0:T(8,128)S(1)} %fusion.49, f32[38,262]{1,0:T(8,128)S(1)} %get-tuple-element.26, f32[38,262]{1,0:T(8,128)S(1)} %get-tuple-element.25, f32[38,262]{1,0:T(8,128)S(1)} %get-tuple-element.24, f32[38,262]{1,0:T(8,128)S(1)} %get-tuple-element.23), kind=kLoop, calls=%fused_computation.63 | loop fusion | flops 1911552 | bytes 3982400 | tf_op jit(solution)/shard_map/sub | solution.py:145
  60.7 1.1 %fusion.33 = f32[16,36,260]{2,1,0:T(8,128)S(1)} fusion(f32[16,38,262]{2,1,0:T(8,128)S(1)} %fusion.41, f32[36,260]{1,0:T(8,128)S(1)} %get-tuple-element.22, f32[36,260]{1,0:T(8,128)S(1)} %get-tuple-element.21, f32[36,260]{1,0:T(8,128)S(1)} %get-tuple-element.20, f32[36,260]{1,0:T(8,128)S(1)} %get-tuple-element.19), kind=kLoop, calls=%fused_computation.51 | loop fusion | flops 1797120 | bytes 3744000 | tf_op jit(solution)/shard_map/sub | solution.py:145
  61.8 1.1 %fusion.25 = f32[16,34,258]{2,1,0:T(8,128)S(1)} fusion(f32[16,36,260]{2,1,0:T(8,128)S(1)} %fusion.33, f32[34,258]{1,0:T(8,128)S(1)} %get-tuple-element.18, f32[34,258]{1,0:T(8,128)S(1)} %get-tuple-element.17, f32[34,258]{1,0:T(8,128)S(1)} %get-tuple-element.16, f32[34,258]{1,0:T(8,128)S(1)} %get-tuple-element.15), kind=kLoop, calls=%fused_computation.39 | loop fusion | flops 1684224 | bytes 3508800 | tf_op jit(solution)/shard_map/sub | solution.py:145
  62.9 1.4 %fusion.57 = f32[16,32,256]{2,1,0:T(8,128)} fusion(f32[16,34,258]{2,1,0:T(8,128)S(1)} %fusion.25, f32[32,256]{1,0:T(8,128)S(1)} %get-tuple-element.14, f32[32,256]{1,0:T(8,128)S(1)} %get-tuple-element.13, f32[32,256]{1,0:T(8,128)S(1)} %get-tuple-element.12, f32[32,256]{1,0:T(8,128)S(1)} %get-tuple-element.11), kind=kLoop, calls=%fused_computation.88 | loop fusion | flops 1572864 | bytes 3276800 | tf_op jit(solution)/shard_map/sub | solution.py:145
  (9 shorter events, 0.1 us)
Async XLA Ops:
  0.0 22.7 %copy-start = (s32[1,16]{1,0:T(1,128)S(1)}, s32[1,16]{1,0:T(1,128)}, u32[]{:S(2)}) copy-start(s32[1,16]{1,0:T(1,128)} %param.13) | copy-start | bytes 196
  3.3 10.9 %copy-start.5 = (s32[1,4096]{1,0:T(1,128)S(1)}, s32[1,4096]{1,0:T(1,128)}, u32[]{:S(2)}) copy-start(s32[1,4096]{1,0:T(1,128)} %param.12) | copy-start | bytes 49156
  3.3 12.2 %copy-start.6 = (s32[32,256]{1,0:T(8,128)S(1)}, s32[32,256]{1,0:T(8,128)}, u32[]{:S(2)}) copy-start(s32[32,256]{1,0:T(8,128)} %param.11) | copy-start | bytes 98308
  4.1 27.3 %all-to-all-start = ((f32[16,16,512]{2,1,0:T(8,128)}), f32[16,16,512]{2,1,0:T(8,128)S(1)}, u32[]{:S(2)}, u32[]{:S(2)}) async-start(f32[16,16,512]{2,1,0:T(8,128)} %maximum_bitcast_fusion), calls=%async_computation | async-start | bytes 1048576 | tf_op jit(solution)/shard_map/all_to_all | solution.py:166
  31.4 0.8 %copy-start.2 = (f32[16,16,512]{2,1,0:T(8,128)}, f32[16,16,512]{2,1,0:T(8,128)S(1)}, u32[]{:S(2)}) copy-start(f32[16,16,512]{2,1,0:T(8,128)S(1)} %all-to-all-done.held_ref) | copy-start | bytes 1572868
  32.2 5.8 %copy-start.3 = (f32[32,256]{1,0:T(8,128)S(1)}, f32[32,256]{1,0:T(8,128)}, u32[]{:S(2)}) copy-start(f32[32,256]{1,0:T(8,128)} %param.10) | copy-start | bytes 98308
  32.2 5.8 %copy-start.4 = (f32[32,256]{1,0:T(8,128)S(1)}, f32[32,256]{1,0:T(8,128)}, u32[]{:S(2)}) copy-start(f32[32,256]{1,0:T(8,128)} %param.9) | copy-start | bytes 98308
  38.0 9.5 %copy-start.1 = (f32[16,32,256]{2,1,0:T(8,128)S(1)}, f32[16,32,256]{2,1,0:T(8,128)}, u32[]{:S(2)}) copy-start(f32[16,32,256]{2,1,0:T(8,128)} %shard_map.83) | copy-start | bytes 1572868
  39.1 8.4 %collective-permute-start = (f32[19,8,256]{2,1,0:T(8,128)S(1)}, f32[19,8,256]{2,1,0:T(8,128)S(1)}, u32[]{:S(2)}, u32[]{:S(2)}) collective-permute-start(f32[19,8,256]{2,1,0:T(8,128)S(1)} %get-tuple-element.9), channel_id=1, source_target_pairs={{0,1},{1,2},{2,3},{3,4},{4,5},{5,6},{6,7},{7,8},{8,9},{9,10},{10,1... | collective-permute-start | bytes 466952 | tf_op jit(solution)/shard_map/ppermute | solution.py:129
  40.4 7.0 %collective-permute-start.1 = (f32[19,8,256]{2,1,0:T(8,128)S(1)}, f32[19,8,256]{2,1,0:T(8,128)S(1)}, u32[]{:S(2)}, u32[]{:S(2)}) collective-permute-start(f32[19,8,256]{2,1,0:T(8,128)S(1)} %get-tuple-element.10), channel_id=1, source_target_pairs={{1,0},{2,1},{3,2},{4,3},{5,4},{6,5},{7,6},{8,7},{9,8},{10,9},{11,1... | collective-permute-start | bytes 466952 | tf_op jit(solution)/shard_map/ppermute | solution.py:130
  48.0 1.2 %collective-permute-start.2 = (f32[57,128]{1,0:T(8,128)S(1)}, f32[57,128]{1,0:T(8,128)S(1)}, u32[]{:S(2)}, u32[]{:S(2)}) collective-permute-start(f32[57,128]{1,0:T(8,128)S(1)} %reshape.107), channel_id=1, source_target_pairs={{0,16},{16,32},{32,48},{48,64},{64,80},{80,96},{96,112},{112,128},... | collective-permute-start | bytes 87560 | tf_op jit(solution)/shard_map/ppermute | solution.py:126
  48.2 3.6 %collective-permute-start.3 = (f32[57,128]{1,0:T(8,128)S(1)}, f32[57,128]{1,0:T(8,128)S(1)}, u32[]{:S(2)}, u32[]{:S(2)}) collective-permute-start(f32[57,128]{1,0:T(8,128)S(1)} %reshape.109), channel_id=1, source_target_pairs={{16,0},{32,16},{48,32},{64,48},{80,64},{96,80},{112,96},{128,112},... | collective-permute-start | bytes 87560 | tf_op jit(solution)/shard_map/ppermute | solution.py:127

commit v19 on v18

--- a/solution.py
+++ b/solution.py
@@ -7,7 +7,7 @@
 
 PASSES = 8
 CHUNK = 512
-SCATTER_CHUNK = 2048
+SCATTER_CHUNK = 4096
 
 
 def three_parts(x):

time: 64.6 us -> 64.3 us (level)
  no operation moved by 1% of the time
where the time goes in v19:
time: 64.3 us; the launch traced here: 64 us
  other arithmetic  18.2 us (28%)
  starting transfers between devices  15.8 us (25%)
  waiting for transfers between devices  14 us (22%)
  Pallas kernels  12.1 us (19%)
  local copies, waits for them, and re-layouts  3.67 us (6%)
    all_to_all x1, starting transfers between devices, body(): lax.all_to_all(held, 'lon', split_axis=0, concat_axis=0, tiled=True)  9.98 us
    sub x8, other arithmetic, one_pass(): centre + east_here * (field[:, 1:-1, 2:] - centre)  9.73 us
    all_to_all x1, waiting for transfers between devices, body(): lax.all_to_all(held, 'lon', split_axis=0, concat_axis=0, tiled=True)  8.01 us
    pallas_call x1, Pallas kernels, onehot_gather(): vmem_call(gather_kernel, shape, flops, 4 * (levels * slots + 2 * slots +...  6.65 us
    pallas_call x1, Pallas kernels, onehot_scatter(): pl.pallas_call(scatter_kernel, out_shape=shape, in_specs=[pl.BlockSpec(me...  5.44 us
    ppermute x1, starting transfers between devices, with_halo(): high = lax.ppermute(high, axis, backward)  3.9 us
    unnamed x2, other arithmetic  3.19 us
    ppermute x1, waiting for transfers between devices, with_halo(): low = lax.ppermute(low, axis, forward)  3.13 us
  transfers between devices with their start and end apart: 5, of which 4 were waited for; matrix products, arithmetic and copies ran while one was open for 5% of the time, Pallas kernels for 10%

profile of v19, /device:TPU:1, one launch (start us, length us, event | category | flops | bytes accessed | tf_op | source)
XLA Modules:
  0.0 64.0 jit_solution(8341738482820829103)
XLA Ops:
  0.0 0.0 copy-start
  0.0 1.6 %reduce.1 = f32[16,4096]{1,0:T(8,128)S(1)} reduce(f32[16,1,4096]{2,1,0:T(1,128)} %param.15, f32[]{:T(128)} %constant.52), dimensions={1}, to_apply=%param.15.reduce_sub_computation | reduce | bytes 524292 | tf_op args[7]
  1.6 1.6 %reduce = f32[16,4096]{1,0:T(8,128)S(1)} reduce(f32[16,1,4096]{2,1,0:T(1,128)} %param.14, f32[]{:T(128)} %constant.52), dimensions={1}, to_apply=%param.14.reduce_sub_computation | reduce | bytes 524292 | tf_op args[6]
  3.2 0.1 copy_bitcast_fusion
  3.3 0.0 copy-start.5
  3.3 0.0 copy-start.6
  3.3 0.9 %maximum_bitcast_fusion = f32[16,16,512]{2,1,0:T(8,128)} fusion(f32[16,16,256]{2,0,1:T(8,128)S(1)} %get-tuple-element.45, f32[16,16,256]{2,0,1:T(8,128)S(1)} %get-tuple-element.46), kind=kLoop, calls=%fused_computation.98 | loop fusion | flops 131072 | bytes 1048576 | tf_op jit(solution)/shard_map/transpose | solution.py:165
  4.1 10.0 %all-to-all-start = ((f32[16,16,512]{2,1,0:T(8,128)}), f32[16,16,512]{2,1,0:T(8,128)S(1)}, u32[]{:S(2)}, u32[]{:S(2)}) async-start(f32[16,16,512]{2,1,0:T(8,128)} %maximum_bitcast_fusion), calls=%async_computation | async-start | bytes 1048576 | tf_op jit(solution)/shard_map/all_to_all | solution.py:166
  14.1 0.0 copy-done.5
  14.1 0.7 %and_select_fusion.1 = (s32[1,4096]{1,0:T(1,128)}, s32[1,4096]{1,0:T(1,128)S(1)}) fusion(s32[1,4096]{1,0:T(1,128)S(1)} %copy-done.5), kind=kLoop, calls=%fused_computation.115 | loop fusion | flops 45056 | bytes 49152 | tf_op jit(solution)/shard_map/jit(remainder)/select_n | solution.py:168
  14.8 0.7 %and_select_fusion.2.rows_ref = s32[1,4096]{1,0:T(1,128)} fusion(s32[1,4096]{1,0:T(1,128)S(1)} %get-tuple-element.6, s32[1,4096]{1,0:T(1,128)S(1)} %copy-done.5), kind=kLoop, calls=%fused_computation.116 | loop fusion | flops 49152 | bytes 49152 | tf_op jit(solution)/shard_map/jit(floor_divide)/jit(_where)/select_n | solution.py:167
  15.4 0.0 copy-done.6
  15.4 0.6 fusion.82
  16.1 6.6 %shard_map.82.seen_ref = f32[16,4096]{1,0:T(8,128)} custom-call(f32[512,256]{1,0:T(8,128)} %bitcast.38, s32[1,4096]{1,0:T(1,128)} %and_select_fusion.2.rows_ref, s32[1,4096]{1,0:T(1,128)} %get-tuple-element.5.cols_ref), custom_call_target="tpu_custom_call" | custom-call | flops 3221225472 | bytes 819200 | tf_op jit(solution)/shard_map/pallas_call | solution.py:113
  22.7 0.0 copy-done
  22.7 0.1 broadcast_bitcast_fusion
  22.8 0.6 compare_select_fusion.usable_ref
  23.4 8.0 %all-to-all-done.held_ref = f32[16,16,512]{2,1,0:T(8,128)S(1)} async-done(((f32[16,16,512]{2,1,0:T(8,128)}), f32[16,16,512]{2,1,0:T(8,128)S(1)}, u32[]{:S(2)}, u32[]{:S(2)}) %all-to-all-start) | async-done | bytes 524320 | tf_op jit(solution)/shard_map/all_to_all | solution.py:166
  31.5 0.8 %copy-done.2 = f32[16,16,512]{2,1,0:T(8,128)} copy-done((f32[16,16,512]{2,1,0:T(8,128)}, f32[16,16,512]{2,1,0:T(8,128)S(1)}, u32[]{:S(2)}) %copy-start.2) | copy-done | bytes 524312
  32.2 5.4 %shard_map.83 = f32[16,32,256]{2,1,0:T(8,128)} custom-call(f32[16,16,512]{2,1,0:T(8,128)} %copy-done.2, f32[16,4096]{1,0:T(8,128)} %shard_map.82.seen_ref, f32[1,4096]{1,0:T(1,128)} %compare_select_fusion.usable_ref, s32[1,4096]{1,0:T(1,128)} %and_select_fusion.2.rows_ref, s32[1,4096]{1,0:T(1,128)} %get-tuple-element.5.cols_ref, ...), custom_call_target="tpu_custom_call" | custom-call | flops 3221225472 | bytes 1359872 | tf_op jit(solution)/shard_map/pallas_call | solution.py:95
  37.7 0.0 copy-done.3
  37.7 0.0 copy-done.4
  37.7 1.0 %pad_maximum_fusion.5 = (f32[19,8,256]{2,1,0:T(8,128)S(1)}, f32[19,8,256]{2,1,0:T(8,128)S(1)}) fusion(f32[1,32,256]{2,1,0:T(8,128)S(1)} %bitcast.31, f32[1,32,256]{2,1,0:T(8,128)S(1)} %bitcast.34, f32[1,32,256]{2,1,0:T(8,128)S(1)} %get-tuple-element.44, f32[16,32,256]{2,1,0:T(8,128)} %shard_map.83), kind=kLoop, calls=%fused_computation.104 | loop fusion | flops 233472 | bytes 933888 | tf_op jit(solution)/shard_map/slice | solution.py:122
  38.7 1.4 %collective-permute-start = (f32[19,8,256]{2,1,0:T(8,128)S(1)}, f32[19,8,256]{2,1,0:T(8,128)S(1)}, u32[]{:S(2)}, u32[]{:S(2)}) collective-permute-start(f32[19,8,256]{2,1,0:T(8,128)S(1)} %get-tuple-element.9), channel_id=1, source_target_pairs={{0,1},{1,2},{2,3},{3,4},{4,5},{5,6},{6,7},{7,8},{8,9},{9,10},{10,1... | collective-permute-start | bytes 466952 | tf_op jit(solution)/shard_map/ppermute | solution.py:129
  40.1 3.9 %collective-permute-start.1 = (f32[19,8,256]{2,1,0:T(8,128)S(1)}, f32[19,8,256]{2,1,0:T(8,128)S(1)}, u32[]{:S(2)}, u32[]{:S(2)}) collective-permute-start(f32[19,8,256]{2,1,0:T(8,128)S(1)} %get-tuple-element.10), channel_id=1, source_target_pairs={{1,0},{2,1},{3,2},{4,3},{5,4},{6,5},{7,6},{8,7},{9,8},{10,9},{11,1... | collective-permute-start | bytes 466952 | tf_op jit(solution)/shard_map/ppermute | solution.py:130
  44.0 3.1 %collective-permute-done = f32[19,8,256]{2,1,0:T(8,128)S(1)} collective-permute-done((f32[19,8,256]{2,1,0:T(8,128)S(1)}, f32[19,8,256]{2,1,0:T(8,128)S(1)}, u32[]{:S(2)}, u32[]{:S(2)}) %collective-permute-start) | collective-permute-done | bytes 155680 | tf_op jit(solution)/shard_map/ppermute | solution.py:129
  47.2 0.0 collective-permute-done.1
  47.2 0.1 pad_maximum_fusion.1
  47.2 0.2 fusion.65
  47.4 0.2 reshape.107
  47.7 0.0 collective-permute-start.2
  47.7 0.2 reshape.109
  47.9 0.5 collective-permute-start.3
  48.4 0.5 collective-permute-done.2
  48.9 0.3 reshape.108
  49.2 2.4 %collective-permute-done.3 = f32[57,128]{1,0:T(8,128)S(1)} collective-permute-done((f32[57,128]{1,0:T(8,128)S(1)}, f32[57,128]{1,0:T(8,128)S(1)}, u32[]{:S(2)}, u32[]{:S(2)}) %collective-permute-start.3) | collective-permute-done | bytes 29216 | tf_op jit(solution)/shard_map/ppermute | solution.py:127
  51.6 0.3 reshape.110
  51.8 0.6 pad_maximum_fusion
  52.4 0.1 fusion.64
  52.5 0.1 slice_multiply_fusion.2
  52.6 0.1 fusion.80
  52.7 0.1 fusion.78
  52.8 0.1 fusion.81
  52.9 0.1 fusion.79
  53.0 0.1 fusion.76
  53.1 0.1 fusion.77
  53.2 0.1 fusion.74
  53.3 0.1 fusion.75
  53.4 0.1 fusion.72
  53.5 0.1 fusion.73
  53.6 0.1 fusion.70
  53.7 0.1 fusion.71
  53.8 0.1 fusion.68
  53.9 0.1 fusion.69
  54.1 0.1 fusion.66
  54.1 0.1 fusion.67
  54.2 1.3 %fusion.17 = f32[16,46,270]{2,1,0:T(8,128)S(1)} fusion(f32[19,48,272]{2,1,0:T(8,128)S(1)} %pad_maximum_fusion, f32[46,270]{1,0:T(8,128)S(1)} %get-tuple-element.42, f32[46,270]{1,0:T(8,128)S(1)} %get-tuple-element.41, f32[46,270]{1,0:T(8,128)S(1)} %get-tuple-element.40, f32[46,270]{1,0:T(8,128)S(1)} %get-tuple-element.39), kind=kLoop, calls=%fused_computation.27 | loop fusion | flops 2384640 | bytes 4968000 | tf_op jit(solution)/shard_map/sub | solution.py:145
  55.5 1.3 %fusion.9 = f32[16,44,268]{2,1,0:T(8,128)S(1)} fusion(f32[16,46,270]{2,1,0:T(8,128)S(1)} %fusion.17, f32[44,268]{1,0:T(8,128)S(1)} %get-tuple-element.38, f32[44,268]{1,0:T(8,128)S(1)} %get-tuple-element.37, f32[44,268]{1,0:T(8,128)S(1)} %get-tuple-element.36, f32[44,268]{1,0:T(8,128)S(1)} %get-tuple-element.35), kind=kLoop, calls=%fused_computation.15 | loop fusion | flops 2264064 | bytes 4716800 | tf_op jit(solution)/shard_map/sub | solution.py:145
  56.8 1.3 %fusion.1 = f32[16,42,266]{2,1,0:T(8,128)S(1)} fusion(f32[16,44,268]{2,1,0:T(8,128)S(1)} %fusion.9, f32[42,266]{1,0:T(8,128)S(1)} %get-tuple-element.34, f32[42,266]{1,0:T(8,128)S(1)} %get-tuple-element.33, f32[42,266]{1,0:T(8,128)S(1)} %get-tuple-element.32, f32[42,266]{1,0:T(8,128)S(1)} %get-tuple-element.31), kind=kLoop, calls=%fused_computation.3 | loop fusion | flops 2145024 | bytes 4468800 | tf_op jit(solution)/shard_map/sub | solution.py:145
  58.2 1.1 %fusion.49 = f32[16,40,264]{2,1,0:T(8,128)S(1)} fusion(f32[16,42,266]{2,1,0:T(8,128)S(1)} %fusion.1, f32[40,264]{1,0:T(8,128)S(1)} %get-tuple-element.30, f32[40,264]{1,0:T(8,128)S(1)} %get-tuple-element.29, f32[40,264]{1,0:T(8,128)S(1)} %get-tuple-element.28, f32[40,264]{1,0:T(8,128)S(1)} %get-tuple-element.27), kind=kLoop, calls=%fused_computation.75 | loop fusion | flops 2027520 | bytes 4224000 | tf_op jit(solution)/shard_map/sub | solution.py:145
  59.3 1.1 %fusion.41 = f32[16,38,262]{2,1,0:T(8,128)S(1)} fusion(f32[16,40,264]{2,1,0:T(8,128)S(1)} %fusion.49, f32[38,262]{1,0:T(8,128)S(1)} %get-tuple-element.26, f32[38,262]{1,0:T(8,128)S(1)} %get-tuple-element.25, f32[38,262]{1,0:T(8,128)S(1)} %get-tuple-element.24, f32[38,262]{1,0:T(8,128)S(1)} %get-tuple-element.23), kind=kLoop, calls=%fused_computation.63 | loop fusion | flops 1911552 | bytes 3982400 | tf_op jit(solution)/shard_map/sub | solution.py:145
  60.4 1.1 %fusion.33 = f32[16,36,260]{2,1,0:T(8,128)S(1)} fusion(f32[16,38,262]{2,1,0:T(8,128)S(1)} %fusion.41, f32[36,260]{1,0:T(8,128)S(1)} %get-tuple-element.22, f32[36,260]{1,0:T(8,128)S(1)} %get-tuple-element.21, f32[36,260]{1,0:T(8,128)S(1)} %get-tuple-element.20, f32[36,260]{1,0:T(8,128)S(1)} %get-tuple-element.19), kind=kLoop, calls=%fused_computation.51 | loop fusion | flops 1797120 | bytes 3744000 | tf_op jit(solution)/shard_map/sub | solution.py:145
  61.5 1.1 %fusion.25 = f32[16,34,258]{2,1,0:T(8,128)S(1)} fusion(f32[16,36,260]{2,1,0:T(8,128)S(1)} %fusion.33, f32[34,258]{1,0:T(8,128)S(1)} %get-tuple-element.18, f32[34,258]{1,0:T(8,128)S(1)} %get-tuple-element.17, f32[34,258]{1,0:T(8,128)S(1)} %get-tuple-element.16, f32[34,258]{1,0:T(8,128)S(1)} %get-tuple-element.15), kind=kLoop, calls=%fused_computation.39 | loop fusion | flops 1684224 | bytes 3508800 | tf_op jit(solution)/shard_map/sub | solution.py:145
  62.6 1.4 %fusion.57 = f32[16,32,256]{2,1,0:T(8,128)} fusion(f32[16,34,258]{2,1,0:T(8,128)S(1)} %fusion.25, f32[32,256]{1,0:T(8,128)S(1)} %get-tuple-element.14, f32[32,256]{1,0:T(8,128)S(1)} %get-tuple-element.13, f32[32,256]{1,0:T(8,128)S(1)} %get-tuple-element.12, f32[32,256]{1,0:T(8,128)S(1)} %get-tuple-element.11), kind=kLoop, calls=%fused_computation.88 | loop fusion | flops 1572864 | bytes 3276800 | tf_op jit(solution)/shard_map/sub | solution.py:145
  (9 shorter events, 0.1 us)
Async XLA Ops:
  0.0 22.7 %copy-start = (s32[1,16]{1,0:T(1,128)S(1)}, s32[1,16]{1,0:T(1,128)}, u32[]{:S(2)}) copy-start(s32[1,16]{1,0:T(1,128)} %param.13) | copy-start | bytes 196
  3.3 10.9 %copy-start.5 = (s32[1,4096]{1,0:T(1,128)S(1)}, s32[1,4096]{1,0:T(1,128)}, u32[]{:S(2)}) copy-start(s32[1,4096]{1,0:T(1,128)} %param.12) | copy-start | bytes 49156
  3.3 12.2 %copy-start.6 = (s32[32,256]{1,0:T(8,128)S(1)}, s32[32,256]{1,0:T(8,128)}, u32[]{:S(2)}) copy-start(s32[32,256]{1,0:T(8,128)} %param.11) | copy-start | bytes 98308
  4.1 27.3 %all-to-all-start = ((f32[16,16,512]{2,1,0:T(8,128)}), f32[16,16,512]{2,1,0:T(8,128)S(1)}, u32[]{:S(2)}, u32[]{:S(2)}) async-start(f32[16,16,512]{2,1,0:T(8,128)} %maximum_bitcast_fusion), calls=%async_computation | async-start | bytes 1048576 | tf_op jit(solution)/shard_map/all_to_all | solution.py:166
  31.4 0.8 %copy-start.2 = (f32[16,16,512]{2,1,0:T(8,128)}, f32[16,16,512]{2,1,0:T(8,128)S(1)}, u32[]{:S(2)}) copy-start(f32[16,16,512]{2,1,0:T(8,128)S(1)} %all-to-all-done.held_ref) | copy-start | bytes 1572868
  32.2 5.4 %copy-start.3 = (f32[32,256]{1,0:T(8,128)S(1)}, f32[32,256]{1,0:T(8,128)}, u32[]{:S(2)}) copy-start(f32[32,256]{1,0:T(8,128)} %param.10) | copy-start | bytes 98308
  32.2 5.4 %copy-start.4 = (f32[32,256]{1,0:T(8,128)S(1)}, f32[32,256]{1,0:T(8,128)}, u32[]{:S(2)}) copy-start(f32[32,256]{1,0:T(8,128)} %param.9) | copy-start | bytes 98308
  37.7 9.5 %copy-start.1 = (f32[16,32,256]{2,1,0:T(8,128)S(1)}, f32[16,32,256]{2,1,0:T(8,128)}, u32[]{:S(2)}) copy-start(f32[16,32,256]{2,1,0:T(8,128)} %shard_map.83) | copy-start | bytes 1572868
  38.7 8.4 %collective-permute-start = (f32[19,8,256]{2,1,0:T(8,128)S(1)}, f32[19,8,256]{2,1,0:T(8,128)S(1)}, u32[]{:S(2)}, u32[]{:S(2)}) collective-permute-start(f32[19,8,256]{2,1,0:T(8,128)S(1)} %get-tuple-element.9), channel_id=1, source_target_pairs={{0,1},{1,2},{2,3},{3,4},{4,5},{5,6},{6,7},{7,8},{8,9},{9,10},{10,1... | collective-permute-start | bytes 466952 | tf_op jit(solution)/shard_map/ppermute | solution.py:129
  40.1 7.0 %collective-permute-start.1 = (f32[19,8,256]{2,1,0:T(8,128)S(1)}, f32[19,8,256]{2,1,0:T(8,128)S(1)}, u32[]{:S(2)}, u32[]{:S(2)}) collective-permute-start(f32[19,8,256]{2,1,0:T(8,128)S(1)} %get-tuple-element.10), channel_id=1, source_target_pairs={{1,0},{2,1},{3,2},{4,3},{5,4},{6,5},{7,6},{8,7},{9,8},{10,9},{11,1... | collective-permute-start | bytes 466952 | tf_op jit(solution)/shard_map/ppermute | solution.py:130
  47.7 1.2 %collective-permute-start.2 = (f32[57,128]{1,0:T(8,128)S(1)}, f32[57,128]{1,0:T(8,128)S(1)}, u32[]{:S(2)}, u32[]{:S(2)}) collective-permute-start(f32[57,128]{1,0:T(8,128)S(1)} %reshape.107), channel_id=1, source_target_pairs={{0,16},{16,32},{32,48},{48,64},{64,80},{80,96},{96,112},{112,128},... | collective-permute-start | bytes 87560 | tf_op jit(solution)/shard_map/ppermute | solution.py:126
  47.9 3.6 %collective-permute-start.3 = (f32[57,128]{1,0:T(8,128)S(1)}, f32[57,128]{1,0:T(8,128)S(1)}, u32[]{:S(2)}, u32[]{:S(2)}) collective-permute-start(f32[57,128]{1,0:T(8,128)S(1)} %reshape.109), channel_id=1, source_target_pairs={{16,0},{32,16},{48,32},{64,48},{80,64},{96,80},{112,96},{128,112},... | collective-permute-start | bytes 87560 | tf_op jit(solution)/shard_map/ppermute | solution.py:127

commit v20 on v18

--- a/solution.py
+++ b/solution.py
@@ -132,21 +132,16 @@
     return block
 
 
-def one_pass(field, east_face, north_face, offset):
+def one_pass(field, faces, offset):
     high, wide = field.shape[1], field.shape[2]
-    rows = slice(offset + 1, offset + high - 1)
-    cols = slice(offset + 1, offset + wide - 1)
+    window = faces[:, offset + 1 : offset + high - 1, offset + 1 : offset + wide - 1]
     centre = field[:, 1:-1, 1:-1]
-    east_here = east_face[rows, cols]
-    east_west = east_face[rows, offset : offset + wide - 2]
-    north_here = north_face[rows, cols]
-    north_south = north_face[offset : offset + high - 2, cols]
     return (
         centre
-        + east_here * (field[:, 1:-1, 2:] - centre)
-        - east_west * (centre - field[:, 1:-1, :-2])
-        + north_here * (field[:, 2:, 1:-1] - centre)
-        - north_south * (centre - field[:, :-2, 1:-1])
+        + window[0] * (field[:, 1:-1, 2:] - centre)
+        - window[1] * (centre - field[:, 1:-1, :-2])
+        + window[2] * (field[:, 2:, 1:-1] - centre)
+        - window[3] * (centre - field[:, :-2, 1:-1])
     )
 
 
@@ -183,8 +178,17 @@
     sea_rim = padded[0] * inside
     east_face = padded[1][:, :-1] * sea_rim[:, :-1] * sea_rim[:, 1:]
     north_face = padded[2][:-1, :] * sea_rim[:-1, :] * sea_rim[1:, :]
+    high, wide = padded.shape[1], padded.shape[2]
+    faces = jnp.stack(
+        [
+            jnp.pad(east_face, ((0, 0), (0, 1))),
+            jnp.pad(east_face, ((0, 0), (1, 0))),
+            jnp.pad(north_face, ((0, 1), (0, 0))),
+            jnp.pad(north_face, ((1, 0), (0, 0))),
+        ]
+    )
     for step_number in range(PASSES):
-        field = one_pass(field, east_face, north_face, step_number)
+        field = one_pass(field, faces, step_number)
     gradient = field
     return gradient
 

time: 64.6 us -> 65.9 us (1.020)
  local copies, waits for them, and re-layouts: 3.67 us -> 4.89 us
    mul x0 -> x32, local copies, waits for them, and re-layouts: none -> 2.63 us  [the longest x8 0.66 us: one_pass(): window[1] * (centre - field[:, 1:-1, :-2])]
    slice x16 -> x0, local copies, waits for them, and re-layouts: 1.5 us -> none  [the longest x8 0.77 us: one_pass(): north_here = north_face[rows, cols]]
where the time goes in v20:
time: 65.9 us; the launch traced here: 65.6 us
  other arithmetic  18.2 us (28%)
  starting transfers between devices  15.8 us (24%)
  waiting for transfers between devices  14 us (21%)
  Pallas kernels  12.4 us (19%)
  local copies, waits for them, and re-layouts  4.89 us (7%)
    all_to_all x1, starting transfers between devices, body(): lax.all_to_all(held, 'lon', split_axis=0, concat_axis=0, tiled=True)  9.98 us
    sub x8, other arithmetic, one_pass(): centre + window[0] * (field[:, 1:-1, 2:] - centre)  9.73 us
    all_to_all x1, waiting for transfers between devices, body(): lax.all_to_all(held, 'lon', split_axis=0, concat_axis=0, tiled=True)  8.02 us
    pallas_call x1, Pallas kernels, onehot_gather(): vmem_call(gather_kernel, shape, flops, 4 * (levels * slots + 2 * slots +...  6.65 us
    pallas_call x1, Pallas kernels, onehot_scatter(): pl.pallas_call(scatter_kernel, out_shape=shape, in_specs=[pl.BlockSpec(me...  5.72 us
    ppermute x1, starting transfers between devices, with_halo(): high = lax.ppermute(high, axis, backward)  3.9 us
    unnamed x2, other arithmetic  3.19 us
    ppermute x1, waiting for transfers between devices, with_halo(): low = lax.ppermute(low, axis, forward)  3.14 us
  transfers between devices with their start and end apart: 5, of which 4 were waited for; matrix products, arithmetic and copies ran while one was open for 5% of the time, Pallas kernels for 10%

profile of v20, /device:TPU:1, one launch (start us, length us, event | category | flops | bytes accessed | tf_op | source)
XLA Modules:
  0.0 65.6 jit_solution(9715509301833443340)
XLA Ops:
  0.0 1.6 %reduce = f32[16,4096]{1,0:T(8,128)S(1)} reduce(f32[16,1,4096]{2,1,0:T(1,128)} %param.14, f32[]{:T(128)} %constant.61), dimensions={1}, to_apply=%param.14.reduce_sub_computation | reduce | bytes 524292 | tf_op args[6]
  1.6 1.6 %reduce.1 = f32[16,4096]{1,0:T(8,128)S(1)} reduce(f32[16,1,4096]{2,1,0:T(1,128)} %param.15, f32[]{:T(128)} %constant.61), dimensions={1}, to_apply=%param.15.reduce_sub_computation | reduce | bytes 524292 | tf_op args[7]
  3.3 0.9 %maximum_bitcast_fusion = f32[16,16,512]{2,1,0:T(8,128)} fusion(f32[16,16,256]{2,0,1:T(8,128)S(1)} %get-tuple-element.17, f32[16,16,256]{2,0,1:T(8,128)S(1)} %get-tuple-element.18), kind=kLoop, calls=%fused_computation.98 | loop fusion | flops 131072 | bytes 1048576 | tf_op jit(solution)/shard_map/transpose | solution.py:160
  4.1 10.0 %all-to-all-start = ((f32[16,16,512]{2,1,0:T(8,128)}), f32[16,16,512]{2,1,0:T(8,128)S(1)}, u32[]{:S(2)}, u32[]{:S(2)}) async-start(f32[16,16,512]{2,1,0:T(8,128)} %maximum_bitcast_fusion), calls=%async_computation | async-start | bytes 1048576 | tf_op jit(solution)/shard_map/all_to_all | solution.py:161
  14.1 0.6 and_select_fusion.1
  14.8 0.7 %and_select_fusion.2.rows_ref = s32[1,4096]{1,0:T(1,128)} fusion(s32[1,4096]{1,0:T(1,128)S(1)} %get-tuple-element.6, s32[1,4096]{1,0:T(1,128)S(1)} %copy-done.5), kind=kLoop, calls=%fused_computation.132 | loop fusion | flops 49152 | bytes 49152 | tf_op jit(solution)/shard_map/jit(floor_divide)/jit(_where)/select_n | solution.py:162
  15.4 0.6 fusion.66
  16.1 6.7 %shard_map.82.seen_ref = f32[16,4096]{1,0:T(8,128)} custom-call(f32[512,256]{1,0:T(8,128)} %bitcast.110, s32[1,4096]{1,0:T(1,128)} %and_select_fusion.2.rows_ref, s32[1,4096]{1,0:T(1,128)} %get-tuple-element.5.cols_ref), custom_call_target="tpu_custom_call" | custom-call | flops 3221225472 | bytes 819200 | tf_op jit(solution)/shard_map/pallas_call | solution.py:113
  22.8 0.6 compare_select_fusion.usable_ref
  23.4 8.0 %all-to-all-done.held_ref = f32[16,16,512]{2,1,0:T(8,128)S(1)} async-done(((f32[16,16,512]{2,1,0:T(8,128)}), f32[16,16,512]{2,1,0:T(8,128)S(1)}, u32[]{:S(2)}, u32[]{:S(2)}) %all-to-all-start) | async-done | bytes 524320 | tf_op jit(solution)/shard_map/all_to_all | solution.py:161
  31.5 0.8 %copy-done.2 = f32[16,16,512]{2,1,0:T(8,128)} copy-done((f32[16,16,512]{2,1,0:T(8,128)}, f32[16,16,512]{2,1,0:T(8,128)S(1)}, u32[]{:S(2)}) %copy-start.2) | copy-done | bytes 524312
  32.2 5.7 %shard_map.83 = f32[16,32,256]{2,1,0:T(8,128)} custom-call(f32[16,16,512]{2,1,0:T(8,128)} %copy-done.2, f32[16,4096]{1,0:T(8,128)} %shard_map.82.seen_ref, f32[1,4096]{1,0:T(1,128)} %compare_select_fusion.usable_ref, s32[1,4096]{1,0:T(1,128)} %and_select_fusion.2.rows_ref, s32[1,4096]{1,0:T(1,128)} %get-tuple-element.5.cols_ref, ...), custom_call_target="tpu_custom_call" | custom-call | flops 3221225472 | bytes 1359872 | tf_op jit(solution)/shard_map/pallas_call | solution.py:95
  38.0 1.0 %pad_maximum_fusion.5 = (f32[19,8,256]{2,1,0:T(8,128)S(1)}, f32[19,8,256]{2,1,0:T(8,128)S(1)}) fusion(f32[1,32,256]{2,1,0:T(8,128)S(1)} %bitcast.103, f32[1,32,256]{2,1,0:T(8,128)S(1)} %bitcast.106, f32[1,32,256]{2,1,0:T(8,128)S(1)} %get-tuple-element.16, f32[16,32,256]{2,1,0:T(8,128)} %shard_map.83), kind=kLoop, calls=%fused_computation.104 | loop fusion | flops 233472 | bytes 933888 | tf_op jit(solution)/shard_map/slice | solution.py:122
  39.0 1.4 %collective-permute-start = (f32[19,8,256]{2,1,0:T(8,128)S(1)}, f32[19,8,256]{2,1,0:T(8,128)S(1)}, u32[]{:S(2)}, u32[]{:S(2)}) collective-permute-start(f32[19,8,256]{2,1,0:T(8,128)S(1)} %get-tuple-element.9), channel_id=1, source_target_pairs={{0,1},{1,2},{2,3},{3,4},{4,5},{5,6},{6,7},{7,8},{8,9},{9,10},{10,1... | collective-permute-start | bytes 466952 | tf_op jit(solution)/shard_map/ppermute | solution.py:129
  40.4 3.9 %collective-permute-start.1 = (f32[19,8,256]{2,1,0:T(8,128)S(1)}, f32[19,8,256]{2,1,0:T(8,128)S(1)}, u32[]{:S(2)}, u32[]{:S(2)}) collective-permute-start(f32[19,8,256]{2,1,0:T(8,128)S(1)} %get-tuple-element.10), channel_id=1, source_target_pairs={{1,0},{2,1},{3,2},{4,3},{5,4},{6,5},{7,6},{8,7},{9,8},{10,9},{11,1... | collective-permute-start | bytes 466952 | tf_op jit(solution)/shard_map/ppermute | solution.py:130
  44.3 3.1 %collective-permute-done = f32[19,8,256]{2,1,0:T(8,128)S(1)} collective-permute-done((f32[19,8,256]{2,1,0:T(8,128)S(1)}, f32[19,8,256]{2,1,0:T(8,128)S(1)}, u32[]{:S(2)}, u32[]{:S(2)}) %collective-permute-start) | collective-permute-done | bytes 155680 | tf_op jit(solution)/shard_map/ppermute | solution.py:129
  47.5 0.2 fusion.65
  47.7 0.2 reshape.75
  48.0 0.2 reshape.77
  48.2 0.5 collective-permute-start.3
  48.7 0.5 collective-permute-done.2
  49.2 0.3 reshape.76
  49.5 2.4 %collective-permute-done.3 = f32[57,128]{1,0:T(8,128)S(1)} collective-permute-done((f32[57,128]{1,0:T(8,128)S(1)}, f32[57,128]{1,0:T(8,128)S(1)}, u32[]{:S(2)}, u32[]{:S(2)}) %collective-permute-start.3) | collective-permute-done | bytes 29216 | tf_op jit(solution)/shard_map/ppermute | solution.py:127
  51.8 0.3 reshape.78
  52.1 0.6 pad_maximum_fusion
  52.8 0.1 slice_multiply_fusion.2
  52.9 0.1 pad_bitcast_fusion.3
  53.0 0.1 slice_bitcast_fusion.11
  53.1 0.1 slice_bitcast_fusion.6
  53.2 0.1 slice_bitcast_fusion.12
  53.3 0.1 slice_bitcast_fusion.7
  53.4 0.1 slice_bitcast_fusion.8
  53.5 0.1 slice_bitcast_fusion.4
  53.5 0.1 slice_bitcast_fusion.9
  53.6 0.1 slice_bitcast_fusion.5
  53.7 0.1 slice_bitcast_fusion.2
  53.8 0.1 slice_bitcast_fusion.3
  53.9 0.1 slice_bitcast_fusion
  54.0 0.1 slice_bitcast_fusion.1
  54.1 0.1 slice_bitcast_fusion.29
  54.2 0.1 slice_bitcast_fusion.30
  54.3 0.1 slice_bitcast_fusion.27
  54.4 0.1 slice_bitcast_fusion.28
  54.4 0.1 slice_bitcast_fusion.25
  54.5 0.1 slice_bitcast_fusion.26
  54.6 0.1 slice_bitcast_fusion.23
  54.7 0.1 slice_bitcast_fusion.24
  54.8 0.1 slice_bitcast_fusion.21
  54.9 0.1 slice_bitcast_fusion.22
  55.0 0.1 slice_bitcast_fusion.19
  55.1 0.1 slice_bitcast_fusion.20
  55.1 0.1 slice_bitcast_fusion.17
  55.2 0.1 slice_bitcast_fusion.18
  55.3 0.1 slice_bitcast_fusion.15
  55.4 0.1 slice_bitcast_fusion.16
  55.7 0.1 slice_bitcast_fusion.32
  55.8 1.3 %fusion.17 = f32[16,46,270]{2,1,0:T(8,128)S(1)} fusion(f32[19,48,272]{2,1,0:T(8,128)S(1)} %pad_maximum_fusion, f32[46,270]{1,0:T(8,128)S(1)} %slice_bitcast_fusion.8, f32[46,270]{1,0:T(8,128)S(1)} %slice_bitcast_fusion.9, f32[46,270]{1,0:T(8,128)S(1)} %slice_bitcast_fusion.11, f32[46,270]{1,0:T(8,128)S(1)} %slice_bitcast_fusion.12), kind=kLoop, calls=%fused_computation.27 | loop fusion | flops 2384640 | bytes 4968000 | tf_op jit(solution)/shard_map/sub | solution.py:140
  57.1 1.3 %fusion.9 = f32[16,44,268]{2,1,0:T(8,128)S(1)} fusion(f32[16,46,270]{2,1,0:T(8,128)S(1)} %fusion.17, f32[44,268]{1,0:T(8,128)S(1)} %slice_bitcast_fusion.4, f32[44,268]{1,0:T(8,128)S(1)} %slice_bitcast_fusion.5, f32[44,268]{1,0:T(8,128)S(1)} %slice_bitcast_fusion.6, f32[44,268]{1,0:T(8,128)S(1)} %slice_bitcast_fusion.7), kind=kLoop, calls=%fused_computation.15 | loop fusion | flops 2264064 | bytes 4716800 | tf_op jit(solution)/shard_map/sub | solution.py:140
  58.4 1.3 %fusion.1 = f32[16,42,266]{2,1,0:T(8,128)S(1)} fusion(f32[16,44,268]{2,1,0:T(8,128)S(1)} %fusion.9, f32[42,266]{1,0:T(8,128)S(1)} %slice_bitcast_fusion, f32[42,266]{1,0:T(8,128)S(1)} %slice_bitcast_fusion.1, f32[42,266]{1,0:T(8,128)S(1)} %slice_bitcast_fusion.2, f32[42,266]{1,0:T(8,128)S(1)} %slice_bitcast_fusion.3), kind=kLoop, calls=%fused_computation.3 | loop fusion | flops 2145024 | bytes 4468800 | tf_op jit(solution)/shard_map/sub | solution.py:140
  59.7 1.1 %fusion.49 = f32[16,40,264]{2,1,0:T(8,128)S(1)} fusion(f32[16,42,266]{2,1,0:T(8,128)S(1)} %fusion.1, f32[40,264]{1,0:T(8,128)S(1)} %slice_bitcast_fusion.27, f32[40,264]{1,0:T(8,128)S(1)} %slice_bitcast_fusion.28, f32[40,264]{1,0:T(8,128)S(1)} %slice_bitcast_fusion.29, f32[40,264]{1,0:T(8,128)S(1)} %slice_bitcast_fusion.30), kind=kLoop, calls=%fused_computation.75 | loop fusion | flops 2027520 | bytes 4224000 | tf_op jit(solution)/shard_map/sub | solution.py:140
  60.8 1.1 %fusion.41 = f32[16,38,262]{2,1,0:T(8,128)S(1)} fusion(f32[16,40,264]{2,1,0:T(8,128)S(1)} %fusion.49, f32[38,262]{1,0:T(8,128)S(1)} %slice_bitcast_fusion.23, f32[38,262]{1,0:T(8,128)S(1)} %slice_bitcast_fusion.24, f32[38,262]{1,0:T(8,128)S(1)} %slice_bitcast_fusion.25, f32[38,262]{1,0:T(8,128)S(1)} %slice_bitcast_fusion.26), kind=kLoop, calls=%fused_computation.63 | loop fusion | flops 1911552 | bytes 3982400 | tf_op jit(solution)/shard_map/sub | solution.py:140
  62.0 1.1 %fusion.33 = f32[16,36,260]{2,1,0:T(8,128)S(1)} fusion(f32[16,38,262]{2,1,0:T(8,128)S(1)} %fusion.41, f32[36,260]{1,0:T(8,128)S(1)} %slice_bitcast_fusion.19, f32[36,260]{1,0:T(8,128)S(1)} %slice_bitcast_fusion.20, f32[36,260]{1,0:T(8,128)S(1)} %slice_bitcast_fusion.21, f32[36,260]{1,0:T(8,128)S(1)} %slice_bitcast_fusion.22), kind=kLoop, calls=%fused_computation.51 | loop fusion | flops 1797120 | bytes 3744000 | tf_op jit(solution)/shard_map/sub | solution.py:140
  63.1 1.1 %fusion.25 = f32[16,34,258]{2,1,0:T(8,128)S(1)} fusion(f32[16,36,260]{2,1,0:T(8,128)S(1)} %fusion.33, f32[34,258]{1,0:T(8,128)S(1)} %slice_bitcast_fusion.15, f32[34,258]{1,0:T(8,128)S(1)} %slice_bitcast_fusion.16, f32[34,258]{1,0:T(8,128)S(1)} %slice_bitcast_fusion.17, f32[34,258]{1,0:T(8,128)S(1)} %slice_bitcast_fusion.18), kind=kLoop, calls=%fused_computation.39 | loop fusion | flops 1684224 | bytes 3508800 | tf_op jit(solution)/shard_map/sub | solution.py:140
  64.2 1.4 %fusion.57 = f32[16,32,256]{2,1,0:T(8,128)} fusion(f32[16,34,258]{2,1,0:T(8,128)S(1)} %fusion.25, f32[32,256]{1,0:T(8,128)S(1)} %slice_bitcast_fusion.31, f32[32,256]{1,0:T(8,128)S(1)} %slice_bitcast_fusion.32, f32[32,256]{1,0:T(8,128)S(1)} %slice_bitcast_fusion.33, f32[32,256]{1,0:T(8,128)S(1)} %slice_bitcast_fusion.34), kind=kLoop, calls=%fused_computation.88 | loop fusion | flops 1572864 | bytes 3276800 | tf_op jit(solution)/shard_map/sub | solution.py:140
  (27 shorter events, 0.6 us)
Async XLA Ops:
  0.0 22.7 %copy-start = (s32[1,16]{1,0:T(1,128)S(1)}, s32[1,16]{1,0:T(1,128)}, u32[]{:S(2)}) copy-start(s32[1,16]{1,0:T(1,128)} %param.13) | copy-start | bytes 196
  3.3 10.9 %copy-start.5 = (s32[1,4096]{1,0:T(1,128)S(1)}, s32[1,4096]{1,0:T(1,128)}, u32[]{:S(2)}) copy-start(s32[1,4096]{1,0:T(1,128)} %param.12) | copy-start | bytes 49156
  3.3 12.2 %copy-start.6 = (s32[32,256]{1,0:T(8,128)S(1)}, s32[32,256]{1,0:T(8,128)}, u32[]{:S(2)}) copy-start(s32[32,256]{1,0:T(8,128)} %param.11) | copy-start | bytes 98308
  4.1 27.3 %all-to-all-start = ((f32[16,16,512]{2,1,0:T(8,128)}), f32[16,16,512]{2,1,0:T(8,128)S(1)}, u32[]{:S(2)}, u32[]{:S(2)}) async-start(f32[16,16,512]{2,1,0:T(8,128)} %maximum_bitcast_fusion), calls=%async_computation | async-start | bytes 1048576 | tf_op jit(solution)/shard_map/all_to_all | solution.py:161
  31.4 0.8 %copy-start.2 = (f32[16,16,512]{2,1,0:T(8,128)}, f32[16,16,512]{2,1,0:T(8,128)S(1)}, u32[]{:S(2)}) copy-start(f32[16,16,512]{2,1,0:T(8,128)S(1)} %all-to-all-done.held_ref) | copy-start | bytes 1572868
  32.2 5.7 %copy-start.3 = (f32[32,256]{1,0:T(8,128)S(1)}, f32[32,256]{1,0:T(8,128)}, u32[]{:S(2)}) copy-start(f32[32,256]{1,0:T(8,128)} %param.10) | copy-start | bytes 98308
  32.2 5.7 %copy-start.4 = (f32[32,256]{1,0:T(8,128)S(1)}, f32[32,256]{1,0:T(8,128)}, u32[]{:S(2)}) copy-start(f32[32,256]{1,0:T(8,128)} %param.9) | copy-start | bytes 98308
  38.0 9.5 %copy-start.1 = (f32[16,32,256]{2,1,0:T(8,128)S(1)}, f32[16,32,256]{2,1,0:T(8,128)}, u32[]{:S(2)}) copy-start(f32[16,32,256]{2,1,0:T(8,128)} %shard_map.83) | copy-start | bytes 1572868
  39.0 8.4 %collective-permute-start = (f32[19,8,256]{2,1,0:T(8,128)S(1)}, f32[19,8,256]{2,1,0:T(8,128)S(1)}, u32[]{:S(2)}, u32[]{:S(2)}) collective-permute-start(f32[19,8,256]{2,1,0:T(8,128)S(1)} %get-tuple-element.9), channel_id=1, source_target_pairs={{0,1},{1,2},{2,3},{3,4},{4,5},{5,6},{6,7},{7,8},{8,9},{9,10},{10,1... | collective-permute-start | bytes 466952 | tf_op jit(solution)/shard_map/ppermute | solution.py:129
  40.4 7.0 %collective-permute-start.1 = (f32[19,8,256]{2,1,0:T(8,128)S(1)}, f32[19,8,256]{2,1,0:T(8,128)S(1)}, u32[]{:S(2)}, u32[]{:S(2)}) collective-permute-start(f32[19,8,256]{2,1,0:T(8,128)S(1)} %get-tuple-element.10), channel_id=1, source_target_pairs={{1,0},{2,1},{3,2},{4,3},{5,4},{6,5},{7,6},{8,7},{9,8},{10,9},{11,1... | collective-permute-start | bytes 466952 | tf_op jit(solution)/shard_map/ppermute | solution.py:130
  47.9 1.2 %collective-permute-start.2 = (f32[57,128]{1,0:T(8,128)S(1)}, f32[57,128]{1,0:T(8,128)S(1)}, u32[]{:S(2)}, u32[]{:S(2)}) collective-permute-start(f32[57,128]{1,0:T(8,128)S(1)} %reshape.75), channel_id=1, source_target_pairs={{0,16},{16,32},{32,48},{48,64},{64,80},{80,96},{96,112},{112,128},... | collective-permute-start | bytes 87560 | tf_op jit(solution)/shard_map/ppermute | solution.py:126
  48.2 3.6 %collective-permute-start.3 = (f32[57,128]{1,0:T(8,128)S(1)}, f32[57,128]{1,0:T(8,128)S(1)}, u32[]{:S(2)}, u32[]{:S(2)}) collective-permute-start(f32[57,128]{1,0:T(8,128)S(1)} %reshape.77), channel_id=1, source_target_pairs={{16,0},{32,16},{48,32},{64,48},{80,64},{96,80},{112,96},{128,112},... | collective-permute-start | bytes 87560 | tf_op jit(solution)/shard_map/ppermute | solution.py:127
